TPU v7x, 32 devices: a whole 2x2x4 slice. The times are simulated.
32 devices in a mesh: groups: 2 (over y), seq: 4 (over z), tensor: 4 (over x, core).
Axes of the slice: x: 2, y: 2, z: 4, core: 2. Of those that a mesh axis runs over, the one named last changes fastest.
Arguments:
- x_in: bfloat16 [4096, 5120], P(('groups', 'seq'), 'tensor'), parts along dimension 0, may hold values from -6 to 6
- z_gate: bfloat16 [4096, 5120], P(('groups', 'seq'), 'tensor'), parts along dimension 0, may hold values from -32 to 32
- bc_in: bfloat16 [4096, 256], P(('groups', 'seq')), parts along dimension 0, may hold values from -6 to 6
- step_size: float32 [80, 4096], P('tensor', ('groups', 'seq')), parts along dimension 1, may hold values from 0 to 0.4
- log_keep: float32 [80, 4096], P('tensor', ('groups', 'seq')), parts along dimension 1, may hold values from -1 to 0
- skip_gain: float32 [80], P('tensor'), may hold values from 0.5 to 2
- conv_x: bfloat16 [4, 5120], P(None, 'tensor'), may hold values from -3 to 3
- conv_bc: bfloat16 [4, 256], replicated, may hold values from -3 to 3
- norm_gain: float32 [5120], P('tensor'), may hold values from 0.1 to 1.9
- seg_ends: int32 [1024], P(('groups', 'seq')), parts along dimension 0, may hold values from 0 to 2047, as said below
- pool_query: bfloat16 [320, 5120], P(('groups', 'seq'), 'tensor'), parts along dimension 0, may hold values from -64 to 64
- pool_start: int32 [320], P(('groups', 'seq')), parts along dimension 0, may hold values from 0 to 255, as said below
- pool_stop: int32 [320], P(('groups', 'seq')), parts along dimension 0, may hold values from 64 to 512
Outputs:
- mixed_seq: bfloat16 [4096, 5120], P(('groups', 'seq'), 'tensor'), parts along dimension 0
- pooled: float32 [320, 5120], P(('groups', 'seq'), 'tensor'), parts along dimension 0
There are 2 independent parts, one for each index of `groups`. A program takes and returns all parts, laid end to end along the dimension named above; an argument that names none is the same for every part. Nothing has to cross between parts.
Inputs may be any that keep to these rules, and one draw needn't show every extreme that they name: The tokens fall into blocks of 512; block b holds exactly the 128 segment ends seg_ends[b * 128] to seg_ends[(b + 1) * 128 - 1], strictly increasing. pool_start < pool_stop for every pooled row.
All inputs are finite; a program needn't handle non-finite values.
Results may differ from a plain program's by a relative error of at most 0.039.
Values may be sent and summed in bfloat16 or wider, within the bound.
No kernel may reach another device: no remote copies, remote signals or barrier semaphores. Data moves between devices by JAX's collectives and lax.ppermute only.
A program may use at most 64 MiB of HBM per device.

v0:
```python
import math

import jax
import jax.numpy as jnp
from jax import lax
from jax.sharding import PartitionSpec as P

STRETCH = 256
POOL_HEADS = 32


EPSILON = 1e-05
MASKED = -1e30


def passed_along(value, axis, steps):
    count = lax.axis_size(axis)
    leading, last = (max(0, -steps), min(count, count - steps))
    return lax.ppermute(value, axis, [(source, source + steps) for source in range(leading, last)])


def prefix(part, axis, combine, identity):
    place = lax.axis_index(axis)
    gathered = jax.tree.map(lambda a: lax.all_gather(a, axis), part)
    state = jax.tree.map(lambda a, e: jnp.zeros_like(a) + jnp.asarray(e, a.dtype), part, identity)

    def one(lap, state):
        return combine(
            state, jax.tree.map(lambda a: lax.dynamic_index_in_dim(a, lap, 0, False), gathered)
        )

    return lax.fori_loop(0, place, one, state)


def silu_act(values):
    return values / (1.0 + jnp.exp(-values))


def causal_conv(before, current, weights):
    kernel_width = weights.shape[0]
    length = current.shape[0]
    padded = jnp.concatenate([before, current], axis=0)
    summed = jnp.zeros(current.shape, jnp.float32)
    for offset in range(kernel_width):
        summed = summed + padded[offset : offset + length].astype(jnp.float32) * weights[
            offset
        ].astype(jnp.float32)
    return silu_act(summed).astype(jnp.bfloat16)


def stretch_local(x_block, b_block, c_block, step_block, keep_block):
    block_len = x_block.shape[0]
    cumul_keep = jnp.cumsum(keep_block, axis=1)
    lower_mask = lax.broadcasted_iota(jnp.int32, (block_len, block_len), 0) >= lax.broadcasted_iota(
        jnp.int32, (block_len, block_len), 1
    )
    inner_prod = jnp.einsum("is,js->ij", c_block, b_block, preferred_element_type=jnp.float32)
    spread = cumul_keep[:, :, None] - cumul_keep[:, None, :]
    decay_mask = jnp.where(lower_mask[None], jnp.exp(jnp.where(lower_mask[None], spread, 0.0)), 0.0)
    mixing = (decay_mask * inner_prod[None] * step_block[:, None, :]).astype(jnp.bfloat16)
    intra_part = jnp.einsum("hij,jhp->ihp", mixing, x_block, preferred_element_type=jnp.float32)
    tail_weight = jnp.exp(cumul_keep[:, -1:] - cumul_keep) * step_block
    weighted = (tail_weight.T[:, :, None] * x_block.astype(jnp.float32)).astype(jnp.bfloat16)
    stretch_state = jnp.einsum("jhp,js->hps", weighted, b_block, preferred_element_type=jnp.float32)
    return (intra_part, stretch_state, cumul_keep)


def combine(earlier, later):
    return (earlier[0] * jnp.exp(later[1])[:, None, None] + later[0], earlier[1] + later[1])


def read_state(c_block, state_in):
    state_high = state_in.astype(jnp.bfloat16)
    state_low = (state_in - state_high.astype(jnp.float32)).astype(jnp.bfloat16)
    high_part = jnp.einsum("is,hps->ihp", c_block, state_high, preferred_element_type=jnp.float32)
    low_part = jnp.einsum("is,hps->ihp", c_block, state_low, preferred_element_type=jnp.float32)
    return high_part + low_part


def local(
    x_in,
    z_gate,
    bc_in,
    step_size,
    log_keep,
    skip_gain,
    conv_x,
    conv_bc,
    norm_gain,
    seg_ends,
    pool_query,
    pool_start,
    pool_stop,
):
    tok_rows = x_in.shape[0]
    channels = x_in.shape[1]
    heads_local = step_size.shape[0]
    head_width = channels // heads_local
    state_width = bc_in.shape[1] // 2
    rim_rows = conv_x.shape[0] - 1
    edge_rows = jnp.concatenate([x_in[tok_rows - rim_rows :], bc_in[tok_rows - rim_rows :]], axis=1)
    before = passed_along(edge_rows, "seq", 1)
    x_conv = causal_conv(before[:, :channels], x_in, conv_x)
    bc_conv = causal_conv(before[:, channels:], bc_in, conv_bc)
    b_mat = bc_conv[:, :state_width]
    c_mat = bc_conv[:, state_width:]
    x_heads = x_conv.reshape(tok_rows, heads_local, head_width)
    stretch_count = tok_rows // STRETCH
    entry_state = jnp.zeros((heads_local, head_width, state_width), jnp.float32)
    decay_total = jnp.zeros((heads_local,), jnp.float32)
    saved_parts = []
    for block_index in range(stretch_count):
        first_row = block_index * STRETCH
        last_row = first_row + STRETCH
        intra_part, stretch_state, cumul_keep = stretch_local(
            x_heads[first_row:last_row],
            b_mat[first_row:last_row],
            c_mat[first_row:last_row],
            step_size[:, first_row:last_row],
            log_keep[:, first_row:last_row],
        )
        saved_parts.append((intra_part, cumul_keep, entry_state, decay_total))
        entry_state = jnp.exp(cumul_keep[:, -1])[:, None, None] * entry_state + stretch_state
        decay_total = decay_total + cumul_keep[:, -1]
    incoming, unused = prefix(
        (entry_state, decay_total),
        "seq",
        combine,
        (jnp.zeros_like(entry_state), jnp.zeros_like(decay_total)),
    )
    pieces_out = []
    for block_index in range(stretch_count):
        intra_part, cumul_keep, entry_part, decay_part = saved_parts[block_index]
        first_row = block_index * STRETCH
        state_in = entry_part + jnp.exp(decay_part)[:, None, None] * incoming
        from_state = read_state(c_mat[first_row : first_row + STRETCH], state_in)
        pieces_out.append(intra_part + jnp.exp(cumul_keep).T[:, :, None] * from_state)
    ssd_out = jnp.concatenate(pieces_out, axis=0) + skip_gain[None, :, None] * x_heads.astype(
        jnp.float32
    )
    gated = ssd_out.reshape(tok_rows, channels) * silu_act(z_gate.astype(jnp.float32))
    square_sum = lax.psum(jnp.sum(gated * gated, axis=1), "tensor")
    width_all = channels * lax.axis_size("tensor")
    mixed_seq = (
        gated * lax.rsqrt(square_sum / width_all + EPSILON)[:, None] * norm_gain[None, :]
    ).astype(jnp.bfloat16)
    local_ends = seg_ends - lax.axis_index("seq") * tok_rows
    summaries = jnp.take(mixed_seq, local_ends, axis=0)
    pool_heads_local = POOL_HEADS // lax.axis_size("tensor")
    pool_width = channels // pool_heads_local
    scale_factor = 1.0 / math.sqrt(pool_width)
    pools_local = pool_query.shape[0]
    queries = pool_query.reshape(pools_local, pool_heads_local, pool_width)
    piece = lax.all_gather(summaries, "seq", axis=0, tiled=True)
    peak = jnp.full((pool_heads_local, pools_local), MASKED, jnp.float32)
    numer = jnp.zeros((pools_local, pool_heads_local, pool_width), jnp.float32)
    count = piece.shape[0]
    seg_index = lax.iota(jnp.int32, count)
    inside = (seg_index[None, :] >= pool_start[:, None]) & (seg_index[None, :] < pool_stop[:, None])
    keys_block = piece.reshape(count, pool_heads_local, pool_width)
    logits = (
        jnp.einsum("pad,rad->apr", queries, keys_block, preferred_element_type=jnp.float32)
        * scale_factor
    )
    logits = jnp.where(inside[None], logits, MASKED)
    new_peak = jnp.maximum(peak, jnp.max(logits, axis=2))
    expo = jnp.where(inside[None], jnp.exp(logits - new_peak[:, :, None]), 0.0)
    rescale = jnp.exp(peak - new_peak)
    denom = jnp.sum(expo, axis=2)
    numer = numer * rescale.T[:, :, None] + jnp.einsum(
        "apr,rad->pad", expo.astype(jnp.bfloat16), keys_block, preferred_element_type=jnp.float32
    )
    peak, denom, numer = (new_peak, denom, numer)
    pooled = (numer / denom.T[:, :, None]).reshape(pools_local, channels)
    return (mixed_seq, pooled)


def solution(mesh):
    in_specs = (
        P(("groups", "seq"), "tensor"),
        P(("groups", "seq"), "tensor"),
        P(("groups", "seq"), None),
        P("tensor", ("groups", "seq")),
        P("tensor", ("groups", "seq")),
        P("tensor"),
        P(None, "tensor"),
        P(),
        P("tensor"),
        P(("groups", "seq")),
        P(("groups", "seq"), "tensor"),
        P(("groups", "seq")),
        P(("groups", "seq")),
    )
    out_specs = (P(("groups", "seq"), "tensor"), P(("groups", "seq"), "tensor"))
    return jax.shard_map(local, mesh=mesh, in_specs=in_specs, out_specs=out_specs, check_vma=False)
```

profile of v0, /device:TPU:0, one launch (start us, length us, event | category | flops | bytes accessed | tf_op | source)
XLA Modules:
  0.0 157.4 jit_solution(5044019205403970520)
XLA Ops:
  7.2 0.7 slice.120
  7.9 0.7 slice.121
  8.7 5.0 %collective-permute-start = (bf16[3,1536]{1,0:T(4,128)(2,1)S(1)}, bf16[3,1536]{1,0:T(4,128)(2,1)S(1)}, u32[]{:S(2)}, u32[]{:S(2)}) collective-permute-start(bf16[3,1536]{1,0:T(4,128)(2,1)S(1)} %pad_maximum_fusion.2), channel_id=1, source_target_pairs={{0,4},{4,8},{8,12},{1,5},{5,9},{9,13},{2,6},{6,10},{10,14},{3,7},{... | collective-permute-start | bytes 27656 | tf_op jit(solution)/shard_map/ppermute | solution.py:19
  13.6 0.8 fusion.71
  16.3 0.8 slice_convert_fusion.3
  17.2 0.8 slice_reduce_fusion.2
  18.5 1.5 fusion.70
  19.9 0.9 convert_reduce_fusion.3
  21.5 4.0 %divide_convert_fusion = bf16[512,1280]{1,0:T(8,128)(2,1)S(1)} fusion(bf16[512,1280]{1,0:T(8,128)(2,1)} %param.15, bf16[3,1280]{1,0:T(4,128)(2,1)S(1)} %slice.158, f32[1280]{0:T(1024)S(1)} %get-tuple-element.52, f32[1280]{0:T(1024)S(1)} %get-tuple-element.53, f32[1280]{0:T(1024)S(1)} %get-tuple-element.51, f32[1280]{0:T(1024)S(1)} %get-tuple-element.50), kind=kLoop, calls=%fused_computation.25 | loop fusion | flops 15728640 | bytes 2649600 | tf_op jit(solution)/shard_map/convert_element_type | solution.py:48
  26.1 1.9 %divide_convert_fusion.1 = bf16[512,256]{1,0:T(8,128)(2,1)S(1)} fusion(bf16[512,256]{1,0:T(8,128)(2,1)} %param.17, bf16[3,256]{1,0:T(4,128)(2,1)S(1)} %slice.165, f32[256]{0:T(256)S(1)} %bitcast.90, f32[256]{0:T(256)S(1)} %bitcast.91, f32[256]{0:T(256)S(1)} %bitcast.89, f32[256]{0:T(256)S(1)} %bitcast.88), kind=kLoop, calls=%fused_computation.59 | loop fusion | flops 3145728 | bytes 529920 | tf_op jit(solution)/shard_map/convert_element_type | solution.py:48
  28.0 1.1 convolution_add_fusion.3
  29.1 1.9 %convolution_add_fusion.2 = f32[20,64,128]{2,1,0:T(8,128)} fusion(bf16[256,20,64]{0,2,1:T(8,128)(2,1)S(1)} %bitcast.75, f32[256,20]{0,1:T(8,128)} %get-tuple-element.72, f32[20,64,128]{2,1,0:T(8,128)S(1)} %convolution_add_fusion.3, f32[20]{0:T(128)} %exp.65, bf16[512,256]{1,0:T(8,128)(2,1)S(1)} %divide_convert_fusion.1), kind=kOutput, calls=%fused_computation.43 | convolution fusion | flops 85196800 | bytes 2052176 | tf_op jit(solution)/shard_map/jhp,js->hps/dot_general | solution.py:64
  31.1 1.2 dynamic-slice
  33.0 0.9 dynamic-update-slice
  33.8 10.1 %all-reduce = f32[80]{0:T(128)S(1)} all-reduce(f32[80]{0:T(128)S(1)} %dynamic-update-slice), channel_id=2, replica_groups=mesh['groups'=2,'seq'=4,'tensor'=4] {'seq'}, use_global_device_ids=true, to_apply=%add | all-reduce | flops 80 | bytes 640
  44.1 0.7 mul.319
  46.5 3.7 %fusion.18 = f32[256,20,64]{0,2,1:T(8,128)} fusion(bf16[256,20,64]{0,2,1:T(8,128)(2,1)S(1)} %bitcast.78, f32[20,256]{1,0:T(8,128)} %get-tuple-element.70, f32[256,256]{1,0:T(8,128)S(1)} %fusion.57, f32[20,256]{1,0:T(8,128)} %bitcast.81, pred[256,256]{1,0:T(8,128)(4,1)S(1)} %iota_compare_fusion), kind=kOutput, calls=%fused_computation.31 | convolution fusion | flops 175636480 | bytes 2334720 | tf_op jit(solution)/shard_map/hij,jhp->ihp/dot_general | solution.py:61
  50.3 2.9 %fusion.17 = f32[256,20,64]{0,2,1:T(8,128)} fusion(bf16[256,20,64]{0,2,1:T(8,128)(2,1)S(1)} %bitcast.76, f32[20,256]{1,0:T(8,128)S(1)} %copy-done.11, f32[256,256]{1,0:T(8,128)S(1)} %fusion.53, f32[20,256]{1,0:T(8,128)S(1)} %bitcast.84, pred[256,256]{1,0:T(8,128)(4,1)S(1)} %iota_compare_fusion), kind=kOutput, calls=%fused_computation.30 | convolution fusion | flops 175636480 | bytes 2334720 | tf_op jit(solution)/shard_map/hij,jhp->ihp/dot_general | solution.py:61
  53.1 33.0 %all-gather.7.cloned.1.call-done = f32[80,64,128]{2,1,0:T(8,128)} async-done(((f32[20,64,128]{2,1,0:T(8,128)}), f32[80,64,128]{2,1,0:T(8,128)}) %all-gather.7.cloned.1.call-update) | async-done | bytes 2621456 | tf_op jit(solution)/shard_map/all_gather | solution.py:24
  87.6 1.4 fusion.21
  89.0 2.8 %copy.40 = f32[256,1280]{1,0:T(8,128)} copy(f32[256,1280]{0,1:T(8,128)} %bitcast.73) | data formatting | bytes 2621440 | tf_op jit(solution)/shard_map/concatenate | solution.py:138
  92.2 0.9 copy-done.2
  93.1 1.4 fusion.22
  94.6 2.9 %copy.41 = f32[256,1280]{1,0:T(8,128)} copy(f32[256,1280]{0,1:T(8,128)} %bitcast.72) | data formatting | bytes 2621440 | tf_op jit(solution)/shard_map/concatenate | solution.py:138
  97.5 4.2 %multiply_reduce_fusion = (f32[512]{0:T(512)S(1)}, f32[512,1280]{1,0:T(8,128)}) fusion(bf16[512,1280]{1,0:T(8,128)(2,1)} %param.16, bf16[512,1280]{1,0:T(8,128)(2,1)S(1)} %divide_convert_fusion, f32[1280]{0:T(1024)S(1)} %copy-done.10, f32[256,1280]{1,0:T(8,128)} %copy.41, f32[256,1280]{1,0:T(8,128)S(1)} %copy-done.1), kind=kLoop, calls=%fused_computation.14 | loop fusion | flops 7208448 | bytes 7871488 | tf_op jit(solution)/shard_map/reduce_sum | solution.py:142
  101.7 6.4 %psum.7 = f32[512]{0:T(512)S(1)} all-reduce(f32[512]{0:T(512)S(1)} %get-tuple-element.66), channel_id=1, replica_groups=mesh['groups'=2,'seq'=4,'tensor'=4] {'tensor'}, use_global_device_ids=true, to_apply=%region_7.8 | all-reduce | flops 512 | bytes 4096 | tf_op jit(solution)/shard_map/psum | solution.py:142
  108.1 2.0 %multiply_convert_fusion.4 = bf16[512,1280]{1,0:T(8,128)(2,1)S(1)} fusion(f32[512,1280]{1,0:T(8,128)} %get-tuple-element.67, f32[1280]{0:T(1024)S(1)} %copy-done.12, f32[512]{0:T(512)S(1)} %add_rsqrt_fusion), kind=kLoop, calls=%fused_computation.13 | loop fusion | flops 1966080 | bytes 3939328 | tf_op jit(solution)/shard_map/convert_element_type | solution.py:146
  110.2 0.9 gather_fusion
  111.1 0.8 broadcast_select_fusion
  112.3 34.4 %all-gather.5.cloned.1.call-done = bf16[512,1280]{1,0:T(8,128)(2,1)} async-done(((bf16[128,1280]{1,0:T(8,128)(2,1)}), bf16[512,1280]{1,0:T(8,128)(2,1)}) %all-gather.5.cloned.1.call-update) | async-done | bytes 1310736 | tf_op jit(solution)/shard_map/all_gather | solution.py:154
  146.7 1.6 %copy.42 = bf16[512,1280]{0,1:T(8,128)(2,1)S(1)} copy(bf16[512,1280]{1,0:T(8,128)(2,1)} %all-gather.5.cloned.1.call-done) | data formatting | bytes 2621440 | tf_op jit(solution)/shard_map/all_gather | solution.py:154
  149.7 0.8 reshape.193
  (84 shorter events, 9.0 us)
Async XLA Ops:
  7.2 79.0 %all-gather.7.cloned.1.call-start = ((), (), s32[]{:S(2)}) async-start(), calls=%async_computation.1 | async-start | bytes 3276800 | tf_op jit(solution)/shard_map/all_gather | solution.py:24
  8.7 12.8 %collective-permute-start = (bf16[3,1536]{1,0:T(4,128)(2,1)S(1)}, bf16[3,1536]{1,0:T(4,128)(2,1)S(1)}, u32[]{:S(2)}, u32[]{:S(2)}) collective-permute-start(bf16[3,1536]{1,0:T(4,128)(2,1)S(1)} %pad_maximum_fusion.2), channel_id=1, source_target_pairs={{0,4},{4,8},{8,12},{1,5},{5,9},{9,13},{2,6},{6,10},{10,14},{3,7},{... | collective-permute-start | bytes 27656 | tf_op jit(solution)/shard_map/ppermute | solution.py:19
  15.3 6.1 %copy-start.4 = (f32[3,8,2,128]{3,1,2,0:T(8,128)}, f32[3,8,2,128]{3,1,2,0:T(8,128)S(1)}, u32[]{:S(2)}) copy-start(f32[3,8,2,128]{3,1,2,0:T(8,128)S(1)} %copy.45) | copy-start | bytes 73732
  16.3 5.1 %copy-start.5 = (f32[3,8,2,128]{3,1,2,0:T(8,128)}, f32[3,8,2,128]{3,1,2,0:T(8,128)S(1)}, u32[]{:S(2)}) copy-start(f32[3,8,2,128]{3,1,2,0:T(8,128)S(1)} %copy.46) | copy-start | bytes 73732
  31.0 115.7 %all-gather.5.cloned.1.call-start = ((), (), s32[]{:S(2)}) async-start(), calls=%async_computation | async-start | bytes 1638400 | tf_op jit(solution)/shard_map/all_gather | solution.py:154
  46.5 3.7 %copy-start.6 = (f32[3,8,2,128]{3,1,2,0:T(8,128)S(1)}, f32[3,8,2,128]{3,1,2,0:T(8,128)}, u32[]{:S(2)}) copy-start(f32[3,8,2,128]{3,1,2,0:T(8,128)} %copy-done.5) | copy-start | bytes 73732
  46.5 3.7 %copy-start.11 = (f32[20,256]{1,0:T(8,128)S(1)}, f32[20,256]{1,0:T(8,128)}, u32[]{:S(2)}) copy-start(f32[20,256]{1,0:T(8,128)} %get-tuple-element.73) | copy-start | bytes 61444
  86.3 0.7 copy-start.9
  86.3 1.3 copy-start.3
  87.6 4.2 %copy-start.13 = (f32[20]{0:T(128)S(1)}, f32[20]{0:T(128)}, u32[]{:S(2)}) copy-start(f32[20]{0:T(128)} %get-tuple-element.84) | copy-start | bytes 244
  89.0 3.2 %copy-start.8 = (f32[256,20]{0,1:T(8,128)S(1)}, f32[256,20]{0,1:T(8,128)}, u32[]{:S(2)}) copy-start(f32[256,20]{0,1:T(8,128)} %get-tuple-element.76) | copy-start | bytes 61444
  91.8 1.3 copy-start.2
  94.6 2.9 %copy-start.1 = (f32[256,1280]{1,0:T(8,128)S(1)}, f32[256,1280]{1,0:T(8,128)}, u32[]{:S(2)}) copy-start(f32[256,1280]{1,0:T(8,128)} %copy.40) | copy-start | bytes 3932164
  94.6 2.9 %copy-start.10 = (f32[1280]{0:T(1024)S(1)}, f32[1280]{0:T(1024)}, u32[]{:S(2)}) copy-start(f32[1280]{0:T(1024)} %mul.320) | copy-start | bytes 15364
  97.5 10.6 %copy-start.12 = (f32[1280]{0:T(1024)S(1)}, f32[1280]{0:T(1024)}, u32[]{:S(2)}) copy-start(f32[1280]{0:T(1024)} %param.23) | copy-start | bytes 15364
  110.1 38.2 %copy-start = (bf16[512,1280]{1,0:T(8,128)(2,1)}, bf16[512,1280]{1,0:T(8,128)(2,1)S(1)}, u32[]{:S(2)}) copy-start(bf16[512,1280]{1,0:T(8,128)(2,1)S(1)} %multiply_convert_fusion.4) | copy-start | bytes 3932164
  110.2 1.8 %copy-start.7 = (bf16[40,1280]{1,0:T(8,128)(2,1)S(1)}, bf16[40,1280]{1,0:T(8,128)(2,1)}, u32[]{:S(2)}) copy-start(bf16[40,1280]{1,0:T(8,128)(2,1)} %param.25) | copy-start | bytes 307204
  110.2 2.0 %copy-start.14 = (s32[40]{0:T(128)S(1)}, s32[40]{0:T(128)}, u32[]{:S(2)}) copy-start(s32[40]{0:T(128)} %param.27) | copy-start | bytes 484
  110.2 2.0 %copy-start.15 = (s32[40]{0:T(128)S(1)}, s32[40]{0:T(128)}, u32[]{:S(2)}) copy-start(s32[40]{0:T(128)} %param.26) | copy-start | bytes 484
Sparse Core Ops, SparseCore 0:
  31.1 55.0 all-gather.6
  112.1 34.5 all-gather.4
where the time goes:
time: 158 us; the launch traced here: 157 us
  waiting for transfers between devices  67.5 us (43%)
  other arithmetic  20 us (13%)
  local copies, waits for them, and re-layouts  18.7 us (12%)
  blocking collectives  16.5 us (10%)
  between operations  15.1 us (10%)
  matrix products  14.5 us (9%)
  starting transfers between devices  5.04 us (3%)
    all_gather x1, waiting for transfers between devices, local(): piece = lax.all_gather(summaries, 'seq', axis=0, tiled=True)  34.4 us
    all_gather x1, waiting for transfers between devices, prefix(): gathered = jax.tree.map(lambda a: lax.all_gather(a, axis), part)  33 us
    unnamed x1, blocking collectives  10.1 us
    dot_general x2, matrix products, stretch_local(): jnp.einsum('hij,jhp->ihp', mixing, x_block, preferred_element_type=jnp.fl...  6.59 us
    psum x1, blocking collectives, local(): square_sum = lax.psum(jnp.sum(gated * gated, axis=1), 'tensor')  6.37 us
    convert_element_type x2, other arithmetic, causal_conv(): return silu_act(summed).astype(jnp.bfloat16)  5.91 us
    concatenate x2, local copies, waits for them, and re-layouts, local(): jnp.concatenate(pieces_out, axis=0)  5.7 us
    ppermute x1, starting transfers between devices, passed_along(): lax.ppermute(value, axis, [(source, source + steps) for source in range(l...  4.96 us
  transfers between devices with their start and end apart: 3, of which 2 were waited for; matrix products, arithmetic and copies ran while one was open for 12% of the time, Pallas kernels for 0%

commit v1 on v0

--- a/solution.py
+++ b/solution.py
@@ -17,19 +17,6 @@
     count = lax.axis_size(axis)
     leading, last = (max(0, -steps), min(count, count - steps))
     return lax.ppermute(value, axis, [(source, source + steps) for source in range(leading, last)])
-
-
-def prefix(part, axis, combine, identity):
-    place = lax.axis_index(axis)
-    gathered = jax.tree.map(lambda a: lax.all_gather(a, axis), part)
-    state = jax.tree.map(lambda a, e: jnp.zeros_like(a) + jnp.asarray(e, a.dtype), part, identity)
-
-    def one(lap, state):
-        return combine(
-            state, jax.tree.map(lambda a: lax.dynamic_index_in_dim(a, lap, 0, False), gathered)
-        )
-
-    return lax.fori_loop(0, place, one, state)
 
 
 def silu_act(values):
@@ -67,6 +54,22 @@
 
 def combine(earlier, later):
     return (earlier[0] * jnp.exp(later[1])[:, None, None] + later[0], earlier[1] + later[1])
+
+
+def exclusive_scan(state, decay, axis):
+    count = lax.axis_size(axis)
+    window = (state, decay)
+    before = (jnp.zeros_like(state), jnp.zeros_like(decay))
+    shift = 1
+    while shift < count:
+        sent_state = passed_along(window[0].astype(jnp.bfloat16), axis, shift)
+        sent_decay = passed_along(window[1], axis, shift)
+        received = (sent_state.astype(jnp.float32), sent_decay)
+        before = combine(received, before)
+        if shift * 2 < count:
+            window = combine(received, window)
+        shift *= 2
+    return before[0]
 
 
 def read_state(c_block, state_in):
@@ -98,6 +101,10 @@
     head_width = channels // heads_local
     state_width = bc_in.shape[1] // 2
     rim_rows = conv_x.shape[0] - 1
+    seq_count = lax.axis_size("seq")
+    queries_all = lax.all_gather(pool_query, "seq", axis=0, tiled=True)
+    start_all = lax.all_gather(pool_start, "seq", axis=0, tiled=True)
+    stop_all = lax.all_gather(pool_stop, "seq", axis=0, tiled=True)
     edge_rows = jnp.concatenate([x_in[tok_rows - rim_rows :], bc_in[tok_rows - rim_rows :]], axis=1)
     before = passed_along(edge_rows, "seq", 1)
     x_conv = causal_conv(before[:, :channels], x_in, conv_x)
@@ -122,12 +129,7 @@
         saved_parts.append((intra_part, cumul_keep, entry_state, decay_total))
         entry_state = jnp.exp(cumul_keep[:, -1])[:, None, None] * entry_state + stretch_state
         decay_total = decay_total + cumul_keep[:, -1]
-    incoming, unused = prefix(
-        (entry_state, decay_total),
-        "seq",
-        combine,
-        (jnp.zeros_like(entry_state), jnp.zeros_like(decay_total)),
-    )
+    incoming = exclusive_scan(entry_state, decay_total, "seq")
     pieces_out = []
     for block_index in range(stretch_count):
         intra_part, cumul_keep, entry_part, decay_part = saved_parts[block_index]
@@ -150,28 +152,39 @@
     pool_width = channels // pool_heads_local
     scale_factor = 1.0 / math.sqrt(pool_width)
     pools_local = pool_query.shape[0]
-    queries = pool_query.reshape(pools_local, pool_heads_local, pool_width)
-    piece = lax.all_gather(summaries, "seq", axis=0, tiled=True)
-    peak = jnp.full((pool_heads_local, pools_local), MASKED, jnp.float32)
-    numer = jnp.zeros((pools_local, pool_heads_local, pool_width), jnp.float32)
-    count = piece.shape[0]
-    seg_index = lax.iota(jnp.int32, count)
-    inside = (seg_index[None, :] >= pool_start[:, None]) & (seg_index[None, :] < pool_stop[:, None])
-    keys_block = piece.reshape(count, pool_heads_local, pool_width)
+    pools_all = queries_all.shape[0]
+    segs_local = summaries.shape[0]
+    queries = queries_all.reshape(pools_all, pool_heads_local, pool_width)
+    seg_index = lax.axis_index("seq") * segs_local + lax.iota(jnp.int32, segs_local)
+    inside = (seg_index[None, :] >= start_all[:, None]) & (seg_index[None, :] < stop_all[:, None])
+    keys_block = summaries.reshape(segs_local, pool_heads_local, pool_width)
     logits = (
         jnp.einsum("pad,rad->apr", queries, keys_block, preferred_element_type=jnp.float32)
         * scale_factor
     )
     logits = jnp.where(inside[None], logits, MASKED)
-    new_peak = jnp.maximum(peak, jnp.max(logits, axis=2))
-    expo = jnp.where(inside[None], jnp.exp(logits - new_peak[:, :, None]), 0.0)
-    rescale = jnp.exp(peak - new_peak)
+    peak = jnp.max(logits, axis=2)
+    expo = jnp.where(inside[None], jnp.exp(logits - peak[:, :, None]), 0.0)
     denom = jnp.sum(expo, axis=2)
-    numer = numer * rescale.T[:, :, None] + jnp.einsum(
+    numer = jnp.einsum(
         "apr,rad->pad", expo.astype(jnp.bfloat16), keys_block, preferred_element_type=jnp.float32
     )
-    peak, denom, numer = (new_peak, denom, numer)
-    pooled = (numer / denom.T[:, :, None]).reshape(pools_local, channels)
+    numer_sent = lax.all_to_all(
+        numer.reshape(pools_all, channels).astype(jnp.bfloat16), "seq", 0, 0, tiled=True
+    )
+    stats = jnp.concatenate([peak.T, denom.T], axis=1)
+    stats_sent = lax.all_to_all(stats, "seq", 0, 0, tiled=True)
+    numer_parts = numer_sent.astype(jnp.float32).reshape(
+        seq_count, pools_local, pool_heads_local, pool_width
+    )
+    stats_parts = stats_sent.reshape(seq_count, pools_local, 2, pool_heads_local)
+    peak_parts = stats_parts[:, :, 0]
+    denom_parts = stats_parts[:, :, 1]
+    peak_all = jnp.max(peak_parts, axis=0)
+    rescale = jnp.exp(peak_parts - peak_all[None])
+    denom_all = jnp.sum(rescale * denom_parts, axis=0)
+    numer_all = jnp.sum(rescale[:, :, :, None] * numer_parts, axis=0)
+    pooled = (numer_all / denom_all[:, :, None]).reshape(pools_local, channels)
     return (mixed_seq, pooled)
 
 

time: 158 us -> 132 us (0.84)
  waiting for transfers between devices: 67.5 us -> 16.9 us
  starting transfers between devices: 5.04 us -> 29.8 us
  between operations: 15.1 us -> 1.73 us
  blocking collectives: 16.5 us -> 27.6 us
  local copies, waits for them, and re-layouts: 18.7 us -> 20.5 us
    all_gather x2 -> x0, waiting for transfers between devices: 67.4 us -> none  [the longest x1 34.4 us: local(): piece = lax.all_gather(summaries, 'seq', axis=0, tiled=True)]
    ppermute x1 -> x4, starting transfers between devices: 4.96 us -> 21.6 us  [passed_along(): lax.ppermute(value, axis, [(source, source + steps) for source in range(l...]
    all_gather x0 -> x1, blocking collectives: none -> 15.2 us  [local(): queries_all = lax.all_gather(pool_query, 'seq', axis=0, tiled=True)]
    all_to_all x0 -> x2, waiting for transfers between devices: none -> 11.4 us  [the longest x1 8.25 us: local(): lax.all_to_all(numer.reshape(pools_all, channels).astype(jnp.bfloat16), '...]
    all_to_all x0 -> x2, starting transfers between devices: none -> 8.11 us  [the longest x1 4.65 us: local(): stats_sent = lax.all_to_all(stats, 'seq', 0, 0, tiled=True)]
    ppermute x1 -> x4, waiting for transfers between devices: 0.01 us -> 5.47 us  [passed_along(): lax.ppermute(value, axis, [(source, source + steps) for source in range(l...]
    unnamed x1, blocking collectives: 10.1 us -> 6.55 us
    convert_element_type x2, other arithmetic: 5.91 us -> 3.73 us  [causal_conv(): return silu_act(summed).astype(jnp.bfloat16)]
  transfers between devices with their start and end apart: 3 -> 6, of which waited for: 2 -> 4; matrix products, arithmetic and copies ran while one was open for 12% -> 19% of each run, Pallas kernels for 0% -> 0%
where the time goes in v1:
time: 132 us; the launch traced here: 130 us
  starting transfers between devices  29.8 us (23%)
  blocking collectives  27.6 us (21%)
  other arithmetic  20.7 us (16%)
  local copies, waits for them, and re-layouts  20.5 us (16%)
  waiting for transfers between devices  16.9 us (13%)
  matrix products  13.3 us (10%)
  between operations  1.73 us (1%)
    ppermute x4, starting transfers between devices, passed_along(): lax.ppermute(value, axis, [(source, source + steps) for source in range(l...  21.6 us
    all_gather x1, blocking collectives, local(): queries_all = lax.all_gather(pool_query, 'seq', axis=0, tiled=True)  15.2 us
    all_to_all x1, waiting for transfers between devices, local(): lax.all_to_all(numer.reshape(pools_all, channels).astype(jnp.bfloat16), '...  8.25 us
    unnamed x1, blocking collectives  6.55 us
    psum x1, blocking collectives, local(): square_sum = lax.psum(jnp.sum(gated * gated, axis=1), 'tensor')  5.81 us
    ppermute x4, waiting for transfers between devices, passed_along(): lax.ppermute(value, axis, [(source, source + steps) for source in range(l...  5.47 us
    unnamed x47, local copies, waits for them, and re-layouts  5.14 us
    all_to_all x1, starting transfers between devices, local(): stats_sent = lax.all_to_all(stats, 'seq', 0, 0, tiled=True)  4.65 us
  transfers between devices with their start and end apart: 6, of which 4 were waited for; matrix products, arithmetic and copies ran while one was open for 19% of the time, Pallas kernels for 0%

profile of v1, /device:TPU:0, one launch (start us, length us, event | category | flops | bytes accessed | tf_op | source)
XLA Modules:
  0.0 130.5 jit_solution(8809013497023641823)
XLA Ops:
  2.2 5.0 %collective-permute-start = (bf16[3,1536]{1,0:T(4,128)(2,1)S(1)}, bf16[3,1536]{1,0:T(4,128)(2,1)S(1)}, u32[]{:S(2)}, u32[]{:S(2)}) collective-permute-start(bf16[3,1536]{1,0:T(4,128)(2,1)S(1)} %pad_maximum_fusion.3), channel_id=1, source_target_pairs={{0,4},{4,8},{8,12},{1,5},{5,9},{9,13},{2,6},{6,10},{10,14},{3,7},{... | collective-permute-start | bytes 27656 | tf_op jit(solution)/shard_map/ppermute | solution.py:19
  10.6 3.5 %collective-permute-start.3 = (f32[20]{0:T(128)S(1)}, f32[20]{0:T(128)S(1)}, u32[]{:S(2)}, u32[]{:S(2)}) collective-permute-start(f32[20]{0:T(128)S(1)} %get-tuple-element.33), channel_id=1, source_target_pairs={{0,4},{4,8},{8,12},{1,5},{5,9},{9,13},{2,6},{6,10},{10,14},{3,7},{... | collective-permute-start | bytes 248 | tf_op jit(solution)/shard_map/ppermute | solution.py:19
  15.7 1.5 %fusion.81 = (f32[20,256]{1,0:T(8,128)}, f32[256,20]{0,1:T(8,128)}, f32[256,20]{0,1:T(8,128)}, f32[20,256]{1,0:T(8,128)}, f32[256,20]{0,1:T(8,128)}, /*index=5*/f32[256,20]{0,1:T(8,128)}) fusion(f32[20,512]{1,0:T(8,128)} %param.16, f32[20,256]{1,0:T(8,128)S(1)} %bitcast.92, f32[20]{0:T(128)S(1)} %get-tuple-element.39, f32[20,256]{1,0:T(8,128)S(1)} %bitcast.95, ...), kind=kLoop, calls=%fused_computation.140 | loop fusion | flops 20480 | bytes 204960 | tf_op jit(solution)/shard_map/slice | solution.py:126
  17.2 1.4 %slice_convert_fusion.3 = (f32[1,256]{1,0:T(1,128)}, f32[1,256]{1,0:T(1,128)}, f32[1,256]{1,0:T(1,128)}, f32[1,256]{1,0:T(1,128)}) fusion(bf16[4,256]{1,0:T(4,128)(2,1)} %param.20), kind=kLoop, calls=%fused_computation.130 | loop fusion | flops 1024 | bytes 6144 | tf_op jit(solution)/shard_map/mul | solution.py:32
  18.6 15.2 %all_gather.11 = bf16[160,1280]{1,0:T(8,128)(2,1)S(1)} all-gather(bf16[40,1280]{1,0:T(8,128)(2,1)} %param.23), channel_id=1, replica_groups=mesh['groups'=2,'seq'=4,'tensor'=4] {'seq'}, dimensions={0}, use_global_device_ids=true | all-gather | bytes 512000 | tf_op jit(solution)/shard_map/all_gather | solution.py:105
  33.8 1.2 compare_and_fusion.1
  35.0 1.2 dynamic-slice
  38.5 6.6 %all-reduce.2 = (s32[160]{0:T(256)S(1)}, s32[160]{0:T(256)S(1)}) all-reduce(s32[160]{0:T(256)S(1)} %dynamic-update-slice.1, s32[160]{0:T(256)S(1)} %dynamic-update-slice), channel_id=1, replica_groups=mesh['groups'=2,'seq'=4,'tensor'=4] {'seq'}, use_global_device_ids=true, to_apply=%add.1 | all-reduce | flops 320 | bytes 2560
  46.5 1.7 %reshape.222 = bf16[160,8,160]{2,1,0:T(8,128)(2,1)} reshape(bf16[160,1280]{1,0:T(8,128)(2,1)S(1)} %all_gather.11) | data formatting | bytes 819200 | tf_op jit(solution)/shard_map/reshape | solution.py:157
  48.2 1.8 %divide_convert_fusion = bf16[512,1280]{1,0:T(8,128)(2,1)S(1)} fusion(bf16[512,1280]{1,0:T(8,128)(2,1)S(1)} %copy-done.1, bf16[3,1280]{1,0:T(4,128)(2,1)S(1)} %slice.166, f32[1280]{0:T(1024)S(1)} %get-tuple-element.4, f32[1280]{0:T(1024)S(1)} %get-tuple-element.5, f32[1280]{0:T(1024)S(1)} %get-tuple-element.3, f32[1280]{0:T(1024)S(1)} %get-tuple-element.2), kind=kLoop, calls=%fused_computation.23 | loop fusion | flops 15728640 | bytes 2649600 | tf_op jit(solution)/shard_map/convert_element_type | solution.py:35
  50.4 1.9 %divide_convert_fusion.1 = bf16[512,256]{1,0:T(8,128)(2,1)S(1)} fusion(bf16[512,256]{1,0:T(8,128)(2,1)} %param.15, bf16[3,256]{1,0:T(4,128)(2,1)S(1)} %slice.173, f32[256]{0:T(256)} %bitcast.104, f32[256]{0:T(256)} %bitcast.105, f32[256]{0:T(256)} %bitcast.103, f32[256]{0:T(256)} %bitcast.102), kind=kLoop, calls=%fused_computation.62 | loop fusion | flops 3145728 | bytes 529920 | tf_op jit(solution)/shard_map/convert_element_type | solution.py:35
  53.5 1.1 convolution_add_fusion.3
  54.6 1.1 fusion.84
  55.7 3.3 %collective-permute-start.1 = (bf16[20,64,128]{2,1,0:T(8,128)(2,1)S(1)}, bf16[20,64,128]{2,1,0:T(8,128)(2,1)S(1)}, u32[]{:S(2)}, u32[]{:S(2)}) collective-permute-start(bf16[20,64,128]{2,1,0:T(8,128)(2,1)S(1)} %get-tuple-element.35), channel_id=1, source_target_pairs={{0,4},{4,8},{8,12},{1,5},{5,9},{9,13},{2,6},{6,10},{10,14},{3,7},{... | collective-permute-start | bytes 983048 | tf_op jit(solution)/shard_map/ppermute | solution.py:19
  59.1 1.7 %fusion.17 = f32[256,20,64]{0,2,1:T(8,128)S(1)} fusion(bf16[256,20,64]{0,2,1:T(8,128)(2,1)S(1)} %bitcast.88, f32[20,256]{1,0:T(8,128)S(1)} %copy-done.13, f32[256,256]{1,0:T(8,128)S(1)} %copy-done.4, f32[20,256]{1,0:T(8,128)S(1)} %bitcast.96, pred[256,256]{1,0:T(8,128)(4,1)S(1)} %copy-done.11), kind=kOutput, calls=%fused_computation.28 | convolution fusion | flops 175636480 | bytes 2334720 | tf_op jit(solution)/shard_map/hij,jhp->ihp/dot_general | solution.py:48
  60.9 3.9 %collective-permute-done.1 = bf16[20,64,128]{2,1,0:T(8,128)(2,1)S(1)} collective-permute-done((bf16[20,64,128]{2,1,0:T(8,128)(2,1)S(1)}, bf16[20,64,128]{2,1,0:T(8,128)(2,1)S(1)}, u32[]{:S(2)}, u32[]{:S(2)}) %collective-permute-start.1) | collective-permute-done | bytes 327712 | tf_op jit(solution)/shard_map/ppermute | solution.py:19
  65.0 10.0 %collective-permute-start.2 = (bf16[20,64,128]{2,1,0:T(8,128)(2,1)S(1)}, bf16[20,64,128]{2,1,0:T(8,128)(2,1)S(1)}, u32[]{:S(2)}, u32[]{:S(2)}) collective-permute-start(bf16[20,64,128]{2,1,0:T(8,128)(2,1)S(1)} %fusion.29), channel_id=1, source_target_pairs={{0,8},{4,12},{1,9},{5,13},{2,10},{6,14},{3,11},{7,15},{16,24},{20,... | collective-permute-start | bytes 983048 | tf_op jit(solution)/shard_map/ppermute | solution.py:19
  75.0 2.9 %fusion.18 = f32[256,20,64]{0,2,1:T(8,128)} fusion(bf16[256,20,64]{0,2,1:T(8,128)(2,1)S(1)} %bitcast.86, f32[20,256]{1,0:T(8,128)S(1)} %copy-done.12, f32[256,256]{1,0:T(8,128)S(1)} %fusion.61, f32[20,256]{1,0:T(8,128)S(1)} %bitcast.93, pred[256,256]{1,0:T(8,128)(4,1)S(1)} %copy-done.11), kind=kOutput, calls=%fused_computation.29 | convolution fusion | flops 175636480 | bytes 2334720 | tf_op jit(solution)/shard_map/hij,jhp->ihp/dot_general | solution.py:48
  77.9 1.6 %collective-permute-done.2 = bf16[20,64,128]{2,1,0:T(8,128)(2,1)S(1)} collective-permute-done((bf16[20,64,128]{2,1,0:T(8,128)(2,1)S(1)}, bf16[20,64,128]{2,1,0:T(8,128)(2,1)S(1)}, u32[]{:S(2)}, u32[]{:S(2)}) %collective-permute-start.2) | collective-permute-done | bytes 327712 | tf_op jit(solution)/shard_map/ppermute | solution.py:19
  79.9 1.5 %fusion.22 = f32[256,20,64]{0,2,1:T(8,128)} fusion(f32[256,20,64]{0,2,1:T(8,128)S(1)} %fusion.17, f32[256,20,64]{0,2,1:T(8,128)S(1)} %fusion.49, f32[256,20]{0,1:T(8,128)S(1)} %copy-done.10, bf16[512,256]{1,0:T(8,128)(2,1)S(1)} %divide_convert_fusion.1, f32[20,64,128]{2,1,0:T(8,128)S(1)} %convolution_add_fusion.3, ...), kind=kOutput, calls=%fused_computation.35 | convolution fusion | flops 86507520 | bytes 5334016 | tf_op jit(solution)/shard_map/is,hps->ihp/dot_general | solution.py:79
  81.4 1.7 %copy.69 = f32[256,1280]{1,0:T(8,128)S(1)} copy(f32[256,1280]{0,1:T(8,128)} %bitcast.84) | data formatting | bytes 2621440 | tf_op jit(solution)/shard_map/concatenate | solution.py:140
  83.5 0.9 copy-done.2
  84.4 2.2 %fusion.21 = f32[256,20,64]{0,2,1:T(8,128)} fusion(f32[256,20,64]{0,2,1:T(8,128)S(1)} %copy-done.2, f32[256,20,64]{0,2,1:T(8,128)S(1)} %fusion.38, f32[256,20]{0,1:T(8,128)} %get-tuple-element.25, bf16[20,64,128]{2,1,0:T(8,128)(2,1)S(1)} %collective-permute-done.1, bf16[20,64,128]{2,1,0:T(8,128)(2,1)S(1)} %collective-permute-done.2, f32[20]{0:T(128)S(1)} %exp.71, ...), kind=kOutput, calls=%fused_computation.34 | convolution fusion | flops 85688320 | bytes 4674048 | tf_op jit(solution)/shard_map/is,hps->ihp/dot_general | solution.py:78
  86.6 2.8 %copy.68 = f32[256,1280]{1,0:T(8,128)} copy(f32[256,1280]{0,1:T(8,128)} %bitcast.83) | data formatting | bytes 2621440 | tf_op jit(solution)/shard_map/concatenate | solution.py:140
  89.4 4.2 %multiply_reduce_fusion = (f32[512]{0:T(512)S(1)}, f32[512,1280]{1,0:T(8,128)}) fusion(bf16[512,1280]{1,0:T(8,128)(2,1)} %param.14, bf16[512,1280]{1,0:T(8,128)(2,1)S(1)} %divide_convert_fusion, f32[1280]{0:T(1024)S(1)} %mul.340, f32[256,1280]{1,0:T(8,128)S(1)} %copy.69, f32[256,1280]{1,0:T(8,128)} %copy.68), kind=kLoop, calls=%fused_computation.12 | loop fusion | flops 7208448 | bytes 7871488 | tf_op jit(solution)/shard_map/reduce_sum | solution.py:144
  93.7 5.8 %psum.7 = f32[512]{0:T(512)S(1)} all-reduce(f32[512]{0:T(512)S(1)} %get-tuple-element.12), channel_id=1, replica_groups=mesh['groups'=2,'seq'=4,'tensor'=4] {'tensor'}, use_global_device_ids=true, to_apply=%region_5.6 | all-reduce | flops 512 | bytes 4096 | tf_op jit(solution)/shard_map/psum | solution.py:144
  99.5 2.0 %multiply_convert_fusion.4 = bf16[512,1280]{1,0:T(8,128)(2,1)S(1)} fusion(f32[512,1280]{1,0:T(8,128)} %get-tuple-element.13, f32[1280]{0:T(1024)S(1)} %copy-done.14, f32[512]{0:T(512)S(1)} %add_rsqrt_fusion), kind=kLoop, calls=%fused_computation.11 | loop fusion | flops 1966080 | bytes 3939328 | tf_op jit(solution)/shard_map/convert_element_type | solution.py:148
  105.1 4.7 %all-to-all-start = ((f32[4,1,640]{2,1,0:T(1,128)}), f32[4,1,640]{2,1,0:T(1,128)S(1)}, u32[]{:S(2)}, u32[]{:S(2)}) async-start(f32[4,1,640]{2,1,0:T(1,128)} %reshape.263), calls=%async_computation | async-start | bytes 20480 | tf_op jit(solution)/shard_map/all_to_all | solution.py:176
  110.7 1.4 %convert_element_type.154 = bf16[4,40,1280]{2,1,0:T(8,128)(2,1)} reshape(bf16[160,8,160]{2,1,0:T(8,128)(2,1)S(1)} %copy.75) | data formatting | bytes 819200 | tf_op jit(solution)/shard_map/convert_element_type | solution.py:173
  112.2 3.2 %all-to-all-done = f32[4,1,640]{2,1,0:T(1,128)S(1)} async-done(((f32[4,1,640]{2,1,0:T(1,128)}), f32[4,1,640]{2,1,0:T(1,128)S(1)}, u32[]{:S(2)}, u32[]{:S(2)}) %all-to-all-start) | async-done | bytes 10272 | tf_op jit(solution)/shard_map/all_to_all | solution.py:176
  115.3 3.5 %all-to-all-start.1 = ((bf16[4,40,1280]{2,1,0:T(8,128)(2,1)}), bf16[4,40,1280]{2,1,0:T(8,128)(2,1)S(1)}, u32[]{:S(2)}, u32[]{:S(2)}) async-start(bf16[4,40,1280]{2,1,0:T(8,128)(2,1)} %convert_element_type.154), calls=%async_computation.1 | async-start | bytes 819200 | tf_op jit(solution)/shard_map/all_to_all | solution.py:172
  121.4 8.3 %all-to-all-done.1 = bf16[4,40,1280]{2,1,0:T(8,128)(2,1)S(1)} async-done(((bf16[4,40,1280]{2,1,0:T(8,128)(2,1)}), bf16[4,40,1280]{2,1,0:T(8,128)(2,1)S(1)}, u32[]{:S(2)}, u32[]{:S(2)}) %all-to-all-start.1) | async-done | bytes 409632 | tf_op jit(solution)/shard_map/all_to_all | solution.py:172
  (110 shorter events, 20.2 us)
Async XLA Ops:
  0.6 47.6 %copy-start.1 = (bf16[512,1280]{1,0:T(8,128)(2,1)S(1)}, bf16[512,1280]{1,0:T(8,128)(2,1)}, u32[]{:S(2)}) copy-start(bf16[512,1280]{1,0:T(8,128)(2,1)} %param.13) | copy-start | bytes 3932164
  2.2 46.0 %collective-permute-start = (bf16[3,1536]{1,0:T(4,128)(2,1)S(1)}, bf16[3,1536]{1,0:T(4,128)(2,1)S(1)}, u32[]{:S(2)}, u32[]{:S(2)}) collective-permute-start(bf16[3,1536]{1,0:T(4,128)(2,1)S(1)} %pad_maximum_fusion.3), channel_id=1, source_target_pairs={{0,4},{4,8},{8,12},{1,5},{5,9},{9,13},{2,6},{6,10},{10,14},{3,7},{... | collective-permute-start | bytes 27656 | tf_op jit(solution)/shard_map/ppermute | solution.py:19
  8.9 9.7 %copy-start.6 = (f32[3,8,2,128]{3,1,2,0:T(8,128)}, f32[3,8,2,128]{3,1,2,0:T(8,128)S(1)}, u32[]{:S(2)}) copy-start(f32[3,8,2,128]{3,1,2,0:T(8,128)S(1)} %copy.80) | copy-start | bytes 73732
  9.8 8.8 %copy-start.8 = (f32[3,8,2,128]{3,1,2,0:T(8,128)}, f32[3,8,2,128]{3,1,2,0:T(8,128)S(1)}, u32[]{:S(2)}) copy-start(f32[3,8,2,128]{3,1,2,0:T(8,128)S(1)} %copy.81) | copy-start | bytes 73732
  10.6 37.6 %collective-permute-start.3 = (f32[20]{0:T(128)S(1)}, f32[20]{0:T(128)S(1)}, u32[]{:S(2)}, u32[]{:S(2)}) collective-permute-start(f32[20]{0:T(128)S(1)} %get-tuple-element.33), channel_id=1, source_target_pairs={{0,4},{4,8},{8,12},{1,5},{5,9},{9,13},{2,6},{6,10},{10,14},{3,7},{... | collective-permute-start | bytes 248 | tf_op jit(solution)/shard_map/ppermute | solution.py:19
  53.5 5.5 %copy-start.4 = (f32[256,256]{1,0:T(8,128)S(1)}, f32[256,256]{1,0:T(8,128)}, u32[]{:S(2)}) copy-start(f32[256,256]{1,0:T(8,128)} %fusion.57) | copy-start | bytes 786436
  53.5 5.5 %copy-start.9 = (f32[3,8,2,128]{3,1,2,0:T(8,128)S(1)}, f32[3,8,2,128]{3,1,2,0:T(8,128)}, u32[]{:S(2)}) copy-start(f32[3,8,2,128]{3,1,2,0:T(8,128)} %copy-done.8) | copy-start | bytes 73732
  53.5 5.5 %copy-start.11 = (pred[256,256]{1,0:T(8,128)(4,1)S(1)}, pred[256,256]{1,0:T(8,128)(4,1)}, u32[]{:S(2)}) copy-start(pred[256,256]{1,0:T(8,128)(4,1)} %iota_compare_fusion) | copy-start | bytes 196612
  53.5 5.5 %copy-start.13 = (f32[20,256]{1,0:T(8,128)S(1)}, f32[20,256]{1,0:T(8,128)}, u32[]{:S(2)}) copy-start(f32[20,256]{1,0:T(8,128)} %get-tuple-element.21) | copy-start | bytes 61444
  55.7 9.1 %collective-permute-start.1 = (bf16[20,64,128]{2,1,0:T(8,128)(2,1)S(1)}, bf16[20,64,128]{2,1,0:T(8,128)(2,1)S(1)}, u32[]{:S(2)}, u32[]{:S(2)}) collective-permute-start(bf16[20,64,128]{2,1,0:T(8,128)(2,1)S(1)} %get-tuple-element.35), channel_id=1, source_target_pairs={{0,4},{4,8},{8,12},{1,5},{5,9},{9,13},{2,6},{6,10},{10,14},{3,7},{... | collective-permute-start | bytes 983048 | tf_op jit(solution)/shard_map/ppermute | solution.py:19
  59.0 5.8 %copy-start.16 = (f32[20]{0:T(128)S(1)}, f32[20]{0:T(128)}, u32[]{:S(2)}) copy-start(f32[20]{0:T(128)} %get-tuple-element.32) | copy-start | bytes 244
  59.0 15.9 %copy-start.7 = (f32[3,8,2,128]{3,1,2,0:T(8,128)S(1)}, f32[3,8,2,128]{3,1,2,0:T(8,128)}, u32[]{:S(2)}) copy-start(f32[3,8,2,128]{3,1,2,0:T(8,128)} %copy-done.6) | copy-start | bytes 73732
  59.0 15.9 %copy-start.12 = (f32[20,256]{1,0:T(8,128)S(1)}, f32[20,256]{1,0:T(8,128)}, u32[]{:S(2)}) copy-start(f32[20,256]{1,0:T(8,128)} %get-tuple-element.18) | copy-start | bytes 61444
  65.0 14.5 %collective-permute-start.2 = (bf16[20,64,128]{2,1,0:T(8,128)(2,1)S(1)}, bf16[20,64,128]{2,1,0:T(8,128)(2,1)S(1)}, u32[]{:S(2)}, u32[]{:S(2)}) collective-permute-start(bf16[20,64,128]{2,1,0:T(8,128)(2,1)S(1)} %fusion.29), channel_id=1, source_target_pairs={{0,8},{4,12},{1,9},{5,13},{2,10},{6,14},{3,11},{7,15},{16,24},{20,... | collective-permute-start | bytes 983048 | tf_op jit(solution)/shard_map/ppermute | solution.py:19
  75.0 4.5 %copy-start.15 = (f32[20]{0:T(128)S(1)}, f32[20]{0:T(128)}, u32[]{:S(2)}) copy-start(f32[20]{0:T(128)} %get-tuple-element.30) | copy-start | bytes 244
  77.9 2.0 %copy-start.10 = (f32[256,20]{0,1:T(8,128)S(1)}, f32[256,20]{0,1:T(8,128)}, u32[]{:S(2)}) copy-start(f32[256,20]{0,1:T(8,128)} %get-tuple-element.24) | copy-start | bytes 61444
  83.1 1.3 %copy-start.2 = (f32[256,20,64]{0,2,1:T(8,128)S(1)}, f32[256,20,64]{0,2,1:T(8,128)}, u32[]{:S(2)}) copy-start(f32[256,20,64]{0,2,1:T(8,128)} %fusion.18) | copy-start | bytes 3932164
  89.4 10.1 %copy-start.14 = (f32[1280]{0:T(1024)S(1)}, f32[1280]{0:T(1024)}, u32[]{:S(2)}) copy-start(f32[1280]{0:T(1024)} %param.21) | copy-start | bytes 15364
  101.5 2.1 %copy-start = (bf16[512,1280]{1,0:T(8,128)(2,1)}, bf16[512,1280]{1,0:T(8,128)(2,1)S(1)}, u32[]{:S(2)}) copy-start(bf16[512,1280]{1,0:T(8,128)(2,1)S(1)} %multiply_convert_fusion.4) | copy-start | bytes 3932164
  101.5 1.6 %copy-start.3 = (bf16[160,8,160]{2,1,0:T(8,128)(2,1)S(1)}, bf16[160,8,160]{2,1,0:T(8,128)(2,1)}, u32[]{:S(2)}) copy-start(bf16[160,8,160]{2,1,0:T(8,128)(2,1)} %reshape.222) | copy-start | bytes 1228804
  101.6 1.6 %copy-start.5 = (pred[160,128]{1,0:T(8,128)(4,1)S(1)}, pred[160,128]{1,0:T(8,128)(4,1)}, u32[]{:S(2)}) copy-start(pred[160,128]{1,0:T(8,128)(4,1)} %compare_and_fusion) | copy-start | bytes 61444
  101.6 1.5 %copy-start.17 = (pred[128]{0:T(512)(128)(4,1)S(1)}, pred[128]{0:T(512)(128)(4,1)}, u32[]{:S(2)}) copy-start(pred[128]{0:T(512)(128)(4,1)} %get-tuple-element.10) | copy-start | bytes 388
  105.1 10.2 %all-to-all-start = ((f32[4,1,640]{2,1,0:T(1,128)}), f32[4,1,640]{2,1,0:T(1,128)S(1)}, u32[]{:S(2)}, u32[]{:S(2)}) async-start(f32[4,1,640]{2,1,0:T(1,128)} %reshape.263), calls=%async_computation | async-start | bytes 20480 | tf_op jit(solution)/shard_map/all_to_all | solution.py:176
  115.3 14.3 %all-to-all-start.1 = ((bf16[4,40,1280]{2,1,0:T(8,128)(2,1)}), bf16[4,40,1280]{2,1,0:T(8,128)(2,1)S(1)}, u32[]{:S(2)}, u32[]{:S(2)}) async-start(bf16[4,40,1280]{2,1,0:T(8,128)(2,1)} %convert_element_type.154), calls=%async_computation.1 | async-start | bytes 819200 | tf_op jit(solution)/shard_map/all_to_all | solution.py:172

commit v2 on v1

--- a/solution.py
+++ b/solution.py
@@ -102,9 +102,18 @@
     state_width = bc_in.shape[1] // 2
     rim_rows = conv_x.shape[0] - 1
     seq_count = lax.axis_size("seq")
-    queries_all = lax.all_gather(pool_query, "seq", axis=0, tiled=True)
-    start_all = lax.all_gather(pool_start, "seq", axis=0, tiled=True)
-    stop_all = lax.all_gather(pool_stop, "seq", axis=0, tiled=True)
+    pools_local = pool_query.shape[0]
+    bounds = jnp.stack([pool_start, pool_stop], axis=1)
+    bounds_split = jnp.concatenate([bounds // 64, bounds % 64], axis=1).astype(jnp.bfloat16)
+    query_rows = jnp.concatenate([pool_query, bounds_split], axis=1)
+    query_rows = jnp.broadcast_to(query_rows[None], (seq_count,) + query_rows.shape)
+    query_rows = lax.all_to_all(
+        query_rows.reshape(seq_count * pools_local, -1), "seq", 0, 0, tiled=True
+    )
+    queries_all = query_rows[:, :channels]
+    bounds_all = query_rows[:, channels:].astype(jnp.int32)
+    start_all = bounds_all[:, 0] * 64 + bounds_all[:, 2]
+    stop_all = bounds_all[:, 1] * 64 + bounds_all[:, 3]
     edge_rows = jnp.concatenate([x_in[tok_rows - rim_rows :], bc_in[tok_rows - rim_rows :]], axis=1)
     before = passed_along(edge_rows, "seq", 1)
     x_conv = causal_conv(before[:, :channels], x_in, conv_x)
@@ -151,7 +160,6 @@
     pool_heads_local = POOL_HEADS // lax.axis_size("tensor")
     pool_width = channels // pool_heads_local
     scale_factor = 1.0 / math.sqrt(pool_width)
-    pools_local = pool_query.shape[0]
     pools_all = queries_all.shape[0]
     segs_local = summaries.shape[0]
     queries = queries_all.reshape(pools_all, pool_heads_local, pool_width)
@@ -163,23 +171,31 @@
         * scale_factor
     )
     logits = jnp.where(inside[None], logits, MASKED)
-    peak = jnp.max(logits, axis=2)
+    peak = jnp.max(logits, axis=2).astype(jnp.bfloat16).astype(jnp.float32)
     expo = jnp.where(inside[None], jnp.exp(logits - peak[:, :, None]), 0.0)
     denom = jnp.sum(expo, axis=2)
     numer = jnp.einsum(
         "apr,rad->pad", expo.astype(jnp.bfloat16), keys_block, preferred_element_type=jnp.float32
     )
-    numer_sent = lax.all_to_all(
-        numer.reshape(pools_all, channels).astype(jnp.bfloat16), "seq", 0, 0, tiled=True
-    )
-    stats = jnp.concatenate([peak.T, denom.T], axis=1)
-    stats_sent = lax.all_to_all(stats, "seq", 0, 0, tiled=True)
-    numer_parts = numer_sent.astype(jnp.float32).reshape(
+    denom_high = denom.astype(jnp.bfloat16)
+    denom_low = (denom - denom_high.astype(jnp.float32)).astype(jnp.bfloat16)
+    parts = jnp.concatenate(
+        [
+            numer.reshape(pools_all, channels).astype(jnp.bfloat16),
+            peak.T.astype(jnp.bfloat16),
+            denom_high.T,
+            denom_low.T,
+        ],
+        axis=1,
+    )
+    parts = lax.all_to_all(parts, "seq", 0, 0, tiled=True).astype(jnp.float32)
+    parts = parts.reshape(seq_count, pools_local, channels + 3 * pool_heads_local)
+    numer_parts = parts[:, :, :channels].reshape(
         seq_count, pools_local, pool_heads_local, pool_width
     )
-    stats_parts = stats_sent.reshape(seq_count, pools_local, 2, pool_heads_local)
+    stats_parts = parts[:, :, channels:].reshape(seq_count, pools_local, 3, pool_heads_local)
     peak_parts = stats_parts[:, :, 0]
-    denom_parts = stats_parts[:, :, 1]
+    denom_parts = stats_parts[:, :, 1] + stats_parts[:, :, 2]
     peak_all = jnp.max(peak_parts, axis=0)
     rescale = jnp.exp(peak_parts - peak_all[None])
     denom_all = jnp.sum(rescale * denom_parts, axis=0)

time: 132 us -> 109 us (0.83)
  waiting for transfers between devices: 16.9 us -> 1.88 us
  starting transfers between devices: 29.8 us -> 21.9 us
  other arithmetic: 20.7 us -> 17.2 us
  blocking collectives: 27.6 us -> 31 us
  matrix products: 13.3 us -> 15.8 us
  local copies, waits for them, and re-layouts: 20.5 us -> 18.6 us
    all_to_all x0 -> x1, blocking collectives: none -> 25.1 us  [local(): parts = lax.all_to_all(parts, 'seq', 0, 0, tiled=True).astype(jnp.float32)]
    all_gather x1 -> x0, blocking collectives: 15.2 us -> none  [local(): queries_all = lax.all_gather(pool_query, 'seq', axis=0, tiled=True)]
    all_to_all x2 -> x1, waiting for transfers between devices: 11.4 us -> 0.01 us  [local(): lax.all_to_all(query_rows.reshape(seq_count * pools_local, -1), 'seq', 0,...]
    unnamed x1 -> x0, blocking collectives: 6.55 us -> none
    unnamed x47 -> x62, local copies, waits for them, and re-layouts: 5.14 us -> 0.59 us
    all_to_all x2 -> x1, starting transfers between devices: 8.11 us -> 4.13 us  [local(): lax.all_to_all(query_rows.reshape(seq_count * pools_local, -1), 'seq', 0,...]
    ppermute x4, starting transfers between devices: 21.6 us -> 17.8 us  [passed_along(): lax.ppermute(value, axis, [(source, source + steps) for source in range(l...]
    ppermute x4, waiting for transfers between devices: 5.47 us -> 1.88 us  [passed_along(): lax.ppermute(value, axis, [(source, source + steps) for source in range(l...]
  transfers between devices with their start and end apart: 6 -> 5, of which waited for: 4 -> 2; matrix products, arithmetic and copies ran while one was open for 19% -> 25% of each run, Pallas kernels for 0% -> 0%
where the time goes in v2:
time: 109 us; the launch traced here: 108 us
  blocking collectives  31 us (28%)
  starting transfers between devices  21.9 us (20%)
  local copies, waits for them, and re-layouts  18.6 us (17%)
  other arithmetic  17.2 us (16%)
  matrix products  15.8 us (14%)
  waiting for transfers between devices  1.88 us (2%)
  between operations  1.29 us (1%)
    all_to_all x1, blocking collectives, local(): parts = lax.all_to_all(parts, 'seq', 0, 0, tiled=True).astype(jnp.float32)  25.1 us
    ppermute x4, starting transfers between devices, passed_along(): lax.ppermute(value, axis, [(source, source + steps) for source in range(l...  17.8 us
    psum x1, blocking collectives, local(): square_sum = lax.psum(jnp.sum(gated * gated, axis=1), 'tensor')  5.81 us
    dot_general x2, matrix products, stretch_local(): jnp.einsum('hij,jhp->ihp', mixing, x_block, preferred_element_type=jnp.fl...  5.8 us
    concatenate x2, local copies, waits for them, and re-layouts, local(): jnp.concatenate(pieces_out, axis=0)  5.71 us
    reduce_sum x1, other arithmetic, local(): square_sum = lax.psum(jnp.sum(gated * gated, axis=1), 'tensor')  4.24 us
    all_to_all x1, starting transfers between devices, local(): lax.all_to_all(query_rows.reshape(seq_count * pools_local, -1), 'seq', 0,...  4.13 us
    dot_general x2, matrix products, read_state(): jnp.einsum('is,hps->ihp', c_block, state_high, preferred_element_type=jnp...  3.15 us
  transfers between devices with their start and end apart: 5, of which 2 were waited for; matrix products, arithmetic and copies ran while one was open for 25% of the time, Pallas kernels for 0%

profile of v2, /device:TPU:0, one launch (start us, length us, event | category | flops | bytes accessed | tf_op | source)
XLA Modules:
  0.0 107.7 jit_solution(17882249819044315914)
XLA Ops:
  0.7 0.8 slice.154
  1.5 0.7 slice.153
  2.3 5.0 %collective-permute-start = (bf16[3,1536]{1,0:T(4,128)(2,1)S(1)}, bf16[3,1536]{1,0:T(4,128)(2,1)S(1)}, u32[]{:S(2)}, u32[]{:S(2)}) collective-permute-start(bf16[3,1536]{1,0:T(4,128)(2,1)S(1)} %pad_maximum_fusion.2), channel_id=1, source_target_pairs={{0,4},{4,8},{8,12},{1,5},{5,9},{9,13},{2,6},{6,10},{10,14},{3,7},{... | collective-permute-start | bytes 27656 | tf_op jit(solution)/shard_map/ppermute | solution.py:19
  7.2 0.8 fusion.87
  10.7 3.5 %collective-permute-start.3 = (f32[20]{0:T(128)S(1)}, f32[20]{0:T(128)S(1)}, u32[]{:S(2)}, u32[]{:S(2)}) collective-permute-start(f32[20]{0:T(128)S(1)} %get-tuple-element.37), channel_id=1, source_target_pairs={{0,4},{4,8},{8,12},{1,5},{5,9},{9,13},{2,6},{6,10},{10,14},{3,7},{... | collective-permute-start | bytes 248 | tf_op jit(solution)/shard_map/ppermute | solution.py:19
  15.1 1.0 concatenate.32
  16.1 0.8 broadcast_in_dim.117
  16.9 4.1 %all-to-all-start = ((bf16[4,40,1284]{2,1,0:T(8,128)(2,1)}), bf16[4,40,1284]{2,1,0:T(8,128)(2,1)}, u32[]{:S(2)}, u32[]{:S(2)}) async-start(bf16[4,40,1284]{2,1,0:T(8,128)(2,1)} %broadcast_in_dim.117), calls=%async_computation | async-start | bytes 901120 | tf_op jit(solution)/shard_map/all_to_all | solution.py:110
  24.2 0.9 fusion.58
  25.0 0.9 fusion.62
  26.0 1.8 %divide_convert_fusion = bf16[512,1280]{1,0:T(8,128)(2,1)S(1)} fusion(bf16[512,1280]{1,0:T(8,128)(2,1)S(1)} %copy-done.4, bf16[3,1280]{1,0:T(4,128)(2,1)S(1)} %slice.202, f32[1280]{0:T(1024)S(1)} %get-tuple-element.6, f32[1280]{0:T(1024)S(1)} %get-tuple-element.7, f32[1280]{0:T(1024)S(1)} %get-tuple-element.5, f32[1280]{0:T(1024)S(1)} %get-tuple-element.4), kind=kLoop, calls=%fused_computation.23 | loop fusion | flops 15728640 | bytes 2649600 | tf_op jit(solution)/shard_map/convert_element_type | solution.py:35
  27.9 1.1 %copy.61 = bf16[256,1280]{0,1:T(8,128)(2,1)} copy(bf16[256,1280]{1,0:T(8,128)(2,1)S(1)} %get-tuple-element.19) | data formatting | bytes 1310720 | tf_op jit(solution)/shard_map/slice | solution.py:132
  29.3 1.2 %convolution_add_fusion.3 = f32[20,64,128]{2,1,0:T(8,128)S(1)} fusion(bf16[256,20,64]{0,2,1:T(8,128)(2,1)S(1)} %bitcast.82, f32[256,20]{0,1:T(8,128)} %get-tuple-element.21, f32[20]{0:T(128)} %get-tuple-element.35, bf16[512,256]{1,0:T(8,128)(2,1)S(1)} %divide_convert_fusion.1), kind=kOutput, calls=%fused_computation.44 | convolution fusion | flops 85032960 | bytes 1396816 | tf_op jit(solution)/shard_map/jhp,js->hps/dot_general | solution.py:51
  30.4 1.1 %fusion.89 = (bf16[20,64,128]{2,1,0:T(8,128)(2,1)S(1)}, f32[20,64,128]{2,1,0:T(8,128)S(1)}) fusion(bf16[512,256]{1,0:T(8,128)(2,1)S(1)} %divide_convert_fusion.1, bf16[256,20,64]{0,2,1:T(8,128)(2,1)S(1)} %bitcast.85, f32[256,20]{0,1:T(8,128)} %get-tuple-element.22, f32[20,64,128]{2,1,0:T(8,128)S(1)} %convolution_add_fusion.3, f32[20]{0:T(128)} %get-tuple-element.38), kind=kOutput, calls=%fused_computation.164 | convolution fusion | flops 85360640 | bytes 2379856 | tf_op jit(solution)/shard_map/jhp,js->hps/dot_general | solution.py:51
  31.5 3.9 %collective-permute-start.1 = (bf16[20,64,128]{2,1,0:T(8,128)(2,1)S(1)}, bf16[20,64,128]{2,1,0:T(8,128)(2,1)S(1)}, u32[]{:S(2)}, u32[]{:S(2)}) collective-permute-start(bf16[20,64,128]{2,1,0:T(8,128)(2,1)S(1)} %get-tuple-element.39), channel_id=1, source_target_pairs={{0,4},{4,8},{8,12},{1,5},{5,9},{9,13},{2,6},{6,10},{10,14},{3,7},{... | collective-permute-start | bytes 983048 | tf_op jit(solution)/shard_map/ppermute | solution.py:19
  35.5 2.9 %fusion.17 = f32[256,20,64]{0,2,1:T(8,128)} fusion(bf16[256,20,64]{0,2,1:T(8,128)(2,1)S(1)} %bitcast.86, f32[20,256]{1,0:T(8,128)S(1)} %copy-done.20, f32[256,256]{1,0:T(8,128)S(1)} %copy-done.9, f32[20,256]{1,0:T(8,128)S(1)} %bitcast.97, pred[256,256]{1,0:T(8,128)(4,1)S(1)} %copy-done.16), kind=kOutput, calls=%fused_computation.28 | convolution fusion | flops 175636480 | bytes 2334720 | tf_op jit(solution)/shard_map/hij,jhp->ihp/dot_general | solution.py:48
  38.4 2.9 %fusion.18 = f32[256,20,64]{0,2,1:T(8,128)} fusion(bf16[256,20,64]{0,2,1:T(8,128)(2,1)S(1)} %bitcast.83, f32[20,256]{1,0:T(8,128)S(1)} %copy-done.19, f32[256,256]{1,0:T(8,128)S(1)} %copy-done.8, f32[20,256]{1,0:T(8,128)S(1)} %bitcast.94, pred[256,256]{1,0:T(8,128)(4,1)S(1)} %copy-done.16), kind=kOutput, calls=%fused_computation.29 | convolution fusion | flops 175636480 | bytes 2334720 | tf_op jit(solution)/shard_map/hij,jhp->ihp/dot_general | solution.py:48
  41.5 0.9 fusion.28
  42.4 5.4 %collective-permute-start.2 = (bf16[20,64,128]{2,1,0:T(8,128)(2,1)}, bf16[20,64,128]{2,1,0:T(8,128)(2,1)S(1)}, u32[]{:S(2)}, u32[]{:S(2)}) collective-permute-start(bf16[20,64,128]{2,1,0:T(8,128)(2,1)} %fusion.28), channel_id=1, source_target_pairs={{0,8},{4,12},{1,9},{5,13},{2,10},{6,14},{3,11},{7,15},{16,24},{20,... | collective-permute-start | bytes 983048 | tf_op jit(solution)/shard_map/ppermute | solution.py:19
  47.8 1.0 slice.227
  48.9 0.8 slice_convert_fusion
  49.7 1.7 %reshape.231 = bf16[160,8,160]{2,1,0:T(8,128)(2,1)} reshape(bf16[160,1280]{1,0:T(8,128)(2,1)S(1)} %slice.227) | data formatting | bytes 819200 | tf_op jit(solution)/shard_map/reshape | solution.py:165
  51.7 1.7 %collective-permute-done.2 = bf16[20,64,128]{2,1,0:T(8,128)(2,1)S(1)} collective-permute-done((bf16[20,64,128]{2,1,0:T(8,128)(2,1)}, bf16[20,64,128]{2,1,0:T(8,128)(2,1)S(1)}, u32[]{:S(2)}, u32[]{:S(2)}) %collective-permute-start.2) | collective-permute-done | bytes 327712 | tf_op jit(solution)/shard_map/ppermute | solution.py:19
  53.8 1.5 %fusion.22 = f32[256,20,64]{0,2,1:T(8,128)} fusion(f32[256,20,64]{0,2,1:T(8,128)S(1)} %copy-done.5, f32[256,20,64]{0,2,1:T(8,128)S(1)} %fusion.48, f32[256,20]{0,1:T(8,128)S(1)} %copy-done.15, bf16[512,256]{1,0:T(8,128)(2,1)S(1)} %divide_convert_fusion.1, f32[20,64,128]{2,1,0:T(8,128)S(1)} %convolution_add_fusion.3, ...), kind=kOutput, calls=%fused_computation.35 | convolution fusion | flops 86507520 | bytes 5334016 | tf_op jit(solution)/shard_map/is,hps->ihp/dot_general | solution.py:79
  55.3 2.8 %copy.63 = f32[256,1280]{1,0:T(8,128)} copy(f32[256,1280]{0,1:T(8,128)} %bitcast.81) | data formatting | bytes 2621440 | tf_op jit(solution)/shard_map/concatenate | solution.py:149
  58.5 2.8 %fusion.21 = f32[256,20,64]{0,2,1:T(8,128)} fusion(f32[256,20,64]{0,2,1:T(8,128)} %fusion.18, f32[256,20,64]{0,2,1:T(8,128)S(1)} %fusion.37, f32[256,20]{0,1:T(8,128)S(1)} %copy-done.14, bf16[20,64,128]{2,1,0:T(8,128)(2,1)S(1)} %collective-permute-done.1, bf16[20,64,128]{2,1,0:T(8,128)(2,1)S(1)} %collective-permute-done.2, f32[20]{0:T(128)S(1)} %exp.71, ...), kind=kOutput, calls=%fused_computation.34 | convolution fusion | flops 85688320 | bytes 4678144 | tf_op jit(solution)/shard_map/is,hps->ihp/dot_general | solution.py:78
  61.3 2.9 %copy.62 = f32[256,1280]{1,0:T(8,128)} copy(f32[256,1280]{0,1:T(8,128)} %bitcast.80) | data formatting | bytes 2621440 | tf_op jit(solution)/shard_map/concatenate | solution.py:149
  64.2 4.2 %multiply_reduce_fusion = (f32[512]{0:T(512)S(1)}, f32[512,1280]{1,0:T(8,128)}) fusion(bf16[512,1280]{1,0:T(8,128)(2,1)} %param.14, bf16[512,1280]{1,0:T(8,128)(2,1)S(1)} %divide_convert_fusion, f32[1280]{0:T(1024)S(1)} %mul.345, f32[256,1280]{1,0:T(8,128)S(1)} %copy-done.1, f32[256,1280]{1,0:T(8,128)} %copy.62), kind=kLoop, calls=%fused_computation.12 | loop fusion | flops 7208448 | bytes 7871488 | tf_op jit(solution)/shard_map/reduce_sum | solution.py:153
  68.5 5.8 %psum.7 = f32[512]{0:T(512)S(1)} all-reduce(f32[512]{0:T(512)S(1)} %get-tuple-element.14), channel_id=1, replica_groups=mesh['groups'=2,'seq'=4,'tensor'=4] {'tensor'}, use_global_device_ids=true, to_apply=%region_5.6 | all-reduce | flops 512 | bytes 4096 | tf_op jit(solution)/shard_map/psum | solution.py:153
  74.3 2.0 %multiply_convert_fusion.4 = bf16[512,1280]{1,0:T(8,128)(2,1)S(1)} fusion(f32[512,1280]{1,0:T(8,128)} %get-tuple-element.15, f32[1280]{0:T(1024)S(1)} %copy-done.21, f32[512]{0:T(512)S(1)} %add_rsqrt_fusion), kind=kLoop, calls=%fused_computation.11 | loop fusion | flops 1966080 | bytes 3939328 | tf_op jit(solution)/shard_map/convert_element_type | solution.py:157
  76.3 0.9 gather_fusion
  80.2 25.1 %all_to_all.18 = bf16[4,40,1304]{2,1,0:T(8,128)(2,1)S(1)} all-to-all(bf16[4,40,1304]{2,1,0:T(8,128)(2,1)S(1)} %bitcast.87), channel_id=1, replica_groups=mesh['groups'=2,'seq'=4,'tensor'=4] {'seq'}, dimensions={0} | all-to-all | bytes 834560 | tf_op jit(solution)/shard_map/all_to_all | solution.py:191
  (132 shorter events, 13.6 us)
Async XLA Ops:
  0.6 23.2 %copy-start.7 = (bf16[512,256]{1,0:T(8,128)(2,1)S(1)}, bf16[512,256]{1,0:T(8,128)(2,1)}, u32[]{:S(2)}) copy-start(bf16[512,256]{1,0:T(8,128)(2,1)} %param.15) | copy-start | bytes 786436
  0.6 25.3 %copy-start.4 = (bf16[512,1280]{1,0:T(8,128)(2,1)S(1)}, bf16[512,1280]{1,0:T(8,128)(2,1)}, u32[]{:S(2)}) copy-start(bf16[512,1280]{1,0:T(8,128)(2,1)} %param.13) | copy-start | bytes 3932164
  0.7 21.0 %copy-start.18 = (bf16[4,1280]{1,0:T(4,128)(2,1)S(1)}, bf16[4,1280]{1,0:T(4,128)(2,1)}, u32[]{:S(2)}) copy-start(bf16[4,1280]{1,0:T(4,128)(2,1)} %param.19) | copy-start | bytes 30724
  0.7 21.1 %copy-start.17 = (f32[20,512]{1,0:T(8,128)S(1)}, f32[20,512]{1,0:T(8,128)}, u32[]{:S(2)}) copy-start(f32[20,512]{1,0:T(8,128)} %param.16) | copy-start | bytes 122884
  0.7 21.8 %copy-start.22 = (bf16[4,256]{1,0:T(4,128)(2,1)S(1)}, bf16[4,256]{1,0:T(4,128)(2,1)}, u32[]{:S(2)}) copy-start(bf16[4,256]{1,0:T(4,128)(2,1)} %param.20) | copy-start | bytes 6148
  0.7 21.8 %copy-start.28 = (s32[128]{0:T(128)S(1)}, s32[128]{0:T(128)}, u32[]{:S(2)}) copy-start(s32[128]{0:T(128)} %param.22) | copy-start | bytes 1540
  0.7 22.9 %copy-start.26 = (f32[20]{0:T(128)S(1)}, f32[20]{0:T(128)}, u32[]{:S(2)}) copy-start(f32[20]{0:T(128)} %param.18) | copy-start | bytes 244
  2.3 21.5 %collective-permute-start = (bf16[3,1536]{1,0:T(4,128)(2,1)S(1)}, bf16[3,1536]{1,0:T(4,128)(2,1)S(1)}, u32[]{:S(2)}, u32[]{:S(2)}) collective-permute-start(bf16[3,1536]{1,0:T(4,128)(2,1)S(1)} %pad_maximum_fusion.2), channel_id=1, source_target_pairs={{0,4},{4,8},{8,12},{1,5},{5,9},{9,13},{2,6},{6,10},{10,14},{3,7},{... | collective-permute-start | bytes 27656 | tf_op jit(solution)/shard_map/ppermute | solution.py:19
  8.9 17.0 %copy-start.10 = (f32[3,8,2,128]{3,1,2,0:T(8,128)}, f32[3,8,2,128]{3,1,2,0:T(8,128)S(1)}, u32[]{:S(2)}) copy-start(f32[3,8,2,128]{3,1,2,0:T(8,128)S(1)} %copy.77) | copy-start | bytes 73732
  9.9 16.0 %copy-start.12 = (f32[3,8,2,128]{3,1,2,0:T(8,128)}, f32[3,8,2,128]{3,1,2,0:T(8,128)S(1)}, u32[]{:S(2)}) copy-start(f32[3,8,2,128]{3,1,2,0:T(8,128)S(1)} %copy.78) | copy-start | bytes 73732
  10.7 13.0 %collective-permute-start.3 = (f32[20]{0:T(128)S(1)}, f32[20]{0:T(128)S(1)}, u32[]{:S(2)}, u32[]{:S(2)}) collective-permute-start(f32[20]{0:T(128)S(1)} %get-tuple-element.37), channel_id=1, source_target_pairs={{0,4},{4,8},{8,12},{1,5},{5,9},{9,13},{2,6},{6,10},{10,14},{3,7},{... | collective-permute-start | bytes 248 | tf_op jit(solution)/shard_map/ppermute | solution.py:19
  16.9 30.9 %all-to-all-start = ((bf16[4,40,1284]{2,1,0:T(8,128)(2,1)}), bf16[4,40,1284]{2,1,0:T(8,128)(2,1)}, u32[]{:S(2)}, u32[]{:S(2)}) async-start(bf16[4,40,1284]{2,1,0:T(8,128)(2,1)} %broadcast_in_dim.117), calls=%async_computation | async-start | bytes 901120 | tf_op jit(solution)/shard_map/all_to_all | solution.py:110
  29.2 6.2 %copy-start.3 = (bf16[256,1280]{0,1:T(8,128)(2,1)S(1)}, bf16[256,1280]{0,1:T(8,128)(2,1)}, u32[]{:S(2)}) copy-start(bf16[256,1280]{0,1:T(8,128)(2,1)} %copy.61) | copy-start | bytes 1966084
  29.2 6.2 %copy-start.9 = (f32[256,256]{1,0:T(8,128)S(1)}, f32[256,256]{1,0:T(8,128)}, u32[]{:S(2)}) copy-start(f32[256,256]{1,0:T(8,128)} %fusion.58) | copy-start | bytes 786436
  29.2 6.2 %copy-start.13 = (f32[3,8,2,128]{3,1,2,0:T(8,128)S(1)}, f32[3,8,2,128]{3,1,2,0:T(8,128)}, u32[]{:S(2)}) copy-start(f32[3,8,2,128]{3,1,2,0:T(8,128)} %copy-done.12) | copy-start | bytes 73732
  29.2 6.2 %copy-start.16 = (pred[256,256]{1,0:T(8,128)(4,1)S(1)}, pred[256,256]{1,0:T(8,128)(4,1)}, u32[]{:S(2)}) copy-start(pred[256,256]{1,0:T(8,128)(4,1)} %iota_compare_fusion) | copy-start | bytes 196612
  29.3 6.2 %copy-start.20 = (f32[20,256]{1,0:T(8,128)S(1)}, f32[20,256]{1,0:T(8,128)}, u32[]{:S(2)}) copy-start(f32[20,256]{1,0:T(8,128)} %get-tuple-element.23) | copy-start | bytes 61444
  31.5 10.0 %collective-permute-start.1 = (bf16[20,64,128]{2,1,0:T(8,128)(2,1)S(1)}, bf16[20,64,128]{2,1,0:T(8,128)(2,1)S(1)}, u32[]{:S(2)}, u32[]{:S(2)}) collective-permute-start(bf16[20,64,128]{2,1,0:T(8,128)(2,1)S(1)} %get-tuple-element.39), channel_id=1, source_target_pairs={{0,4},{4,8},{8,12},{1,5},{5,9},{9,13},{2,6},{6,10},{10,14},{3,7},{... | collective-permute-start | bytes 983048 | tf_op jit(solution)/shard_map/ppermute | solution.py:19
  35.5 2.9 %copy-start.8 = (f32[256,256]{1,0:T(8,128)S(1)}, f32[256,256]{1,0:T(8,128)}, u32[]{:S(2)}) copy-start(f32[256,256]{1,0:T(8,128)} %fusion.62) | copy-start | bytes 786436
  35.5 2.9 %copy-start.11 = (f32[3,8,2,128]{3,1,2,0:T(8,128)S(1)}, f32[3,8,2,128]{3,1,2,0:T(8,128)}, u32[]{:S(2)}) copy-start(f32[3,8,2,128]{3,1,2,0:T(8,128)} %copy-done.10) | copy-start | bytes 73732
  35.5 2.9 %copy-start.19 = (f32[20,256]{1,0:T(8,128)S(1)}, f32[20,256]{1,0:T(8,128)}, u32[]{:S(2)}) copy-start(f32[20,256]{1,0:T(8,128)} %get-tuple-element.20) | copy-start | bytes 61444
  38.4 3.1 %copy-start.24 = (f32[20]{0:T(128)S(1)}, f32[20]{0:T(128)}, u32[]{:S(2)}) copy-start(f32[20]{0:T(128)} %get-tuple-element.36) | copy-start | bytes 244
  41.3 10.3 %copy-start.27 = (s32[128]{0:T(128)S(1)}, s32[128]{0:T(128)}, u32[]{:S(2)}) copy-start(s32[128]{0:T(128)} %iota_add_fusion) | copy-start | bytes 1540
  41.3 12.1 %copy-start.23 = (f32[20]{0:T(128)S(1)}, f32[20]{0:T(128)}, u32[]{:S(2)}) copy-start(f32[20]{0:T(128)} %get-tuple-element.34) | copy-start | bytes 244
  42.4 11.4 %copy-start.15 = (f32[256,20]{0,1:T(8,128)S(1)}, f32[256,20]{0,1:T(8,128)}, u32[]{:S(2)}) copy-start(f32[256,20]{0,1:T(8,128)} %get-tuple-element.26) | copy-start | bytes 61444
  42.4 11.0 %collective-permute-start.2 = (bf16[20,64,128]{2,1,0:T(8,128)(2,1)}, bf16[20,64,128]{2,1,0:T(8,128)(2,1)S(1)}, u32[]{:S(2)}, u32[]{:S(2)}) collective-permute-start(bf16[20,64,128]{2,1,0:T(8,128)(2,1)} %fusion.28), channel_id=1, source_target_pairs={{0,8},{4,12},{1,9},{5,13},{2,10},{6,14},{3,11},{7,15},{16,24},{20,... | collective-permute-start | bytes 983048 | tf_op jit(solution)/shard_map/ppermute | solution.py:19
  51.3 2.5 %copy-start.5 = (f32[256,20,64]{0,2,1:T(8,128)S(1)}, f32[256,20,64]{0,2,1:T(8,128)}, u32[]{:S(2)}) copy-start(f32[256,20,64]{0,2,1:T(8,128)} %fusion.17) | copy-start | bytes 3932164
  55.3 3.2 %copy-start.14 = (f32[256,20]{0,1:T(8,128)S(1)}, f32[256,20]{0,1:T(8,128)}, u32[]{:S(2)}) copy-start(f32[256,20]{0,1:T(8,128)} %get-tuple-element.27) | copy-start | bytes 61444
  61.3 2.9 %copy-start.1 = (f32[256,1280]{1,0:T(8,128)S(1)}, f32[256,1280]{1,0:T(8,128)}, u32[]{:S(2)}) copy-start(f32[256,1280]{1,0:T(8,128)} %copy.63) | copy-start | bytes 3932164
  64.2 10.1 %copy-start.21 = (f32[1280]{0:T(1024)S(1)}, f32[1280]{0:T(1024)}, u32[]{:S(2)}) copy-start(f32[1280]{0:T(1024)} %param.21) | copy-start | bytes 15364
  76.3 2.1 %copy-start = (bf16[512,1280]{1,0:T(8,128)(2,1)}, bf16[512,1280]{1,0:T(8,128)(2,1)S(1)}, u32[]{:S(2)}) copy-start(bf16[512,1280]{1,0:T(8,128)(2,1)S(1)} %multiply_convert_fusion.4) | copy-start | bytes 3932164
  76.3 1.6 %copy-start.6 = (bf16[160,8,160]{2,1,0:T(8,128)(2,1)S(1)}, bf16[160,8,160]{2,1,0:T(8,128)(2,1)}, u32[]{:S(2)}) copy-start(bf16[160,8,160]{2,1,0:T(8,128)(2,1)} %reshape.231) | copy-start | bytes 1228804
  (2 other events, 3.0 us)

commit v3 on v2

--- a/solution.py
+++ b/solution.py
@@ -73,11 +73,12 @@
 
 
 def read_state(c_block, state_in):
-    state_high = state_in.astype(jnp.bfloat16)
-    state_low = (state_in - state_high.astype(jnp.float32)).astype(jnp.bfloat16)
-    high_part = jnp.einsum("is,hps->ihp", c_block, state_high, preferred_element_type=jnp.float32)
-    low_part = jnp.einsum("is,hps->ihp", c_block, state_low, preferred_element_type=jnp.float32)
-    return high_part + low_part
+    flat = state_in.reshape(-1, state_in.shape[-1])
+    state_high = flat.astype(jnp.bfloat16)
+    state_low = (flat - state_high.astype(jnp.float32)).astype(jnp.bfloat16)
+    high_part = jnp.einsum("is,cs->ic", c_block, state_high, preferred_element_type=jnp.float32)
+    low_part = jnp.einsum("is,cs->ic", c_block, state_low, preferred_element_type=jnp.float32)
+    return (high_part + low_part).reshape(c_block.shape[0], state_in.shape[0], state_in.shape[1])
 
 
 def local(
@@ -106,16 +107,21 @@
     bounds = jnp.stack([pool_start, pool_stop], axis=1)
     bounds_split = jnp.concatenate([bounds // 64, bounds % 64], axis=1).astype(jnp.bfloat16)
     query_rows = jnp.concatenate([pool_query, bounds_split], axis=1)
-    query_rows = jnp.broadcast_to(query_rows[None], (seq_count,) + query_rows.shape)
-    query_rows = lax.all_to_all(
-        query_rows.reshape(seq_count * pools_local, -1), "seq", 0, 0, tiled=True
-    )
+    edge_rows = jnp.concatenate([x_in[tok_rows - rim_rows :], bc_in[tok_rows - rim_rows :]], axis=1)
+    query_width = query_rows.shape[1]
+    payload = jnp.concatenate([query_rows.reshape(-1), edge_rows.reshape(-1)])
+    payload = jnp.broadcast_to(payload[None], (seq_count,) + payload.shape)
+    payload = lax.all_to_all(payload, "seq", 0, 0, tiled=True)
+    query_size = pools_local * query_width
+    query_rows = payload[:, :query_size].reshape(seq_count * pools_local, query_width)
     queries_all = query_rows[:, :channels]
     bounds_all = query_rows[:, channels:].astype(jnp.int32)
     start_all = bounds_all[:, 0] * 64 + bounds_all[:, 2]
     stop_all = bounds_all[:, 1] * 64 + bounds_all[:, 3]
-    edge_rows = jnp.concatenate([x_in[tok_rows - rim_rows :], bc_in[tok_rows - rim_rows :]], axis=1)
-    before = passed_along(edge_rows, "seq", 1)
+    place = lax.axis_index("seq")
+    edges_all = payload[:, query_size:].reshape(seq_count, rim_rows, edge_rows.shape[1])
+    before = lax.dynamic_index_in_dim(edges_all, jnp.maximum(place - 1, 0), 0, False)
+    before = jnp.where(place > 0, before, jnp.zeros_like(before))
     x_conv = causal_conv(before[:, :channels], x_in, conv_x)
     bc_conv = causal_conv(before[:, channels:], bc_in, conv_bc)
     b_mat = bc_conv[:, :state_width]
@@ -138,6 +144,10 @@
         saved_parts.append((intra_part, cumul_keep, entry_state, decay_total))
         entry_state = jnp.exp(cumul_keep[:, -1])[:, None, None] * entry_state + stretch_state
         decay_total = decay_total + cumul_keep[:, -1]
+    base = jnp.concatenate([part[0] for part in saved_parts], axis=0) + skip_gain[
+        None, :, None
+    ] * x_heads.astype(jnp.float32)
+    base = lax.optimization_barrier(base.reshape(tok_rows, channels))
     incoming = exclusive_scan(entry_state, decay_total, "seq")
     pieces_out = []
     for block_index in range(stretch_count):
@@ -145,10 +155,10 @@
         first_row = block_index * STRETCH
         state_in = entry_part + jnp.exp(decay_part)[:, None, None] * incoming
         from_state = read_state(c_mat[first_row : first_row + STRETCH], state_in)
-        pieces_out.append(intra_part + jnp.exp(cumul_keep).T[:, :, None] * from_state)
-    ssd_out = jnp.concatenate(pieces_out, axis=0) + skip_gain[None, :, None] * x_heads.astype(
-        jnp.float32
-    )
+        pieces_out.append(
+            (jnp.exp(cumul_keep).T[:, :, None] * from_state).reshape(STRETCH, channels)
+        )
+    ssd_out = jnp.concatenate(pieces_out, axis=0) + base
     gated = ssd_out.reshape(tok_rows, channels) * silu_act(z_gate.astype(jnp.float32))
     square_sum = lax.psum(jnp.sum(gated * gated, axis=1), "tensor")
     width_all = channels * lax.axis_size("tensor")

time: 109 us -> 124 us (1.14)
  local copies, waits for them, and re-layouts: 18.6 us -> 31.8 us
  other arithmetic: 17.2 us -> 22.1 us
  starting transfers between devices: 21.9 us -> 17.1 us
  waiting for transfers between devices: 1.88 us -> 4.95 us
    ppermute x4 -> x3, starting transfers between devices: 17.8 us -> 10.8 us  [passed_along(): lax.ppermute(value, axis, [(source, source + steps) for source in range(l...]
    unnamed x62 -> x59, local copies, waits for them, and re-layouts: 0.59 us -> 5.56 us
    dot_general x4, matrix products: 5.01 us -> 1.32 us  [the longest x2 0.67 us: read_state(): jnp.einsum('is,cs->ic', c_block, state_low, preferred_element_type=jnp.fl...]
    broadcast_in_dim x0 -> x1, other arithmetic: none -> 3.53 us  [local(): payload = jnp.broadcast_to(payload[None], (seq_count,) + payload.shape)]
    add x0 -> x2, other arithmetic: none -> 3.04 us  [the longest x1 1.82 us: local(): jnp.concatenate([part[0] for part in saved_parts], axis=0)]
    slice x3, local copies, waits for them, and re-layouts: 1.4 us -> 4.18 us  [local(): x_heads[first_row:last_row]]
    ppermute x4 -> x3, waiting for transfers between devices: 1.88 us -> 4.28 us  [passed_along(): lax.ppermute(value, axis, [(source, source + steps) for source in range(l...]
    all_to_all x1, starting transfers between devices: 4.13 us -> 6.35 us  [local(): payload = lax.all_to_all(payload, 'seq', 0, 0, tiled=True)]
  transfers between devices with their start and end apart: 5 -> 4, of which waited for: 2 -> 2; matrix products, arithmetic and copies ran while one was open for 25% -> 14% of each run, Pallas kernels for 0% -> 0%
where the time goes in v3:
time: 124 us; the launch traced here: 123 us
  local copies, waits for them, and re-layouts  31.8 us (26%)
  blocking collectives  29.9 us (24%)
  other arithmetic  22.1 us (18%)
  starting transfers between devices  17.1 us (14%)
  matrix products  16.1 us (13%)
  waiting for transfers between devices  4.95 us (4%)
  between operations  1.3 us (1%)
    all_to_all x1, blocking collectives, local(): parts = lax.all_to_all(parts, 'seq', 0, 0, tiled=True).astype(jnp.float32)  24.1 us
    ppermute x3, starting transfers between devices, passed_along(): lax.ppermute(value, axis, [(source, source + steps) for source in range(l...  10.8 us
    dot_general x2, matrix products, stretch_local(): jnp.einsum('hij,jhp->ihp', mixing, x_block, preferred_element_type=jnp.fl...  8.02 us
    all_to_all x1, starting transfers between devices, local(): payload = lax.all_to_all(payload, 'seq', 0, 0, tiled=True)  6.35 us
    psum x1, blocking collectives, local(): square_sum = lax.psum(jnp.sum(gated * gated, axis=1), 'tensor')  5.85 us
    concatenate x2, local copies, waits for them, and re-layouts, local(): jnp.concatenate([part[0] for part in saved_parts], axis=0)  5.58 us
    unnamed x59, local copies, waits for them, and re-layouts  5.56 us
    ppermute x3, waiting for transfers between devices, passed_along(): lax.ppermute(value, axis, [(source, source + steps) for source in range(l...  4.28 us
  transfers between devices with their start and end apart: 4, of which 2 were waited for; matrix products, arithmetic and copies ran while one was open for 14% of the time, Pallas kernels for 0%

profile of v3, /device:TPU:0, one launch (start us, length us, event | category | flops | bytes accessed | tf_op | source)
XLA Modules:
  0.0 123.3 jit_solution(16082110591801562320)
XLA Ops:
  3.0 1.0 concatenate.32
  5.3 3.5 %reduce.22 = bf16[4,55968]{1,0:T(4,128)(2,1)S(1)} reduce(bf16[4,1,55968]{2,1,0:T(2,128)(2,1)S(1)} %broadcast_in_dim.66, bf16[]{:T(256)} %broadcast.166), dimensions={1}, to_apply=%broadcast_in_dim.66.reduce_sub_computation | reduce | bytes 895490 | tf_op jit(solution)/shard_map/broadcast_in_dim | solution.py:113
  8.8 1.2 reshape.296
  10.1 6.3 %all-to-all-start = ((bf16[4,2,27984]{2,1,0:T(2,128)(2,1)}), bf16[4,2,27984]{2,1,0:T(2,128)(2,1)S(1)}, u32[]{:S(2)}, u32[]{:S(2)}) async-start(bf16[4,2,27984]{2,1,0:T(2,128)(2,1)} %reshape.296), calls=%async_computation | async-start | bytes 897024 | tf_op jit(solution)/shard_map/all_to_all | solution.py:114
  19.2 4.1 %collective-permute-start.2 = (f32[20]{0:T(128)S(1)}, f32[20]{0:T(128)S(1)}, u32[]{:S(2)}, u32[]{:S(2)}) collective-permute-start(f32[20]{0:T(128)S(1)} %get-tuple-element.23), channel_id=1, source_target_pairs={{0,4},{4,8},{8,12},{1,5},{5,9},{9,13},{2,6},{6,10},{10,14},{3,7},{... | collective-permute-start | bytes 248 | tf_op jit(solution)/shard_map/ppermute | solution.py:19
  26.6 1.5 %copy.98 = f32[256,1280]{1,0:T(8,128)} copy(f32[256,1280]{0,1:T(8,128)S(1)} %bitcast.94) | data formatting | bytes 2621440 | tf_op jit(solution)/shard_map/mul | solution.py:159
  29.3 1.7 %reshape.297 = bf16[4,1,55968]{2,1,0:T(2,128)(2,1)S(1)} reshape(bf16[4,2,27984]{2,1,0:T(2,128)(2,1)S(1)} %all-to-all-done) | data formatting | bytes 895488
  31.8 0.9 fusion.44
  32.7 0.9 fusion.47
  33.6 1.8 %divide_convert_fusion = bf16[512,1280]{1,0:T(8,128)(2,1)S(1)} fusion(bf16[512,1280]{1,0:T(8,128)(2,1)S(1)} %copy-done.8, bf16[3,1280]{1,0:T(4,128)(2,1)S(1)} %slice.221, f32[1280]{0:T(1024)S(1)} %get-tuple-element.6, f32[1280]{0:T(1024)S(1)} %get-tuple-element.7, f32[1280]{0:T(1024)S(1)} %get-tuple-element.5, f32[1280]{0:T(1024)S(1)} %get-tuple-element.4), kind=kLoop, calls=%fused_computation.28 | loop fusion | flops 15728640 | bytes 2649600 | tf_op jit(solution)/shard_map/convert_element_type | solution.py:35
  35.4 0.9 fusion.74
  36.3 2.2 %copy.97 = bf16[256,1280]{0,1:T(8,128)(2,1)} copy(bf16[256,1280]{1,0:T(8,128)(2,1)} %get-tuple-element.25) | data formatting | bytes 1310720 | tf_op jit(solution)/shard_map/slice | solution.py:138
  38.5 4.0 %fusion.3 = f32[20,64,256]{2,1,0:T(8,128)} fusion(bf16[256,20,64]{0,2,1:T(8,128)(2,1)} %bitcast.98, f32[20,256]{1,0:T(8,128)} %get-tuple-element.28, f32[256,256]{1,0:T(8,128)} %fusion.44, f32[20,256]{1,0:T(8,128)} %bitcast.111, pred[256,256]{1,0:T(8,128)(4,1)} %iota_compare_fusion), kind=kOutput, calls=%fused_computation.10 | convolution fusion | flops 175636480 | bytes 2334720 | tf_op jit(solution)/shard_map/hij,jhp->ihp/dot_general | solution.py:48
  42.5 2.8 %copy.101 = f32[256,1280]{1,0:T(8,128)} copy(f32[256,1280]{0,1:T(8,128)} %bitcast.104) | data formatting | bytes 2621440 | tf_op jit(solution)/shard_map/concatenate | solution.py:147
  45.3 1.1 copy.96
  46.4 4.0 %fusion.2 = f32[20,64,256]{2,1,0:T(8,128)} fusion(bf16[256,20,64]{0,2,1:T(8,128)(2,1)} %bitcast.95, f32[20,256]{1,0:T(8,128)} %get-tuple-element.29, f32[256,256]{1,0:T(8,128)} %fusion.47, f32[20,256]{1,0:T(8,128)} %bitcast.114, pred[256,256]{1,0:T(8,128)(4,1)} %iota_compare_fusion), kind=kOutput, calls=%fused_computation.9 | convolution fusion | flops 175636480 | bytes 2334720 | tf_op jit(solution)/shard_map/hij,jhp->ihp/dot_general | solution.py:48
  50.4 2.8 %copy.100 = f32[256,1280]{1,0:T(8,128)} copy(f32[256,1280]{0,1:T(8,128)} %bitcast.103) | data formatting | bytes 2621440 | tf_op jit(solution)/shard_map/concatenate | solution.py:147
  53.2 1.6 %convolution_add_fusion.3 = f32[20,64,128]{2,1,0:T(8,128)S(1)} fusion(bf16[256,20,64]{0,2,1:T(8,128)(2,1)} %bitcast.96, f32[256,20]{0,1:T(8,128)} %get-tuple-element.27, f32[20]{0:T(128)S(1)} %get-tuple-element.41, bf16[512,256]{1,0:T(8,128)(2,1)S(1)} %divide_convert_fusion.1), kind=kOutput, calls=%fused_computation.41 | convolution fusion | flops 85032960 | bytes 1397248 | tf_op jit(solution)/shard_map/jhp,js->hps/dot_general | solution.py:51
  54.8 2.4 %fusion.76 = (bf16[20,64,128]{2,1,0:T(8,128)(2,1)}, f32[20,64,128]{2,1,0:T(8,128)}) fusion(bf16[512,256]{1,0:T(8,128)(2,1)S(1)} %divide_convert_fusion.1, bf16[256,20,64]{0,2,1:T(8,128)(2,1)} %bitcast.99, f32[256,20]{0,1:T(8,128)} %get-tuple-element.26, f32[20,64,128]{2,1,0:T(8,128)S(1)} %convolution_add_fusion.3, f32[20]{0:T(128)} %get-tuple-element.40), kind=kOutput, calls=%fused_computation.159 | convolution fusion | flops 85360640 | bytes 2379856 | tf_op jit(solution)/shard_map/jhp,js->hps/dot_general | solution.py:51
  57.2 3.6 %collective-permute-start = (bf16[20,64,128]{2,1,0:T(8,128)(2,1)}, bf16[20,64,128]{2,1,0:T(8,128)(2,1)}, u32[]{:S(2)}, u32[]{:S(2)}) collective-permute-start(bf16[20,64,128]{2,1,0:T(8,128)(2,1)} %get-tuple-element.43), channel_id=1, source_target_pairs={{0,4},{4,8},{8,12},{1,5},{5,9},{9,13},{2,6},{6,10},{10,14},{3,7},{... | collective-permute-start | bytes 983048 | tf_op jit(solution)/shard_map/ppermute | solution.py:19
  60.7 1.8 %maximum_add_fusion.1 = f32[512,1280]{1,0:T(8,128)} fusion(f32[256,1280]{1,0:T(8,128)S(1)} %copy-done.3, f32[256,1280]{1,0:T(8,128)S(1)} %copy-done.4, bf16[512,1280]{1,0:T(8,128)(2,1)S(1)} %divide_convert_fusion, f32[1280]{0:T(1024)S(1)} %mul.353), kind=kLoop, calls=%fused_computation.15 | loop fusion | flops 2621440 | bytes 6558720 | tf_op jit(solution)/shard_map/add | solution.py:147
  63.5 1.7 %reshape.264 = bf16[160,1284]{1,0:T(8,128)(2,1)S(1)} reshape(bf16[4,51360]{1,0:T(4,128)(2,1)} %slice.231) | data formatting | bytes 821760 | tf_op jit(solution)/shard_map/reshape | solution.py:116
  65.9 2.7 %reshape.265 = bf16[160,8,160]{2,1,0:T(8,128)(2,1)} reshape(bf16[160,1280]{1,0:T(8,128)(2,1)} %slice.237) | data formatting | bytes 819200 | tf_op jit(solution)/shard_map/reshape | solution.py:175
  68.6 1.1 fusion.24
  69.8 3.1 %collective-permute-start.1 = (bf16[20,64,128]{2,1,0:T(8,128)(2,1)S(1)}, bf16[20,64,128]{2,1,0:T(8,128)(2,1)S(1)}, u32[]{:S(2)}, u32[]{:S(2)}) collective-permute-start(bf16[20,64,128]{2,1,0:T(8,128)(2,1)S(1)} %fusion.24), channel_id=1, source_target_pairs={{0,8},{4,12},{1,9},{5,13},{2,10},{6,14},{3,11},{7,15},{16,24},{20,... | collective-permute-start | bytes 983048 | tf_op jit(solution)/shard_map/ppermute | solution.py:19
  73.9 4.3 %collective-permute-done.1 = bf16[20,64,128]{2,1,0:T(8,128)(2,1)S(1)} collective-permute-done((bf16[20,64,128]{2,1,0:T(8,128)(2,1)S(1)}, bf16[20,64,128]{2,1,0:T(8,128)(2,1)S(1)}, u32[]{:S(2)}, u32[]{:S(2)}) %collective-permute-start.1) | collective-permute-done | bytes 327712 | tf_op jit(solution)/shard_map/ppermute | solution.py:19
  78.2 1.2 multiply_add_fusion
  82.8 2.4 %multiply_reduce_fusion = (f32[512]{0:T(512)S(1)}, f32[512,1280]{1,0:T(8,128)}) fusion(bf16[512,1280]{1,0:T(8,128)(2,1)S(1)} %copy-done.9, f32[512,1280]{1,0:T(8,128)S(1)} %copy-done.1, f32[256,1280]{1,0:T(8,128)S(1)} %fusion.1, f32[256,1280]{1,0:T(8,128)S(1)} %fusion), kind=kLoop, calls=%fused_computation.17 | loop fusion | flops 5897728 | bytes 9177088 | tf_op jit(solution)/shard_map/reduce_sum | solution.py:163
  85.2 5.9 %psum.7 = f32[512]{0:T(512)S(1)} all-reduce(f32[512]{0:T(512)S(1)} %get-tuple-element.14), channel_id=1, replica_groups=mesh['groups'=2,'seq'=4,'tensor'=4] {'tensor'}, use_global_device_ids=true, to_apply=%region_5.6 | all-reduce | flops 512 | bytes 4096 | tf_op jit(solution)/shard_map/psum | solution.py:163
  91.0 2.0 %multiply_convert_fusion.4 = bf16[512,1280]{1,0:T(8,128)(2,1)S(1)} fusion(f32[512,1280]{1,0:T(8,128)} %get-tuple-element.15, f32[1280]{0:T(1024)S(1)} %copy-done.18, f32[512]{0:T(512)S(1)} %add_rsqrt_fusion), kind=kLoop, calls=%fused_computation.16 | loop fusion | flops 1966080 | bytes 3939328 | tf_op jit(solution)/shard_map/convert_element_type | solution.py:167
  93.1 0.9 gather_fusion
  97.0 24.1 %all_to_all.18 = bf16[4,40,1304]{2,1,0:T(8,128)(2,1)S(1)} all-to-all(bf16[4,40,1304]{2,1,0:T(8,128)(2,1)S(1)} %bitcast.100), channel_id=1, replica_groups=mesh['groups'=2,'seq'=4,'tensor'=4] {'seq'}, dimensions={0} | all-to-all | bytes 834560 | tf_op jit(solution)/shard_map/all_to_all | solution.py:201
  (145 shorter events, 22.7 us)
Async XLA Ops:
  0.6 15.8 %copy-start.15 = (f32[20,512]{1,0:T(8,128)S(1)}, f32[20,512]{1,0:T(8,128)}, u32[]{:S(2)}) copy-start(f32[20,512]{1,0:T(8,128)} %param.17) | copy-start | bytes 122884
  4.2 19.1 %copy-start.16 = (f32[20,512]{1,0:T(8,128)S(1)}, f32[20,512]{1,0:T(8,128)}, u32[]{:S(2)}) copy-start(f32[20,512]{1,0:T(8,128)} %param.16) | copy-start | bytes 122884
  4.3 19.7 %copy-start.23 = (f32[20]{0:T(128)S(1)}, f32[20]{0:T(128)}, u32[]{:S(2)}) copy-start(f32[20]{0:T(128)} %param.18) | copy-start | bytes 244
  10.1 19.2 %all-to-all-start = ((bf16[4,2,27984]{2,1,0:T(2,128)(2,1)}), bf16[4,2,27984]{2,1,0:T(2,128)(2,1)S(1)}, u32[]{:S(2)}, u32[]{:S(2)}) async-start(bf16[4,2,27984]{2,1,0:T(2,128)(2,1)} %reshape.296), calls=%async_computation | async-start | bytes 897024 | tf_op jit(solution)/shard_map/all_to_all | solution.py:114
  16.4 8.3 %copy-start.25 = (s32[128]{0:T(128)S(1)}, s32[128]{0:T(128)}, u32[]{:S(2)}) copy-start(s32[128]{0:T(128)} %param.22) | copy-start | bytes 1540
  16.4 10.0 %copy-start.17 = (bf16[4,1280]{1,0:T(4,128)(2,1)S(1)}, bf16[4,1280]{1,0:T(4,128)(2,1)}, u32[]{:S(2)}) copy-start(bf16[4,1280]{1,0:T(4,128)(2,1)} %param.19) | copy-start | bytes 30724
  16.4 10.0 %copy-start.19 = (bf16[4,256]{1,0:T(4,128)(2,1)S(1)}, bf16[4,256]{1,0:T(4,128)(2,1)}, u32[]{:S(2)}) copy-start(bf16[4,256]{1,0:T(4,128)(2,1)} %param.20) | copy-start | bytes 6148
  17.4 6.9 %copy-start.13 = (f32[3,8,2,128]{3,1,2,0:T(8,128)}, f32[3,8,2,128]{3,1,2,0:T(8,128)S(1)}, u32[]{:S(2)}) copy-start(f32[3,8,2,128]{3,1,2,0:T(8,128)S(1)} %copy.116) | copy-start | bytes 73732
  18.4 5.9 %copy-start.14 = (f32[3,8,2,128]{3,1,2,0:T(8,128)}, f32[3,8,2,128]{3,1,2,0:T(8,128)S(1)}, u32[]{:S(2)}) copy-start(f32[3,8,2,128]{3,1,2,0:T(8,128)S(1)} %copy.115) | copy-start | bytes 73732
  19.2 8.9 %collective-permute-start.2 = (f32[20]{0:T(128)S(1)}, f32[20]{0:T(128)S(1)}, u32[]{:S(2)}, u32[]{:S(2)}) collective-permute-start(f32[20]{0:T(128)S(1)} %get-tuple-element.23), channel_id=1, source_target_pairs={{0,4},{4,8},{8,12},{1,5},{5,9},{9,13},{2,6},{6,10},{10,14},{3,7},{... | collective-permute-start | bytes 248 | tf_op jit(solution)/shard_map/ppermute | solution.py:19
  26.6 4.9 %copy-start.11 = (bf16[512,256]{1,0:T(8,128)(2,1)S(1)}, bf16[512,256]{1,0:T(8,128)(2,1)}, u32[]{:S(2)}) copy-start(bf16[512,256]{1,0:T(8,128)(2,1)} %param.15) | copy-start | bytes 786436
  31.0 2.6 %copy-start.8 = (bf16[512,1280]{1,0:T(8,128)(2,1)S(1)}, bf16[512,1280]{1,0:T(8,128)(2,1)}, u32[]{:S(2)}) copy-start(bf16[512,1280]{1,0:T(8,128)(2,1)} %param.13) | copy-start | bytes 3932164
  31.2 2.4 %copy-start.6 = (bf16[4,1,55968]{2,0,1:T(4,128)(2,1)}, bf16[4,1,55968]{2,0,1:T(4,128)(2,1)S(1)}, u32[]{:S(2)}) copy-start(bf16[4,1,55968]{2,0,1:T(4,128)(2,1)S(1)} %copy.125) | copy-start | bytes 1343236
  53.2 7.6 %copy-start.3 = (f32[256,1280]{1,0:T(8,128)S(1)}, f32[256,1280]{1,0:T(8,128)}, u32[]{:S(2)}) copy-start(f32[256,1280]{1,0:T(8,128)} %copy.101) | copy-start | bytes 3932164
  53.2 7.6 %copy-start.4 = (f32[256,1280]{1,0:T(8,128)S(1)}, f32[256,1280]{1,0:T(8,128)}, u32[]{:S(2)}) copy-start(f32[256,1280]{1,0:T(8,128)} %copy.100) | copy-start | bytes 3932164
  57.2 5.4 %copy-start.7 = (bf16[4,1,55968]{2,0,1:T(4,128)(2,1)S(1)}, bf16[4,1,55968]{2,0,1:T(4,128)(2,1)}, u32[]{:S(2)}) copy-start(bf16[4,1,55968]{2,0,1:T(4,128)(2,1)} %copy-done.6) | copy-start | bytes 1343236
  57.2 11.4 %collective-permute-start = (bf16[20,64,128]{2,1,0:T(8,128)(2,1)}, bf16[20,64,128]{2,1,0:T(8,128)(2,1)}, u32[]{:S(2)}, u32[]{:S(2)}) collective-permute-start(bf16[20,64,128]{2,1,0:T(8,128)(2,1)} %get-tuple-element.43), channel_id=1, source_target_pairs={{0,4},{4,8},{8,12},{1,5},{5,9},{9,13},{2,6},{6,10},{10,14},{3,7},{... | collective-permute-start | bytes 983048 | tf_op jit(solution)/shard_map/ppermute | solution.py:19
  62.6 6.0 %copy-start.5 = (f32[20,64,128]{2,1,0:T(8,128)S(1)}, f32[20,64,128]{2,1,0:T(8,128)}, u32[]{:S(2)}) copy-start(f32[20,64,128]{2,1,0:T(8,128)} %get-tuple-element.44) | copy-start | bytes 1966084
  62.6 6.1 %copy-start.21 = (f32[20]{0:T(128)S(1)}, f32[20]{0:T(128)}, u32[]{:S(2)}) copy-start(f32[20]{0:T(128)} %get-tuple-element.22) | copy-start | bytes 244
  62.6 10.6 %copy-start.24 = (s32[128]{0:T(128)S(1)}, s32[128]{0:T(128)}, u32[]{:S(2)}) copy-start(s32[128]{0:T(128)} %iota_add_fusion) | copy-start | bytes 1540
  62.6 15.6 %copy-start.20 = (f32[20]{0:T(128)S(1)}, f32[20]{0:T(128)}, u32[]{:S(2)}) copy-start(f32[20]{0:T(128)} %get-tuple-element.42) | copy-start | bytes 244
  69.8 8.4 %collective-permute-start.1 = (bf16[20,64,128]{2,1,0:T(8,128)(2,1)S(1)}, bf16[20,64,128]{2,1,0:T(8,128)(2,1)S(1)}, u32[]{:S(2)}, u32[]{:S(2)}) collective-permute-start(bf16[20,64,128]{2,1,0:T(8,128)(2,1)S(1)} %fusion.24), channel_id=1, source_target_pairs={{0,8},{4,12},{1,9},{5,13},{2,10},{6,14},{3,11},{7,15},{16,24},{20,... | collective-permute-start | bytes 983048 | tf_op jit(solution)/shard_map/ppermute | solution.py:19
  79.9 1.3 %copy-start.2 = (f32[256,1280]{1,0:T(8,128)S(1)}, f32[256,1280]{1,0:T(8,128)}, u32[]{:S(2)}) copy-start(f32[256,1280]{1,0:T(8,128)} %copy.98) | copy-start | bytes 3932164
  80.6 1.8 %copy-start.1 = (f32[512,1280]{1,0:T(8,128)S(1)}, f32[512,1280]{1,0:T(8,128)}, u32[]{:S(2)}) copy-start(f32[512,1280]{1,0:T(8,128)} %maximum_add_fusion.1) | copy-start | bytes 7864324
  80.6 2.2 %copy-start.9 = (bf16[512,1280]{1,0:T(8,128)(2,1)S(1)}, bf16[512,1280]{1,0:T(8,128)(2,1)}, u32[]{:S(2)}) copy-start(bf16[512,1280]{1,0:T(8,128)(2,1)} %param.14) | copy-start | bytes 3932164
  82.8 8.2 %copy-start.18 = (f32[1280]{0:T(1024)S(1)}, f32[1280]{0:T(1024)}, u32[]{:S(2)}) copy-start(f32[1280]{0:T(1024)} %param.21) | copy-start | bytes 15364
  93.0 2.2 %copy-start = (bf16[512,1280]{1,0:T(8,128)(2,1)}, bf16[512,1280]{1,0:T(8,128)(2,1)S(1)}, u32[]{:S(2)}) copy-start(bf16[512,1280]{1,0:T(8,128)(2,1)S(1)} %multiply_convert_fusion.4) | copy-start | bytes 3932164
  93.1 1.6 %copy-start.10 = (bf16[160,8,160]{2,1,0:T(8,128)(2,1)S(1)}, bf16[160,8,160]{2,1,0:T(8,128)(2,1)}, u32[]{:S(2)}) copy-start(bf16[160,8,160]{2,1,0:T(8,128)(2,1)} %reshape.265) | copy-start | bytes 1228804
  93.1 1.6 %copy-start.12 = (pred[160,128]{1,0:T(8,128)(4,1)S(1)}, pred[160,128]{1,0:T(8,128)(4,1)}, u32[]{:S(2)}) copy-start(pred[160,128]{1,0:T(8,128)(4,1)} %compare_and_fusion) | copy-start | bytes 61444
  93.1 1.5 %copy-start.22 = (pred[128]{0:T(512)(128)(4,1)S(1)}, pred[128]{0:T(512)(128)(4,1)}, u32[]{:S(2)}) copy-start(pred[128]{0:T(512)(128)(4,1)} %get-tuple-element.12) | copy-start | bytes 388

commit v4 on v3

--- a/solution.py
+++ b/solution.py
@@ -56,7 +56,7 @@
     return (earlier[0] * jnp.exp(later[1])[:, None, None] + later[0], earlier[1] + later[1])
 
 
-def exclusive_scan(state, decay, axis):
+def exclusive_scan(state, decay, axis, rider):
     count = lax.axis_size(axis)
     window = (state, decay)
     before = (jnp.zeros_like(state), jnp.zeros_like(decay))
@@ -64,12 +64,14 @@
     while shift < count:
         sent_state = passed_along(window[0].astype(jnp.bfloat16), axis, shift)
         sent_decay = passed_along(window[1], axis, shift)
+        if shift == 1:
+            sent_state, rider = lax.optimization_barrier((sent_state, rider))
         received = (sent_state.astype(jnp.float32), sent_decay)
         before = combine(received, before)
         if shift * 2 < count:
             window = combine(received, window)
         shift *= 2
-    return before[0]
+    return before[0], rider
 
 
 def read_state(c_block, state_in):
@@ -134,24 +136,41 @@
     for block_index in range(stretch_count):
         first_row = block_index * STRETCH
         last_row = first_row + STRETCH
-        intra_part, stretch_state, cumul_keep = stretch_local(
-            x_heads[first_row:last_row],
-            b_mat[first_row:last_row],
-            c_mat[first_row:last_row],
-            step_size[:, first_row:last_row],
-            log_keep[:, first_row:last_row],
+        cumul_keep = jnp.cumsum(log_keep[:, first_row:last_row], axis=1)
+        step_block = step_size[:, first_row:last_row]
+        tail_weight = jnp.exp(cumul_keep[:, -1:] - cumul_keep) * step_block
+        weighted = (
+            tail_weight.T[:, :, None] * x_heads[first_row:last_row].astype(jnp.float32)
+        ).astype(jnp.bfloat16)
+        stretch_state = jnp.einsum(
+            "jhp,js->hps", weighted, b_mat[first_row:last_row], preferred_element_type=jnp.float32
         )
-        saved_parts.append((intra_part, cumul_keep, entry_state, decay_total))
+        saved_parts.append((cumul_keep, entry_state, decay_total))
         entry_state = jnp.exp(cumul_keep[:, -1])[:, None, None] * entry_state + stretch_state
         decay_total = decay_total + cumul_keep[:, -1]
-    base = jnp.concatenate([part[0] for part in saved_parts], axis=0) + skip_gain[
-        None, :, None
-    ] * x_heads.astype(jnp.float32)
+    incoming, rider = exclusive_scan(
+        entry_state, decay_total, "seq", (x_heads, b_mat, c_mat, step_size, log_keep)
+    )
+    x_late, b_late, c_late, step_late, keep_late = rider
+    intra_parts = []
+    for block_index in range(stretch_count):
+        first_row = block_index * STRETCH
+        last_row = first_row + STRETCH
+        intra_part, unused_state, unused_cumul = stretch_local(
+            x_late[first_row:last_row],
+            b_late[first_row:last_row],
+            c_late[first_row:last_row],
+            step_late[:, first_row:last_row],
+            keep_late[:, first_row:last_row],
+        )
+        intra_parts.append(intra_part)
+    base = jnp.concatenate(intra_parts, axis=0) + skip_gain[None, :, None] * x_late.astype(
+        jnp.float32
+    )
     base = lax.optimization_barrier(base.reshape(tok_rows, channels))
-    incoming = exclusive_scan(entry_state, decay_total, "seq")
     pieces_out = []
     for block_index in range(stretch_count):
-        intra_part, cumul_keep, entry_part, decay_part = saved_parts[block_index]
+        cumul_keep, entry_part, decay_part = saved_parts[block_index]
         first_row = block_index * STRETCH
         state_in = entry_part + jnp.exp(decay_part)[:, None, None] * incoming
         from_state = read_state(c_mat[first_row : first_row + STRETCH], state_in)

time: 124 us -> 121 us (0.976)
  other arithmetic: 22.1 us -> 29.1 us
  waiting for transfers between devices: 4.95 us -> 0.01 us
  matrix products: 16.1 us -> 12.2 us
  blocking collectives: 29.9 us -> 26.3 us
  starting transfers between devices: 17.1 us -> 19.4 us
    concatenate x2 -> x0, local copies, waits for them, and re-layouts: 5.58 us -> none  [local(): jnp.concatenate([part[0] for part in saved_parts], axis=0)]
    convert_element_type x0 -> x3, local copies, waits for them, and re-layouts: none -> 5.18 us  [the longest x2 4.54 us: local(): x_heads[first_row:last_row].astype(jnp.float32)]
    ppermute x3, waiting for transfers between devices: 4.28 us -> 0.01 us  [passed_along(): lax.ppermute(value, axis, [(source, source + steps) for source in range(l...]
    dot_general x2, matrix products: 8.02 us -> 4.35 us  [stretch_local(): jnp.einsum('hij,jhp->ihp', mixing, x_block, preferred_element_type=jnp.fl...]
    slice x5, local copies, waits for them, and re-layouts: 4.34 us -> 0.81 us  [the longest x1 0.62 us: local(): step_late[:, first_row:last_row]]
    all_to_all x1, blocking collectives: 24.1 us -> 20.6 us  [local(): parts = lax.all_to_all(parts, 'seq', 0, 0, tiled=True).astype(jnp.float32)]
    ppermute x3, starting transfers between devices: 10.8 us -> 13.1 us  [passed_along(): lax.ppermute(value, axis, [(source, source + steps) for source in range(l...]
    optimization_barrier x0 -> x1, local copies, waits for them, and re-layouts: none -> 2.15 us  [local(): base = lax.optimization_barrier(base.reshape(tok_rows, channels))]
  transfers between devices with their start and end apart: 4 -> 4, of which waited for: 2 -> 0; matrix products, arithmetic and copies ran while one was open for 14% -> 20% of each run, Pallas kernels for 0% -> 0%
where the time goes in v4:
time: 121 us; the launch traced here: 120 us
  local copies, waits for them, and re-layouts  31.5 us (26%)
  other arithmetic  29.1 us (24%)
  blocking collectives  26.3 us (22%)
  starting transfers between devices  19.4 us (16%)
  matrix products  12.2 us (10%)
  between operations  1.39 us (1%)
    all_to_all x1, blocking collectives, local(): parts = lax.all_to_all(parts, 'seq', 0, 0, tiled=True).astype(jnp.float32)  20.6 us
    ppermute x3, starting transfers between devices, passed_along(): lax.ppermute(value, axis, [(source, source + steps) for source in range(l...  13.1 us
    unnamed x67, local copies, waits for them, and re-layouts  6.37 us
    all_to_all x1, starting transfers between devices, local(): payload = lax.all_to_all(payload, 'seq', 0, 0, tiled=True)  6.35 us
    psum x1, blocking collectives, local(): square_sum = lax.psum(jnp.sum(gated * gated, axis=1), 'tensor')  5.63 us
    convert_element_type x2, local copies, waits for them, and re-layouts, local(): x_heads[first_row:last_row].astype(jnp.float32)  4.54 us
    dot_general x2, matrix products, stretch_local(): jnp.einsum('hij,jhp->ihp', mixing, x_block, preferred_element_type=jnp.fl...  4.35 us
    convert_element_type x2, other arithmetic, causal_conv(): return silu_act(summed).astype(jnp.bfloat16)  4.29 us
  transfers between devices with their start and end apart: 4, of which 0 were waited for; matrix products, arithmetic and copies ran while one was open for 20% of the time, Pallas kernels for 0%

profile of v4, /device:TPU:0, one launch (start us, length us, event | category | flops | bytes accessed | tf_op | source)
XLA Modules:
  0.0 119.9 jit_solution(6349732159716406702)
XLA Ops:
  3.0 1.0 concatenate.27
  5.3 3.5 %reduce.26 = bf16[4,55968]{1,0:T(4,128)(2,1)S(1)} reduce(bf16[4,1,55968]{2,1,0:T(2,128)(2,1)S(1)} %broadcast_in_dim.66, bf16[]{:T(256)} %broadcast.176), dimensions={1}, to_apply=%broadcast_in_dim.66.reduce_sub_computation | reduce | bytes 895490 | tf_op jit(solution)/shard_map/broadcast_in_dim | solution.py:115
  8.8 1.2 %reshape.327 = bf16[4,2,27984]{2,1,0:T(2,128)(2,1)} reshape(bf16[4,55968]{1,0:T(4,128)(2,1)S(1)} %reduce.26) | data formatting | bytes 895488
  10.1 6.3 %all-to-all-start = ((bf16[4,2,27984]{2,1,0:T(2,128)(2,1)}), bf16[4,2,27984]{2,1,0:T(2,128)(2,1)S(1)}, u32[]{:S(2)}, u32[]{:S(2)}) async-start(bf16[4,2,27984]{2,1,0:T(2,128)(2,1)} %reshape.327), calls=%async_computation | async-start | bytes 897024 | tf_op jit(solution)/shard_map/all_to_all | solution.py:116
  19.1 3.9 %collective-permute-start.2 = (f32[20]{0:T(128)S(1)}, f32[20]{0:T(128)S(1)}, u32[]{:S(2)}, u32[]{:S(2)}) collective-permute-start(f32[20]{0:T(128)S(1)} %get-tuple-element.35), channel_id=1, source_target_pairs={{0,4},{4,8},{8,12},{1,5},{5,9},{9,13},{2,6},{6,10},{10,14},{3,7},{... | collective-permute-start | bytes 248 | tf_op jit(solution)/shard_map/ppermute | solution.py:19
  23.9 1.5 %copy.114 = f32[256,1280]{1,0:T(8,128)} copy(f32[256,1280]{0,1:T(8,128)S(1)} %bitcast.100) | data formatting | bytes 2621440 | tf_op jit(solution)/shard_map/mul | solution.py:178
  27.9 1.5 %copy.113 = f32[256,1280]{1,0:T(8,128)} copy(f32[256,1280]{0,1:T(8,128)S(1)} %bitcast.101) | data formatting | bytes 2621440 | tf_op jit(solution)/shard_map/mul | solution.py:178
  30.0 1.7 %reshape.328 = bf16[4,1,55968]{2,1,0:T(2,128)(2,1)S(1)} reshape(bf16[4,2,27984]{2,1,0:T(2,128)(2,1)S(1)} %all-to-all-done) | data formatting | bytes 895488
  32.1 0.9 slice.289
  33.0 3.9 %divide_convert_fusion = bf16[512,1280]{1,0:T(8,128)(2,1)S(1)} fusion(bf16[512,1280]{1,0:T(8,128)(2,1)} %param.13, bf16[3,1280]{1,0:T(4,128)(2,1)S(1)} %slice.275, f32[1280]{0:T(1024)S(1)} %get-tuple-element.18, f32[1280]{0:T(1024)S(1)} %get-tuple-element.19, f32[1280]{0:T(1024)S(1)} %get-tuple-element.17, f32[1280]{0:T(1024)S(1)} %get-tuple-element.16), kind=kLoop, calls=%fused_computation.28 | loop fusion | flops 15728640 | bytes 2649600 | tf_op jit(solution)/shard_map/convert_element_type | solution.py:35
  37.0 1.7 %slice_convert_fusion.1 = (f32[256,1280]{1,0:T(8,128)}, f32[256,1280]{1,0:T(8,128)}) fusion(bf16[512,1280]{1,0:T(8,128)(2,1)S(1)} %divide_convert_fusion), kind=kLoop, calls=%fused_computation.52 | loop fusion | flops 655360 | bytes 3932160 | tf_op jit(solution)/shard_map/convert_element_type | solution.py:143
  38.7 1.8 %copy.111 = f32[256,1280]{0,1:T(8,128)S(1)} copy(f32[256,1280]{1,0:T(8,128)} %get-tuple-element.37) | data formatting | bytes 2621440 | tf_op jit(solution)/shard_map/convert_element_type | solution.py:143
  40.4 2.8 %copy.110 = f32[256,1280]{0,1:T(8,128)} copy(f32[256,1280]{1,0:T(8,128)} %get-tuple-element.36) | data formatting | bytes 2621440 | tf_op jit(solution)/shard_map/convert_element_type | solution.py:143
  43.6 1.7 %convolution_add_fusion.3 = f32[20,64,128]{2,1,0:T(8,128)S(1)} fusion(f32[256,20,64]{0,2,1:T(8,128)} %bitcast.99, f32[256,20]{0,1:T(8,128)} %get-tuple-element.44, f32[20]{0:T(128)} %get-tuple-element.57, bf16[512,256]{1,0:T(8,128)(2,1)S(1)} %divide_convert_fusion.1), kind=kOutput, calls=%fused_computation.43 | convolution fusion | flops 84705280 | bytes 2052176 | tf_op jit(solution)/shard_map/jhp,js->hps/dot_general | solution.py:145
  45.3 2.0 %fusion.78 = (bf16[20,64,128]{2,1,0:T(8,128)(2,1)}, f32[20,64,128]{2,1,0:T(8,128)}) fusion(bf16[512,256]{1,0:T(8,128)(2,1)S(1)} %divide_convert_fusion.1, f32[256,20,64]{0,2,1:T(8,128)S(1)} %bitcast.98, f32[256,20]{0,1:T(8,128)} %get-tuple-element.45, f32[20,64,128]{2,1,0:T(8,128)S(1)} %convolution_add_fusion.3, f32[20]{0:T(128)} %get-tuple-element.56), kind=kOutput, calls=%fused_computation.169 | convolution fusion | flops 85032960 | bytes 3035216 | tf_op jit(solution)/shard_map/jhp,js->hps/dot_general | solution.py:145
  47.3 4.1 %collective-permute-start = (bf16[20,64,128]{2,1,0:T(8,128)(2,1)}, bf16[20,64,128]{2,1,0:T(8,128)(2,1)}, u32[]{:S(2)}, u32[]{:S(2)}) collective-permute-start(bf16[20,64,128]{2,1,0:T(8,128)(2,1)} %get-tuple-element.59), channel_id=1, source_target_pairs={{0,4},{4,8},{8,12},{1,5},{5,9},{9,13},{2,6},{6,10},{10,14},{3,7},{... | collective-permute-start | bytes 983048 | tf_op jit(solution)/shard_map/ppermute | solution.py:19
  51.4 1.7 %reshape.291 = bf16[160,1284]{1,0:T(8,128)(2,1)S(1)} reshape(bf16[4,51360]{1,0:T(4,128)(2,1)} %slice.289) | data formatting | bytes 821760 | tf_op jit(solution)/shard_map/reshape | solution.py:118
  55.2 1.1 slice.295
  56.3 1.7 %reshape.292 = bf16[160,8,160]{2,1,0:T(8,128)(2,1)} reshape(bf16[160,1280]{1,0:T(8,128)(2,1)S(1)} %slice.295) | data formatting | bytes 819200 | tf_op jit(solution)/shard_map/reshape | solution.py:194
  58.9 0.9 fusion.49
  63.0 1.9 %fusion.26 = bf16[20,64,128]{2,1,0:T(8,128)(2,1)} fusion(f32[20,64,128]{2,1,0:T(8,128)S(1)} %copy-done.3, bf16[20,64,128]{2,1,0:T(8,128)(2,1)} %collective-permute-done, f32[20]{0:T(128)S(1)} %copy-done.22), kind=kLoop, calls=%fused_computation.50 | loop fusion | flops 655360 | bytes 1310800 | tf_op jit(solution)/shard_map/convert_element_type | solution.py:65
  64.8 5.1 %collective-permute-start.1 = (bf16[20,64,128]{2,1,0:T(8,128)(2,1)}, bf16[20,64,128]{2,1,0:T(8,128)(2,1)}, u32[]{:S(2)}, u32[]{:S(2)}) collective-permute-start(bf16[20,64,128]{2,1,0:T(8,128)(2,1)} %fusion.26), channel_id=1, source_target_pairs={{0,8},{4,12},{1,9},{5,13},{2,10},{6,14},{3,11},{7,15},{16,24},{20,... | collective-permute-start | bytes 983048 | tf_op jit(solution)/shard_map/ppermute | solution.py:19
  69.9 2.7 %fusion.19 = f32[256,20,64]{0,2,1:T(8,128)S(1)} fusion(f32[20,256]{1,0:T(8,128)} %get-tuple-element.43, f32[256,256]{1,0:T(8,128)} %fusion.46, f32[20,256]{1,0:T(8,128)} %bitcast.122, pred[256,256]{1,0:T(8,128)(4,1)} %iota_compare_fusion, bf16[512,20,64]{0,2,1:T(8,128)(2,1)S(1)} %bitcast.102), kind=kOutput, calls=%fused_computation.33 | convolution fusion | flops 175636480 | bytes 2367488 | tf_op jit(solution)/shard_map/hij,jhp->ihp/dot_general | solution.py:48
  72.6 1.7 %fusion.20 = f32[256,20,64]{0,2,1:T(8,128)S(1)} fusion(f32[20,256]{1,0:T(8,128)S(1)} %copy-done.17, f32[256,256]{1,0:T(8,128)S(1)} %copy-done.8, f32[20,256]{1,0:T(8,128)S(1)} %bitcast.123, pred[256,256]{1,0:T(8,128)(4,1)S(1)} %copy-done.14, bf16[512,20,64]{0,2,1:T(8,128)(2,1)S(1)} %bitcast.103), kind=kOutput, calls=%fused_computation.34 | convolution fusion | flops 175636480 | bytes 2367488 | tf_op jit(solution)/shard_map/hij,jhp->ihp/dot_general | solution.py:48
  74.3 2.0 %maximum_add_fusion.1 = f32[512,20,64]{0,2,1:T(8,128)} fusion(f32[256,20,64]{0,2,1:T(8,128)S(1)} %fusion.19, f32[256,20,64]{0,2,1:T(8,128)S(1)} %fusion.20, bf16[512,20,64]{0,2,1:T(8,128)(2,1)S(1)} %bitcast.104, f32[20]{0:T(128)S(1)} %copy-done.27), kind=kLoop, calls=%fused_computation.15 | loop fusion | flops 2621440 | bytes 6553680 | tf_op jit(solution)/shard_map/add | solution.py:167
  76.3 2.1 %copy.119 = f32[512,1280]{1,0:T(8,128)S(1)} copy(f32[512,1280]{0,1:T(8,128)} %bitcast.97) | data formatting | bytes 5242880 | tf_op jit(solution)/shard_map/optimization_barrier | solution.py:170
  78.5 1.3 %multiply_add_fusion = (f32[20,64,128]{2,1,0:T(8,128)S(1)}, f32[20,64,128]{2,1,0:T(8,128)S(1)}) fusion(f32[20,64,128]{2,1,0:T(8,128)S(1)} %convolution_add_fusion.3, f32[20]{0:T(128)S(1)} %copy-done.21, bf16[20,64,128]{2,1,0:T(8,128)(2,1)} %collective-permute-done, f32[20]{0:T(128)S(1)} %copy-done.24, bf16[20,64,128]{2,1,0:T(8,128)(2,1)} %collective-permute-done.1), kind=kLoop, calls=%fused_computation.63 | loop fusion | flops 983040 | bytes 2621600 | tf_op jit(solution)/shard_map/add | solution.py:175
  83.0 2.4 %multiply_reduce_fusion = (f32[512]{0:T(512)S(1)}, f32[512,1280]{1,0:T(8,128)}) fusion(bf16[512,1280]{1,0:T(8,128)(2,1)S(1)} %copy-done.5, f32[512,1280]{1,0:T(8,128)S(1)} %copy.119, f32[256,1280]{1,0:T(8,128)S(1)} %fusion.1, f32[256,1280]{1,0:T(8,128)S(1)} %fusion), kind=kLoop, calls=%fused_computation.17 | loop fusion | flops 5897728 | bytes 9177088 | tf_op jit(solution)/shard_map/reduce_sum | solution.py:182
  85.4 5.6 %psum.7 = f32[512]{0:T(512)S(1)} all-reduce(f32[512]{0:T(512)S(1)} %get-tuple-element.26), channel_id=1, replica_groups=mesh['groups'=2,'seq'=4,'tensor'=4] {'tensor'}, use_global_device_ids=true, to_apply=%region_9.10 | all-reduce | flops 512 | bytes 4096 | tf_op jit(solution)/shard_map/psum | solution.py:182
  91.0 2.0 %multiply_convert_fusion.4 = bf16[512,1280]{1,0:T(8,128)(2,1)S(1)} fusion(f32[512,1280]{1,0:T(8,128)} %get-tuple-element.27, f32[1280]{0:T(1024)S(1)} %copy-done.18, f32[512]{0:T(512)S(1)} %add_rsqrt_fusion), kind=kLoop, calls=%fused_computation.16 | loop fusion | flops 1966080 | bytes 3939328 | tf_op jit(solution)/shard_map/convert_element_type | solution.py:186
  93.1 0.9 gather_fusion
  97.0 20.6 %all_to_all.18 = bf16[4,40,1304]{2,1,0:T(8,128)(2,1)S(1)} all-to-all(bf16[4,40,1304]{2,1,0:T(8,128)(2,1)S(1)} %bitcast.106), channel_id=1, replica_groups=mesh['groups'=2,'seq'=4,'tensor'=4] {'seq'}, dimensions={0} | all-to-all | bytes 834560 | tf_op jit(solution)/shard_map/all_to_all | solution.py:220
  (171 shorter events, 25.3 us)
Async XLA Ops:
  0.6 15.8 %copy-start.9 = (f32[20,512]{1,0:T(8,128)S(1)}, f32[20,512]{1,0:T(8,128)}, u32[]{:S(2)}) copy-start(f32[20,512]{1,0:T(8,128)} %param.17) | copy-start | bytes 122884
  4.2 18.8 %copy-start.11 = (f32[20,512]{1,0:T(8,128)S(1)}, f32[20,512]{1,0:T(8,128)}, u32[]{:S(2)}) copy-start(f32[20,512]{1,0:T(8,128)} %param.16) | copy-start | bytes 122884
  10.1 19.9 %all-to-all-start = ((bf16[4,2,27984]{2,1,0:T(2,128)(2,1)}), bf16[4,2,27984]{2,1,0:T(2,128)(2,1)S(1)}, u32[]{:S(2)}, u32[]{:S(2)}) async-start(bf16[4,2,27984]{2,1,0:T(2,128)(2,1)} %reshape.327), calls=%async_computation | async-start | bytes 897024 | tf_op jit(solution)/shard_map/all_to_all | solution.py:116
  16.4 8.9 %copy-start.26 = (s32[128]{0:T(128)S(1)}, s32[128]{0:T(128)}, u32[]{:S(2)}) copy-start(s32[128]{0:T(128)} %param.22) | copy-start | bytes 1540
  16.4 10.7 %copy-start.16 = (bf16[4,1280]{1,0:T(4,128)(2,1)S(1)}, bf16[4,1280]{1,0:T(4,128)(2,1)}, u32[]{:S(2)}) copy-start(bf16[4,1280]{1,0:T(4,128)(2,1)} %param.19) | copy-start | bytes 30724
  16.4 10.8 %copy-start.19 = (bf16[4,256]{1,0:T(4,128)(2,1)S(1)}, bf16[4,256]{1,0:T(4,128)(2,1)}, u32[]{:S(2)}) copy-start(bf16[4,256]{1,0:T(4,128)(2,1)} %param.20) | copy-start | bytes 6148
  19.1 10.3 %collective-permute-start.2 = (f32[20]{0:T(128)S(1)}, f32[20]{0:T(128)S(1)}, u32[]{:S(2)}, u32[]{:S(2)}) collective-permute-start(f32[20]{0:T(128)S(1)} %get-tuple-element.35), channel_id=1, source_target_pairs={{0,4},{4,8},{8,12},{1,5},{5,9},{9,13},{2,6},{6,10},{10,14},{3,7},{... | collective-permute-start | bytes 248 | tf_op jit(solution)/shard_map/ppermute | solution.py:19
  32.1 6.5 %copy-start.15 = (bf16[3,1536]{1,0:T(4,128)(2,1)}, bf16[3,1536]{1,0:T(4,128)(2,1)S(1)}, u32[]{:S(2)}) copy-start(bf16[3,1536]{1,0:T(4,128)(2,1)S(1)} %fusion.62) | copy-start | bytes 27652
  38.6 4.6 %copy-start.7 = (bf16[512,256]{1,0:T(8,128)(2,1)S(1)}, bf16[512,256]{1,0:T(8,128)(2,1)}, u32[]{:S(2)}) copy-start(bf16[512,256]{1,0:T(8,128)(2,1)} %param.15) | copy-start | bytes 786436
  38.6 4.6 %slice-start = ((bf16[3,1536]{1,0:T(4,128)(2,1)}), bf16[3,256]{1,0:T(4,128)(2,1)S(1)}, s32[]{:S(2)}) async-start(bf16[3,1536]{1,0:T(4,128)(2,1)} %copy-done.15), calls=%async_computation.2 | async-start | bytes 4096 | tf_op jit(solution)/shard_map/slice | solution.py:128
  38.6 4.6 %copy-start.20 = (f32[1,256]{1,0:T(1,128)S(1)}, f32[1,256]{1,0:T(1,128)}, u32[]{:S(2)}) copy-start(f32[1,256]{1,0:T(1,128)} %get-tuple-element.53) | copy-start | bytes 3076
  45.3 8.6 %copy-start.25 = (s32[128]{0:T(128)S(1)}, s32[128]{0:T(128)}, u32[]{:S(2)}) copy-start(s32[128]{0:T(128)} %iota_add_fusion) | copy-start | bytes 1540
  47.3 10.7 %collective-permute-start = (bf16[20,64,128]{2,1,0:T(8,128)(2,1)}, bf16[20,64,128]{2,1,0:T(8,128)(2,1)}, u32[]{:S(2)}, u32[]{:S(2)}) collective-permute-start(bf16[20,64,128]{2,1,0:T(8,128)(2,1)} %get-tuple-element.59), channel_id=1, source_target_pairs={{0,4},{4,8},{8,12},{1,5},{5,9},{9,13},{2,6},{6,10},{10,14},{3,7},{... | collective-permute-start | bytes 983048 | tf_op jit(solution)/shard_map/ppermute | solution.py:19
  55.2 4.6 %copy-start.12 = (f32[20,512]{1,0:T(8,128)S(1)}, f32[20,512]{1,0:T(8,128)}, u32[]{:S(2)}) copy-start(f32[20,512]{1,0:T(8,128)} %param.16) | copy-start | bytes 122884
  55.2 5.2 %copy-start.10 = (f32[20,512]{1,0:T(8,128)S(1)}, f32[20,512]{1,0:T(8,128)}, u32[]{:S(2)}) copy-start(f32[20,512]{1,0:T(8,128)} %param.17) | copy-start | bytes 122884
  55.2 7.7 %copy-start.3 = (f32[20,64,128]{2,1,0:T(8,128)S(1)}, f32[20,64,128]{2,1,0:T(8,128)}, u32[]{:S(2)}) copy-start(f32[20,64,128]{2,1,0:T(8,128)} %get-tuple-element.60) | copy-start | bytes 1966084
  55.2 7.7 %copy-start.22 = (f32[20]{0:T(128)S(1)}, f32[20]{0:T(128)}, u32[]{:S(2)}) copy-start(f32[20]{0:T(128)} %get-tuple-element.34) | copy-start | bytes 244
  64.8 13.6 %collective-permute-start.1 = (bf16[20,64,128]{2,1,0:T(8,128)(2,1)}, bf16[20,64,128]{2,1,0:T(8,128)(2,1)}, u32[]{:S(2)}, u32[]{:S(2)}) collective-permute-start(bf16[20,64,128]{2,1,0:T(8,128)(2,1)} %fusion.26), channel_id=1, source_target_pairs={{0,8},{4,12},{1,9},{5,13},{2,10},{6,14},{3,11},{7,15},{16,24},{20,... | collective-permute-start | bytes 983048 | tf_op jit(solution)/shard_map/ppermute | solution.py:19
  69.9 2.7 %copy-start.8 = (f32[256,256]{1,0:T(8,128)S(1)}, f32[256,256]{1,0:T(8,128)}, u32[]{:S(2)}) copy-start(f32[256,256]{1,0:T(8,128)} %fusion.49) | copy-start | bytes 786436
  69.9 2.7 %copy-start.14 = (pred[256,256]{1,0:T(8,128)(4,1)S(1)}, pred[256,256]{1,0:T(8,128)(4,1)}, u32[]{:S(2)}) copy-start(pred[256,256]{1,0:T(8,128)(4,1)} %iota_compare_fusion) | copy-start | bytes 196612
  69.9 2.7 %copy-start.17 = (f32[20,256]{1,0:T(8,128)S(1)}, f32[20,256]{1,0:T(8,128)}, u32[]{:S(2)}) copy-start(f32[20,256]{1,0:T(8,128)} %get-tuple-element.42) | copy-start | bytes 61444
  72.6 1.7 %copy-start.27 = (f32[20]{0:T(128)S(1)}, f32[20]{0:T(128)}, u32[]{:S(2)}) copy-start(f32[20]{0:T(128)} %param.18) | copy-start | bytes 244
  76.3 2.2 %copy-start.21 = (f32[20]{0:T(128)S(1)}, f32[20]{0:T(128)}, u32[]{:S(2)}) copy-start(f32[20]{0:T(128)} %get-tuple-element.58) | copy-start | bytes 244
  76.3 2.2 %copy-start.24 = (f32[20]{0:T(128)S(1)}, f32[20]{0:T(128)}, u32[]{:S(2)}) copy-start(f32[20]{0:T(128)} %exp.70) | copy-start | bytes 244
  79.9 1.3 %copy-start.1 = (f32[256,1280]{1,0:T(8,128)S(1)}, f32[256,1280]{1,0:T(8,128)}, u32[]{:S(2)}) copy-start(f32[256,1280]{1,0:T(8,128)} %copy.114) | copy-start | bytes 3932164
  80.4 1.4 %copy-start.2 = (f32[256,1280]{1,0:T(8,128)S(1)}, f32[256,1280]{1,0:T(8,128)}, u32[]{:S(2)}) copy-start(f32[256,1280]{1,0:T(8,128)} %copy.113) | copy-start | bytes 3932164
  81.6 1.4 %copy-start.5 = (bf16[512,1280]{1,0:T(8,128)(2,1)S(1)}, bf16[512,1280]{1,0:T(8,128)(2,1)}, u32[]{:S(2)}) copy-start(bf16[512,1280]{1,0:T(8,128)(2,1)} %param.14) | copy-start | bytes 3932164
  83.0 8.1 %copy-start.18 = (f32[1280]{0:T(1024)S(1)}, f32[1280]{0:T(1024)}, u32[]{:S(2)}) copy-start(f32[1280]{0:T(1024)} %param.21) | copy-start | bytes 15364
  93.1 2.2 %copy-start = (bf16[512,1280]{1,0:T(8,128)(2,1)}, bf16[512,1280]{1,0:T(8,128)(2,1)S(1)}, u32[]{:S(2)}) copy-start(bf16[512,1280]{1,0:T(8,128)(2,1)S(1)} %multiply_convert_fusion.4) | copy-start | bytes 3932164
  93.1 1.6 %copy-start.6 = (bf16[160,8,160]{2,1,0:T(8,128)(2,1)S(1)}, bf16[160,8,160]{2,1,0:T(8,128)(2,1)}, u32[]{:S(2)}) copy-start(bf16[160,8,160]{2,1,0:T(8,128)(2,1)} %reshape.292) | copy-start | bytes 1228804
  93.1 1.6 %copy-start.13 = (pred[160,128]{1,0:T(8,128)(4,1)S(1)}, pred[160,128]{1,0:T(8,128)(4,1)}, u32[]{:S(2)}) copy-start(pred[160,128]{1,0:T(8,128)(4,1)} %compare_and_fusion) | copy-start | bytes 61444
  93.1 1.5 %copy-start.23 = (pred[128]{0:T(512)(128)(4,1)S(1)}, pred[128]{0:T(512)(128)(4,1)}, u32[]{:S(2)}) copy-start(pred[128]{0:T(512)(128)(4,1)} %get-tuple-element.24) | copy-start | bytes 388
  (1 other events, 0.8 us)

commit v5 on v4

--- a/solution.py
+++ b/solution.py
@@ -109,21 +109,16 @@
     bounds = jnp.stack([pool_start, pool_stop], axis=1)
     bounds_split = jnp.concatenate([bounds // 64, bounds % 64], axis=1).astype(jnp.bfloat16)
     query_rows = jnp.concatenate([pool_query, bounds_split], axis=1)
-    edge_rows = jnp.concatenate([x_in[tok_rows - rim_rows :], bc_in[tok_rows - rim_rows :]], axis=1)
-    query_width = query_rows.shape[1]
-    payload = jnp.concatenate([query_rows.reshape(-1), edge_rows.reshape(-1)])
-    payload = jnp.broadcast_to(payload[None], (seq_count,) + payload.shape)
-    payload = lax.all_to_all(payload, "seq", 0, 0, tiled=True)
-    query_size = pools_local * query_width
-    query_rows = payload[:, :query_size].reshape(seq_count * pools_local, query_width)
+    query_rows = jnp.broadcast_to(query_rows[None], (seq_count,) + query_rows.shape)
+    query_rows = lax.all_to_all(
+        query_rows.reshape(seq_count * pools_local, -1), "seq", 0, 0, tiled=True
+    )
     queries_all = query_rows[:, :channels]
     bounds_all = query_rows[:, channels:].astype(jnp.int32)
     start_all = bounds_all[:, 0] * 64 + bounds_all[:, 2]
     stop_all = bounds_all[:, 1] * 64 + bounds_all[:, 3]
-    place = lax.axis_index("seq")
-    edges_all = payload[:, query_size:].reshape(seq_count, rim_rows, edge_rows.shape[1])
-    before = lax.dynamic_index_in_dim(edges_all, jnp.maximum(place - 1, 0), 0, False)
-    before = jnp.where(place > 0, before, jnp.zeros_like(before))
+    edge_rows = jnp.concatenate([x_in[tok_rows - rim_rows :], bc_in[tok_rows - rim_rows :]], axis=1)
+    before = passed_along(edge_rows, "seq", 1)
     x_conv = causal_conv(before[:, :channels], x_in, conv_x)
     bc_conv = causal_conv(before[:, channels:], bc_in, conv_bc)
     b_mat = bc_conv[:, :state_width]

time: 121 us -> 125 us (1.033)
  starting transfers between devices: 19.4 us -> 23.7 us
  local copies, waits for them, and re-layouts: 31.5 us -> 28.8 us
  waiting for transfers between devices: 0.01 us -> 2.19 us
    ppermute x3 -> x4, starting transfers between devices: 13.1 us -> 19.6 us  [passed_along(): lax.ppermute(value, axis, [(source, source + steps) for source in range(l...]
    unnamed x67 -> x50, local copies, waits for them, and re-layouts: 6.37 us -> 2.72 us
    broadcast_in_dim x1 -> x0, other arithmetic: 3.53 us -> none  [local(): payload = jnp.broadcast_to(payload[None], (seq_count,) + payload.shape)]
    all_to_all x1, starting transfers between devices: 6.35 us -> 4.13 us  [local(): lax.all_to_all(query_rows.reshape(seq_count * pools_local, -1), 'seq', 0,...]
    ppermute x3 -> x4, waiting for transfers between devices: 0.01 us -> 2.19 us  [passed_along(): lax.ppermute(value, axis, [(source, source + steps) for source in range(l...]
    reshape x5 -> x2, local copies, waits for them, and re-layouts: 1.9 us -> 0.02 us  [the longest x1 1.66 us: local(): payload[:, :query_size].reshape(seq_count * pools_local, query_width)]
    convert_element_type x1, other arithmetic: 0.01 us -> 1.42 us  [local(): bounds_all = query_rows[:, channels:].astype(jnp.int32)]
  transfers between devices with their start and end apart: 4 -> 5, of which waited for: 0 -> 1; matrix products, arithmetic and copies ran while one was open for 20% -> 43% of each run, Pallas kernels for 0% -> 0%
where the time goes in v5:
time: 125 us; the launch traced here: 124 us
  other arithmetic  28.9 us (23%)
  local copies, waits for them, and re-layouts  28.8 us (23%)
  blocking collectives  27.2 us (22%)
  starting transfers between devices  23.7 us (19%)
  matrix products  12.1 us (10%)
  waiting for transfers between devices  2.19 us (2%)
    all_to_all x1, blocking collectives, local(): parts = lax.all_to_all(parts, 'seq', 0, 0, tiled=True).astype(jnp.float32)  21.6 us
    ppermute x4, starting transfers between devices, passed_along(): lax.ppermute(value, axis, [(source, source + steps) for source in range(l...  19.6 us
    psum x1, blocking collectives, local(): square_sum = lax.psum(jnp.sum(gated * gated, axis=1), 'tensor')  5.63 us
    convert_element_type x2, local copies, waits for them, and re-layouts, local(): x_heads[first_row:last_row].astype(jnp.float32)  4.54 us
    dot_general x2, matrix products, stretch_local(): jnp.einsum('hij,jhp->ihp', mixing, x_block, preferred_element_type=jnp.fl...  4.35 us
    convert_element_type x2, other arithmetic, causal_conv(): return silu_act(summed).astype(jnp.bfloat16)  4.3 us
    all_to_all x1, starting transfers between devices, local(): lax.all_to_all(query_rows.reshape(seq_count * pools_local, -1), 'seq', 0,...  4.13 us
    dot_general x2, matrix products, local(): jnp.einsum('jhp,js->hps', weighted, b_mat[first_row:last_row], preferred_...  3.7 us
  transfers between devices with their start and end apart: 5, of which 1 were waited for; matrix products, arithmetic and copies ran while one was open for 43% of the time, Pallas kernels for 0%

profile of v5, /device:TPU:0, one launch (start us, length us, event | category | flops | bytes accessed | tf_op | source)
XLA Modules:
  0.0 124.2 jit_solution(6417077865066585093)
XLA Ops:
  2.1 5.0 %collective-permute-start = (bf16[3,1536]{1,0:T(4,128)(2,1)S(1)}, bf16[3,1536]{1,0:T(4,128)(2,1)S(1)}, u32[]{:S(2)}, u32[]{:S(2)}) collective-permute-start(bf16[3,1536]{1,0:T(4,128)(2,1)S(1)} %pad_maximum_fusion.2), channel_id=1, source_target_pairs={{0,4},{4,8},{8,12},{1,5},{5,9},{9,13},{2,6},{6,10},{10,14},{3,7},{... | collective-permute-start | bytes 27656 | tf_op jit(solution)/shard_map/ppermute | solution.py:19
  10.6 4.0 %collective-permute-start.3 = (f32[20]{0:T(128)}, f32[20]{0:T(128)}, u32[]{:S(2)}, u32[]{:S(2)}) collective-permute-start(f32[20]{0:T(128)} %get-tuple-element.35), channel_id=1, source_target_pairs={{0,4},{4,8},{8,12},{1,5},{5,9},{9,13},{2,6},{6,10},{10,14},{3,7},{... | collective-permute-start | bytes 248 | tf_op jit(solution)/shard_map/ppermute | solution.py:19
  15.5 1.0 concatenate.29
  17.3 4.1 %all-to-all-start = ((bf16[4,40,1284]{2,1,0:T(8,128)(2,1)}), bf16[4,40,1284]{2,1,0:T(8,128)(2,1)}, u32[]{:S(2)}, u32[]{:S(2)}) async-start(bf16[4,40,1284]{2,1,0:T(8,128)(2,1)} %broadcast_in_dim.117), calls=%async_computation | async-start | bytes 901120 | tf_op jit(solution)/shard_map/all_to_all | solution.py:113
  24.1 1.5 %copy.82 = f32[256,1280]{1,0:T(8,128)} copy(f32[256,1280]{0,1:T(8,128)S(1)} %bitcast.95) | data formatting | bytes 2621440 | tf_op jit(solution)/shard_map/mul | solution.py:173
  25.6 4.0 %divide_convert_fusion = bf16[512,1280]{1,0:T(8,128)(2,1)S(1)} fusion(bf16[512,1280]{1,0:T(8,128)(2,1)} %param.13, bf16[3,1280]{1,0:T(4,128)(2,1)S(1)} %slice.266, f32[1280]{0:T(1024)S(1)} %get-tuple-element.18, f32[1280]{0:T(1024)S(1)} %get-tuple-element.19, f32[1280]{0:T(1024)S(1)} %get-tuple-element.17, f32[1280]{0:T(1024)S(1)} %get-tuple-element.16), kind=kLoop, calls=%fused_computation.28 | loop fusion | flops 15728640 | bytes 2649600 | tf_op jit(solution)/shard_map/convert_element_type | solution.py:35
  29.5 1.7 %slice_convert_fusion.1 = (f32[256,1280]{1,0:T(8,128)}, f32[256,1280]{1,0:T(8,128)}) fusion(bf16[512,1280]{1,0:T(8,128)(2,1)S(1)} %divide_convert_fusion), kind=kLoop, calls=%fused_computation.52 | loop fusion | flops 655360 | bytes 3932160 | tf_op jit(solution)/shard_map/convert_element_type | solution.py:138
  31.2 1.8 %copy.79 = f32[256,1280]{0,1:T(8,128)S(1)} copy(f32[256,1280]{1,0:T(8,128)} %get-tuple-element.37) | data formatting | bytes 2621440 | tf_op jit(solution)/shard_map/convert_element_type | solution.py:138
  33.0 2.8 %copy.78 = f32[256,1280]{0,1:T(8,128)} copy(f32[256,1280]{1,0:T(8,128)} %get-tuple-element.36) | data formatting | bytes 2621440 | tf_op jit(solution)/shard_map/convert_element_type | solution.py:138
  36.2 1.7 %convolution_add_fusion.3 = f32[20,64,128]{2,1,0:T(8,128)S(1)} fusion(f32[256,20,64]{0,2,1:T(8,128)} %bitcast.94, f32[256,20]{0,1:T(8,128)} %get-tuple-element.44, f32[20]{0:T(128)} %get-tuple-element.57, bf16[512,256]{1,0:T(8,128)(2,1)S(1)} %divide_convert_fusion.1), kind=kOutput, calls=%fused_computation.43 | convolution fusion | flops 84705280 | bytes 2052176 | tf_op jit(solution)/shard_map/jhp,js->hps/dot_general | solution.py:140
  37.8 2.0 %fusion.77 = (bf16[20,64,128]{2,1,0:T(8,128)(2,1)}, f32[20,64,128]{2,1,0:T(8,128)}) fusion(bf16[512,256]{1,0:T(8,128)(2,1)S(1)} %divide_convert_fusion.1, f32[256,20,64]{0,2,1:T(8,128)S(1)} %bitcast.93, f32[256,20]{0,1:T(8,128)} %get-tuple-element.45, f32[20,64,128]{2,1,0:T(8,128)S(1)} %convolution_add_fusion.3, f32[20]{0:T(128)} %get-tuple-element.56), kind=kOutput, calls=%fused_computation.164 | convolution fusion | flops 85032960 | bytes 3035216 | tf_op jit(solution)/shard_map/jhp,js->hps/dot_general | solution.py:140
  39.9 4.6 %collective-permute-start.1 = (bf16[20,64,128]{2,1,0:T(8,128)(2,1)}, bf16[20,64,128]{2,1,0:T(8,128)(2,1)}, u32[]{:S(2)}, u32[]{:S(2)}) collective-permute-start(bf16[20,64,128]{2,1,0:T(8,128)(2,1)} %get-tuple-element.59), channel_id=1, source_target_pairs={{0,4},{4,8},{8,12},{1,5},{5,9},{9,13},{2,6},{6,10},{10,14},{3,7},{... | collective-permute-start | bytes 983048 | tf_op jit(solution)/shard_map/ppermute | solution.py:19
  45.2 1.5 %copy.81 = f32[256,1280]{1,0:T(8,128)} copy(f32[256,1280]{0,1:T(8,128)S(1)} %bitcast.96) | data formatting | bytes 2621440 | tf_op jit(solution)/shard_map/mul | solution.py:173
  48.0 2.2 %collective-permute-done.1 = bf16[20,64,128]{2,1,0:T(8,128)(2,1)} collective-permute-done((bf16[20,64,128]{2,1,0:T(8,128)(2,1)}, bf16[20,64,128]{2,1,0:T(8,128)(2,1)}, u32[]{:S(2)}, u32[]{:S(2)}) %collective-permute-start.1) | collective-permute-done | bytes 327712 | tf_op jit(solution)/shard_map/ppermute | solution.py:19
  51.9 1.4 %fusion.75 = (f32[20,256]{1,0:T(8,128)}, f32[20,256]{1,0:T(8,128)}) fusion(f32[20,512]{1,0:T(8,128)} %param.16), kind=kLoop, calls=%fused_computation.162 | loop fusion | bytes 81920 | tf_op jit(solution)/shard_map/slice | solution.py:158
  56.6 2.7 %fusion.19 = f32[256,20,64]{0,2,1:T(8,128)S(1)} fusion(f32[20,256]{1,0:T(8,128)} %get-tuple-element.43, f32[256,256]{1,0:T(8,128)} %fusion.46, f32[20,256]{1,0:T(8,128)} %bitcast.114, pred[256,256]{1,0:T(8,128)(4,1)} %iota_compare_fusion, bf16[512,20,64]{0,2,1:T(8,128)(2,1)S(1)} %bitcast.97), kind=kOutput, calls=%fused_computation.33 | convolution fusion | flops 175636480 | bytes 2367488 | tf_op jit(solution)/shard_map/hij,jhp->ihp/dot_general | solution.py:48
  59.3 1.7 %fusion.20 = f32[256,20,64]{0,2,1:T(8,128)S(1)} fusion(f32[20,256]{1,0:T(8,128)S(1)} %copy-done.12, f32[256,256]{1,0:T(8,128)S(1)} %copy-done.6, f32[20,256]{1,0:T(8,128)S(1)} %bitcast.115, pred[256,256]{1,0:T(8,128)(4,1)S(1)} %copy-done.10, bf16[512,20,64]{0,2,1:T(8,128)(2,1)S(1)} %bitcast.98), kind=kOutput, calls=%fused_computation.34 | convolution fusion | flops 175636480 | bytes 2367488 | tf_op jit(solution)/shard_map/hij,jhp->ihp/dot_general | solution.py:48
  61.0 2.0 %maximum_add_fusion.1 = f32[512,20,64]{0,2,1:T(8,128)} fusion(f32[256,20,64]{0,2,1:T(8,128)S(1)} %fusion.19, f32[256,20,64]{0,2,1:T(8,128)S(1)} %fusion.20, bf16[512,20,64]{0,2,1:T(8,128)(2,1)S(1)} %bitcast.99, f32[20]{0:T(128)S(1)} %copy-done.20), kind=kLoop, calls=%fused_computation.15 | loop fusion | flops 2621440 | bytes 6553680 | tf_op jit(solution)/shard_map/add | solution.py:162
  63.0 2.1 %copy.87 = f32[512,1280]{1,0:T(8,128)S(1)} copy(f32[512,1280]{0,1:T(8,128)} %bitcast.92) | data formatting | bytes 5242880 | tf_op jit(solution)/shard_map/optimization_barrier | solution.py:165
  65.2 2.1 %fusion.26 = bf16[20,64,128]{2,1,0:T(8,128)(2,1)} fusion(f32[20,64,128]{2,1,0:T(8,128)} %get-tuple-element.60, bf16[20,64,128]{2,1,0:T(8,128)(2,1)} %collective-permute-done.1, f32[20]{0:T(128)S(1)} %copy-done.17), kind=kLoop, calls=%fused_computation.50 | loop fusion | flops 655360 | bytes 1310800 | tf_op jit(solution)/shard_map/convert_element_type | solution.py:65
  67.2 6.0 %collective-permute-start.2 = (bf16[20,64,128]{2,1,0:T(8,128)(2,1)}, bf16[20,64,128]{2,1,0:T(8,128)(2,1)}, u32[]{:S(2)}, u32[]{:S(2)}) collective-permute-start(bf16[20,64,128]{2,1,0:T(8,128)(2,1)} %fusion.26), channel_id=1, source_target_pairs={{0,8},{4,12},{1,9},{5,13},{2,10},{6,14},{3,11},{7,15},{16,24},{20,... | collective-permute-start | bytes 983048 | tf_op jit(solution)/shard_map/ppermute | solution.py:19
  73.3 1.8 %slice.285 = bf16[160,1280]{1,0:T(8,128)(2,1)} slice(bf16[160,1284]{1,0:T(8,128)(2,1)} %bitcast.23), slice={[0:160], [0:1280]} | slice | bytes 819200 | tf_op jit(solution)/shard_map/slice | solution.py:116
  75.0 1.4 %slice_convert_fusion.2 = s32[160,4]{1,0:T(8,128)} fusion(bf16[160,1284]{1,0:T(8,128)(2,1)} %bitcast.23), kind=kLoop, calls=%fused_computation.102 | loop fusion | flops 640 | bytes 3840 | tf_op jit(solution)/shard_map/convert_element_type | solution.py:117
  76.4 2.7 %reshape.272 = bf16[160,8,160]{2,1,0:T(8,128)(2,1)} reshape(bf16[160,1280]{1,0:T(8,128)(2,1)} %slice.285) | data formatting | bytes 819200 | tf_op jit(solution)/shard_map/reshape | solution.py:189
  79.1 1.3 %fusion.45 = (s32[160]{0:T(256)S(1)}, s32[160]{0:T(256)S(1)}) fusion(s32[160,4]{1,0:T(8,128)} %slice_convert_fusion.2), kind=kLoop, calls=%fused_computation.85 | loop fusion | flops 640 | bytes 3840 | tf_op jit(solution)/shard_map/add | solution.py:118
  80.4 1.4 %compare_and_fusion = pred[160,128]{1,0:T(8,128)(4,1)} fusion(s32[128]{0:T(128)} %iota_add_fusion, s32[160]{0:T(256)S(1)} %get-tuple-element.15, s32[160]{0:T(256)S(1)} %get-tuple-element.14), kind=kLoop, calls=%fused_computation.87 | loop fusion | flops 61440 | bytes 22272 | tf_op jit(solution)/shard_map/and | solution.py:191
  81.8 1.3 %multiply_add_fusion = (f32[20,64,128]{2,1,0:T(8,128)S(1)}, f32[20,64,128]{2,1,0:T(8,128)S(1)}) fusion(f32[20,64,128]{2,1,0:T(8,128)S(1)} %convolution_add_fusion.3, f32[20]{0:T(128)S(1)} %copy-done.16, bf16[20,64,128]{2,1,0:T(8,128)(2,1)} %collective-permute-done.1, f32[20]{0:T(128)S(1)} %exp.70, bf16[20,64,128]{2,1,0:T(8,128)(2,1)} %collective-permute-done.2), kind=kLoop, calls=%fused_computation.63 | loop fusion | flops 983040 | bytes 2621600 | tf_op jit(solution)/shard_map/add | solution.py:170
  86.3 2.4 %multiply_reduce_fusion = (f32[512]{0:T(512)S(1)}, f32[512,1280]{1,0:T(8,128)}) fusion(bf16[512,1280]{1,0:T(8,128)(2,1)S(1)} %copy-done.3, f32[512,1280]{1,0:T(8,128)S(1)} %copy.87, f32[256,1280]{1,0:T(8,128)S(1)} %fusion.1, f32[256,1280]{1,0:T(8,128)S(1)} %fusion), kind=kLoop, calls=%fused_computation.17 | loop fusion | flops 5897728 | bytes 9177088 | tf_op jit(solution)/shard_map/reduce_sum | solution.py:177
  88.7 5.6 %psum.7 = f32[512]{0:T(512)S(1)} all-reduce(f32[512]{0:T(512)S(1)} %get-tuple-element.26), channel_id=1, replica_groups=mesh['groups'=2,'seq'=4,'tensor'=4] {'tensor'}, use_global_device_ids=true, to_apply=%region_9.10 | all-reduce | flops 512 | bytes 4096 | tf_op jit(solution)/shard_map/psum | solution.py:177
  94.4 2.0 %multiply_convert_fusion.4 = bf16[512,1280]{1,0:T(8,128)(2,1)S(1)} fusion(f32[512,1280]{1,0:T(8,128)} %get-tuple-element.27, f32[1280]{0:T(1024)S(1)} %copy-done.13, f32[512]{0:T(512)S(1)} %add_rsqrt_fusion), kind=kLoop, calls=%fused_computation.16 | loop fusion | flops 1966080 | bytes 3939328 | tf_op jit(solution)/shard_map/convert_element_type | solution.py:181
  96.4 0.9 gather_fusion
  100.3 21.6 %all_to_all.18 = bf16[4,40,1304]{2,1,0:T(8,128)(2,1)S(1)} all-to-all(bf16[4,40,1304]{2,1,0:T(8,128)(2,1)S(1)} %bitcast.101), channel_id=1, replica_groups=mesh['groups'=2,'seq'=4,'tensor'=4] {'seq'}, dimensions={0} | all-to-all | bytes 834560 | tf_op jit(solution)/shard_map/all_to_all | solution.py:215
  (145 shorter events, 24.8 us)
Async XLA Ops:
  0.6 21.4 %copy-start.14 = (bf16[4,256]{1,0:T(4,128)(2,1)S(1)}, bf16[4,256]{1,0:T(4,128)(2,1)}, u32[]{:S(2)}) copy-start(bf16[4,256]{1,0:T(4,128)(2,1)} %param.20) | copy-start | bytes 6148
  0.6 22.0 %copy-start.11 = (bf16[4,1280]{1,0:T(4,128)(2,1)S(1)}, bf16[4,1280]{1,0:T(4,128)(2,1)}, u32[]{:S(2)}) copy-start(bf16[4,1280]{1,0:T(4,128)(2,1)} %param.19) | copy-start | bytes 30724
  0.7 22.1 %copy-start.7 = (f32[20,512]{1,0:T(8,128)S(1)}, f32[20,512]{1,0:T(8,128)}, u32[]{:S(2)}) copy-start(f32[20,512]{1,0:T(8,128)} %param.16) | copy-start | bytes 122884
  0.7 22.8 %copy-start.19 = (s32[128]{0:T(128)S(1)}, s32[128]{0:T(128)}, u32[]{:S(2)}) copy-start(s32[128]{0:T(128)} %param.22) | copy-start | bytes 1540
  2.1 23.4 %collective-permute-start = (bf16[3,1536]{1,0:T(4,128)(2,1)S(1)}, bf16[3,1536]{1,0:T(4,128)(2,1)S(1)}, u32[]{:S(2)}, u32[]{:S(2)}) collective-permute-start(bf16[3,1536]{1,0:T(4,128)(2,1)S(1)} %pad_maximum_fusion.2), channel_id=1, source_target_pairs={{0,4},{4,8},{8,12},{1,5},{5,9},{9,13},{2,6},{6,10},{10,14},{3,7},{... | collective-permute-start | bytes 27656 | tf_op jit(solution)/shard_map/ppermute | solution.py:19
  10.6 36.1 %collective-permute-start.3 = (f32[20]{0:T(128)}, f32[20]{0:T(128)}, u32[]{:S(2)}, u32[]{:S(2)}) collective-permute-start(f32[20]{0:T(128)} %get-tuple-element.35), channel_id=1, source_target_pairs={{0,4},{4,8},{8,12},{1,5},{5,9},{9,13},{2,6},{6,10},{10,14},{3,7},{... | collective-permute-start | bytes 248 | tf_op jit(solution)/shard_map/ppermute | solution.py:19
  17.3 56.0 %all-to-all-start = ((bf16[4,40,1284]{2,1,0:T(8,128)(2,1)}), bf16[4,40,1284]{2,1,0:T(8,128)(2,1)}, u32[]{:S(2)}, u32[]{:S(2)}) async-start(bf16[4,40,1284]{2,1,0:T(8,128)(2,1)} %broadcast_in_dim.117), calls=%async_computation | async-start | bytes 901120 | tf_op jit(solution)/shard_map/all_to_all | solution.py:113
  31.2 4.6 %copy-start.5 = (bf16[512,256]{1,0:T(8,128)(2,1)S(1)}, bf16[512,256]{1,0:T(8,128)(2,1)}, u32[]{:S(2)}) copy-start(bf16[512,256]{1,0:T(8,128)(2,1)} %param.15) | copy-start | bytes 786436
  31.2 4.6 %copy-start.15 = (f32[1,256]{1,0:T(1,128)S(1)}, f32[1,256]{1,0:T(1,128)}, u32[]{:S(2)}) copy-start(f32[1,256]{1,0:T(1,128)} %get-tuple-element.53) | copy-start | bytes 3076
  36.1 8.9 %copy-start.9 = (f32[256,20]{0,1:T(8,128)S(1)}, f32[256,20]{0,1:T(8,128)}, u32[]{:S(2)}) copy-start(f32[256,20]{0,1:T(8,128)} %get-tuple-element.49) | copy-start | bytes 61444
  39.9 10.3 %collective-permute-start.1 = (bf16[20,64,128]{2,1,0:T(8,128)(2,1)}, bf16[20,64,128]{2,1,0:T(8,128)(2,1)}, u32[]{:S(2)}, u32[]{:S(2)}) collective-permute-start(bf16[20,64,128]{2,1,0:T(8,128)(2,1)} %get-tuple-element.59), channel_id=1, source_target_pairs={{0,4},{4,8},{8,12},{1,5},{5,9},{9,13},{2,6},{6,10},{10,14},{3,7},{... | collective-permute-start | bytes 983048 | tf_op jit(solution)/shard_map/ppermute | solution.py:19
  56.6 2.7 %copy-start.6 = (f32[256,256]{1,0:T(8,128)S(1)}, f32[256,256]{1,0:T(8,128)}, u32[]{:S(2)}) copy-start(f32[256,256]{1,0:T(8,128)} %fusion.49) | copy-start | bytes 786436
  56.6 2.7 %copy-start.10 = (pred[256,256]{1,0:T(8,128)(4,1)S(1)}, pred[256,256]{1,0:T(8,128)(4,1)}, u32[]{:S(2)}) copy-start(pred[256,256]{1,0:T(8,128)(4,1)} %iota_compare_fusion) | copy-start | bytes 196612
  56.6 2.7 %copy-start.12 = (f32[20,256]{1,0:T(8,128)S(1)}, f32[20,256]{1,0:T(8,128)}, u32[]{:S(2)}) copy-start(f32[20,256]{1,0:T(8,128)} %get-tuple-element.42) | copy-start | bytes 61444
  59.3 1.7 %copy-start.20 = (f32[20]{0:T(128)S(1)}, f32[20]{0:T(128)}, u32[]{:S(2)}) copy-start(f32[20]{0:T(128)} %param.18) | copy-start | bytes 244
  63.0 2.2 %copy-start.17 = (f32[20]{0:T(128)S(1)}, f32[20]{0:T(128)}, u32[]{:S(2)}) copy-start(f32[20]{0:T(128)} %get-tuple-element.34) | copy-start | bytes 244
  65.2 16.7 %copy-start.16 = (f32[20]{0:T(128)S(1)}, f32[20]{0:T(128)}, u32[]{:S(2)}) copy-start(f32[20]{0:T(128)} %get-tuple-element.58) | copy-start | bytes 244
  67.2 14.6 %collective-permute-start.2 = (bf16[20,64,128]{2,1,0:T(8,128)(2,1)}, bf16[20,64,128]{2,1,0:T(8,128)(2,1)}, u32[]{:S(2)}, u32[]{:S(2)}) collective-permute-start(bf16[20,64,128]{2,1,0:T(8,128)(2,1)} %fusion.26), channel_id=1, source_target_pairs={{0,8},{4,12},{1,9},{5,13},{2,10},{6,14},{3,11},{7,15},{16,24},{20,... | collective-permute-start | bytes 983048 | tf_op jit(solution)/shard_map/ppermute | solution.py:19
  83.3 1.3 %copy-start.1 = (f32[256,1280]{1,0:T(8,128)S(1)}, f32[256,1280]{1,0:T(8,128)}, u32[]{:S(2)}) copy-start(f32[256,1280]{1,0:T(8,128)} %copy.82) | copy-start | bytes 3932164
  83.7 1.4 %copy-start.2 = (f32[256,1280]{1,0:T(8,128)S(1)}, f32[256,1280]{1,0:T(8,128)}, u32[]{:S(2)}) copy-start(f32[256,1280]{1,0:T(8,128)} %copy.81) | copy-start | bytes 3932164
  84.9 1.4 %copy-start.3 = (bf16[512,1280]{1,0:T(8,128)(2,1)S(1)}, bf16[512,1280]{1,0:T(8,128)(2,1)}, u32[]{:S(2)}) copy-start(bf16[512,1280]{1,0:T(8,128)(2,1)} %param.14) | copy-start | bytes 3932164
  86.3 8.1 %copy-start.13 = (f32[1280]{0:T(1024)S(1)}, f32[1280]{0:T(1024)}, u32[]{:S(2)}) copy-start(f32[1280]{0:T(1024)} %param.21) | copy-start | bytes 15364
  96.4 2.1 %copy-start = (bf16[512,1280]{1,0:T(8,128)(2,1)}, bf16[512,1280]{1,0:T(8,128)(2,1)S(1)}, u32[]{:S(2)}) copy-start(bf16[512,1280]{1,0:T(8,128)(2,1)S(1)} %multiply_convert_fusion.4) | copy-start | bytes 3932164
  96.4 1.6 %copy-start.4 = (bf16[160,8,160]{2,1,0:T(8,128)(2,1)S(1)}, bf16[160,8,160]{2,1,0:T(8,128)(2,1)}, u32[]{:S(2)}) copy-start(bf16[160,8,160]{2,1,0:T(8,128)(2,1)} %reshape.272) | copy-start | bytes 1228804
  96.4 1.6 %copy-start.8 = (pred[160,128]{1,0:T(8,128)(4,1)S(1)}, pred[160,128]{1,0:T(8,128)(4,1)}, u32[]{:S(2)}) copy-start(pred[160,128]{1,0:T(8,128)(4,1)} %compare_and_fusion) | copy-start | bytes 61444
  96.4 1.5 %copy-start.18 = (pred[128]{0:T(512)(128)(4,1)S(1)}, pred[128]{0:T(512)(128)(4,1)}, u32[]{:S(2)}) copy-start(pred[128]{0:T(512)(128)(4,1)} %get-tuple-element.24) | copy-start | bytes 388

commit v6 on v2

--- a/solution.py
+++ b/solution.py
@@ -58,13 +58,18 @@
 
 def exclusive_scan(state, decay, axis):
     count = lax.axis_size(axis)
+    heads, rows, cols = state.shape
     window = (state, decay)
     before = (jnp.zeros_like(state), jnp.zeros_like(decay))
     shift = 1
     while shift < count:
-        sent_state = passed_along(window[0].astype(jnp.bfloat16), axis, shift)
-        sent_decay = passed_along(window[1], axis, shift)
-        received = (sent_state.astype(jnp.float32), sent_decay)
+        decay_high = window[1].astype(jnp.bfloat16)
+        decay_low = (window[1] - decay_high.astype(jnp.float32)).astype(jnp.bfloat16)
+        decay_rows = jnp.zeros((1, rows, cols), jnp.bfloat16)
+        decay_rows = decay_rows.at[0, 0, :heads].set(decay_high).at[0, 1, :heads].set(decay_low)
+        sent = jnp.concatenate([window[0].astype(jnp.bfloat16), decay_rows], axis=0)
+        sent = passed_along(sent, axis, shift).astype(jnp.float32)
+        received = (sent[:heads], sent[heads, 0, :heads] + sent[heads, 1, :heads])
         before = combine(received, before)
         if shift * 2 < count:
             window = combine(received, window)

time: 109 us -> 112 us (1.028)
  starting transfers between devices: 21.9 us -> 18.3 us
  other arithmetic: 17.2 us -> 20.6 us
  matrix products: 15.8 us -> 17.5 us
  local copies, waits for them, and re-layouts: 18.6 us -> 20.1 us
    ppermute x4 -> x3, starting transfers between devices: 17.8 us -> 14.2 us  [passed_along(): lax.ppermute(value, axis, [(source, source + steps) for source in range(l...]
    dot_general x2, matrix products: 2.24 us -> 3.82 us  [stretch_local(): jnp.einsum('jhp,js->hps', weighted, b_block, preferred_element_type=jnp.f...]
    concatenate x2, local copies, waits for them, and re-layouts: 5.71 us -> 4.52 us  [local(): jnp.concatenate(pieces_out, axis=0)]
  transfers between devices with their start and end apart: 5 -> 4, of which waited for: 2 -> 2; matrix products, arithmetic and copies ran while one was open for 25% -> 31% of each run, Pallas kernels for 0% -> 0%
where the time goes in v6:
time: 112 us; the launch traced here: 111 us
  blocking collectives  31.3 us (28%)
  other arithmetic  20.6 us (18%)
  local copies, waits for them, and re-layouts  20.1 us (18%)
  starting transfers between devices  18.3 us (16%)
  matrix products  17.5 us (16%)
  waiting for transfers between devices  1.39 us (1%)
  between operations  1.35 us (1%)
    all_to_all x1, blocking collectives, local(): parts = lax.all_to_all(parts, 'seq', 0, 0, tiled=True).astype(jnp.float32)  25.5 us
    ppermute x3, starting transfers between devices, passed_along(): lax.ppermute(value, axis, [(source, source + steps) for source in range(l...  14.2 us
    psum x1, blocking collectives, local(): square_sum = lax.psum(jnp.sum(gated * gated, axis=1), 'tensor')  5.81 us
    dot_general x2, matrix products, stretch_local(): jnp.einsum('hij,jhp->ihp', mixing, x_block, preferred_element_type=jnp.fl...  5.8 us
    concatenate x2, local copies, waits for them, and re-layouts, local(): jnp.concatenate(pieces_out, axis=0)  4.52 us
    reduce_sum x1, other arithmetic, local(): square_sum = lax.psum(jnp.sum(gated * gated, axis=1), 'tensor')  4.26 us
    all_to_all x1, starting transfers between devices, local(): lax.all_to_all(query_rows.reshape(seq_count * pools_local, -1), 'seq', 0,...  4.13 us
    dot_general x2, matrix products, stretch_local(): jnp.einsum('jhp,js->hps', weighted, b_block, preferred_element_type=jnp.f...  3.82 us
  transfers between devices with their start and end apart: 4, of which 2 were waited for; matrix products, arithmetic and copies ran while one was open for 31% of the time, Pallas kernels for 0%

profile of v6, /device:TPU:0, one launch (start us, length us, event | category | flops | bytes accessed | tf_op | source)
XLA Modules:
  0.0 110.6 jit_solution(2656350478321249316)
XLA Ops:
  0.7 0.8 slice.258
  2.3 5.0 %collective-permute-start = (bf16[3,1536]{1,0:T(4,128)(2,1)S(1)}, bf16[3,1536]{1,0:T(4,128)(2,1)S(1)}, u32[]{:S(2)}, u32[]{:S(2)}) collective-permute-start(bf16[3,1536]{1,0:T(4,128)(2,1)S(1)} %pad_maximum_fusion.4), channel_id=1, source_target_pairs={{0,4},{4,8},{8,12},{1,5},{5,9},{9,13},{2,6},{6,10},{10,14},{3,7},{... | collective-permute-start | bytes 27656 | tf_op jit(solution)/shard_map/ppermute | solution.py:19
  8.1 1.0 concatenate.49
  9.1 0.8 broadcast_in_dim.117
  9.9 4.1 %all-to-all-start = ((bf16[4,40,1284]{2,1,0:T(8,128)(2,1)}), bf16[4,40,1284]{2,1,0:T(8,128)(2,1)}, u32[]{:S(2)}, u32[]{:S(2)}) async-start(bf16[4,40,1284]{2,1,0:T(8,128)(2,1)} %broadcast_in_dim.117), calls=%async_computation | async-start | bytes 901120 | tf_op jit(solution)/shard_map/all_to_all | solution.py:115
  14.7 0.8 fusion.84
  22.1 0.9 fusion.54
  23.2 2.6 %divide_convert_fusion = bf16[512,1280]{1,0:T(8,128)(2,1)S(1)} fusion(bf16[512,1280]{1,0:T(8,128)(2,1)S(1)} %copy-done.5, bf16[3,1280]{1,0:T(4,128)(2,1)S(1)} %slice.311, f32[1280]{0:T(1024)} %get-tuple-element.57, f32[1280]{0:T(1024)} %get-tuple-element.58, f32[1280]{0:T(1024)} %get-tuple-element.56, f32[1280]{0:T(1024)S(1)} %get-tuple-element.55), kind=kLoop, calls=%fused_computation.23 | loop fusion | flops 15728640 | bytes 2649600 | tf_op jit(solution)/shard_map/convert_element_type | solution.py:35
  25.9 1.1 copy.61
  26.9 1.1 copy.56
  28.0 1.5 %convolution_add_fusion.3 = f32[20,64,128]{2,1,0:T(8,128)S(1)} fusion(bf16[256,20,64]{0,2,1:T(8,128)(2,1)} %bitcast.98, f32[256,20]{0,1:T(8,128)S(1)} %get-tuple-element.73, f32[20]{0:T(128)S(1)} %copy-done.23, bf16[512,256]{1,0:T(8,128)(2,1)S(1)} %divide_convert_fusion.1), kind=kOutput, calls=%fused_computation.44 | convolution fusion | flops 85032960 | bytes 1401344 | tf_op jit(solution)/shard_map/jhp,js->hps/dot_general | solution.py:51
  29.5 2.3 %fusion.85 = (bf16[20,64,128]{2,1,0:T(8,128)(2,1)S(1)}, f32[20,64,128]{2,1,0:T(8,128)}) fusion(bf16[512,256]{1,0:T(8,128)(2,1)S(1)} %divide_convert_fusion.1, bf16[256,20,64]{0,2,1:T(8,128)(2,1)} %bitcast.101, f32[256,20]{0,1:T(8,128)} %get-tuple-element.74, f32[20,64,128]{2,1,0:T(8,128)S(1)} %convolution_add_fusion.3, f32[20]{0:T(128)} %get-tuple-element.87), kind=kOutput, calls=%fused_computation.171 | convolution fusion | flops 85360640 | bytes 2379856 | tf_op jit(solution)/shard_map/jhp,js->hps/dot_general | solution.py:51
  31.9 3.9 %collective-permute-start.1 = (bf16[21,64,128]{2,1,0:T(8,128)(2,1)S(1)}, bf16[21,64,128]{2,1,0:T(8,128)(2,1)S(1)}, u32[]{:S(2)}, u32[]{:S(2)}) collective-permute-start(bf16[21,64,128]{2,1,0:T(8,128)(2,1)S(1)} %pad_maximum_fusion.1), channel_id=1, source_target_pairs={{0,4},{4,8},{8,12},{1,5},{5,9},{9,13},{2,6},{6,10},{10,14},{3,7},{... | collective-permute-start | bytes 1032200 | tf_op jit(solution)/shard_map/ppermute | solution.py:19
  35.9 2.9 %fusion.17 = f32[256,20,64]{0,2,1:T(8,128)} fusion(bf16[256,20,64]{0,2,1:T(8,128)(2,1)S(1)} %bitcast.102, f32[20,256]{1,0:T(8,128)S(1)} %copy-done.19, f32[256,256]{1,0:T(8,128)S(1)} %copy-done.10, f32[20,256]{1,0:T(8,128)S(1)} %bitcast.113, pred[256,256]{1,0:T(8,128)(4,1)S(1)} %copy-done.15), kind=kOutput, calls=%fused_computation.28 | convolution fusion | flops 175636480 | bytes 2334720 | tf_op jit(solution)/shard_map/hij,jhp->ihp/dot_general | solution.py:48
  38.8 2.9 %fusion.18 = f32[256,20,64]{0,2,1:T(8,128)} fusion(bf16[256,20,64]{0,2,1:T(8,128)(2,1)S(1)} %bitcast.99, f32[20,256]{1,0:T(8,128)S(1)} %copy-done.18, f32[256,256]{1,0:T(8,128)S(1)} %fusion.58, f32[20,256]{1,0:T(8,128)S(1)} %bitcast.110, pred[256,256]{1,0:T(8,128)(4,1)S(1)} %copy-done.15), kind=kOutput, calls=%fused_computation.29 | convolution fusion | flops 175636480 | bytes 2334720 | tf_op jit(solution)/shard_map/hij,jhp->ihp/dot_general | solution.py:48
  41.7 0.8 collective-permute-done.1
  42.8 1.2 %add_convert_fusion = bf16[20,64,128]{2,1,0:T(8,128)(2,1)S(1)} fusion(f32[20,64,128]{2,1,0:T(8,128)} %get-tuple-element.91, f32[21,64,128]{2,1,0:T(8,128)S(1)} %convert_element_type.214, f32[20]{0:T(128)} %get-tuple-element.86), kind=kLoop, calls=%fused_computation.54 | loop fusion | flops 491520 | bytes 1638480 | tf_op jit(solution)/shard_map/convert_element_type | solution.py:70
  44.1 0.8 pad_maximum_fusion.2
  44.8 5.3 %collective-permute-start.2 = (bf16[21,64,128]{2,1,0:T(8,128)(2,1)}, bf16[21,64,128]{2,1,0:T(8,128)(2,1)S(1)}, u32[]{:S(2)}, u32[]{:S(2)}) collective-permute-start(bf16[21,64,128]{2,1,0:T(8,128)(2,1)} %pad_maximum_fusion.2), channel_id=1, source_target_pairs={{0,8},{4,12},{1,9},{5,13},{2,10},{6,14},{3,11},{7,15},{16,24},{20,... | collective-permute-start | bytes 1032200 | tf_op jit(solution)/shard_map/ppermute | solution.py:19
  50.2 0.8 slice_convert_fusion
  51.0 1.8 %slice.340 = bf16[160,1280]{1,0:T(8,128)(2,1)} slice(bf16[160,1284]{1,0:T(8,128)(2,1)} %bitcast.22), slice={[0:160], [0:1280]} | slice | bytes 819200 | tf_op jit(solution)/shard_map/slice | solution.py:118
  52.8 2.7 %reshape.391 = bf16[160,8,160]{2,1,0:T(8,128)(2,1)} reshape(bf16[160,1280]{1,0:T(8,128)(2,1)} %slice.340) | data formatting | bytes 819200 | tf_op jit(solution)/shard_map/reshape | solution.py:170
  56.8 1.5 %fusion.22 = f32[256,20,64]{0,2,1:T(8,128)} fusion(f32[256,20,64]{0,2,1:T(8,128)S(1)} %copy-done.7, f32[256,20,64]{0,2,1:T(8,128)S(1)} %fusion.42, f32[256,20]{0,1:T(8,128)S(1)} %copy-done.14, f32[20,64,128]{2,1,0:T(8,128)S(1)} %convolution_add_fusion.3, f32[20]{0:T(128)S(1)} %copy-done.22, bf16[512,256]{1,0:T(8,128)(2,1)S(1)} %divide_convert_fusion.1, ...), kind=kOutput, calls=%fused_computation.35 | convolution fusion | flops 86343680 | bytes 5661696 | tf_op jit(solution)/shard_map/is,hps->ihp/dot_general | solution.py:84
  58.3 1.7 %copy.63 = f32[256,1280]{1,0:T(8,128)S(1)} copy(f32[256,1280]{0,1:T(8,128)} %bitcast.97) | data formatting | bytes 2621440 | tf_op jit(solution)/shard_map/concatenate | solution.py:154
  60.0 1.5 %fusion.33 = f32[256,20,64]{0,2,1:T(8,128)S(1)} fusion(bf16[512,256]{1,0:T(8,128)(2,1)} %copy-done.2, f32[21,64,128]{2,1,0:T(8,128)S(1)} %convert_element_type.214, bf16[21,64,128]{2,1,0:T(8,128)(2,1)} %copy-done.1, f32[20]{0:T(128)S(1)} %get-tuple-element.71), kind=kOutput, calls=%fused_computation.64 | convolution fusion | flops 85032960 | bytes 2359808 | tf_op jit(solution)/shard_map/is,hps->ihp/dot_general | solution.py:84
  61.5 2.5 %fusion.21 = f32[256,20,64]{0,2,1:T(8,128)} fusion(f32[256,20,64]{0,2,1:T(8,128)S(1)} %copy-done.6, f32[256,20,64]{0,2,1:T(8,128)S(1)} %fusion.33, f32[256,20]{0,1:T(8,128)S(1)} %copy-done.13, bf16[512,256]{1,0:T(8,128)(2,1)} %copy-done.2, f32[21,64,128]{2,1,0:T(8,128)S(1)} %convert_element_type.214, bf16[21,64,128]{2,1,0:T(8,128)(2,1)} %copy-done.1, ...), kind=kOutput, calls=%fused_computation.34 | convolution fusion | flops 85524480 | bytes 5005824 | tf_op jit(solution)/shard_map/is,hps->ihp/dot_general | solution.py:83
  64.0 2.8 %copy.62 = f32[256,1280]{1,0:T(8,128)} copy(f32[256,1280]{0,1:T(8,128)} %bitcast.96) | data formatting | bytes 2621440 | tf_op jit(solution)/shard_map/concatenate | solution.py:154
  66.8 4.3 %multiply_reduce_fusion = (f32[512]{0:T(512)S(1)}, f32[512,1280]{1,0:T(8,128)}) fusion(bf16[512,1280]{1,0:T(8,128)(2,1)} %param.22, bf16[512,1280]{1,0:T(8,128)(2,1)S(1)} %divide_convert_fusion, f32[1280]{0:T(1024)S(1)} %mul.345, f32[256,1280]{1,0:T(8,128)S(1)} %copy.63, f32[256,1280]{1,0:T(8,128)} %copy.62), kind=kLoop, calls=%fused_computation.12 | loop fusion | flops 7208448 | bytes 7871488 | tf_op jit(solution)/shard_map/reduce_sum | solution.py:158
  71.0 5.8 %psum.7 = f32[512]{0:T(512)S(1)} all-reduce(f32[512]{0:T(512)S(1)} %get-tuple-element.65), channel_id=1, replica_groups=mesh['groups'=2,'seq'=4,'tensor'=4] {'tensor'}, use_global_device_ids=true, to_apply=%region_5.6 | all-reduce | flops 512 | bytes 4096 | tf_op jit(solution)/shard_map/psum | solution.py:158
  76.9 2.0 %multiply_convert_fusion.4 = bf16[512,1280]{1,0:T(8,128)(2,1)S(1)} fusion(f32[512,1280]{1,0:T(8,128)} %get-tuple-element.66, f32[1280]{0:T(1024)S(1)} %copy-done.20, f32[512]{0:T(512)S(1)} %add_rsqrt_fusion), kind=kLoop, calls=%fused_computation.11 | loop fusion | flops 1966080 | bytes 3939328 | tf_op jit(solution)/shard_map/convert_element_type | solution.py:162
  78.9 1.1 %gather_fusion = bf16[128,1280]{1,0:T(8,128)(2,1)S(1)} fusion(bf16[512,1280]{1,0:T(8,128)(2,1)S(1)} %multiply_convert_fusion.4, s32[1024]{0:T(1024)} %pad_clamp_fusion), kind=kCustom, calls=%fused_computation | custom fusion | bytes 655872 | tf_op jit(solution)/shard_map/jit(_take)/gather | solution.py:164
  82.8 25.5 %all_to_all.18 = bf16[4,40,1304]{2,1,0:T(8,128)(2,1)S(1)} all-to-all(bf16[4,40,1304]{2,1,0:T(8,128)(2,1)S(1)} %bitcast.103), channel_id=1, replica_groups=mesh['groups'=2,'seq'=4,'tensor'=4] {'seq'}, dimensions={0} | all-to-all | bytes 834560 | tf_op jit(solution)/shard_map/all_to_all | solution.py:196
  (141 shorter events, 15.6 us)
Async XLA Ops:
  0.6 21.1 %copy-start.9 = (bf16[512,256]{1,0:T(8,128)(2,1)S(1)}, bf16[512,256]{1,0:T(8,128)(2,1)}, u32[]{:S(2)}) copy-start(bf16[512,256]{1,0:T(8,128)(2,1)} %param.23) | copy-start | bytes 786436
  0.6 22.5 %copy-start.5 = (bf16[512,1280]{1,0:T(8,128)(2,1)S(1)}, bf16[512,1280]{1,0:T(8,128)(2,1)}, u32[]{:S(2)}) copy-start(bf16[512,1280]{1,0:T(8,128)(2,1)} %param.21) | copy-start | bytes 3932164
  0.7 17.0 %copy-start.17 = (bf16[4,1280]{1,0:T(4,128)(2,1)S(1)}, bf16[4,1280]{1,0:T(4,128)(2,1)}, u32[]{:S(2)}) copy-start(bf16[4,1280]{1,0:T(4,128)(2,1)} %param.27) | copy-start | bytes 30724
  0.7 18.3 %copy-start.16 = (f32[20,512]{1,0:T(8,128)S(1)}, f32[20,512]{1,0:T(8,128)}, u32[]{:S(2)}) copy-start(f32[20,512]{1,0:T(8,128)} %param.24) | copy-start | bytes 122884
  0.7 19.0 %copy-start.21 = (bf16[4,256]{1,0:T(4,128)(2,1)S(1)}, bf16[4,256]{1,0:T(4,128)(2,1)}, u32[]{:S(2)}) copy-start(bf16[4,256]{1,0:T(4,128)(2,1)} %param.28) | copy-start | bytes 6148
  0.7 19.0 %copy-start.29 = (s32[128]{0:T(128)S(1)}, s32[128]{0:T(128)}, u32[]{:S(2)}) copy-start(s32[128]{0:T(128)} %param.30) | copy-start | bytes 1540
  0.7 20.7 %copy-start.27 = (f32[20]{0:T(128)S(1)}, f32[20]{0:T(128)}, u32[]{:S(2)}) copy-start(f32[20]{0:T(128)} %param.26) | copy-start | bytes 244
  2.3 19.4 %collective-permute-start = (bf16[3,1536]{1,0:T(4,128)(2,1)S(1)}, bf16[3,1536]{1,0:T(4,128)(2,1)S(1)}, u32[]{:S(2)}, u32[]{:S(2)}) collective-permute-start(bf16[3,1536]{1,0:T(4,128)(2,1)S(1)} %pad_maximum_fusion.4), channel_id=1, source_target_pairs={{0,4},{4,8},{8,12},{1,5},{5,9},{9,13},{2,6},{6,10},{10,14},{3,7},{... | collective-permute-start | bytes 27656 | tf_op jit(solution)/shard_map/ppermute | solution.py:19
  9.9 40.2 %all-to-all-start = ((bf16[4,40,1284]{2,1,0:T(8,128)(2,1)}), bf16[4,40,1284]{2,1,0:T(8,128)(2,1)}, u32[]{:S(2)}, u32[]{:S(2)}) async-start(bf16[4,40,1284]{2,1,0:T(8,128)(2,1)} %broadcast_in_dim.117), calls=%async_computation | async-start | bytes 901120 | tf_op jit(solution)/shard_map/all_to_all | solution.py:115
  17.4 8.5 %copy-start.11 = (f32[3,8,2,128]{3,1,2,0:T(8,128)}, f32[3,8,2,128]{3,1,2,0:T(8,128)S(1)}, u32[]{:S(2)}) copy-start(f32[3,8,2,128]{3,1,2,0:T(8,128)S(1)} %copy.78) | copy-start | bytes 73732
  17.6 3.2 %copy-start.25 = (f32[20]{0:T(128)}, f32[20]{0:T(128)S(1)}, u32[]{:S(2)}) copy-start(f32[20]{0:T(128)S(1)} %get-tuple-element.53) | copy-start | bytes 244
  22.0 34.7 %copy-start.2 = (bf16[512,256]{1,0:T(8,128)(2,1)}, bf16[512,256]{1,0:T(8,128)(2,1)S(1)}, u32[]{:S(2)}) copy-start(bf16[512,256]{1,0:T(8,128)(2,1)S(1)} %divide_convert_fusion.1) | copy-start | bytes 786436
  25.8 2.3 %copy-start.23 = (f32[20]{0:T(128)S(1)}, f32[20]{0:T(128)}, u32[]{:S(2)}) copy-start(f32[20]{0:T(128)} %get-tuple-element.88) | copy-start | bytes 244
  26.9 8.9 %copy-start.12 = (f32[3,8,2,128]{3,1,2,0:T(8,128)S(1)}, f32[3,8,2,128]{3,1,2,0:T(8,128)}, u32[]{:S(2)}) copy-start(f32[3,8,2,128]{3,1,2,0:T(8,128)} %copy-done.11) | copy-start | bytes 73732
  28.0 7.8 %copy-start.4 = (bf16[256,1280]{0,1:T(8,128)(2,1)S(1)}, bf16[256,1280]{0,1:T(8,128)(2,1)}, u32[]{:S(2)}) copy-start(bf16[256,1280]{0,1:T(8,128)(2,1)} %copy.61) | copy-start | bytes 1966084
  28.0 7.8 %copy-start.10 = (f32[256,256]{1,0:T(8,128)S(1)}, f32[256,256]{1,0:T(8,128)}, u32[]{:S(2)}) copy-start(f32[256,256]{1,0:T(8,128)} %fusion.54) | copy-start | bytes 786436
  28.0 7.8 %copy-start.15 = (pred[256,256]{1,0:T(8,128)(4,1)S(1)}, pred[256,256]{1,0:T(8,128)(4,1)}, u32[]{:S(2)}) copy-start(pred[256,256]{1,0:T(8,128)(4,1)} %iota_compare_fusion) | copy-start | bytes 196612
  28.0 7.8 %copy-start.19 = (f32[20,256]{1,0:T(8,128)S(1)}, f32[20,256]{1,0:T(8,128)}, u32[]{:S(2)}) copy-start(f32[20,256]{1,0:T(8,128)} %get-tuple-element.75) | copy-start | bytes 61444
  31.9 10.6 %collective-permute-start.1 = (bf16[21,64,128]{2,1,0:T(8,128)(2,1)S(1)}, bf16[21,64,128]{2,1,0:T(8,128)(2,1)S(1)}, u32[]{:S(2)}, u32[]{:S(2)}) collective-permute-start(bf16[21,64,128]{2,1,0:T(8,128)(2,1)S(1)} %pad_maximum_fusion.1), channel_id=1, source_target_pairs={{0,4},{4,8},{8,12},{1,5},{5,9},{9,13},{2,6},{6,10},{10,14},{3,7},{... | collective-permute-start | bytes 1032200 | tf_op jit(solution)/shard_map/ppermute | solution.py:19
  35.9 2.9 %copy-start.3 = (bf16[256,1280]{0,1:T(8,128)(2,1)S(1)}, bf16[256,1280]{0,1:T(8,128)(2,1)}, u32[]{:S(2)}) copy-start(bf16[256,1280]{0,1:T(8,128)(2,1)} %copy.56) | copy-start | bytes 1966084
  35.9 2.9 %copy-start.18 = (f32[20,256]{1,0:T(8,128)S(1)}, f32[20,256]{1,0:T(8,128)}, u32[]{:S(2)}) copy-start(f32[20,256]{1,0:T(8,128)} %get-tuple-element.72) | copy-start | bytes 61444
  38.8 3.8 %copy-start.26 = (f32[20]{0:T(128)S(1)}, f32[20]{0:T(128)}, u32[]{:S(2)}) copy-start(f32[20]{0:T(128)} %copy-done.25) | copy-start | bytes 244
  41.7 14.0 %copy-start.28 = (s32[128]{0:T(128)S(1)}, s32[128]{0:T(128)}, u32[]{:S(2)}) copy-start(s32[128]{0:T(128)} %iota_add_fusion) | copy-start | bytes 1540
  42.6 13.8 %copy-start.22 = (f32[20]{0:T(128)S(1)}, f32[20]{0:T(128)}, u32[]{:S(2)}) copy-start(f32[20]{0:T(128)} %get-tuple-element.89) | copy-start | bytes 244
  44.8 11.5 %collective-permute-start.2 = (bf16[21,64,128]{2,1,0:T(8,128)(2,1)}, bf16[21,64,128]{2,1,0:T(8,128)(2,1)S(1)}, u32[]{:S(2)}, u32[]{:S(2)}) collective-permute-start(bf16[21,64,128]{2,1,0:T(8,128)(2,1)} %pad_maximum_fusion.2), channel_id=1, source_target_pairs={{0,8},{4,12},{1,9},{5,13},{2,10},{6,14},{3,11},{7,15},{16,24},{20,... | collective-permute-start | bytes 1032200 | tf_op jit(solution)/shard_map/ppermute | solution.py:19
  50.9 5.8 %copy-start.14 = (f32[256,20]{0,1:T(8,128)S(1)}, f32[256,20]{0,1:T(8,128)}, u32[]{:S(2)}) copy-start(f32[256,20]{0,1:T(8,128)} %get-tuple-element.78) | copy-start | bytes 61444
  56.4 1.9 %copy-start.1 = (bf16[21,64,128]{2,1,0:T(8,128)(2,1)}, bf16[21,64,128]{2,1,0:T(8,128)(2,1)S(1)}, u32[]{:S(2)}) copy-start(bf16[21,64,128]{2,1,0:T(8,128)(2,1)S(1)} %collective-permute-done.2) | copy-start | bytes 1032196
  58.3 3.2 %copy-start.13 = (f32[256,20]{0,1:T(8,128)S(1)}, f32[256,20]{0,1:T(8,128)}, u32[]{:S(2)}) copy-start(f32[256,20]{0,1:T(8,128)} %get-tuple-element.79) | copy-start | bytes 61444
  66.8 10.1 %copy-start.20 = (f32[1280]{0:T(1024)S(1)}, f32[1280]{0:T(1024)}, u32[]{:S(2)}) copy-start(f32[1280]{0:T(1024)} %param.29) | copy-start | bytes 15364
  78.9 2.1 %copy-start = (bf16[512,1280]{1,0:T(8,128)(2,1)}, bf16[512,1280]{1,0:T(8,128)(2,1)S(1)}, u32[]{:S(2)}) copy-start(bf16[512,1280]{1,0:T(8,128)(2,1)S(1)} %multiply_convert_fusion.4) | copy-start | bytes 3932164
  78.9 1.6 %copy-start.8 = (bf16[160,8,160]{2,1,0:T(8,128)(2,1)S(1)}, bf16[160,8,160]{2,1,0:T(8,128)(2,1)}, u32[]{:S(2)}) copy-start(bf16[160,8,160]{2,1,0:T(8,128)(2,1)} %reshape.391) | copy-start | bytes 1228804
  78.9 1.6 %copy-start.24 = (pred[128]{0:T(512)(128)(4,1)S(1)}, pred[128]{0:T(512)(128)(4,1)}, u32[]{:S(2)}) copy-start(pred[128]{0:T(512)(128)(4,1)} %get-tuple-element.63) | copy-start | bytes 388
  (2 other events, 2.9 us)

commit v7 on v2

--- a/solution.py
+++ b/solution.py
@@ -70,6 +70,18 @@
             window = combine(received, window)
         shift *= 2
     return before[0]
+
+
+def butterfly_sum(value, axis):
+    count = lax.axis_size(axis)
+    if count & (count - 1):
+        return lax.psum(value, axis)
+    stride = 1
+    while stride < count:
+        partner = lax.ppermute(value, axis, [(i, i ^ stride) for i in range(count)])
+        value = value + partner
+        stride *= 2
+    return value
 
 
 def read_state(c_block, state_in):
@@ -150,7 +162,7 @@
         jnp.float32
     )
     gated = ssd_out.reshape(tok_rows, channels) * silu_act(z_gate.astype(jnp.float32))
-    square_sum = lax.psum(jnp.sum(gated * gated, axis=1), "tensor")
+    square_sum = butterfly_sum(jnp.sum(gated * gated, axis=1), "tensor")
     width_all = channels * lax.axis_size("tensor")
     mixed_seq = (
         gated * lax.rsqrt(square_sum / width_all + EPSILON)[:, None] * norm_gain[None, :]

time: 109 us -> 106 us (0.972)
  blocking collectives: 31 us -> 25.1 us
  waiting for transfers between devices: 1.88 us -> 5.49 us
  starting transfers between devices: 21.9 us -> 23.4 us
  matrix products: 15.8 us -> 14.5 us
    psum x1 -> x0, blocking collectives: 5.81 us -> none  [local(): square_sum = lax.psum(jnp.sum(gated * gated, axis=1), 'tensor')]
    ppermute x4, waiting for transfers between devices: 1.88 us -> 4.48 us  [passed_along(): lax.ppermute(value, axis, [(source, source + steps) for source in range(l...]
    ppermute x0 -> x2, starting transfers between devices: none -> 1.49 us  [butterfly_sum(): partner = lax.ppermute(value, axis, [(i, i ^ stride) for i in range(count)])]
  transfers between devices with their start and end apart: 5 -> 7, of which waited for: 2 -> 4; matrix products, arithmetic and copies ran while one was open for 25% -> 24% of each run, Pallas kernels for 0% -> 0%
where the time goes in v7:
time: 106 us; the launch traced here: 105 us
  blocking collectives  25.1 us (24%)
  starting transfers between devices  23.4 us (22%)
  local copies, waits for them, and re-layouts  18.2 us (17%)
  other arithmetic  17.4 us (16%)
  matrix products  14.5 us (14%)
  waiting for transfers between devices  5.49 us (5%)
  between operations  1.31 us (1%)
    all_to_all x1, blocking collectives, local(): parts = lax.all_to_all(parts, 'seq', 0, 0, tiled=True).astype(jnp.float32)  25.1 us
    ppermute x4, starting transfers between devices, passed_along(): lax.ppermute(value, axis, [(source, source + steps) for source in range(l...  17.8 us
    dot_general x2, matrix products, stretch_local(): jnp.einsum('hij,jhp->ihp', mixing, x_block, preferred_element_type=jnp.fl...  5.82 us
    concatenate x2, local copies, waits for them, and re-layouts, local(): jnp.concatenate(pieces_out, axis=0)  5.71 us
    ppermute x4, waiting for transfers between devices, passed_along(): lax.ppermute(value, axis, [(source, source + steps) for source in range(l...  4.48 us
    reduce_sum x1, other arithmetic, local(): square_sum = butterfly_sum(jnp.sum(gated * gated, axis=1), 'tensor')  4.24 us
    all_to_all x1, starting transfers between devices, local(): lax.all_to_all(query_rows.reshape(seq_count * pools_local, -1), 'seq', 0,...  4.12 us
    dot_general x2, matrix products, read_state(): jnp.einsum('is,hps->ihp', c_block, state_high, preferred_element_type=jnp...  2.49 us
  transfers between devices with their start and end apart: 7, of which 4 were waited for; matrix products, arithmetic and copies ran while one was open for 24% of the time, Pallas kernels for 0%

profile of v7, /device:TPU:0, one launch (start us, length us, event | category | flops | bytes accessed | tf_op | source)
XLA Modules:
  0.0 105.4 jit_solution(4616297774633751183)
XLA Ops:
  2.2 5.0 %collective-permute-start = (bf16[3,1536]{1,0:T(4,128)(2,1)S(1)}, bf16[3,1536]{1,0:T(4,128)(2,1)S(1)}, u32[]{:S(2)}, u32[]{:S(2)}) collective-permute-start(bf16[3,1536]{1,0:T(4,128)(2,1)S(1)} %pad_maximum_fusion.2), channel_id=1, source_target_pairs={{0,4},{4,8},{8,12},{1,5},{5,9},{9,13},{2,6},{6,10},{10,14},{3,7},{... | collective-permute-start | bytes 27656 | tf_op jit(solution)/shard_map/ppermute | solution.py:19
  10.7 3.5 %collective-permute-start.3 = (f32[20]{0:T(128)S(1)}, f32[20]{0:T(128)S(1)}, u32[]{:S(2)}, u32[]{:S(2)}) collective-permute-start(f32[20]{0:T(128)S(1)} %get-tuple-element.37), channel_id=1, source_target_pairs={{0,4},{4,8},{8,12},{1,5},{5,9},{9,13},{2,6},{6,10},{10,14},{3,7},{... | collective-permute-start | bytes 248 | tf_op jit(solution)/shard_map/ppermute | solution.py:19
  15.1 1.0 concatenate.32
  16.1 0.8 broadcast_in_dim.117
  16.9 4.1 %all-to-all-start = ((bf16[4,40,1284]{2,1,0:T(8,128)(2,1)}), bf16[4,40,1284]{2,1,0:T(8,128)(2,1)}, u32[]{:S(2)}, u32[]{:S(2)}) async-start(bf16[4,40,1284]{2,1,0:T(8,128)(2,1)} %broadcast_in_dim.117), calls=%async_computation | async-start | bytes 901120 | tf_op jit(solution)/shard_map/all_to_all | solution.py:122
  23.8 1.8 %divide_convert_fusion = bf16[512,1280]{1,0:T(8,128)(2,1)S(1)} fusion(bf16[512,1280]{1,0:T(8,128)(2,1)S(1)} %copy-done.4, bf16[3,1280]{1,0:T(4,128)(2,1)S(1)} %slice.202, f32[1280]{0:T(1024)S(1)} %get-tuple-element.6, f32[1280]{0:T(1024)S(1)} %get-tuple-element.7, f32[1280]{0:T(1024)S(1)} %get-tuple-element.5, f32[1280]{0:T(1024)S(1)} %get-tuple-element.4), kind=kLoop, calls=%fused_computation.23 | loop fusion | flops 15728640 | bytes 2649600 | tf_op jit(solution)/shard_map/convert_element_type | solution.py:35
  25.8 1.1 %copy.61 = bf16[256,1280]{0,1:T(8,128)(2,1)} copy(bf16[256,1280]{1,0:T(8,128)(2,1)S(1)} %get-tuple-element.19) | data formatting | bytes 1310720 | tf_op jit(solution)/shard_map/slice | solution.py:144
  27.2 0.9 fusion.58
  28.4 1.2 %convolution_add_fusion.3 = f32[20,64,128]{2,1,0:T(8,128)S(1)} fusion(bf16[256,20,64]{0,2,1:T(8,128)(2,1)S(1)} %bitcast.82, f32[256,20]{0,1:T(8,128)} %get-tuple-element.21, f32[20]{0:T(128)} %get-tuple-element.35, bf16[512,256]{1,0:T(8,128)(2,1)S(1)} %divide_convert_fusion.1), kind=kOutput, calls=%fused_computation.44 | convolution fusion | flops 85032960 | bytes 1396816 | tf_op jit(solution)/shard_map/jhp,js->hps/dot_general | solution.py:51
  29.6 1.1 %fusion.89 = (bf16[20,64,128]{2,1,0:T(8,128)(2,1)S(1)}, f32[20,64,128]{2,1,0:T(8,128)S(1)}) fusion(bf16[512,256]{1,0:T(8,128)(2,1)S(1)} %divide_convert_fusion.1, bf16[256,20,64]{0,2,1:T(8,128)(2,1)S(1)} %bitcast.85, f32[256,20]{0,1:T(8,128)} %get-tuple-element.22, f32[20,64,128]{2,1,0:T(8,128)S(1)} %convolution_add_fusion.3, f32[20]{0:T(128)} %get-tuple-element.38), kind=kOutput, calls=%fused_computation.164 | convolution fusion | flops 85360640 | bytes 2379856 | tf_op jit(solution)/shard_map/jhp,js->hps/dot_general | solution.py:51
  30.7 3.9 %collective-permute-start.1 = (bf16[20,64,128]{2,1,0:T(8,128)(2,1)S(1)}, bf16[20,64,128]{2,1,0:T(8,128)(2,1)S(1)}, u32[]{:S(2)}, u32[]{:S(2)}) collective-permute-start(bf16[20,64,128]{2,1,0:T(8,128)(2,1)S(1)} %get-tuple-element.39), channel_id=1, source_target_pairs={{0,4},{4,8},{8,12},{1,5},{5,9},{9,13},{2,6},{6,10},{10,14},{3,7},{... | collective-permute-start | bytes 983048 | tf_op jit(solution)/shard_map/ppermute | solution.py:19
  34.6 2.9 %fusion.17 = f32[256,20,64]{0,2,1:T(8,128)} fusion(bf16[256,20,64]{0,2,1:T(8,128)(2,1)S(1)} %bitcast.86, f32[20,256]{1,0:T(8,128)S(1)} %copy-done.19, f32[256,256]{1,0:T(8,128)S(1)} %copy-done.8, f32[20,256]{1,0:T(8,128)S(1)} %bitcast.97, pred[256,256]{1,0:T(8,128)(4,1)S(1)} %copy-done.15), kind=kOutput, calls=%fused_computation.28 | convolution fusion | flops 175636480 | bytes 2334720 | tf_op jit(solution)/shard_map/hij,jhp->ihp/dot_general | solution.py:48
  37.7 2.9 %collective-permute-done.1 = bf16[20,64,128]{2,1,0:T(8,128)(2,1)S(1)} collective-permute-done((bf16[20,64,128]{2,1,0:T(8,128)(2,1)S(1)}, bf16[20,64,128]{2,1,0:T(8,128)(2,1)S(1)}, u32[]{:S(2)}, u32[]{:S(2)}) %collective-permute-start.1) | collective-permute-done | bytes 327712 | tf_op jit(solution)/shard_map/ppermute | solution.py:19
  40.7 0.9 fusion.28
  41.6 5.5 %collective-permute-start.2 = (bf16[20,64,128]{2,1,0:T(8,128)(2,1)}, bf16[20,64,128]{2,1,0:T(8,128)(2,1)S(1)}, u32[]{:S(2)}, u32[]{:S(2)}) collective-permute-start(bf16[20,64,128]{2,1,0:T(8,128)(2,1)} %fusion.28), channel_id=1, source_target_pairs={{0,8},{4,12},{1,9},{5,13},{2,10},{6,14},{3,11},{7,15},{16,24},{20,... | collective-permute-start | bytes 983048 | tf_op jit(solution)/shard_map/ppermute | solution.py:19
  47.1 2.9 %fusion.18 = f32[256,20,64]{0,2,1:T(8,128)} fusion(bf16[256,20,64]{0,2,1:T(8,128)(2,1)S(1)} %bitcast.83, f32[20,256]{1,0:T(8,128)S(1)} %copy-done.18, f32[256,256]{1,0:T(8,128)S(1)} %fusion.62, f32[20,256]{1,0:T(8,128)S(1)} %bitcast.94, pred[256,256]{1,0:T(8,128)(4,1)S(1)} %copy-done.15), kind=kOutput, calls=%fused_computation.29 | convolution fusion | flops 175636480 | bytes 2334720 | tf_op jit(solution)/shard_map/hij,jhp->ihp/dot_general | solution.py:48
  50.0 0.9 slice_convert_fusion
  50.9 1.5 %collective-permute-done.2 = bf16[20,64,128]{2,1,0:T(8,128)(2,1)S(1)} collective-permute-done((bf16[20,64,128]{2,1,0:T(8,128)(2,1)}, bf16[20,64,128]{2,1,0:T(8,128)(2,1)S(1)}, u32[]{:S(2)}, u32[]{:S(2)}) %collective-permute-start.2) | collective-permute-done | bytes 327712 | tf_op jit(solution)/shard_map/ppermute | solution.py:19
  52.5 1.0 fusion.48
  53.5 1.5 %fusion.22 = f32[256,20,64]{0,2,1:T(8,128)} fusion(f32[256,20,64]{0,2,1:T(8,128)S(1)} %copy-done.6, f32[256,20,64]{0,2,1:T(8,128)S(1)} %fusion.48, f32[256,20]{0,1:T(8,128)S(1)} %copy-done.14, bf16[512,256]{1,0:T(8,128)(2,1)S(1)} %divide_convert_fusion.1, f32[20,64,128]{2,1,0:T(8,128)S(1)} %convolution_add_fusion.3, ...), kind=kOutput, calls=%fused_computation.35 | convolution fusion | flops 86507520 | bytes 5334016 | tf_op jit(solution)/shard_map/is,hps->ihp/dot_general | solution.py:91
  55.0 2.8 %copy.63 = f32[256,1280]{1,0:T(8,128)} copy(f32[256,1280]{0,1:T(8,128)} %bitcast.81) | data formatting | bytes 2621440 | tf_op jit(solution)/shard_map/concatenate | solution.py:161
  58.2 0.9 copy-done.5
  59.1 1.4 %fusion.21 = f32[256,20,64]{0,2,1:T(8,128)} fusion(f32[256,20,64]{0,2,1:T(8,128)S(1)} %copy-done.5, f32[256,20,64]{0,2,1:T(8,128)S(1)} %fusion.37, f32[256,20]{0,1:T(8,128)S(1)} %copy-done.13, bf16[20,64,128]{2,1,0:T(8,128)(2,1)S(1)} %collective-permute-done.1, bf16[20,64,128]{2,1,0:T(8,128)(2,1)S(1)} %collective-permute-done.2, f32[20]{0:T(128)S(1)} %exp.71, ...), kind=kOutput, calls=%fused_computation.34 | convolution fusion | flops 85688320 | bytes 4678144 | tf_op jit(solution)/shard_map/is,hps->ihp/dot_general | solution.py:90
  60.6 2.9 %copy.62 = f32[256,1280]{1,0:T(8,128)} copy(f32[256,1280]{0,1:T(8,128)} %bitcast.80) | data formatting | bytes 2621440 | tf_op jit(solution)/shard_map/concatenate | solution.py:161
  63.5 4.2 %multiply_reduce_fusion = (f32[512]{0:T(512)S(1)}, f32[512,1280]{1,0:T(8,128)}) fusion(bf16[512,1280]{1,0:T(8,128)(2,1)} %param.14, bf16[512,1280]{1,0:T(8,128)(2,1)S(1)} %divide_convert_fusion, f32[1280]{0:T(1024)S(1)} %mul.345, f32[256,1280]{1,0:T(8,128)S(1)} %copy-done.1, f32[256,1280]{1,0:T(8,128)} %copy.62), kind=kLoop, calls=%fused_computation.12 | loop fusion | flops 7208448 | bytes 7871488 | tf_op jit(solution)/shard_map/reduce_sum | solution.py:165
  68.0 0.9 collective-permute-done.4
  68.9 1.5 %collective-permute-start.5 = (f32[512]{0:T(512)S(1)}, f32[512]{0:T(512)S(1)}, u32[]{:S(2)}, u32[]{:S(2)}) collective-permute-start(f32[512]{0:T(512)S(1)} %add.140), channel_id=1, source_target_pairs={{0,2},{1,3},{2,0},{3,1},{4,6},{5,7},{6,4},{7,5},{8,10},{9,11},{10,... | collective-permute-start | bytes 6152 | tf_op jit(solution)/shard_map/ppermute | solution.py:81
  70.5 1.0 slice.227
  71.6 0.8 reshape.231
  72.5 2.0 %multiply_convert_fusion.4 = bf16[512,1280]{1,0:T(8,128)(2,1)S(1)} fusion(f32[512,1280]{1,0:T(8,128)} %get-tuple-element.15, f32[1280]{0:T(1024)S(1)} %copy-done.20, f32[512]{0:T(512)S(1)} %add_rsqrt_fusion), kind=kLoop, calls=%fused_computation.11 | loop fusion | flops 1966080 | bytes 3939328 | tf_op jit(solution)/shard_map/convert_element_type | solution.py:169
  74.6 0.9 gather_fusion
  78.0 25.1 %all_to_all.18 = bf16[4,40,1304]{2,1,0:T(8,128)(2,1)S(1)} all-to-all(bf16[4,40,1304]{2,1,0:T(8,128)(2,1)S(1)} %bitcast.87), channel_id=1, replica_groups=mesh['groups'=2,'seq'=4,'tensor'=4] {'seq'}, dimensions={0} | all-to-all | bytes 834560 | tf_op jit(solution)/shard_map/all_to_all | solution.py:203
  (134 shorter events, 15.2 us)
Async XLA Ops:
  0.6 23.2 %copy-start.4 = (bf16[512,1280]{1,0:T(8,128)(2,1)S(1)}, bf16[512,1280]{1,0:T(8,128)(2,1)}, u32[]{:S(2)}) copy-start(bf16[512,1280]{1,0:T(8,128)(2,1)} %param.13) | copy-start | bytes 3932164
  0.6 21.0 %copy-start.17 = (bf16[4,1280]{1,0:T(4,128)(2,1)S(1)}, bf16[4,1280]{1,0:T(4,128)(2,1)}, u32[]{:S(2)}) copy-start(bf16[4,1280]{1,0:T(4,128)(2,1)} %param.19) | copy-start | bytes 30724
  0.7 21.1 %copy-start.16 = (f32[20,512]{1,0:T(8,128)S(1)}, f32[20,512]{1,0:T(8,128)}, u32[]{:S(2)}) copy-start(f32[20,512]{1,0:T(8,128)} %param.16) | copy-start | bytes 122884
  0.7 21.8 %copy-start.21 = (bf16[4,256]{1,0:T(4,128)(2,1)S(1)}, bf16[4,256]{1,0:T(4,128)(2,1)}, u32[]{:S(2)}) copy-start(bf16[4,256]{1,0:T(4,128)(2,1)} %param.20) | copy-start | bytes 6148
  0.7 21.8 %copy-start.27 = (s32[128]{0:T(128)S(1)}, s32[128]{0:T(128)}, u32[]{:S(2)}) copy-start(s32[128]{0:T(128)} %param.22) | copy-start | bytes 1540
  0.7 22.9 %copy-start.25 = (f32[20]{0:T(128)S(1)}, f32[20]{0:T(128)}, u32[]{:S(2)}) copy-start(f32[20]{0:T(128)} %param.18) | copy-start | bytes 244
  2.2 21.6 %collective-permute-start = (bf16[3,1536]{1,0:T(4,128)(2,1)S(1)}, bf16[3,1536]{1,0:T(4,128)(2,1)S(1)}, u32[]{:S(2)}, u32[]{:S(2)}) collective-permute-start(bf16[3,1536]{1,0:T(4,128)(2,1)S(1)} %pad_maximum_fusion.2), channel_id=1, source_target_pairs={{0,4},{4,8},{8,12},{1,5},{5,9},{9,13},{2,6},{6,10},{10,14},{3,7},{... | collective-permute-start | bytes 27656 | tf_op jit(solution)/shard_map/ppermute | solution.py:19
  8.9 14.9 %copy-start.9 = (f32[3,8,2,128]{3,1,2,0:T(8,128)}, f32[3,8,2,128]{3,1,2,0:T(8,128)S(1)}, u32[]{:S(2)}) copy-start(f32[3,8,2,128]{3,1,2,0:T(8,128)S(1)} %copy.77) | copy-start | bytes 73732
  9.9 13.9 %copy-start.11 = (f32[3,8,2,128]{3,1,2,0:T(8,128)}, f32[3,8,2,128]{3,1,2,0:T(8,128)S(1)}, u32[]{:S(2)}) copy-start(f32[3,8,2,128]{3,1,2,0:T(8,128)S(1)} %copy.78) | copy-start | bytes 73732
  10.7 13.1 %collective-permute-start.3 = (f32[20]{0:T(128)S(1)}, f32[20]{0:T(128)S(1)}, u32[]{:S(2)}, u32[]{:S(2)}) collective-permute-start(f32[20]{0:T(128)S(1)} %get-tuple-element.37), channel_id=1, source_target_pairs={{0,4},{4,8},{8,12},{1,5},{5,9},{9,13},{2,6},{6,10},{10,14},{3,7},{... | collective-permute-start | bytes 248 | tf_op jit(solution)/shard_map/ppermute | solution.py:19
  16.9 33.1 %all-to-all-start = ((bf16[4,40,1284]{2,1,0:T(8,128)(2,1)}), bf16[4,40,1284]{2,1,0:T(8,128)(2,1)}, u32[]{:S(2)}, u32[]{:S(2)}) async-start(bf16[4,40,1284]{2,1,0:T(8,128)(2,1)} %broadcast_in_dim.117), calls=%async_computation | async-start | bytes 901120 | tf_op jit(solution)/shard_map/all_to_all | solution.py:122
  26.9 2.7 %copy-start.2 = (bf16[256,1280]{0,1:T(8,128)(2,1)S(1)}, bf16[256,1280]{0,1:T(8,128)(2,1)}, u32[]{:S(2)}) copy-start(bf16[256,1280]{0,1:T(8,128)(2,1)} %copy.61) | copy-start | bytes 1966084
  28.3 6.2 %copy-start.3 = (bf16[256,1280]{0,1:T(8,128)(2,1)S(1)}, bf16[256,1280]{0,1:T(8,128)(2,1)}, u32[]{:S(2)}) copy-start(bf16[256,1280]{0,1:T(8,128)(2,1)} %copy.61) | copy-start | bytes 1966084
  28.4 6.2 %copy-start.8 = (f32[256,256]{1,0:T(8,128)S(1)}, f32[256,256]{1,0:T(8,128)}, u32[]{:S(2)}) copy-start(f32[256,256]{1,0:T(8,128)} %fusion.58) | copy-start | bytes 786436
  28.4 6.2 %copy-start.12 = (f32[3,8,2,128]{3,1,2,0:T(8,128)S(1)}, f32[3,8,2,128]{3,1,2,0:T(8,128)}, u32[]{:S(2)}) copy-start(f32[3,8,2,128]{3,1,2,0:T(8,128)} %copy-done.11) | copy-start | bytes 73732
  28.4 6.2 %copy-start.15 = (pred[256,256]{1,0:T(8,128)(4,1)S(1)}, pred[256,256]{1,0:T(8,128)(4,1)}, u32[]{:S(2)}) copy-start(pred[256,256]{1,0:T(8,128)(4,1)} %iota_compare_fusion) | copy-start | bytes 196612
  28.4 6.2 %copy-start.19 = (f32[20,256]{1,0:T(8,128)S(1)}, f32[20,256]{1,0:T(8,128)}, u32[]{:S(2)}) copy-start(f32[20,256]{1,0:T(8,128)} %get-tuple-element.23) | copy-start | bytes 61444
  30.7 10.0 %collective-permute-start.1 = (bf16[20,64,128]{2,1,0:T(8,128)(2,1)S(1)}, bf16[20,64,128]{2,1,0:T(8,128)(2,1)S(1)}, u32[]{:S(2)}, u32[]{:S(2)}) collective-permute-start(bf16[20,64,128]{2,1,0:T(8,128)(2,1)S(1)} %get-tuple-element.39), channel_id=1, source_target_pairs={{0,4},{4,8},{8,12},{1,5},{5,9},{9,13},{2,6},{6,10},{10,14},{3,7},{... | collective-permute-start | bytes 983048 | tf_op jit(solution)/shard_map/ppermute | solution.py:19
  34.6 6.0 %copy-start.23 = (f32[20]{0:T(128)S(1)}, f32[20]{0:T(128)}, u32[]{:S(2)}) copy-start(f32[20]{0:T(128)} %get-tuple-element.36) | copy-start | bytes 244
  34.6 12.4 %copy-start.10 = (f32[3,8,2,128]{3,1,2,0:T(8,128)S(1)}, f32[3,8,2,128]{3,1,2,0:T(8,128)}, u32[]{:S(2)}) copy-start(f32[3,8,2,128]{3,1,2,0:T(8,128)} %copy-done.9) | copy-start | bytes 73732
  34.6 12.4 %copy-start.18 = (f32[20,256]{1,0:T(8,128)S(1)}, f32[20,256]{1,0:T(8,128)}, u32[]{:S(2)}) copy-start(f32[20,256]{1,0:T(8,128)} %get-tuple-element.20) | copy-start | bytes 61444
  41.6 10.9 %collective-permute-start.2 = (bf16[20,64,128]{2,1,0:T(8,128)(2,1)}, bf16[20,64,128]{2,1,0:T(8,128)(2,1)S(1)}, u32[]{:S(2)}, u32[]{:S(2)}) collective-permute-start(bf16[20,64,128]{2,1,0:T(8,128)(2,1)} %fusion.28), channel_id=1, source_target_pairs={{0,8},{4,12},{1,9},{5,13},{2,10},{6,14},{3,11},{7,15},{16,24},{20,... | collective-permute-start | bytes 983048 | tf_op jit(solution)/shard_map/ppermute | solution.py:19
  50.0 3.5 %copy-start.14 = (f32[256,20]{0,1:T(8,128)S(1)}, f32[256,20]{0,1:T(8,128)}, u32[]{:S(2)}) copy-start(f32[256,20]{0,1:T(8,128)} %get-tuple-element.26) | copy-start | bytes 61444
  50.0 3.5 %copy-start.22 = (f32[20]{0:T(128)S(1)}, f32[20]{0:T(128)}, u32[]{:S(2)}) copy-start(f32[20]{0:T(128)} %get-tuple-element.34) | copy-start | bytes 244
  50.0 3.5 %copy-start.6 = (f32[256,20,64]{0,2,1:T(8,128)S(1)}, f32[256,20,64]{0,2,1:T(8,128)}, u32[]{:S(2)}) copy-start(f32[256,20,64]{0,2,1:T(8,128)} %fusion.17) | copy-start | bytes 3932164
  55.0 3.2 %copy-start.13 = (f32[256,20]{0,1:T(8,128)S(1)}, f32[256,20]{0,1:T(8,128)}, u32[]{:S(2)}) copy-start(f32[256,20]{0,1:T(8,128)} %get-tuple-element.27) | copy-start | bytes 61444
  60.6 2.9 %copy-start.1 = (f32[256,1280]{1,0:T(8,128)S(1)}, f32[256,1280]{1,0:T(8,128)}, u32[]{:S(2)}) copy-start(f32[256,1280]{1,0:T(8,128)} %copy.63) | copy-start | bytes 3932164
  63.5 6.9 %copy-start.26 = (s32[128]{0:T(128)S(1)}, s32[128]{0:T(128)}, u32[]{:S(2)}) copy-start(s32[128]{0:T(128)} %iota_add_fusion) | copy-start | bytes 1540
  63.5 9.0 %copy-start.20 = (f32[1280]{0:T(1024)S(1)}, f32[1280]{0:T(1024)}, u32[]{:S(2)}) copy-start(f32[1280]{0:T(1024)} %param.21) | copy-start | bytes 15364
  67.8 1.2 %collective-permute-start.4 = (f32[512]{0:T(512)S(1)}, f32[512]{0:T(512)S(1)}, u32[]{:S(2)}, u32[]{:S(2)}) collective-permute-start(f32[512]{0:T(512)S(1)} %get-tuple-element.14), channel_id=1, source_target_pairs={{0,1},{1,0},{2,3},{3,2},{4,5},{5,4},{6,7},{7,6},{8,9},{9,8},{10,11... | collective-permute-start | bytes 6152 | tf_op jit(solution)/shard_map/ppermute | solution.py:81
  68.9 3.6 %collective-permute-start.5 = (f32[512]{0:T(512)S(1)}, f32[512]{0:T(512)S(1)}, u32[]{:S(2)}, u32[]{:S(2)}) collective-permute-start(f32[512]{0:T(512)S(1)} %add.140), channel_id=1, source_target_pairs={{0,2},{1,3},{2,0},{3,1},{4,6},{5,7},{6,4},{7,5},{8,10},{9,11},{10,... | collective-permute-start | bytes 6152 | tf_op jit(solution)/shard_map/ppermute | solution.py:81
  74.6 1.7 %copy-start = (bf16[512,1280]{1,0:T(8,128)(2,1)}, bf16[512,1280]{1,0:T(8,128)(2,1)S(1)}, u32[]{:S(2)}) copy-start(bf16[512,1280]{1,0:T(8,128)(2,1)S(1)} %multiply_convert_fusion.4) | copy-start | bytes 3932164
  (3 other events, 3.6 us)

commit v8 on v7

--- a/solution.py
+++ b/solution.py
@@ -3,6 +3,7 @@
 import jax
 import jax.numpy as jnp
 from jax import lax
+from jax.experimental.layout import Layout, with_layout_constraint
 from jax.sharding import PartitionSpec as P
 
 STRETCH = 256
@@ -45,7 +46,7 @@
     spread = cumul_keep[:, :, None] - cumul_keep[:, None, :]
     decay_mask = jnp.where(lower_mask[None], jnp.exp(jnp.where(lower_mask[None], spread, 0.0)), 0.0)
     mixing = (decay_mask * inner_prod[None] * step_block[:, None, :]).astype(jnp.bfloat16)
-    intra_part = jnp.einsum("hij,jhp->ihp", mixing, x_block, preferred_element_type=jnp.float32)
+    intra_part = jnp.einsum("hij,jhp->hpi", mixing, x_block, preferred_element_type=jnp.float32)
     tail_weight = jnp.exp(cumul_keep[:, -1:] - cumul_keep) * step_block
     weighted = (tail_weight.T[:, :, None] * x_block.astype(jnp.float32)).astype(jnp.bfloat16)
     stretch_state = jnp.einsum("jhp,js->hps", weighted, b_block, preferred_element_type=jnp.float32)
@@ -87,8 +88,8 @@
 def read_state(c_block, state_in):
     state_high = state_in.astype(jnp.bfloat16)
     state_low = (state_in - state_high.astype(jnp.float32)).astype(jnp.bfloat16)
-    high_part = jnp.einsum("is,hps->ihp", c_block, state_high, preferred_element_type=jnp.float32)
-    low_part = jnp.einsum("is,hps->ihp", c_block, state_low, preferred_element_type=jnp.float32)
+    high_part = jnp.einsum("hps,is->hpi", state_high, c_block, preferred_element_type=jnp.float32)
+    low_part = jnp.einsum("hps,is->hpi", state_low, c_block, preferred_element_type=jnp.float32)
     return high_part + low_part
 
 
@@ -151,22 +152,26 @@
         entry_state = jnp.exp(cumul_keep[:, -1])[:, None, None] * entry_state + stretch_state
         decay_total = decay_total + cumul_keep[:, -1]
     incoming = exclusive_scan(entry_state, decay_total, "seq")
+    x_major = x_conv.T.reshape(heads_local, head_width, tok_rows)
+    z_major = z_gate.T
     pieces_out = []
     for block_index in range(stretch_count):
         intra_part, cumul_keep, entry_part, decay_part = saved_parts[block_index]
         first_row = block_index * STRETCH
         state_in = entry_part + jnp.exp(decay_part)[:, None, None] * incoming
         from_state = read_state(c_mat[first_row : first_row + STRETCH], state_in)
-        pieces_out.append(intra_part + jnp.exp(cumul_keep).T[:, :, None] * from_state)
-    ssd_out = jnp.concatenate(pieces_out, axis=0) + skip_gain[None, :, None] * x_heads.astype(
+        pieces_out.append(intra_part + jnp.exp(cumul_keep)[:, None, :] * from_state)
+    ssd_out = jnp.concatenate(pieces_out, axis=2) + skip_gain[:, None, None] * x_major.astype(
         jnp.float32
     )
-    gated = ssd_out.reshape(tok_rows, channels) * silu_act(z_gate.astype(jnp.float32))
-    square_sum = butterfly_sum(jnp.sum(gated * gated, axis=1), "tensor")
+    gated = ssd_out.reshape(channels, tok_rows) * silu_act(z_major.astype(jnp.float32))
+    gated = with_layout_constraint(gated, Layout(major_to_minor=(0, 1)))
+    square_sum = butterfly_sum(jnp.sum(gated * gated, axis=0), "tensor")
     width_all = channels * lax.axis_size("tensor")
-    mixed_seq = (
-        gated * lax.rsqrt(square_sum / width_all + EPSILON)[:, None] * norm_gain[None, :]
+    mixed_major = (
+        gated * lax.rsqrt(square_sum / width_all + EPSILON)[None, :] * norm_gain[:, None]
     ).astype(jnp.bfloat16)
+    mixed_seq = mixed_major.T
     local_ends = seg_ends - lax.axis_index("seq") * tok_rows
     summaries = jnp.take(mixed_seq, local_ends, axis=0)
     pool_heads_local = POOL_HEADS // lax.axis_size("tensor")

time: 106 us -> 104 us (0.981)
  matrix products: 14.5 us -> 9.59 us
  other arithmetic: 17.4 us -> 18.6 us
    concatenate x2 -> x1, local copies, waits for them, and re-layouts: 5.71 us -> 0.96 us  [local(): jnp.concatenate([x_in[tok_rows - rim_rows:], bc_in[tok_rows - rim_rows:]]...]
    unnamed x60 -> x69, local copies, waits for them, and re-layouts: 1.07 us -> 5.78 us
    dot_general x6, matrix products: 10.2 us -> 7.5 us  [the longest x2 5.88 us: stretch_local(): jnp.einsum('hij,jhp->hpi', mixing, x_block, preferred_element_type=jnp.fl...]
    transpose x0 -> x1, other arithmetic: none -> 2.04 us  [local(): mixed_seq = mixed_major.T]
    convert_element_type x1 -> x0, other arithmetic: 2.02 us -> none  [local(): mixed_seq = (gated * lax.rsqrt(square_sum / width_all + EPSILON)[:, None]...]
    convert_element_type x2, other arithmetic: 2.18 us -> 4.15 us  [causal_conv(): return silu_act(summed).astype(jnp.bfloat16)]
    reduce_sum x1, other arithmetic: 4.24 us -> 2.56 us  [local(): square_sum = butterfly_sum(jnp.sum(gated * gated, axis=0), 'tensor')]
    dot_general x2, matrix products: 2.24 us -> 0.71 us  [stretch_local(): jnp.einsum('jhp,js->hps', weighted, b_block, preferred_element_type=jnp.f...]
  transfers between devices with their start and end apart: 7 -> 7, of which waited for: 4 -> 4; matrix products, arithmetic and copies ran while one was open for 24% -> 29% of each run, Pallas kernels for 0% -> 0%
where the time goes in v8:
time: 104 us; the launch traced here: 103 us
  blocking collectives  24.9 us (24%)
  starting transfers between devices  23.3 us (22%)
  local copies, waits for them, and re-layouts  18.9 us (18%)
  other arithmetic  18.6 us (18%)
  matrix products  9.59 us (9%)
  waiting for transfers between devices  6.49 us (6%)
  between operations  1.34 us (1%)
    all_to_all x1, blocking collectives, local(): parts = lax.all_to_all(parts, 'seq', 0, 0, tiled=True).astype(jnp.float32)  24.9 us
    ppermute x4, starting transfers between devices, passed_along(): lax.ppermute(value, axis, [(source, source + steps) for source in range(l...  18.3 us
    dot_general x2, matrix products, stretch_local(): jnp.einsum('hij,jhp->hpi', mixing, x_block, preferred_element_type=jnp.fl...  5.88 us
    unnamed x69, local copies, waits for them, and re-layouts  5.78 us
    ppermute x4, waiting for transfers between devices, passed_along(): lax.ppermute(value, axis, [(source, source + steps) for source in range(l...  5.34 us
    convert_element_type x2, other arithmetic, causal_conv(): return silu_act(summed).astype(jnp.bfloat16)  4.15 us
    all_to_all x1, starting transfers between devices, local(): lax.all_to_all(query_rows.reshape(seq_count * pools_local, -1), 'seq', 0,...  3.46 us
    reduce_sum x1, other arithmetic, local(): square_sum = butterfly_sum(jnp.sum(gated * gated, axis=0), 'tensor')  2.56 us
  transfers between devices with their start and end apart: 7, of which 4 were waited for; matrix products, arithmetic and copies ran while one was open for 29% of the time, Pallas kernels for 0%

profile of v8, /device:TPU:0, one launch (start us, length us, event | category | flops | bytes accessed | tf_op | source)
XLA Modules:
  0.0 103.1 jit_solution(8360167507262547399)
XLA Ops:
  0.7 0.8 slice.153
  1.5 0.7 slice.154
  2.2 1.0 copy.68
  3.2 5.0 %collective-permute-start = (bf16[3,1536]{0,1:T(8,128)(2,1)}, bf16[3,1536]{0,1:T(8,128)(2,1)S(1)}, u32[]{:S(2)}, u32[]{:S(2)}) collective-permute-start(bf16[3,1536]{0,1:T(8,128)(2,1)} %copy.68), channel_id=1, source_target_pairs={{0,4},{4,8},{8,12},{1,5},{5,9},{9,13},{2,6},{6,10},{10,14},{3,7},{... | collective-permute-start | bytes 27656 | tf_op jit(solution)/shard_map/ppermute | solution.py:20
  8.1 0.8 fusion.86
  11.6 4.0 %collective-permute-start.3 = (f32[20]{0:T(128)}, f32[20]{0:T(128)}, u32[]{:S(2)}, u32[]{:S(2)}) collective-permute-start(f32[20]{0:T(128)} %get-tuple-element.45), channel_id=1, source_target_pairs={{0,4},{4,8},{8,12},{1,5},{5,9},{9,13},{2,6},{6,10},{10,14},{3,7},{... | collective-permute-start | bytes 248 | tf_op jit(solution)/shard_map/ppermute | solution.py:20
  15.6 0.7 fusion.74
  16.5 1.0 concatenate.32
  17.5 0.8 broadcast_in_dim.117
  18.3 3.5 %all-to-all-start = ((bf16[4,40,1284]{2,1,0:T(8,128)(2,1)}), bf16[4,40,1284]{2,1,0:T(8,128)(2,1)S(1)}, u32[]{:S(2)}, u32[]{:S(2)}) async-start(bf16[4,40,1284]{2,1,0:T(8,128)(2,1)} %broadcast_in_dim.117), calls=%async_computation | async-start | bytes 901120 | tf_op jit(solution)/shard_map/all_to_all | solution.py:123
  22.4 0.7 fusion.85
  26.8 2.4 %copy.76 = bf16[512,1280]{0,1:T(8,128)(2,1)} copy(bf16[512,1280]{1,0:T(8,128)(2,1)} %param.14) | data formatting | bytes 2621440 | tf_op args[1]
  29.4 1.2 %exp.79 = f32[20]{0:T(128)} exponential(f32[20]{0:T(128)} %collective-permute-done.3) | non-fusion elementwise | bytes 160 | tf_op jit(solution)/shard_map/exp | solution.py:57
  30.6 0.7 copy.73
  31.4 3.8 %divide_convert_fusion = bf16[512,1280]{0,1:T(8,128)(2,1)S(1)} fusion(bf16[512,1280]{0,1:T(8,128)(2,1)S(1)} %copy.69, bf16[3,1280]{0,1:T(8,128)(2,1)S(1)} %slice.202, f32[1280]{0:T(1024)} %get-tuple-element.14, f32[1280]{0:T(1024)} %get-tuple-element.15, f32[1280]{0:T(1024)} %get-tuple-element.13, f32[1280]{0:T(1024)S(1)} %get-tuple-element.12), kind=kLoop, calls=%fused_computation.23 | loop fusion | flops 15728640 | bytes 2649600 | tf_op jit(solution)/shard_map/convert_element_type | solution.py:36
  36.7 3.9 %collective-permute-start.1 = (bf16[20,64,128]{2,1,0:T(8,128)(2,1)S(1)}, bf16[20,64,128]{2,1,0:T(8,128)(2,1)S(1)}, u32[]{:S(2)}, u32[]{:S(2)}) collective-permute-start(bf16[20,64,128]{2,1,0:T(8,128)(2,1)S(1)} %get-tuple-element.47), channel_id=1, source_target_pairs={{0,4},{4,8},{8,12},{1,5},{5,9},{9,13},{2,6},{6,10},{10,14},{3,7},{... | collective-permute-start | bytes 983048 | tf_op jit(solution)/shard_map/ppermute | solution.py:20
  40.6 2.9 %fusion = f32[20,64,256]{2,1,0:T(8,128)} fusion(bf16[256,20,64]{0,2,1:T(8,128)(2,1)S(1)} %bitcast.92, f32[20,256]{1,0:T(8,128)S(1)} %copy-done.14, f32[256,256]{1,0:T(8,128)S(1)} %fusion.61, f32[20,256]{1,0:T(8,128)S(1)} %bitcast.105, pred[256,256]{1,0:T(8,128)(4,1)S(1)} %copy-done.10), kind=kOutput, calls=%fused_computation.3 | convolution fusion | flops 175636480 | bytes 2334720 | tf_op jit(solution)/shard_map/hij,jhp->hpi/dot_general | solution.py:49
  43.8 2.9 %collective-permute-done.1 = bf16[20,64,128]{2,1,0:T(8,128)(2,1)S(1)} collective-permute-done((bf16[20,64,128]{2,1,0:T(8,128)(2,1)S(1)}, bf16[20,64,128]{2,1,0:T(8,128)(2,1)S(1)}, u32[]{:S(2)}, u32[]{:S(2)}) %collective-permute-start.1) | collective-permute-done | bytes 327712 | tf_op jit(solution)/shard_map/ppermute | solution.py:20
  46.7 0.9 fusion.27
  47.6 5.5 %collective-permute-start.2 = (bf16[20,64,128]{2,1,0:T(8,128)(2,1)}, bf16[20,64,128]{2,1,0:T(8,128)(2,1)S(1)}, u32[]{:S(2)}, u32[]{:S(2)}) collective-permute-start(bf16[20,64,128]{2,1,0:T(8,128)(2,1)} %fusion.27), channel_id=1, source_target_pairs={{0,8},{4,12},{1,9},{5,13},{2,10},{6,14},{3,11},{7,15},{16,24},{20,... | collective-permute-start | bytes 983048 | tf_op jit(solution)/shard_map/ppermute | solution.py:20
  53.1 2.9 %fusion.1 = f32[20,64,256]{2,1,0:T(8,128)} fusion(bf16[256,20,64]{0,2,1:T(8,128)(2,1)S(1)} %bitcast.94, f32[20,256]{1,0:T(8,128)S(1)} %copy-done.13, f32[256,256]{1,0:T(8,128)S(1)} %fusion.57, f32[20,256]{1,0:T(8,128)S(1)} %bitcast.108, pred[256,256]{1,0:T(8,128)(4,1)S(1)} %copy-done.10), kind=kOutput, calls=%fused_computation.4 | convolution fusion | flops 175636480 | bytes 2334720 | tf_op jit(solution)/shard_map/hij,jhp->hpi/dot_general | solution.py:49
  56.1 2.4 %collective-permute-done.2 = bf16[20,64,128]{2,1,0:T(8,128)(2,1)S(1)} collective-permute-done((bf16[20,64,128]{2,1,0:T(8,128)(2,1)}, bf16[20,64,128]{2,1,0:T(8,128)(2,1)S(1)}, u32[]{:S(2)}, u32[]{:S(2)}) %collective-permute-start.2) | collective-permute-done | bytes 327712 | tf_op jit(solution)/shard_map/ppermute | solution.py:20
  59.7 0.9 copy-done.4
  61.1 0.8 copy-done.1
  61.9 2.6 %multiply_reduce_fusion = (f32[512]{0:T(512)S(1)}, f32[1280,512]{1,0:T(8,128)}) fusion(bf16[512,1280]{0,1:T(8,128)(2,1)S(1)} %copy-done.1, bf16[512,1280]{0,1:T(8,128)(2,1)S(1)} %divide_convert_fusion, f32[1280]{0:T(1024)S(1)} %mul.348, f32[1280,256]{1,0:T(8,128)S(1)} %bitcast.90, f32[1280,256]{1,0:T(8,128)S(1)} %bitcast.89), kind=kLoop, calls=%fused_computation.12 | loop fusion | flops 7208448 | bytes 7871488 | tf_op jit(solution)/shard_map/reduce_sum | solution.py:169
  64.7 0.9 collective-permute-done.4
  65.6 1.5 %collective-permute-start.5 = (f32[512]{0:T(512)S(1)}, f32[512]{0:T(512)S(1)}, u32[]{:S(2)}, u32[]{:S(2)}) collective-permute-start(f32[512]{0:T(512)S(1)} %add.148), channel_id=1, source_target_pairs={{0,2},{1,3},{2,0},{3,1},{4,6},{5,7},{6,4},{7,5},{8,10},{9,11},{10,... | collective-permute-start | bytes 6152 | tf_op jit(solution)/shard_map/ppermute | solution.py:82
  67.3 1.7 %reshape.244 = bf16[160,8,160]{2,1,0:T(8,128)(2,1)} reshape(bf16[160,1280]{1,0:T(8,128)(2,1)S(1)} %slice.227) | data formatting | bytes 819200 | tf_op jit(solution)/shard_map/reshape | solution.py:182
  69.2 2.0 %fusion.23 = bf16[512,1280]{0,1:T(8,128)(2,1)S(1)} fusion(f32[1280,512]{1,0:T(8,128)} %get-tuple-element.23, f32[1280]{0:T(1024)S(1)} %copy-done.15, f32[512]{0:T(512)S(1)} %add_rsqrt_fusion), kind=kLoop, calls=%fused_computation.39 | loop fusion | flops 1966080 | bytes 3939328 | tf_op jit(solution)/shard_map/transpose | solution.py:174
  71.9 1.1 %gather_fusion = bf16[128,1280]{1,0:T(8,128)(2,1)S(1)} fusion(bf16[512,1280]{1,0:T(8,128)(2,1)S(1)} %copy.90, s32[1024]{0:T(1024)} %pad_clamp_fusion), kind=kCustom, calls=%fused_computation | custom fusion | bytes 655872 | tf_op jit(solution)/shard_map/jit(_take)/gather | solution.py:176
  75.9 24.9 %all_to_all.18 = bf16[4,40,1304]{2,1,0:T(8,128)(2,1)S(1)} all-to-all(bf16[4,40,1304]{2,1,0:T(8,128)(2,1)S(1)} %bitcast.98), channel_id=1, replica_groups=mesh['groups'=2,'seq'=4,'tensor'=4] {'seq'}, dimensions={0} | all-to-all | bytes 834560 | tf_op jit(solution)/shard_map/all_to_all | solution.py:208
  102.4 0.7 div.49
  (141 shorter events, 16.1 us)
Async XLA Ops:
  0.6 25.5 %copy-start.2 = (bf16[512,1280]{1,0:T(8,128)(2,1)S(1)}, bf16[512,1280]{1,0:T(8,128)(2,1)}, u32[]{:S(2)}) copy-start(bf16[512,1280]{1,0:T(8,128)(2,1)} %param.13) | copy-start | bytes 3932164
  0.6 21.8 %copy-start.11 = (f32[20,512]{1,0:T(8,128)S(1)}, f32[20,512]{1,0:T(8,128)}, u32[]{:S(2)}) copy-start(f32[20,512]{1,0:T(8,128)} %param.16) | copy-start | bytes 122884
  0.7 22.5 %copy-start.18 = (bf16[4,256]{1,0:T(4,128)(2,1)S(1)}, bf16[4,256]{1,0:T(4,128)(2,1)}, u32[]{:S(2)}) copy-start(bf16[4,256]{1,0:T(4,128)(2,1)} %param.20) | copy-start | bytes 6148
  0.7 23.1 %copy-start.12 = (bf16[4,1280]{1,0:T(4,128)(2,1)S(1)}, bf16[4,1280]{1,0:T(4,128)(2,1)}, u32[]{:S(2)}) copy-start(bf16[4,1280]{1,0:T(4,128)(2,1)} %param.19) | copy-start | bytes 30724
  0.7 23.7 %copy-start.30 = (s32[128]{0:T(128)S(1)}, s32[128]{0:T(128)}, u32[]{:S(2)}) copy-start(s32[128]{0:T(128)} %param.22) | copy-start | bytes 1540
  3.2 27.4 %collective-permute-start = (bf16[3,1536]{0,1:T(8,128)(2,1)}, bf16[3,1536]{0,1:T(8,128)(2,1)S(1)}, u32[]{:S(2)}, u32[]{:S(2)}) collective-permute-start(bf16[3,1536]{0,1:T(8,128)(2,1)} %copy.68), channel_id=1, source_target_pairs={{0,4},{4,8},{8,12},{1,5},{5,9},{9,13},{2,6},{6,10},{10,14},{3,7},{... | collective-permute-start | bytes 27656 | tf_op jit(solution)/shard_map/ppermute | solution.py:20
  11.6 17.7 %collective-permute-start.3 = (f32[20]{0:T(128)}, f32[20]{0:T(128)}, u32[]{:S(2)}, u32[]{:S(2)}) collective-permute-start(f32[20]{0:T(128)} %get-tuple-element.45), channel_id=1, source_target_pairs={{0,4},{4,8},{8,12},{1,5},{5,9},{9,13},{2,6},{6,10},{10,14},{3,7},{... | collective-permute-start | bytes 248 | tf_op jit(solution)/shard_map/ppermute | solution.py:20
  18.3 37.7 %all-to-all-start = ((bf16[4,40,1284]{2,1,0:T(8,128)(2,1)}), bf16[4,40,1284]{2,1,0:T(8,128)(2,1)S(1)}, u32[]{:S(2)}, u32[]{:S(2)}) async-start(bf16[4,40,1284]{2,1,0:T(8,128)(2,1)} %broadcast_in_dim.117), calls=%async_computation | async-start | bytes 901120 | tf_op jit(solution)/shard_map/all_to_all | solution.py:123
  26.1 3.1 %copy-start.28 = (f32[20]{0:T(128)S(1)}, f32[20]{0:T(128)}, u32[]{:S(2)}) copy-start(f32[20]{0:T(128)} %param.18) | copy-start | bytes 244
  31.3 4.0 %copy-start.6 = (bf16[512,256]{1,0:T(8,128)(2,1)S(1)}, bf16[512,256]{1,0:T(8,128)(2,1)}, u32[]{:S(2)}) copy-start(bf16[512,256]{1,0:T(8,128)(2,1)} %param.15) | copy-start | bytes 786436
  31.3 4.0 %copy-start.17 = (bf16[3,256]{1,0:T(4,128)(2,1)S(1)}, bf16[3,256]{1,0:T(4,128)(2,1)}, u32[]{:S(2)}) copy-start(bf16[3,256]{1,0:T(4,128)(2,1)} %copy.73) | copy-start | bytes 4612
  31.3 4.0 %copy-start.20 = (f32[1,256]{1,0:T(1,128)S(1)}, f32[1,256]{1,0:T(1,128)}, u32[]{:S(2)}) copy-start(f32[1,256]{1,0:T(1,128)} %get-tuple-element.36) | copy-start | bytes 3076
  31.3 4.0 %copy-start.21 = (f32[1,256]{1,0:T(1,128)S(1)}, f32[1,256]{1,0:T(1,128)}, u32[]{:S(2)}) copy-start(f32[1,256]{1,0:T(1,128)} %get-tuple-element.37) | copy-start | bytes 3076
  31.3 4.0 %copy-start.22 = (f32[1,256]{1,0:T(1,128)S(1)}, f32[1,256]{1,0:T(1,128)}, u32[]{:S(2)}) copy-start(f32[1,256]{1,0:T(1,128)} %get-tuple-element.38) | copy-start | bytes 3076
  31.3 4.0 %copy-start.23 = (f32[1,256]{1,0:T(1,128)S(1)}, f32[1,256]{1,0:T(1,128)}, u32[]{:S(2)}) copy-start(f32[1,256]{1,0:T(1,128)} %get-tuple-element.39) | copy-start | bytes 3076
  31.3 4.6 %copy-start.8 = (f32[256,20]{0,1:T(8,128)S(1)}, f32[256,20]{0,1:T(8,128)}, u32[]{:S(2)}) copy-start(f32[256,20]{0,1:T(8,128)} %get-tuple-element.29) | copy-start | bytes 61444
  31.4 4.6 %copy-start.24 = (f32[20]{0:T(128)S(1)}, f32[20]{0:T(128)}, u32[]{:S(2)}) copy-start(f32[20]{0:T(128)} %get-tuple-element.43) | copy-start | bytes 244
  35.3 5.3 %copy-start.10 = (pred[256,256]{1,0:T(8,128)(4,1)S(1)}, pred[256,256]{1,0:T(8,128)(4,1)}, u32[]{:S(2)}) copy-start(pred[256,256]{1,0:T(8,128)(4,1)} %iota_compare_fusion) | copy-start | bytes 196612
  35.3 5.3 %copy-start.14 = (f32[20,256]{1,0:T(8,128)S(1)}, f32[20,256]{1,0:T(8,128)}, u32[]{:S(2)}) copy-start(f32[20,256]{1,0:T(8,128)} %get-tuple-element.28) | copy-start | bytes 61444
  36.7 10.0 %collective-permute-start.1 = (bf16[20,64,128]{2,1,0:T(8,128)(2,1)S(1)}, bf16[20,64,128]{2,1,0:T(8,128)(2,1)S(1)}, u32[]{:S(2)}, u32[]{:S(2)}) collective-permute-start(bf16[20,64,128]{2,1,0:T(8,128)(2,1)S(1)} %get-tuple-element.47), channel_id=1, source_target_pairs={{0,4},{4,8},{8,12},{1,5},{5,9},{9,13},{2,6},{6,10},{10,14},{3,7},{... | collective-permute-start | bytes 983048 | tf_op jit(solution)/shard_map/ppermute | solution.py:20
  40.6 6.1 %copy-start.25 = (f32[20]{0:T(128)S(1)}, f32[20]{0:T(128)}, u32[]{:S(2)}) copy-start(f32[20]{0:T(128)} %get-tuple-element.44) | copy-start | bytes 244
  40.6 12.5 %copy-start.13 = (f32[20,256]{1,0:T(8,128)S(1)}, f32[20,256]{1,0:T(8,128)}, u32[]{:S(2)}) copy-start(f32[20,256]{1,0:T(8,128)} %get-tuple-element.31) | copy-start | bytes 61444
  47.6 10.9 %collective-permute-start.2 = (bf16[20,64,128]{2,1,0:T(8,128)(2,1)}, bf16[20,64,128]{2,1,0:T(8,128)(2,1)S(1)}, u32[]{:S(2)}, u32[]{:S(2)}) collective-permute-start(bf16[20,64,128]{2,1,0:T(8,128)(2,1)} %fusion.27), channel_id=1, source_target_pairs={{0,8},{4,12},{1,9},{5,13},{2,10},{6,14},{3,11},{7,15},{16,24},{20,... | collective-permute-start | bytes 983048 | tf_op jit(solution)/shard_map/ppermute | solution.py:20
  53.1 5.4 %copy-start.16 = (f32[20]{0:T(128)S(1)}, f32[20]{0:T(128)}, u32[]{:S(2)}) copy-start(f32[20]{0:T(128)} %exp.79) | copy-start | bytes 244
  53.1 5.8 %copy-start.19 = (f32[20]{0:T(128)S(1)}, f32[20]{0:T(128)}, u32[]{:S(2)}) copy-start(f32[20]{0:T(128)} %get-tuple-element.42) | copy-start | bytes 244
  56.0 3.3 %copy-start.7 = (f32[20,256]{1,0:T(8,128)S(1)}, f32[20,256]{1,0:T(8,128)}, u32[]{:S(2)}) copy-start(f32[20,256]{1,0:T(8,128)} %get-tuple-element.35) | copy-start | bytes 61444
  56.0 3.3 %copy-start.3 = (f32[20,64,256]{2,1,0:T(8,128)S(1)}, f32[20,64,256]{2,1,0:T(8,128)}, u32[]{:S(2)}) copy-start(f32[20,64,256]{2,1,0:T(8,128)} %fusion) | copy-start | bytes 3932164
  61.9 5.2 %copy-start.29 = (s32[128]{0:T(128)S(1)}, s32[128]{0:T(128)}, u32[]{:S(2)}) copy-start(s32[128]{0:T(128)} %iota_add_fusion) | copy-start | bytes 1540
  61.9 7.3 %copy-start.15 = (f32[1280]{0:T(1024)S(1)}, f32[1280]{0:T(1024)}, u32[]{:S(2)}) copy-start(f32[1280]{0:T(1024)} %param.21) | copy-start | bytes 15364
  64.5 1.2 %collective-permute-start.4 = (f32[512]{0:T(512)S(1)}, f32[512]{0:T(512)S(1)}, u32[]{:S(2)}, u32[]{:S(2)}) collective-permute-start(f32[512]{0:T(512)S(1)} %get-tuple-element.22), channel_id=1, source_target_pairs={{0,1},{1,0},{2,3},{3,2},{4,5},{5,4},{6,7},{7,6},{8,9},{9,8},{10,11... | collective-permute-start | bytes 6152 | tf_op jit(solution)/shard_map/ppermute | solution.py:82
  65.6 3.6 %collective-permute-start.5 = (f32[512]{0:T(512)S(1)}, f32[512]{0:T(512)S(1)}, u32[]{:S(2)}, u32[]{:S(2)}) collective-permute-start(f32[512]{0:T(512)S(1)} %add.148), channel_id=1, source_target_pairs={{0,2},{1,3},{2,0},{3,1},{4,6},{5,7},{6,4},{7,5},{8,10},{9,11},{10,... | collective-permute-start | bytes 6152 | tf_op jit(solution)/shard_map/ppermute | solution.py:82
  71.9 2.1 %copy-start = (bf16[512,1280]{1,0:T(8,128)(2,1)}, bf16[512,1280]{1,0:T(8,128)(2,1)S(1)}, u32[]{:S(2)}) copy-start(bf16[512,1280]{1,0:T(8,128)(2,1)S(1)} %copy.90) | copy-start | bytes 3932164
  (6 other events, 8.4 us)

commit v9 on v8

--- a/solution.py
+++ b/solution.py
@@ -57,7 +57,7 @@
     return (earlier[0] * jnp.exp(later[1])[:, None, None] + later[0], earlier[1] + later[1])
 
 
-def exclusive_scan(state, decay, axis):
+def exclusive_scan(state, decay, axis, rider):
     count = lax.axis_size(axis)
     window = (state, decay)
     before = (jnp.zeros_like(state), jnp.zeros_like(decay))
@@ -65,12 +65,14 @@
     while shift < count:
         sent_state = passed_along(window[0].astype(jnp.bfloat16), axis, shift)
         sent_decay = passed_along(window[1], axis, shift)
+        if shift == 1:
+            sent_state, rider = lax.optimization_barrier((sent_state, rider))
         received = (sent_state.astype(jnp.float32), sent_decay)
         before = combine(received, before)
         if shift * 2 < count:
             window = combine(received, window)
         shift *= 2
-    return before[0]
+    return before[0], rider
 
 
 def butterfly_sum(value, axis):
@@ -130,6 +132,7 @@
     edge_rows = jnp.concatenate([x_in[tok_rows - rim_rows :], bc_in[tok_rows - rim_rows :]], axis=1)
     before = passed_along(edge_rows, "seq", 1)
     x_conv = causal_conv(before[:, :channels], x_in, conv_x)
+    x_conv = with_layout_constraint(x_conv, Layout(major_to_minor=(0, 1)))
     bc_conv = causal_conv(before[:, channels:], bc_in, conv_bc)
     b_mat = bc_conv[:, :state_width]
     c_mat = bc_conv[:, state_width:]
@@ -151,9 +154,9 @@
         saved_parts.append((intra_part, cumul_keep, entry_state, decay_total))
         entry_state = jnp.exp(cumul_keep[:, -1])[:, None, None] * entry_state + stretch_state
         decay_total = decay_total + cumul_keep[:, -1]
-    incoming = exclusive_scan(entry_state, decay_total, "seq")
+    incoming, z_late = exclusive_scan(entry_state, decay_total, "seq", z_gate)
     x_major = x_conv.T.reshape(heads_local, head_width, tok_rows)
-    z_major = z_gate.T
+    z_major = z_late.T
     pieces_out = []
     for block_index in range(stretch_count):
         intra_part, cumul_keep, entry_part, decay_part = saved_parts[block_index]

time: 104 us -> 97.6 us (0.938)
  other arithmetic: 18.6 us -> 15.4 us
  waiting for transfers between devices: 6.49 us -> 3.77 us
  blocking collectives: 24.9 us -> 22.6 us
  matrix products: 9.59 us -> 10.9 us
    ppermute x4, waiting for transfers between devices: 5.34 us -> 2.89 us  [passed_along(): lax.ppermute(value, axis, [(source, source + steps) for source in range(l...]
    optimization_barrier x0 -> x1, local copies, waits for them, and re-layouts: none -> 2.43 us  [exclusive_scan(): sent_state, rider = lax.optimization_barrier((sent_state, rider))]
    all_to_all x1, blocking collectives: 24.9 us -> 22.6 us  [local(): parts = lax.all_to_all(parts, 'seq', 0, 0, tiled=True).astype(jnp.float32)]
    unnamed x69 -> x61, local copies, waits for them, and re-layouts: 5.78 us -> 3.97 us
    another operation x9 -> x10, local copies, waits for them, and re-layouts: 0.44 us -> 1.92 us  [the longest x1 1.48 us: local(): x_conv = with_layout_constraint(x_conv, Layout(major_to_minor=(0, 1)))]
    dot_general x2, matrix products: 0.71 us -> 2.16 us  [stretch_local(): jnp.einsum('jhp,js->hps', weighted, b_block, preferred_element_type=jnp.f...]
    exp x1, local copies, waits for them, and re-layouts: 1.21 us -> 0.01 us  [combine(): jnp.exp(later[1])[:, None, None]]
    reduce_sum x1, other arithmetic: 2.56 us -> 1.47 us  [local(): square_sum = butterfly_sum(jnp.sum(gated * gated, axis=0), 'tensor')]
  transfers between devices with their start and end apart: 7 -> 7, of which waited for: 4 -> 2; matrix products, arithmetic and copies ran while one was open for 29% -> 31% of each run, Pallas kernels for 0% -> 0%
where the time goes in v9:
time: 97.6 us; the launch traced here: 96.9 us
  starting transfers between devices  23.5 us (24%)
  blocking collectives  22.6 us (23%)
  local copies, waits for them, and re-layouts  19.3 us (20%)
  other arithmetic  15.4 us (16%)
  matrix products  10.9 us (11%)
  waiting for transfers between devices  3.77 us (4%)
  between operations  1.35 us (1%)
    all_to_all x1, blocking collectives, local(): parts = lax.all_to_all(parts, 'seq', 0, 0, tiled=True).astype(jnp.float32)  22.6 us
    ppermute x4, starting transfers between devices, passed_along(): lax.ppermute(value, axis, [(source, source + steps) for source in range(l...  17.8 us
    dot_general x2, matrix products, stretch_local(): jnp.einsum('hij,jhp->hpi', mixing, x_block, preferred_element_type=jnp.fl...  5.85 us
    all_to_all x1, starting transfers between devices, local(): lax.all_to_all(query_rows.reshape(seq_count * pools_local, -1), 'seq', 0,...  4.12 us
    unnamed x61, local copies, waits for them, and re-layouts  3.97 us
    convert_element_type x2, other arithmetic, causal_conv(): return silu_act(summed).astype(jnp.bfloat16)  3.73 us
    ppermute x4, waiting for transfers between devices, passed_along(): lax.ppermute(value, axis, [(source, source + steps) for source in range(l...  2.89 us
    optimization_barrier x1, local copies, waits for them, and re-layouts, exclusive_scan(): sent_state, rider = lax.optimization_barrier((sent_state, rider))  2.43 us
  transfers between devices with their start and end apart: 7, of which 2 were waited for; matrix products, arithmetic and copies ran while one was open for 31% of the time, Pallas kernels for 0%

profile of v9, /device:TPU:0, one launch (start us, length us, event | category | flops | bytes accessed | tf_op | source)
XLA Modules:
  0.0 96.9 jit_solution(6520542925429075998)
XLA Ops:
  0.7 0.8 slice.153
  2.2 5.0 %collective-permute-start = (bf16[3,1536]{1,0:T(4,128)(2,1)S(1)}, bf16[3,1536]{1,0:T(4,128)(2,1)S(1)}, u32[]{:S(2)}, u32[]{:S(2)}) collective-permute-start(bf16[3,1536]{1,0:T(4,128)(2,1)S(1)} %pad_maximum_fusion.2), channel_id=1, source_target_pairs={{0,4},{4,8},{8,12},{1,5},{5,9},{9,13},{2,6},{6,10},{10,14},{3,7},{... | collective-permute-start | bytes 27656 | tf_op jit(solution)/shard_map/ppermute | solution.py:20
  7.2 0.8 fusion.86
  10.7 3.5 %collective-permute-start.3 = (f32[20]{0:T(128)S(1)}, f32[20]{0:T(128)S(1)}, u32[]{:S(2)}, u32[]{:S(2)}) collective-permute-start(f32[20]{0:T(128)S(1)} %get-tuple-element.49), channel_id=1, source_target_pairs={{0,4},{4,8},{8,12},{1,5},{5,9},{9,13},{2,6},{6,10},{10,14},{3,7},{... | collective-permute-start | bytes 248 | tf_op jit(solution)/shard_map/ppermute | solution.py:20
  15.1 1.0 %concatenate.32 = bf16[40,1284]{1,0:T(8,128)(2,1)S(1)} concatenate(bf16[40,1280]{1,0:T(8,128)(2,1)} %param.23, bf16[40,2]{1,0:T(8,128)(2,1)S(1)} %copy.74, bf16[40,2]{1,0:T(8,128)(2,1)S(1)} %copy.75), dimensions={1} | concatenate | bytes 205440 | tf_op jit(solution)/shard_map/concatenate | solution.py:123
  16.0 0.8 broadcast_in_dim.117
  16.9 4.1 %all-to-all-start = ((bf16[4,40,1284]{2,1,0:T(8,128)(2,1)}), bf16[4,40,1284]{2,1,0:T(8,128)(2,1)}, u32[]{:S(2)}, u32[]{:S(2)}) async-start(bf16[4,40,1284]{2,1,0:T(8,128)(2,1)} %broadcast_in_dim.117), calls=%async_computation | async-start | bytes 901120 | tf_op jit(solution)/shard_map/all_to_all | solution.py:125
  21.6 0.7 fusion.85
  24.4 1.8 %divide_convert_fusion = bf16[512,1280]{1,0:T(8,128)(2,1)S(1)} fusion(bf16[512,1280]{1,0:T(8,128)(2,1)S(1)} %copy-done.5, bf16[3,1280]{1,0:T(4,128)(2,1)S(1)} %slice.202, f32[1280]{0:T(1024)S(1)} %get-tuple-element.18, f32[1280]{0:T(1024)S(1)} %get-tuple-element.19, f32[1280]{0:T(1024)S(1)} %get-tuple-element.17, f32[1280]{0:T(1024)S(1)} %get-tuple-element.16), kind=kLoop, calls=%fused_computation.23 | loop fusion | flops 15728640 | bytes 2649600 | tf_op jit(solution)/shard_map/convert_element_type | solution.py:36
  26.9 1.9 %divide_convert_fusion.1 = bf16[512,256]{1,0:T(8,128)(2,1)S(1)} fusion(bf16[512,256]{1,0:T(8,128)(2,1)} %param.15, bf16[3,256]{1,0:T(4,128)(2,1)S(1)} %slice.209, f32[256]{0:T(256)} %bitcast.112, f32[256]{0:T(256)} %bitcast.113, f32[256]{0:T(256)} %bitcast.111, f32[256]{0:T(256)} %bitcast.110), kind=kLoop, calls=%fused_computation.60 | loop fusion | flops 3145728 | bytes 529920 | tf_op jit(solution)/shard_map/convert_element_type | solution.py:36
  29.0 1.1 %convolution_add_fusion.3 = f32[20,64,128]{2,1,0:T(8,128)S(1)} fusion(bf16[256,20,64]{0,2,1:T(8,128)(2,1)S(1)} %bitcast.91, f32[256,20]{0,1:T(8,128)} %get-tuple-element.33, f32[20]{0:T(128)} %get-tuple-element.47, bf16[512,256]{1,0:T(8,128)(2,1)S(1)} %divide_convert_fusion.1), kind=kOutput, calls=%fused_computation.43 | convolution fusion | flops 85032960 | bytes 1396816 | tf_op jit(solution)/shard_map/jhp,js->hps/dot_general | solution.py:52
  30.1 1.1 %fusion.88 = (bf16[20,64,128]{2,1,0:T(8,128)(2,1)S(1)}, f32[20,64,128]{2,1,0:T(8,128)S(1)}) fusion(bf16[512,256]{1,0:T(8,128)(2,1)S(1)} %divide_convert_fusion.1, bf16[256,20,64]{0,2,1:T(8,128)(2,1)S(1)} %bitcast.94, f32[256,20]{0,1:T(8,128)} %get-tuple-element.34, f32[20,64,128]{2,1,0:T(8,128)S(1)} %convolution_add_fusion.3, f32[20]{0:T(128)} %get-tuple-element.50), kind=kOutput, calls=%fused_computation.161 | convolution fusion | flops 85360640 | bytes 2379856 | tf_op jit(solution)/shard_map/jhp,js->hps/dot_general | solution.py:52
  31.1 3.9 %collective-permute-start.1 = (bf16[20,64,128]{2,1,0:T(8,128)(2,1)S(1)}, bf16[20,64,128]{2,1,0:T(8,128)(2,1)S(1)}, u32[]{:S(2)}, u32[]{:S(2)}) collective-permute-start(bf16[20,64,128]{2,1,0:T(8,128)(2,1)S(1)} %get-tuple-element.51), channel_id=1, source_target_pairs={{0,4},{4,8},{8,12},{1,5},{5,9},{9,13},{2,6},{6,10},{10,14},{3,7},{... | collective-permute-start | bytes 983048 | tf_op jit(solution)/shard_map/ppermute | solution.py:20
  35.1 3.0 %fusion = f32[20,64,256]{2,1,0:T(8,128)} fusion(bf16[256,20,64]{0,2,1:T(8,128)(2,1)S(1)} %bitcast.92, f32[20,256]{1,0:T(8,128)S(1)} %copy-done.19, f32[256,256]{1,0:T(8,128)S(1)} %fusion.61, f32[20,256]{1,0:T(8,128)S(1)} %bitcast.103, pred[256,256]{1,0:T(8,128)(4,1)S(1)} %copy-done.15), kind=kOutput, calls=%fused_computation.3 | convolution fusion | flops 175636480 | bytes 2334720 | tf_op jit(solution)/shard_map/hij,jhp->hpi/dot_general | solution.py:49
  38.3 2.9 %collective-permute-done.1 = bf16[20,64,128]{2,1,0:T(8,128)(2,1)S(1)} collective-permute-done((bf16[20,64,128]{2,1,0:T(8,128)(2,1)S(1)}, bf16[20,64,128]{2,1,0:T(8,128)(2,1)S(1)}, u32[]{:S(2)}, u32[]{:S(2)}) %collective-permute-start.1) | collective-permute-done | bytes 327712 | tf_op jit(solution)/shard_map/ppermute | solution.py:20
  41.3 5.5 %collective-permute-start.2 = (bf16[20,64,128]{2,1,0:T(8,128)(2,1)S(1)}, bf16[20,64,128]{2,1,0:T(8,128)(2,1)S(1)}, u32[]{:S(2)}, u32[]{:S(2)}) collective-permute-start(bf16[20,64,128]{2,1,0:T(8,128)(2,1)S(1)} %fusion.27), channel_id=1, source_target_pairs={{0,8},{4,12},{1,9},{5,13},{2,10},{6,14},{3,11},{7,15},{16,24},{20,... | collective-permute-start | bytes 983048 | tf_op jit(solution)/shard_map/ppermute | solution.py:20
  46.8 2.9 %fusion.1 = f32[20,64,256]{2,1,0:T(8,128)} fusion(bf16[256,20,64]{0,2,1:T(8,128)(2,1)S(1)} %bitcast.95, f32[20,256]{1,0:T(8,128)S(1)} %copy-done.18, f32[256,256]{1,0:T(8,128)S(1)} %fusion.57, f32[20,256]{1,0:T(8,128)S(1)} %bitcast.106, pred[256,256]{1,0:T(8,128)(4,1)S(1)} %copy-done.15), kind=kOutput, calls=%fused_computation.4 | convolution fusion | flops 175636480 | bytes 2334720 | tf_op jit(solution)/shard_map/hij,jhp->hpi/dot_general | solution.py:49
  49.7 1.5 %copy.70 = bf16[512,1280]{0,1:T(8,128)(2,1)} copy(bf16[512,1280]{1,0:T(8,128)(2,1)S(1)} %divide_convert_fusion) | data formatting | bytes 2621440 | tf_op jit(solution)/shard_map/layout_constraint | solution.py:135
  51.2 2.4 %copy.71 = bf16[512,1280]{0,1:T(8,128)(2,1)} copy(bf16[512,1280]{1,0:T(8,128)(2,1)} %param.14) | data formatting | bytes 2621440 | tf_op jit(solution)/shard_map/optimization_barrier | solution.py:69
  53.7 0.9 slice_convert_fusion
  55.8 0.9 copy-done.7
  57.1 0.9 copy-done.1
  58.4 1.5 %multiply_reduce_fusion = (f32[512]{0:T(512)S(1)}, f32[1280,512]{1,0:T(8,128)S(1)}) fusion(bf16[512,1280]{0,1:T(8,128)(2,1)S(1)} %copy-done.2, bf16[512,1280]{0,1:T(8,128)(2,1)S(1)} %copy-done.1, f32[1280]{0:T(1024)S(1)} %mul.348, f32[1280,256]{1,0:T(8,128)S(1)} %bitcast.90, f32[1280,256]{1,0:T(8,128)S(1)} %bitcast.89), kind=kLoop, calls=%fused_computation.12 | loop fusion | flops 7208448 | bytes 7871488 | tf_op jit(solution)/shard_map/reduce_sum | solution.py:172
  60.2 0.9 collective-permute-done.4
  61.1 1.5 %collective-permute-start.5 = (f32[512]{0:T(512)S(1)}, f32[512]{0:T(512)S(1)}, u32[]{:S(2)}, u32[]{:S(2)}) collective-permute-start(f32[512]{0:T(512)S(1)} %add.148), channel_id=1, source_target_pairs={{0,2},{1,3},{2,0},{3,1},{4,6},{5,7},{6,4},{7,5},{8,10},{9,11},{10,... | collective-permute-start | bytes 6152 | tf_op jit(solution)/shard_map/ppermute | solution.py:84
  62.7 1.0 %slice.227 = bf16[160,1280]{1,0:T(8,128)(2,1)S(1)} slice(bf16[160,1284]{1,0:T(8,128)(2,1)} %bitcast.20), slice={[0:160], [0:1280]} | slice | bytes 819200 | tf_op jit(solution)/shard_map/slice | solution.py:128
  63.7 1.7 %reshape.244 = bf16[160,8,160]{2,1,0:T(8,128)(2,1)} reshape(bf16[160,1280]{1,0:T(8,128)(2,1)S(1)} %slice.227) | data formatting | bytes 819200 | tf_op jit(solution)/shard_map/reshape | solution.py:185
  65.4 1.4 %fusion.23 = bf16[512,1280]{0,1:T(8,128)(2,1)} fusion(f32[1280,512]{1,0:T(8,128)S(1)} %get-tuple-element.27, f32[1280]{0:T(1024)S(1)} %copy-done.20, f32[512]{0:T(512)S(1)} %add_rsqrt_fusion), kind=kLoop, calls=%fused_computation.37 | loop fusion | flops 1966080 | bytes 3939328 | tf_op jit(solution)/shard_map/transpose | solution.py:177
  66.8 1.7 %copy.85 = bf16[512,1280]{1,0:T(8,128)(2,1)S(1)} copy(bf16[512,1280]{0,1:T(8,128)(2,1)} %fusion.23) | data formatting | bytes 2621440
  68.5 0.9 gather_fusion
  72.0 22.6 %all_to_all.18 = bf16[4,40,1304]{2,1,0:T(8,128)(2,1)S(1)} all-to-all(bf16[4,40,1304]{2,1,0:T(8,128)(2,1)S(1)} %bitcast.96), channel_id=1, replica_groups=mesh['groups'=2,'seq'=4,'tensor'=4] {'seq'}, dimensions={0} | all-to-all | bytes 834560 | tf_op jit(solution)/shard_map/all_to_all | solution.py:211
  96.2 0.7 div.49
  (135 shorter events, 14.5 us)
Async XLA Ops:
  0.6 23.8 %copy-start.5 = (bf16[512,1280]{1,0:T(8,128)(2,1)S(1)}, bf16[512,1280]{1,0:T(8,128)(2,1)}, u32[]{:S(2)}) copy-start(bf16[512,1280]{1,0:T(8,128)(2,1)} %param.13) | copy-start | bytes 3932164
  0.6 21.0 %copy-start.16 = (f32[20,512]{1,0:T(8,128)S(1)}, f32[20,512]{1,0:T(8,128)}, u32[]{:S(2)}) copy-start(f32[20,512]{1,0:T(8,128)} %param.16) | copy-start | bytes 122884
  0.7 21.7 %copy-start.21 = (bf16[4,256]{1,0:T(4,128)(2,1)S(1)}, bf16[4,256]{1,0:T(4,128)(2,1)}, u32[]{:S(2)}) copy-start(bf16[4,256]{1,0:T(4,128)(2,1)} %param.20) | copy-start | bytes 6148
  0.7 22.3 %copy-start.17 = (bf16[4,1280]{1,0:T(4,128)(2,1)S(1)}, bf16[4,1280]{1,0:T(4,128)(2,1)}, u32[]{:S(2)}) copy-start(bf16[4,1280]{1,0:T(4,128)(2,1)} %param.19) | copy-start | bytes 30724
  0.7 22.4 %copy-start.27 = (s32[128]{0:T(128)S(1)}, s32[128]{0:T(128)}, u32[]{:S(2)}) copy-start(s32[128]{0:T(128)} %param.22) | copy-start | bytes 1540
  0.7 23.5 %copy-start.25 = (f32[20]{0:T(128)S(1)}, f32[20]{0:T(128)}, u32[]{:S(2)}) copy-start(f32[20]{0:T(128)} %param.18) | copy-start | bytes 244
  2.2 22.1 %collective-permute-start = (bf16[3,1536]{1,0:T(4,128)(2,1)S(1)}, bf16[3,1536]{1,0:T(4,128)(2,1)S(1)}, u32[]{:S(2)}, u32[]{:S(2)}) collective-permute-start(bf16[3,1536]{1,0:T(4,128)(2,1)S(1)} %pad_maximum_fusion.2), channel_id=1, source_target_pairs={{0,4},{4,8},{8,12},{1,5},{5,9},{9,13},{2,6},{6,10},{10,14},{3,7},{... | collective-permute-start | bytes 27656 | tf_op jit(solution)/shard_map/ppermute | solution.py:20
  8.9 15.5 %copy-start.9 = (f32[3,8,2,128]{3,1,2,0:T(8,128)}, f32[3,8,2,128]{3,1,2,0:T(8,128)S(1)}, u32[]{:S(2)}) copy-start(f32[3,8,2,128]{3,1,2,0:T(8,128)S(1)} %copy.87) | copy-start | bytes 73732
  9.9 14.5 %copy-start.11 = (f32[3,8,2,128]{3,1,2,0:T(8,128)}, f32[3,8,2,128]{3,1,2,0:T(8,128)S(1)}, u32[]{:S(2)}) copy-start(f32[3,8,2,128]{3,1,2,0:T(8,128)S(1)} %copy.88) | copy-start | bytes 73732
  10.7 13.7 %collective-permute-start.3 = (f32[20]{0:T(128)S(1)}, f32[20]{0:T(128)S(1)}, u32[]{:S(2)}, u32[]{:S(2)}) collective-permute-start(f32[20]{0:T(128)S(1)} %get-tuple-element.49), channel_id=1, source_target_pairs={{0,4},{4,8},{8,12},{1,5},{5,9},{9,13},{2,6},{6,10},{10,14},{3,7},{... | collective-permute-start | bytes 248 | tf_op jit(solution)/shard_map/ppermute | solution.py:20
  16.9 36.8 %all-to-all-start = ((bf16[4,40,1284]{2,1,0:T(8,128)(2,1)}), bf16[4,40,1284]{2,1,0:T(8,128)(2,1)}, u32[]{:S(2)}, u32[]{:S(2)}) async-start(bf16[4,40,1284]{2,1,0:T(8,128)(2,1)} %broadcast_in_dim.117), calls=%async_computation | async-start | bytes 901120 | tf_op jit(solution)/shard_map/all_to_all | solution.py:125
  26.8 4.3 %copy-start.3 = (bf16[256,1280]{0,1:T(8,128)(2,1)}, bf16[256,1280]{0,1:T(8,128)(2,1)S(1)}, u32[]{:S(2)}) copy-start(bf16[256,1280]{0,1:T(8,128)(2,1)S(1)} %copy.69) | copy-start | bytes 1966084
  26.8 8.2 %copy-start.10 = (f32[3,8,2,128]{3,1,2,0:T(8,128)S(1)}, f32[3,8,2,128]{3,1,2,0:T(8,128)}, u32[]{:S(2)}) copy-start(f32[3,8,2,128]{3,1,2,0:T(8,128)} %copy-done.9) | copy-start | bytes 73732
  26.8 8.2 %copy-start.15 = (pred[256,256]{1,0:T(8,128)(4,1)S(1)}, pred[256,256]{1,0:T(8,128)(4,1)}, u32[]{:S(2)}) copy-start(pred[256,256]{1,0:T(8,128)(4,1)} %iota_compare_fusion) | copy-start | bytes 196612
  26.8 8.2 %copy-start.19 = (f32[20,256]{1,0:T(8,128)S(1)}, f32[20,256]{1,0:T(8,128)}, u32[]{:S(2)}) copy-start(f32[20,256]{1,0:T(8,128)} %get-tuple-element.32) | copy-start | bytes 61444
  31.1 10.0 %collective-permute-start.1 = (bf16[20,64,128]{2,1,0:T(8,128)(2,1)S(1)}, bf16[20,64,128]{2,1,0:T(8,128)(2,1)S(1)}, u32[]{:S(2)}, u32[]{:S(2)}) collective-permute-start(bf16[20,64,128]{2,1,0:T(8,128)(2,1)S(1)} %get-tuple-element.51), channel_id=1, source_target_pairs={{0,4},{4,8},{8,12},{1,5},{5,9},{9,13},{2,6},{6,10},{10,14},{3,7},{... | collective-permute-start | bytes 983048 | tf_op jit(solution)/shard_map/ppermute | solution.py:20
  35.1 6.1 %copy-start.23 = (f32[20]{0:T(128)S(1)}, f32[20]{0:T(128)}, u32[]{:S(2)}) copy-start(f32[20]{0:T(128)} %get-tuple-element.48) | copy-start | bytes 244
  35.1 11.7 %copy-start.4 = (bf16[256,1280]{0,1:T(8,128)(2,1)S(1)}, bf16[256,1280]{0,1:T(8,128)(2,1)}, u32[]{:S(2)}) copy-start(bf16[256,1280]{0,1:T(8,128)(2,1)} %copy-done.3) | copy-start | bytes 1966084
  35.1 11.7 %copy-start.12 = (f32[3,8,2,128]{3,1,2,0:T(8,128)S(1)}, f32[3,8,2,128]{3,1,2,0:T(8,128)}, u32[]{:S(2)}) copy-start(f32[3,8,2,128]{3,1,2,0:T(8,128)} %copy-done.11) | copy-start | bytes 73732
  35.1 11.7 %copy-start.18 = (f32[20,256]{1,0:T(8,128)S(1)}, f32[20,256]{1,0:T(8,128)}, u32[]{:S(2)}) copy-start(f32[20,256]{1,0:T(8,128)} %get-tuple-element.35) | copy-start | bytes 61444
  41.3 13.2 %collective-permute-start.2 = (bf16[20,64,128]{2,1,0:T(8,128)(2,1)S(1)}, bf16[20,64,128]{2,1,0:T(8,128)(2,1)S(1)}, u32[]{:S(2)}, u32[]{:S(2)}) collective-permute-start(bf16[20,64,128]{2,1,0:T(8,128)(2,1)S(1)} %fusion.27), channel_id=1, source_target_pairs={{0,8},{4,12},{1,9},{5,13},{2,10},{6,14},{3,11},{7,15},{16,24},{20,... | collective-permute-start | bytes 983048 | tf_op jit(solution)/shard_map/ppermute | solution.py:20
  51.2 3.7 %copy-start.22 = (f32[20]{0:T(128)S(1)}, f32[20]{0:T(128)}, u32[]{:S(2)}) copy-start(f32[20]{0:T(128)} %get-tuple-element.46) | copy-start | bytes 244
  53.6 1.7 %copy-start.6 = (f32[20,64,256]{2,1,0:T(8,128)S(1)}, f32[20,64,256]{2,1,0:T(8,128)}, u32[]{:S(2)}) copy-start(f32[20,64,256]{2,1,0:T(8,128)} %fusion) | copy-start | bytes 3932164
  53.6 1.7 %copy-start.14 = (f32[20,256]{1,0:T(8,128)S(1)}, f32[20,256]{1,0:T(8,128)}, u32[]{:S(2)}) copy-start(f32[20,256]{1,0:T(8,128)} %get-tuple-element.39) | copy-start | bytes 61444
  56.7 1.7 %copy-start.2 = (bf16[512,1280]{0,1:T(8,128)(2,1)S(1)}, bf16[512,1280]{0,1:T(8,128)(2,1)}, u32[]{:S(2)}) copy-start(bf16[512,1280]{0,1:T(8,128)(2,1)} %copy.71) | copy-start | bytes 3932164
  58.4 4.2 %copy-start.26 = (s32[128]{0:T(128)S(1)}, s32[128]{0:T(128)}, u32[]{:S(2)}) copy-start(s32[128]{0:T(128)} %iota_add_fusion) | copy-start | bytes 1540
  58.4 7.0 %copy-start.20 = (f32[1280]{0:T(1024)S(1)}, f32[1280]{0:T(1024)}, u32[]{:S(2)}) copy-start(f32[1280]{0:T(1024)} %param.21) | copy-start | bytes 15364
  59.9 1.2 %collective-permute-start.4 = (f32[512]{0:T(512)S(1)}, f32[512]{0:T(512)S(1)}, u32[]{:S(2)}, u32[]{:S(2)}) collective-permute-start(f32[512]{0:T(512)S(1)} %get-tuple-element.26), channel_id=1, source_target_pairs={{0,1},{1,0},{2,3},{3,2},{4,5},{5,4},{6,7},{7,6},{8,9},{9,8},{10,11... | collective-permute-start | bytes 6152 | tf_op jit(solution)/shard_map/ppermute | solution.py:84
  61.1 4.3 %collective-permute-start.5 = (f32[512]{0:T(512)S(1)}, f32[512]{0:T(512)S(1)}, u32[]{:S(2)}, u32[]{:S(2)}) collective-permute-start(f32[512]{0:T(512)S(1)} %add.148), channel_id=1, source_target_pairs={{0,2},{1,3},{2,0},{3,1},{4,6},{5,7},{6,4},{7,5},{8,10},{9,11},{10,... | collective-permute-start | bytes 6152 | tf_op jit(solution)/shard_map/ppermute | solution.py:84
  66.8 2.8 %copy-start.8 = (bf16[160,8,160]{2,1,0:T(8,128)(2,1)S(1)}, bf16[160,8,160]{2,1,0:T(8,128)(2,1)}, u32[]{:S(2)}) copy-start(bf16[160,8,160]{2,1,0:T(8,128)(2,1)} %reshape.244) | copy-start | bytes 1228804
  66.8 2.8 %copy-start.24 = (pred[128]{0:T(512)(128)(4,1)S(1)}, pred[128]{0:T(512)(128)(4,1)}, u32[]{:S(2)}) copy-start(pred[128]{0:T(512)(128)(4,1)} %get-tuple-element.24) | copy-start | bytes 388
  68.5 1.7 %copy-start = (bf16[512,1280]{1,0:T(8,128)(2,1)}, bf16[512,1280]{1,0:T(8,128)(2,1)S(1)}, u32[]{:S(2)}) copy-start(bf16[512,1280]{1,0:T(8,128)(2,1)S(1)} %copy.85) | copy-start | bytes 3932164
  (3 other events, 3.9 us)

commit v10 on v9

--- a/solution.py
+++ b/solution.py
@@ -208,8 +208,17 @@
         ],
         axis=1,
     )
-    parts = lax.all_to_all(parts, "seq", 0, 0, tiled=True).astype(jnp.float32)
     parts = parts.reshape(seq_count, pools_local, channels + 3 * pool_heads_local)
+    place = lax.axis_index("seq")
+    gathered = [lax.dynamic_index_in_dim(parts, place, 0, False)]
+    for shift in range(1, seq_count):
+        chunk = lax.dynamic_index_in_dim(parts, (place + shift) % seq_count, 0, False)
+        gathered.append(
+            lax.ppermute(
+                chunk, "seq", [(i, (i + shift) % seq_count) for i in range(seq_count)]
+            )
+        )
+    parts = jnp.stack(gathered).astype(jnp.float32)
     numer_parts = parts[:, :, :channels].reshape(
         seq_count, pools_local, pool_heads_local, pool_width
     )

time: 97.6 us -> 91.7 us (0.940)
  blocking collectives: 22.6 us -> 0 us
  starting transfers between devices: 23.5 us -> 32.7 us
  waiting for transfers between devices: 3.77 us -> 11.3 us
    all_to_all x1 -> x0, blocking collectives: 22.6 us -> none  [local(): parts = lax.all_to_all(parts, 'seq', 0, 0, tiled=True).astype(jnp.float32)]
    ppermute x0 -> x3, starting transfers between devices: none -> 9.22 us  [local(): lax.ppermute(chunk, 'seq', [(i, (i + shift) % seq_count) for i in range(s...]
    ppermute x0 -> x3, waiting for transfers between devices: none -> 7.51 us  [local(): lax.ppermute(chunk, 'seq', [(i, (i + shift) % seq_count) for i in range(s...]
  transfers between devices with their start and end apart: 7 -> 10, of which waited for: 2 -> 4; matrix products, arithmetic and copies ran while one was open for 31% -> 33% of each run, Pallas kernels for 0% -> 0%
where the time goes in v10:
time: 91.7 us; the launch traced here: 91 us
  starting transfers between devices  32.7 us (36%)
  local copies, waits for them, and re-layouts  19.4 us (21%)
  other arithmetic  15.3 us (17%)
  waiting for transfers between devices  11.3 us (12%)
  matrix products  10.9 us (12%)
  between operations  1.34 us (1%)
    ppermute x4, starting transfers between devices, passed_along(): lax.ppermute(value, axis, [(source, source + steps) for source in range(l...  17.8 us
    ppermute x3, starting transfers between devices, local(): lax.ppermute(chunk, 'seq', [(i, (i + shift) % seq_count) for i in range(s...  9.22 us
    ppermute x3, waiting for transfers between devices, local(): lax.ppermute(chunk, 'seq', [(i, (i + shift) % seq_count) for i in range(s...  7.51 us
    dot_general x2, matrix products, stretch_local(): jnp.einsum('hij,jhp->hpi', mixing, x_block, preferred_element_type=jnp.fl...  5.85 us
    all_to_all x1, starting transfers between devices, local(): lax.all_to_all(query_rows.reshape(seq_count * pools_local, -1), 'seq', 0,...  4.12 us
    unnamed x61, local copies, waits for them, and re-layouts  3.97 us
    convert_element_type x2, other arithmetic, causal_conv(): return silu_act(summed).astype(jnp.bfloat16)  3.73 us
    ppermute x4, waiting for transfers between devices, passed_along(): lax.ppermute(value, axis, [(source, source + steps) for source in range(l...  2.89 us
  transfers between devices with their start and end apart: 10, of which 4 were waited for; matrix products, arithmetic and copies ran while one was open for 33% of the time, Pallas kernels for 0%

profile of v10, /device:TPU:0, one launch (start us, length us, event | category | flops | bytes accessed | tf_op | source)
XLA Modules:
  0.0 91.0 jit_solution(506859335095620243)
XLA Ops:
  0.7 0.8 slice.153
  2.2 5.0 %collective-permute-start = (bf16[3,1536]{1,0:T(4,128)(2,1)S(1)}, bf16[3,1536]{1,0:T(4,128)(2,1)S(1)}, u32[]{:S(2)}, u32[]{:S(2)}) collective-permute-start(bf16[3,1536]{1,0:T(4,128)(2,1)S(1)} %pad_maximum_fusion.5), channel_id=1, source_target_pairs={{0,4},{4,8},{8,12},{1,5},{5,9},{9,13},{2,6},{6,10},{10,14},{3,7},{... | collective-permute-start | bytes 27656 | tf_op jit(solution)/shard_map/ppermute | solution.py:20
  10.7 3.5 %collective-permute-start.3 = (f32[20]{0:T(128)S(1)}, f32[20]{0:T(128)S(1)}, u32[]{:S(2)}, u32[]{:S(2)}) collective-permute-start(f32[20]{0:T(128)S(1)} %get-tuple-element.53), channel_id=1, source_target_pairs={{0,4},{4,8},{8,12},{1,5},{5,9},{9,13},{2,6},{6,10},{10,14},{3,7},{... | collective-permute-start | bytes 248 | tf_op jit(solution)/shard_map/ppermute | solution.py:20
  15.1 1.0 %concatenate.32 = bf16[40,1284]{1,0:T(8,128)(2,1)S(1)} concatenate(bf16[40,1280]{1,0:T(8,128)(2,1)} %param.23, bf16[40,2]{1,0:T(8,128)(2,1)S(1)} %copy.74, bf16[40,2]{1,0:T(8,128)(2,1)S(1)} %copy.75), dimensions={1} | concatenate | bytes 205440 | tf_op jit(solution)/shard_map/concatenate | solution.py:123
  16.0 0.8 broadcast_in_dim.117
  16.9 4.1 %all-to-all-start = ((bf16[4,40,1284]{2,1,0:T(8,128)(2,1)}), bf16[4,40,1284]{2,1,0:T(8,128)(2,1)}, u32[]{:S(2)}, u32[]{:S(2)}) async-start(bf16[4,40,1284]{2,1,0:T(8,128)(2,1)} %broadcast_in_dim.117), calls=%async_computation | async-start | bytes 901120 | tf_op jit(solution)/shard_map/all_to_all | solution.py:125
  24.4 1.8 %divide_convert_fusion = bf16[512,1280]{1,0:T(8,128)(2,1)S(1)} fusion(bf16[512,1280]{1,0:T(8,128)(2,1)S(1)} %copy-done.5, bf16[3,1280]{1,0:T(4,128)(2,1)S(1)} %slice.202, f32[1280]{0:T(1024)S(1)} %get-tuple-element.18, f32[1280]{0:T(1024)S(1)} %get-tuple-element.19, f32[1280]{0:T(1024)S(1)} %get-tuple-element.17, f32[1280]{0:T(1024)S(1)} %get-tuple-element.16), kind=kLoop, calls=%fused_computation.23 | loop fusion | flops 15728640 | bytes 2649600 | tf_op jit(solution)/shard_map/convert_element_type | solution.py:36
  26.9 1.9 %divide_convert_fusion.1 = bf16[512,256]{1,0:T(8,128)(2,1)S(1)} fusion(bf16[512,256]{1,0:T(8,128)(2,1)} %param.15, bf16[3,256]{1,0:T(4,128)(2,1)S(1)} %slice.209, f32[256]{0:T(256)} %bitcast.127, f32[256]{0:T(256)} %bitcast.128, f32[256]{0:T(256)} %bitcast.126, f32[256]{0:T(256)} %bitcast.125), kind=kLoop, calls=%fused_computation.59 | loop fusion | flops 3145728 | bytes 529920 | tf_op jit(solution)/shard_map/convert_element_type | solution.py:36
  29.0 1.1 %convolution_add_fusion.3 = f32[20,64,128]{2,1,0:T(8,128)S(1)} fusion(bf16[256,20,64]{0,2,1:T(8,128)(2,1)S(1)} %bitcast.100, f32[256,20]{0,1:T(8,128)} %get-tuple-element.37, f32[20]{0:T(128)} %get-tuple-element.51, bf16[512,256]{1,0:T(8,128)(2,1)S(1)} %divide_convert_fusion.1), kind=kOutput, calls=%fused_computation.43 | convolution fusion | flops 85032960 | bytes 1396816 | tf_op jit(solution)/shard_map/jhp,js->hps/dot_general | solution.py:52
  30.1 1.1 %fusion.87 = (bf16[20,64,128]{2,1,0:T(8,128)(2,1)S(1)}, f32[20,64,128]{2,1,0:T(8,128)S(1)}) fusion(bf16[512,256]{1,0:T(8,128)(2,1)S(1)} %divide_convert_fusion.1, bf16[256,20,64]{0,2,1:T(8,128)(2,1)S(1)} %bitcast.103, f32[256,20]{0,1:T(8,128)} %get-tuple-element.38, f32[20,64,128]{2,1,0:T(8,128)S(1)} %convolution_add_fusion.3, f32[20]{0:T(128)} %get-tuple-element.54), kind=kOutput, calls=%fused_computation.168 | convolution fusion | flops 85360640 | bytes 2379856 | tf_op jit(solution)/shard_map/jhp,js->hps/dot_general | solution.py:52
  31.1 3.9 %collective-permute-start.1 = (bf16[20,64,128]{2,1,0:T(8,128)(2,1)S(1)}, bf16[20,64,128]{2,1,0:T(8,128)(2,1)S(1)}, u32[]{:S(2)}, u32[]{:S(2)}) collective-permute-start(bf16[20,64,128]{2,1,0:T(8,128)(2,1)S(1)} %get-tuple-element.55), channel_id=1, source_target_pairs={{0,4},{4,8},{8,12},{1,5},{5,9},{9,13},{2,6},{6,10},{10,14},{3,7},{... | collective-permute-start | bytes 983048 | tf_op jit(solution)/shard_map/ppermute | solution.py:20
  35.1 3.0 %fusion = f32[20,64,256]{2,1,0:T(8,128)} fusion(bf16[256,20,64]{0,2,1:T(8,128)(2,1)S(1)} %bitcast.101, f32[20,256]{1,0:T(8,128)S(1)} %copy-done.19, f32[256,256]{1,0:T(8,128)S(1)} %fusion.60, f32[20,256]{1,0:T(8,128)S(1)} %bitcast.118, pred[256,256]{1,0:T(8,128)(4,1)S(1)} %copy-done.15), kind=kOutput, calls=%fused_computation.3 | convolution fusion | flops 175636480 | bytes 2334720 | tf_op jit(solution)/shard_map/hij,jhp->hpi/dot_general | solution.py:49
  38.3 2.9 %collective-permute-done.1 = bf16[20,64,128]{2,1,0:T(8,128)(2,1)S(1)} collective-permute-done((bf16[20,64,128]{2,1,0:T(8,128)(2,1)S(1)}, bf16[20,64,128]{2,1,0:T(8,128)(2,1)S(1)}, u32[]{:S(2)}, u32[]{:S(2)}) %collective-permute-start.1) | collective-permute-done | bytes 327712 | tf_op jit(solution)/shard_map/ppermute | solution.py:20
  41.3 5.5 %collective-permute-start.2 = (bf16[20,64,128]{2,1,0:T(8,128)(2,1)S(1)}, bf16[20,64,128]{2,1,0:T(8,128)(2,1)S(1)}, u32[]{:S(2)}, u32[]{:S(2)}) collective-permute-start(bf16[20,64,128]{2,1,0:T(8,128)(2,1)S(1)} %fusion.26), channel_id=1, source_target_pairs={{0,8},{4,12},{1,9},{5,13},{2,10},{6,14},{3,11},{7,15},{16,24},{20,... | collective-permute-start | bytes 983048 | tf_op jit(solution)/shard_map/ppermute | solution.py:20
  46.8 2.9 %fusion.1 = f32[20,64,256]{2,1,0:T(8,128)} fusion(bf16[256,20,64]{0,2,1:T(8,128)(2,1)S(1)} %bitcast.104, f32[20,256]{1,0:T(8,128)S(1)} %copy-done.18, f32[256,256]{1,0:T(8,128)S(1)} %fusion.56, f32[20,256]{1,0:T(8,128)S(1)} %bitcast.121, pred[256,256]{1,0:T(8,128)(4,1)S(1)} %copy-done.15), kind=kOutput, calls=%fused_computation.4 | convolution fusion | flops 175636480 | bytes 2334720 | tf_op jit(solution)/shard_map/hij,jhp->hpi/dot_general | solution.py:49
  49.7 1.5 %copy.70 = bf16[512,1280]{0,1:T(8,128)(2,1)} copy(bf16[512,1280]{1,0:T(8,128)(2,1)S(1)} %divide_convert_fusion) | data formatting | bytes 2621440 | tf_op jit(solution)/shard_map/layout_constraint | solution.py:135
  51.2 2.4 %copy.71 = bf16[512,1280]{0,1:T(8,128)(2,1)} copy(bf16[512,1280]{1,0:T(8,128)(2,1)} %param.14) | data formatting | bytes 2621440 | tf_op jit(solution)/shard_map/optimization_barrier | solution.py:69
  53.7 0.9 slice_convert_fusion
  55.8 0.9 copy-done.7
  57.1 0.9 copy-done.1
  58.4 1.5 %multiply_reduce_fusion = (f32[512]{0:T(512)S(1)}, f32[1280,512]{1,0:T(8,128)S(1)}) fusion(bf16[512,1280]{0,1:T(8,128)(2,1)S(1)} %copy-done.2, bf16[512,1280]{0,1:T(8,128)(2,1)S(1)} %copy-done.1, f32[1280]{0:T(1024)S(1)} %mul.348, f32[1280,256]{1,0:T(8,128)S(1)} %bitcast.99, f32[1280,256]{1,0:T(8,128)S(1)} %bitcast.98), kind=kLoop, calls=%fused_computation.12 | loop fusion | flops 7208448 | bytes 7871488 | tf_op jit(solution)/shard_map/reduce_sum | solution.py:172
  60.2 0.9 collective-permute-done.4
  61.1 1.5 %collective-permute-start.5 = (f32[512]{0:T(512)S(1)}, f32[512]{0:T(512)S(1)}, u32[]{:S(2)}, u32[]{:S(2)}) collective-permute-start(f32[512]{0:T(512)S(1)} %add.180), channel_id=1, source_target_pairs={{0,2},{1,3},{2,0},{3,1},{4,6},{5,7},{6,4},{7,5},{8,10},{9,11},{10,... | collective-permute-start | bytes 6152 | tf_op jit(solution)/shard_map/ppermute | solution.py:84
  62.7 1.0 %slice.227 = bf16[160,1280]{1,0:T(8,128)(2,1)S(1)} slice(bf16[160,1284]{1,0:T(8,128)(2,1)} %bitcast.20), slice={[0:160], [0:1280]} | slice | bytes 819200 | tf_op jit(solution)/shard_map/slice | solution.py:128
  63.7 1.7 %reshape.244 = bf16[160,8,160]{2,1,0:T(8,128)(2,1)} reshape(bf16[160,1280]{1,0:T(8,128)(2,1)S(1)} %slice.227) | data formatting | bytes 819200 | tf_op jit(solution)/shard_map/reshape | solution.py:185
  65.4 1.4 %fusion.23 = bf16[512,1280]{0,1:T(8,128)(2,1)} fusion(f32[1280,512]{1,0:T(8,128)S(1)} %get-tuple-element.27, f32[1280]{0:T(1024)S(1)} %copy-done.20, f32[512]{0:T(512)S(1)} %add_rsqrt_fusion), kind=kLoop, calls=%fused_computation.37 | loop fusion | flops 1966080 | bytes 3939328 | tf_op jit(solution)/shard_map/transpose | solution.py:177
  66.8 1.7 %copy.85 = bf16[512,1280]{1,0:T(8,128)(2,1)S(1)} copy(bf16[512,1280]{0,1:T(8,128)(2,1)} %fusion.23) | data formatting | bytes 2621440
  68.5 0.9 gather_fusion
  72.0 5.8 %collective-permute-start.6 = (bf16[40,1304]{1,0:T(8,128)(2,1)S(1)}, bf16[40,1304]{1,0:T(8,128)(2,1)S(1)}, u32[]{:S(2)}, u32[]{:S(2)}) collective-permute-start(bf16[40,1304]{1,0:T(8,128)(2,1)S(1)} %get-tuple-element.35), channel_id=1, source_target_pairs={{0,4},{4,8},{8,12},{12,0},{1,5},{5,9},{9,13},{13,1},{2,6},{6,10},{... | collective-permute-start | bytes 312968 | tf_op jit(solution)/shard_map/ppermute | solution.py:217
  77.8 3.4 %collective-permute-start.7 = (bf16[40,1304]{1,0:T(8,128)(2,1)S(1)}, bf16[40,1304]{1,0:T(8,128)(2,1)S(1)}, u32[]{:S(2)}, u32[]{:S(2)}) collective-permute-start(bf16[40,1304]{1,0:T(8,128)(2,1)S(1)} %get-tuple-element.34), channel_id=1, source_target_pairs={{0,8},{4,12},{8,0},{12,4},{1,9},{5,13},{9,1},{13,5},{2,10},{6,14},... | collective-permute-start | bytes 312968 | tf_op jit(solution)/shard_map/ppermute | solution.py:217
  81.3 3.5 %collective-permute-done.6 = bf16[40,1304]{1,0:T(8,128)(2,1)S(1)} collective-permute-done((bf16[40,1304]{1,0:T(8,128)(2,1)S(1)}, bf16[40,1304]{1,0:T(8,128)(2,1)S(1)}, u32[]{:S(2)}, u32[]{:S(2)}) %collective-permute-start.6) | collective-permute-done | bytes 104352 | tf_op jit(solution)/shard_map/ppermute | solution.py:217
  84.7 4.0 %collective-permute-done.7 = bf16[40,1304]{1,0:T(8,128)(2,1)S(1)} collective-permute-done((bf16[40,1304]{1,0:T(8,128)(2,1)S(1)}, bf16[40,1304]{1,0:T(8,128)(2,1)S(1)}, u32[]{:S(2)}, u32[]{:S(2)}) %collective-permute-start.7) | collective-permute-done | bytes 104352 | tf_op jit(solution)/shard_map/ppermute | solution.py:217
  (140 shorter events, 16.7 us)
Async XLA Ops:
  0.6 23.8 %copy-start.5 = (bf16[512,1280]{1,0:T(8,128)(2,1)S(1)}, bf16[512,1280]{1,0:T(8,128)(2,1)}, u32[]{:S(2)}) copy-start(bf16[512,1280]{1,0:T(8,128)(2,1)} %param.13) | copy-start | bytes 3932164
  0.6 21.0 %copy-start.16 = (f32[20,512]{1,0:T(8,128)S(1)}, f32[20,512]{1,0:T(8,128)}, u32[]{:S(2)}) copy-start(f32[20,512]{1,0:T(8,128)} %param.16) | copy-start | bytes 122884
  0.7 21.7 %copy-start.21 = (bf16[4,256]{1,0:T(4,128)(2,1)S(1)}, bf16[4,256]{1,0:T(4,128)(2,1)}, u32[]{:S(2)}) copy-start(bf16[4,256]{1,0:T(4,128)(2,1)} %param.20) | copy-start | bytes 6148
  0.7 22.3 %copy-start.17 = (bf16[4,1280]{1,0:T(4,128)(2,1)S(1)}, bf16[4,1280]{1,0:T(4,128)(2,1)}, u32[]{:S(2)}) copy-start(bf16[4,1280]{1,0:T(4,128)(2,1)} %param.19) | copy-start | bytes 30724
  0.7 22.4 %copy-start.27 = (s32[128]{0:T(128)S(1)}, s32[128]{0:T(128)}, u32[]{:S(2)}) copy-start(s32[128]{0:T(128)} %param.22) | copy-start | bytes 1540
  0.7 23.5 %copy-start.25 = (f32[20]{0:T(128)S(1)}, f32[20]{0:T(128)}, u32[]{:S(2)}) copy-start(f32[20]{0:T(128)} %param.18) | copy-start | bytes 244
  2.2 22.1 %collective-permute-start = (bf16[3,1536]{1,0:T(4,128)(2,1)S(1)}, bf16[3,1536]{1,0:T(4,128)(2,1)S(1)}, u32[]{:S(2)}, u32[]{:S(2)}) collective-permute-start(bf16[3,1536]{1,0:T(4,128)(2,1)S(1)} %pad_maximum_fusion.5), channel_id=1, source_target_pairs={{0,4},{4,8},{8,12},{1,5},{5,9},{9,13},{2,6},{6,10},{10,14},{3,7},{... | collective-permute-start | bytes 27656 | tf_op jit(solution)/shard_map/ppermute | solution.py:20
  8.9 15.5 %copy-start.9 = (f32[3,8,2,128]{3,1,2,0:T(8,128)}, f32[3,8,2,128]{3,1,2,0:T(8,128)S(1)}, u32[]{:S(2)}) copy-start(f32[3,8,2,128]{3,1,2,0:T(8,128)S(1)} %copy.87) | copy-start | bytes 73732
  9.9 14.5 %copy-start.11 = (f32[3,8,2,128]{3,1,2,0:T(8,128)}, f32[3,8,2,128]{3,1,2,0:T(8,128)S(1)}, u32[]{:S(2)}) copy-start(f32[3,8,2,128]{3,1,2,0:T(8,128)S(1)} %copy.88) | copy-start | bytes 73732
  10.7 13.7 %collective-permute-start.3 = (f32[20]{0:T(128)S(1)}, f32[20]{0:T(128)S(1)}, u32[]{:S(2)}, u32[]{:S(2)}) collective-permute-start(f32[20]{0:T(128)S(1)} %get-tuple-element.53), channel_id=1, source_target_pairs={{0,4},{4,8},{8,12},{1,5},{5,9},{9,13},{2,6},{6,10},{10,14},{3,7},{... | collective-permute-start | bytes 248 | tf_op jit(solution)/shard_map/ppermute | solution.py:20
  16.9 36.8 %all-to-all-start = ((bf16[4,40,1284]{2,1,0:T(8,128)(2,1)}), bf16[4,40,1284]{2,1,0:T(8,128)(2,1)}, u32[]{:S(2)}, u32[]{:S(2)}) async-start(bf16[4,40,1284]{2,1,0:T(8,128)(2,1)} %broadcast_in_dim.117), calls=%async_computation | async-start | bytes 901120 | tf_op jit(solution)/shard_map/all_to_all | solution.py:125
  26.8 4.3 %copy-start.3 = (bf16[256,1280]{0,1:T(8,128)(2,1)}, bf16[256,1280]{0,1:T(8,128)(2,1)S(1)}, u32[]{:S(2)}) copy-start(bf16[256,1280]{0,1:T(8,128)(2,1)S(1)} %copy.69) | copy-start | bytes 1966084
  26.8 8.2 %copy-start.10 = (f32[3,8,2,128]{3,1,2,0:T(8,128)S(1)}, f32[3,8,2,128]{3,1,2,0:T(8,128)}, u32[]{:S(2)}) copy-start(f32[3,8,2,128]{3,1,2,0:T(8,128)} %copy-done.9) | copy-start | bytes 73732
  26.8 8.2 %copy-start.15 = (pred[256,256]{1,0:T(8,128)(4,1)S(1)}, pred[256,256]{1,0:T(8,128)(4,1)}, u32[]{:S(2)}) copy-start(pred[256,256]{1,0:T(8,128)(4,1)} %iota_compare_fusion) | copy-start | bytes 196612
  26.8 8.2 %copy-start.19 = (f32[20,256]{1,0:T(8,128)S(1)}, f32[20,256]{1,0:T(8,128)}, u32[]{:S(2)}) copy-start(f32[20,256]{1,0:T(8,128)} %get-tuple-element.36) | copy-start | bytes 61444
  31.1 10.0 %collective-permute-start.1 = (bf16[20,64,128]{2,1,0:T(8,128)(2,1)S(1)}, bf16[20,64,128]{2,1,0:T(8,128)(2,1)S(1)}, u32[]{:S(2)}, u32[]{:S(2)}) collective-permute-start(bf16[20,64,128]{2,1,0:T(8,128)(2,1)S(1)} %get-tuple-element.55), channel_id=1, source_target_pairs={{0,4},{4,8},{8,12},{1,5},{5,9},{9,13},{2,6},{6,10},{10,14},{3,7},{... | collective-permute-start | bytes 983048 | tf_op jit(solution)/shard_map/ppermute | solution.py:20
  35.1 6.1 %copy-start.23 = (f32[20]{0:T(128)S(1)}, f32[20]{0:T(128)}, u32[]{:S(2)}) copy-start(f32[20]{0:T(128)} %get-tuple-element.52) | copy-start | bytes 244
  35.1 11.7 %copy-start.4 = (bf16[256,1280]{0,1:T(8,128)(2,1)S(1)}, bf16[256,1280]{0,1:T(8,128)(2,1)}, u32[]{:S(2)}) copy-start(bf16[256,1280]{0,1:T(8,128)(2,1)} %copy-done.3) | copy-start | bytes 1966084
  35.1 11.7 %copy-start.12 = (f32[3,8,2,128]{3,1,2,0:T(8,128)S(1)}, f32[3,8,2,128]{3,1,2,0:T(8,128)}, u32[]{:S(2)}) copy-start(f32[3,8,2,128]{3,1,2,0:T(8,128)} %copy-done.11) | copy-start | bytes 73732
  35.1 11.7 %copy-start.18 = (f32[20,256]{1,0:T(8,128)S(1)}, f32[20,256]{1,0:T(8,128)}, u32[]{:S(2)}) copy-start(f32[20,256]{1,0:T(8,128)} %get-tuple-element.39) | copy-start | bytes 61444
  41.3 13.2 %collective-permute-start.2 = (bf16[20,64,128]{2,1,0:T(8,128)(2,1)S(1)}, bf16[20,64,128]{2,1,0:T(8,128)(2,1)S(1)}, u32[]{:S(2)}, u32[]{:S(2)}) collective-permute-start(bf16[20,64,128]{2,1,0:T(8,128)(2,1)S(1)} %fusion.26), channel_id=1, source_target_pairs={{0,8},{4,12},{1,9},{5,13},{2,10},{6,14},{3,11},{7,15},{16,24},{20,... | collective-permute-start | bytes 983048 | tf_op jit(solution)/shard_map/ppermute | solution.py:20
  51.2 3.7 %copy-start.22 = (f32[20]{0:T(128)S(1)}, f32[20]{0:T(128)}, u32[]{:S(2)}) copy-start(f32[20]{0:T(128)} %get-tuple-element.50) | copy-start | bytes 244
  53.6 1.7 %copy-start.14 = (f32[20,256]{1,0:T(8,128)S(1)}, f32[20,256]{1,0:T(8,128)}, u32[]{:S(2)}) copy-start(f32[20,256]{1,0:T(8,128)} %get-tuple-element.43) | copy-start | bytes 61444
  58.4 4.2 %copy-start.26 = (s32[128]{0:T(128)S(1)}, s32[128]{0:T(128)}, u32[]{:S(2)}) copy-start(s32[128]{0:T(128)} %iota_add_fusion) | copy-start | bytes 1540
  58.4 7.0 %copy-start.20 = (f32[1280]{0:T(1024)S(1)}, f32[1280]{0:T(1024)}, u32[]{:S(2)}) copy-start(f32[1280]{0:T(1024)} %param.21) | copy-start | bytes 15364
  59.9 1.2 %collective-permute-start.4 = (f32[512]{0:T(512)S(1)}, f32[512]{0:T(512)S(1)}, u32[]{:S(2)}, u32[]{:S(2)}) collective-permute-start(f32[512]{0:T(512)S(1)} %get-tuple-element.26), channel_id=1, source_target_pairs={{0,1},{1,0},{2,3},{3,2},{4,5},{5,4},{6,7},{7,6},{8,9},{9,8},{10,11... | collective-permute-start | bytes 6152 | tf_op jit(solution)/shard_map/ppermute | solution.py:84
  61.1 4.3 %collective-permute-start.5 = (f32[512]{0:T(512)S(1)}, f32[512]{0:T(512)S(1)}, u32[]{:S(2)}, u32[]{:S(2)}) collective-permute-start(f32[512]{0:T(512)S(1)} %add.180), channel_id=1, source_target_pairs={{0,2},{1,3},{2,0},{3,1},{4,6},{5,7},{6,4},{7,5},{8,10},{9,11},{10,... | collective-permute-start | bytes 6152 | tf_op jit(solution)/shard_map/ppermute | solution.py:84
  66.8 2.8 %copy-start.8 = (bf16[160,8,160]{2,1,0:T(8,128)(2,1)S(1)}, bf16[160,8,160]{2,1,0:T(8,128)(2,1)}, u32[]{:S(2)}) copy-start(bf16[160,8,160]{2,1,0:T(8,128)(2,1)} %reshape.244) | copy-start | bytes 1228804
  66.8 2.8 %copy-start.24 = (pred[128]{0:T(512)(128)(4,1)S(1)}, pred[128]{0:T(512)(128)(4,1)}, u32[]{:S(2)}) copy-start(pred[128]{0:T(512)(128)(4,1)} %get-tuple-element.24) | copy-start | bytes 388
  72.0 12.7 %collective-permute-start.6 = (bf16[40,1304]{1,0:T(8,128)(2,1)S(1)}, bf16[40,1304]{1,0:T(8,128)(2,1)S(1)}, u32[]{:S(2)}, u32[]{:S(2)}) collective-permute-start(bf16[40,1304]{1,0:T(8,128)(2,1)S(1)} %get-tuple-element.35), channel_id=1, source_target_pairs={{0,4},{4,8},{8,12},{12,0},{1,5},{5,9},{9,13},{13,1},{2,6},{6,10},{... | collective-permute-start | bytes 312968 | tf_op jit(solution)/shard_map/ppermute | solution.py:217
  77.8 10.9 %collective-permute-start.7 = (bf16[40,1304]{1,0:T(8,128)(2,1)S(1)}, bf16[40,1304]{1,0:T(8,128)(2,1)S(1)}, u32[]{:S(2)}, u32[]{:S(2)}) collective-permute-start(bf16[40,1304]{1,0:T(8,128)(2,1)S(1)} %get-tuple-element.34), channel_id=1, source_target_pairs={{0,8},{4,12},{8,0},{12,4},{1,9},{5,13},{9,1},{13,5},{2,10},{6,14},... | collective-permute-start | bytes 312968 | tf_op jit(solution)/shard_map/ppermute | solution.py:217
  81.3 7.5 %collective-permute-start.8 = (bf16[40,1304]{1,0:T(8,128)(2,1)S(1)}, bf16[40,1304]{1,0:T(8,128)(2,1)S(1)}, u32[]{:S(2)}, u32[]{:S(2)}) collective-permute-start(bf16[40,1304]{1,0:T(8,128)(2,1)S(1)} %get-tuple-element.33), channel_id=1, source_target_pairs={{0,12},{4,0},{8,4},{12,8},{1,13},{5,1},{9,5},{13,9},{2,14},{6,2},{... | collective-permute-start | bytes 312968 | tf_op jit(solution)/shard_map/ppermute | solution.py:217
  (6 other events, 9.1 us)

commit v11 on v10

--- a/solution.py
+++ b/solution.py
@@ -121,9 +121,13 @@
     bounds = jnp.stack([pool_start, pool_stop], axis=1)
     bounds_split = jnp.concatenate([bounds // 64, bounds % 64], axis=1).astype(jnp.bfloat16)
     query_rows = jnp.concatenate([pool_query, bounds_split], axis=1)
-    query_rows = jnp.broadcast_to(query_rows[None], (seq_count,) + query_rows.shape)
-    query_rows = lax.all_to_all(
-        query_rows.reshape(seq_count * pools_local, -1), "seq", 0, 0, tiled=True
+    query_rows = jnp.concatenate(
+        [query_rows]
+        + [
+            lax.ppermute(query_rows, "seq", [(i, (i + shift) % seq_count) for i in range(seq_count)])
+            for shift in range(1, seq_count)
+        ],
+        axis=0,
     )
     queries_all = query_rows[:, :channels]
     bounds_all = query_rows[:, channels:].astype(jnp.int32)
@@ -209,13 +213,11 @@
         axis=1,
     )
     parts = parts.reshape(seq_count, pools_local, channels + 3 * pool_heads_local)
-    place = lax.axis_index("seq")
-    gathered = [lax.dynamic_index_in_dim(parts, place, 0, False)]
+    gathered = [parts[0]]
     for shift in range(1, seq_count):
-        chunk = lax.dynamic_index_in_dim(parts, (place + shift) % seq_count, 0, False)
         gathered.append(
             lax.ppermute(
-                chunk, "seq", [(i, (i + shift) % seq_count) for i in range(seq_count)]
+                parts[shift], "seq", [(i, (i - shift) % seq_count) for i in range(seq_count)]
             )
         )
     parts = jnp.stack(gathered).astype(jnp.float32)

time: 91.7 us -> 92.2 us (level)
  other arithmetic: 15.3 us -> 18.6 us
  starting transfers between devices: 32.7 us -> 29.9 us
  matrix products: 10.9 us -> 11.9 us
    ppermute x3 -> x6, starting transfers between devices: 9.22 us -> 18.1 us  [the longest x3 11.1 us: local(): lax.ppermute(parts[shift], 'seq', [(i, (i - shift) % seq_count) for i in...]
    ppermute x4, starting transfers between devices: 17.8 us -> 10.3 us  [passed_along(): lax.ppermute(value, axis, [(source, source + steps) for source in range(l...]
    all_to_all x1 -> x0, starting transfers between devices: 4.12 us -> none  [local(): lax.all_to_all(query_rows.reshape(seq_count * pools_local, -1), 'seq', 0,...]
    ppermute x4, waiting for transfers between devices: 2.89 us -> 0.5 us  [passed_along(): lax.ppermute(value, axis, [(source, source + steps) for source in range(l...]
    dot_general x2, matrix products: 2.16 us -> 0.69 us  [stretch_local(): jnp.einsum('jhp,js->hps', weighted, b_block, preferred_element_type=jnp.f...]
    dot_general x2, matrix products: 0.36 us -> 1.78 us  [stretch_local(): jnp.einsum('is,js->ij', c_block, b_block, preferred_element_type=jnp.floa...]
    ppermute x3 -> x6, waiting for transfers between devices: 7.51 us -> 8.89 us  [the longest x3 8.88 us: local(): lax.ppermute(parts[shift], 'seq', [(i, (i - shift) % seq_count) for i in...]
    mul x2, other arithmetic: 0.64 us -> 1.75 us  [causal_conv(): padded[offset:offset + length].astype(jnp.float32)]
  transfers between devices with their start and end apart: 10 -> 12, of which waited for: 4 -> 5; matrix products, arithmetic and copies ran while one was open for 33% -> 36% of each run, Pallas kernels for 0% -> 0%
where the time goes in v11:
time: 92.2 us; the launch traced here: 91.4 us
  starting transfers between devices  29.9 us (32%)
  local copies, waits for them, and re-layouts  19.2 us (21%)
  other arithmetic  18.6 us (20%)
  matrix products  11.9 us (13%)
  waiting for transfers between devices  10.6 us (11%)
  between operations  1.22 us (1%)
    ppermute x3, starting transfers between devices, local(): lax.ppermute(parts[shift], 'seq', [(i, (i - shift) % seq_count) for i in...  11.1 us
    ppermute x4, starting transfers between devices, passed_along(): lax.ppermute(value, axis, [(source, source + steps) for source in range(l...  10.3 us
    ppermute x3, waiting for transfers between devices, local(): lax.ppermute(parts[shift], 'seq', [(i, (i - shift) % seq_count) for i in...  8.88 us
    ppermute x3, starting transfers between devices, local(): lax.ppermute(query_rows, 'seq', [(i, (i + shift) % seq_count) for i in ra...  6.99 us
    dot_general x2, matrix products, stretch_local(): jnp.einsum('hij,jhp->hpi', mixing, x_block, preferred_element_type=jnp.fl...  6.8 us
    unnamed x54, local copies, waits for them, and re-layouts  5.06 us
    convert_element_type x2, other arithmetic, causal_conv(): return silu_act(summed).astype(jnp.bfloat16)  3.73 us
    optimization_barrier x1, local copies, waits for them, and re-layouts, exclusive_scan(): sent_state, rider = lax.optimization_barrier((sent_state, rider))  2.43 us
  transfers between devices with their start and end apart: 12, of which 5 were waited for; matrix products, arithmetic and copies ran while one was open for 36% of the time, Pallas kernels for 0%

profile of v11, /device:TPU:0, one launch (start us, length us, event | category | flops | bytes accessed | tf_op | source)
XLA Modules:
  0.0 91.4 jit_solution(8346436635209358367)
XLA Ops:
  1.6 1.6 %concatenate.35 = bf16[40,1284]{1,0:T(8,128)(2,1)} concatenate(bf16[40,1280]{1,0:T(8,128)(2,1)} %param.23, bf16[40,2]{1,0:T(8,128)(2,1)S(1)} %copy.95, bf16[40,2]{1,0:T(8,128)(2,1)S(1)} %copy.96), dimensions={1} | concatenate | bytes 205440 | tf_op jit(solution)/shard_map/concatenate | solution.py:123
  3.3 3.1 %collective-permute-start.6 = (bf16[40,1284]{1,0:T(8,128)(2,1)}, bf16[40,1284]{1,0:T(8,128)(2,1)}, u32[]{:S(2)}, u32[]{:S(2)}) collective-permute-start(bf16[40,1284]{1,0:T(8,128)(2,1)} %concatenate.35), channel_id=1, source_target_pairs={{0,4},{4,8},{8,12},{12,0},{1,5},{5,9},{9,13},{13,1},{2,6},{6,10},{... | collective-permute-start | bytes 308168 | tf_op jit(solution)/shard_map/ppermute | solution.py:127
  6.3 2.6 %collective-permute-start.7 = (bf16[40,1284]{1,0:T(8,128)(2,1)}, bf16[40,1284]{1,0:T(8,128)(2,1)}, u32[]{:S(2)}, u32[]{:S(2)}) collective-permute-start(bf16[40,1284]{1,0:T(8,128)(2,1)} %concatenate.35), channel_id=1, source_target_pairs={{0,8},{4,12},{8,0},{12,4},{1,9},{5,13},{9,1},{13,5},{2,10},{6,14},... | collective-permute-start | bytes 308168 | tf_op jit(solution)/shard_map/ppermute | solution.py:127
  8.9 1.3 %collective-permute-start.8 = (bf16[40,1284]{1,0:T(8,128)(2,1)}, bf16[40,1284]{1,0:T(8,128)(2,1)}, u32[]{:S(2)}, u32[]{:S(2)}) collective-permute-start(bf16[40,1284]{1,0:T(8,128)(2,1)} %concatenate.35), channel_id=1, source_target_pairs={{0,12},{4,0},{8,4},{12,8},{1,13},{5,1},{9,5},{13,9},{2,14},{6,2},{... | collective-permute-start | bytes 308168 | tf_op jit(solution)/shard_map/ppermute | solution.py:127
  11.7 2.6 %collective-permute-start = (bf16[3,1536]{1,0:T(4,128)(2,1)S(1)}, bf16[3,1536]{1,0:T(4,128)(2,1)S(1)}, u32[]{:S(2)}, u32[]{:S(2)}) collective-permute-start(bf16[3,1536]{1,0:T(4,128)(2,1)S(1)} %pad_maximum_fusion.6), channel_id=1, source_target_pairs={{0,4},{4,8},{8,12},{1,5},{5,9},{9,13},{2,6},{6,10},{10,14},{3,7},{... | collective-permute-start | bytes 27656 | tf_op jit(solution)/shard_map/ppermute | solution.py:20
  17.8 1.9 %collective-permute-start.3 = (f32[20]{0:T(128)S(1)}, f32[20]{0:T(128)S(1)}, u32[]{:S(2)}, u32[]{:S(2)}) collective-permute-start(f32[20]{0:T(128)S(1)} %get-tuple-element.55), channel_id=1, source_target_pairs={{0,4},{4,8},{8,12},{1,5},{5,9},{9,13},{2,6},{6,10},{10,14},{3,7},{... | collective-permute-start | bytes 248 | tf_op jit(solution)/shard_map/ppermute | solution.py:20
  20.3 1.5 %fusion.85 = (f32[20,256]{1,0:T(8,128)}, f32[256,20]{0,1:T(8,128)}, f32[256,20]{0,1:T(8,128)}, f32[20,256]{1,0:T(8,128)}, f32[20,256]{1,0:T(8,128)}, /*index=5*/f32[20,256]{1,0:T(8,128)}) fusion(f32[20,512]{1,0:T(8,128)} %param.16, f32[20,256]{1,0:T(8,128)S(1)} %bitcast.105, f32[20]{0:T(128)S(1)} %get-tuple-element.61, f32[20,256]{1,0:T(8,128)S(1)} %bitcast.108, ...), kind=kLoop, calls=%fused_computation.165 | loop fusion | flops 20480 | bytes 204960 | tf_op jit(solution)/shard_map/slice | solution.py:155
  22.7 0.9 convert_reduce_fusion.3
  23.6 1.2 %compare_and_fusion.1 = (pred[128]{0:T(512)(128)(4,1)}, s32[128]{0:T(128)S(1)}) fusion(s32[128]{0:T(128)} %param.22, s32[]{:T(128)S(6)} %mul.358), kind=kLoop, calls=%fused_computation.143 | loop fusion | flops 896 | bytes 1156 | tf_op jit(solution)/shard_map/jit(_take)/and | solution.py:183
  26.1 1.9 %divide_convert_fusion.1 = bf16[512,256]{1,0:T(8,128)(2,1)S(1)} fusion(bf16[512,256]{1,0:T(8,128)(2,1)} %param.15, bf16[3,256]{1,0:T(4,128)(2,1)S(1)} %slice.232, f32[256]{0:T(256)S(1)} %bitcast.118, f32[256]{0:T(256)S(1)} %bitcast.119, f32[256]{0:T(256)S(1)} %bitcast.117, f32[256]{0:T(256)S(1)} %bitcast.116), kind=kLoop, calls=%fused_computation.61 | loop fusion | flops 3145728 | bytes 529920 | tf_op jit(solution)/shard_map/convert_element_type | solution.py:36
  28.0 0.9 fusion.61
  28.9 0.9 fusion.57
  29.8 1.8 %divide_convert_fusion = bf16[512,1280]{1,0:T(8,128)(2,1)S(1)} fusion(bf16[512,1280]{1,0:T(8,128)(2,1)S(1)} %copy-done.3, bf16[3,1280]{1,0:T(4,128)(2,1)S(1)} %slice.225, f32[1280]{0:T(1024)S(1)} %get-tuple-element.20, f32[1280]{0:T(1024)S(1)} %get-tuple-element.21, f32[1280]{0:T(1024)S(1)} %get-tuple-element.19, f32[1280]{0:T(1024)S(1)} %get-tuple-element.18), kind=kLoop, calls=%fused_computation.25 | loop fusion | flops 15728640 | bytes 2649600 | tf_op jit(solution)/shard_map/convert_element_type | solution.py:36
  31.8 1.5 %copy.91 = bf16[512,1280]{0,1:T(8,128)(2,1)} copy(bf16[512,1280]{1,0:T(8,128)(2,1)S(1)} %divide_convert_fusion) | data formatting | bytes 2621440 | tf_op jit(solution)/shard_map/layout_constraint | solution.py:139
  34.7 2.8 %collective-permute-start.1 = (bf16[20,64,128]{2,1,0:T(8,128)(2,1)S(1)}, bf16[20,64,128]{2,1,0:T(8,128)(2,1)S(1)}, u32[]{:S(2)}, u32[]{:S(2)}) collective-permute-start(bf16[20,64,128]{2,1,0:T(8,128)(2,1)S(1)} %get-tuple-element.57), channel_id=1, source_target_pairs={{0,4},{4,8},{8,12},{1,5},{5,9},{9,13},{2,6},{6,10},{10,14},{3,7},{... | collective-permute-start | bytes 983048 | tf_op jit(solution)/shard_map/ppermute | solution.py:20
  37.6 3.9 %fusion = f32[20,64,256]{2,1,0:T(8,128)} fusion(bf16[256,20,64]{0,2,1:T(8,128)(2,1)S(1)} %bitcast.98, f32[20,256]{1,0:T(8,128)} %get-tuple-element.38, f32[256,256]{1,0:T(8,128)} %fusion.61, f32[20,256]{1,0:T(8,128)} %bitcast.106, pred[256,256]{1,0:T(8,128)(4,1)} %iota_compare_fusion), kind=kOutput, calls=%fused_computation.3 | convolution fusion | flops 175636480 | bytes 2334720 | tf_op jit(solution)/shard_map/hij,jhp->hpi/dot_general | solution.py:49
  41.5 2.9 %fusion.1 = f32[20,64,256]{2,1,0:T(8,128)} fusion(bf16[256,20,64]{0,2,1:T(8,128)(2,1)S(1)} %bitcast.101, f32[20,256]{1,0:T(8,128)S(1)} %copy-done.16, f32[256,256]{1,0:T(8,128)S(1)} %copy-done.7, f32[20,256]{1,0:T(8,128)S(1)} %bitcast.109, pred[256,256]{1,0:T(8,128)(4,1)S(1)} %copy-done.15), kind=kOutput, calls=%fused_computation.4 | convolution fusion | flops 175636480 | bytes 2334720 | tf_op jit(solution)/shard_map/hij,jhp->hpi/dot_general | solution.py:49
  44.6 3.0 %collective-permute-start.2 = (bf16[20,64,128]{2,1,0:T(8,128)(2,1)S(1)}, bf16[20,64,128]{2,1,0:T(8,128)(2,1)S(1)}, u32[]{:S(2)}, u32[]{:S(2)}) collective-permute-start(bf16[20,64,128]{2,1,0:T(8,128)(2,1)S(1)} %fusion.27), channel_id=1, source_target_pairs={{0,8},{4,12},{1,9},{5,13},{2,10},{6,14},{3,11},{7,15},{16,24},{20,... | collective-permute-start | bytes 983048 | tf_op jit(solution)/shard_map/ppermute | solution.py:20
  48.4 1.1 %pad_maximum_fusion.2 = bf16[160,1280]{1,0:T(8,128)(2,1)S(1)} fusion(bf16[40,1284]{1,0:T(8,128)(2,1)} %collective-permute-done.8, bf16[40,1284]{1,0:T(8,128)(2,1)} %collective-permute-done.7, bf16[40,1284]{1,0:T(8,128)(2,1)} %collective-permute-done.6, bf16[40,1284]{1,0:T(8,128)(2,1)} %concatenate.35), kind=kLoop, calls=%fused_computation.64 | loop fusion | flops 1638400 | bytes 820480 | tf_op jit(solution)/shard_map/concatenate | solution.py:124
  49.5 2.4 %copy.92 = bf16[512,1280]{0,1:T(8,128)(2,1)} copy(bf16[512,1280]{1,0:T(8,128)(2,1)} %param.14) | data formatting | bytes 2621440 | tf_op jit(solution)/shard_map/optimization_barrier | solution.py:69
  53.6 0.9 copy-done.5
  56.2 1.5 %multiply_reduce_fusion = (f32[512]{0:T(512)S(1)}, f32[1280,512]{1,0:T(8,128)S(1)}) fusion(bf16[512,1280]{0,1:T(8,128)(2,1)S(1)} %copy-done.2, bf16[512,1280]{0,1:T(8,128)(2,1)S(1)} %copy-done.1, f32[1280]{0:T(1024)S(1)} %mul.348, f32[1280,256]{1,0:T(8,128)S(1)} %bitcast.96, f32[1280,256]{1,0:T(8,128)S(1)} %bitcast.95), kind=kLoop, calls=%fused_computation.14 | loop fusion | flops 7208448 | bytes 7871488 | tf_op jit(solution)/shard_map/reduce_sum | solution.py:176
  58.0 0.9 collective-permute-done.4
  58.9 1.5 %collective-permute-start.5 = (f32[512]{0:T(512)S(1)}, f32[512]{0:T(512)S(1)}, u32[]{:S(2)}, u32[]{:S(2)}) collective-permute-start(f32[512]{0:T(512)S(1)} %add.148), channel_id=1, source_target_pairs={{0,2},{1,3},{2,0},{3,1},{4,6},{5,7},{6,4},{7,5},{8,10},{9,11},{10,... | collective-permute-start | bytes 6152 | tf_op jit(solution)/shard_map/ppermute | solution.py:84
  60.5 1.7 %reshape.244 = bf16[160,8,160]{2,1,0:T(8,128)(2,1)} reshape(bf16[160,1280]{1,0:T(8,128)(2,1)S(1)} %pad_maximum_fusion.2) | data formatting | bytes 819200 | tf_op jit(solution)/shard_map/reshape | solution.py:189
  62.5 1.4 %fusion.24 = bf16[512,1280]{0,1:T(8,128)(2,1)} fusion(f32[1280,512]{1,0:T(8,128)S(1)} %get-tuple-element.29, f32[1280]{0:T(1024)S(1)} %copy-done.17, f32[512]{0:T(512)S(1)} %add_rsqrt_fusion), kind=kLoop, calls=%fused_computation.39 | loop fusion | flops 1966080 | bytes 3939328 | tf_op jit(solution)/shard_map/transpose | solution.py:181
  63.9 1.7 %copy.104 = bf16[512,1280]{1,0:T(8,128)(2,1)S(1)} copy(bf16[512,1280]{0,1:T(8,128)(2,1)} %fusion.24) | data formatting | bytes 2621440
  65.6 0.9 gather_fusion
  69.1 10.4 %collective-permute-start.9 = (bf16[40,1304]{1,0:T(8,128)(2,1)S(1)}, bf16[40,1304]{1,0:T(8,128)(2,1)S(1)}, u32[]{:S(2)}, u32[]{:S(2)}) collective-permute-start(bf16[40,1304]{1,0:T(8,128)(2,1)S(1)} %get-tuple-element.37), channel_id=1, source_target_pairs={{0,12},{4,0},{8,4},{12,8},{1,13},{5,1},{9,5},{13,9},{2,14},{6,2},{... | collective-permute-start | bytes 312968 | tf_op jit(solution)/shard_map/ppermute | solution.py:219
  80.2 2.8 %collective-permute-done.9 = bf16[40,1304]{1,0:T(8,128)(2,1)S(1)} collective-permute-done((bf16[40,1304]{1,0:T(8,128)(2,1)S(1)}, bf16[40,1304]{1,0:T(8,128)(2,1)S(1)}, u32[]{:S(2)}, u32[]{:S(2)}) %collective-permute-start.9) | collective-permute-done | bytes 104352 | tf_op jit(solution)/shard_map/ppermute | solution.py:219
  83.0 6.0 %collective-permute-done.10 = bf16[40,1304]{1,0:T(8,128)(2,1)S(1)} collective-permute-done((bf16[40,1304]{1,0:T(8,128)(2,1)S(1)}, bf16[40,1304]{1,0:T(8,128)(2,1)S(1)}, u32[]{:S(2)}, u32[]{:S(2)}) %collective-permute-start.10) | collective-permute-done | bytes 104352 | tf_op jit(solution)/shard_map/ppermute | solution.py:219
  90.5 0.9 copy.105
  (132 shorter events, 19.9 us)
Async XLA Ops:
  0.6 29.2 %copy-start.3 = (bf16[512,1280]{1,0:T(8,128)(2,1)S(1)}, bf16[512,1280]{1,0:T(8,128)(2,1)}, u32[]{:S(2)}) copy-start(bf16[512,1280]{1,0:T(8,128)(2,1)} %param.13) | copy-start | bytes 3932164
  3.3 44.3 %collective-permute-start.6 = (bf16[40,1284]{1,0:T(8,128)(2,1)}, bf16[40,1284]{1,0:T(8,128)(2,1)}, u32[]{:S(2)}, u32[]{:S(2)}) collective-permute-start(bf16[40,1284]{1,0:T(8,128)(2,1)} %concatenate.35), channel_id=1, source_target_pairs={{0,4},{4,8},{8,12},{12,0},{1,5},{5,9},{9,13},{13,1},{2,6},{6,10},{... | collective-permute-start | bytes 308168 | tf_op jit(solution)/shard_map/ppermute | solution.py:127
  6.3 41.2 %collective-permute-start.7 = (bf16[40,1284]{1,0:T(8,128)(2,1)}, bf16[40,1284]{1,0:T(8,128)(2,1)}, u32[]{:S(2)}, u32[]{:S(2)}) collective-permute-start(bf16[40,1284]{1,0:T(8,128)(2,1)} %concatenate.35), channel_id=1, source_target_pairs={{0,8},{4,12},{8,0},{12,4},{1,9},{5,13},{9,1},{13,5},{2,10},{6,14},... | collective-permute-start | bytes 308168 | tf_op jit(solution)/shard_map/ppermute | solution.py:127
  8.9 38.7 %collective-permute-start.8 = (bf16[40,1284]{1,0:T(8,128)(2,1)}, bf16[40,1284]{1,0:T(8,128)(2,1)}, u32[]{:S(2)}, u32[]{:S(2)}) collective-permute-start(bf16[40,1284]{1,0:T(8,128)(2,1)} %concatenate.35), channel_id=1, source_target_pairs={{0,12},{4,0},{8,4},{12,8},{1,13},{5,1},{9,5},{13,9},{2,14},{6,2},{... | collective-permute-start | bytes 308168 | tf_op jit(solution)/shard_map/ppermute | solution.py:127
  11.7 14.4 %collective-permute-start = (bf16[3,1536]{1,0:T(4,128)(2,1)S(1)}, bf16[3,1536]{1,0:T(4,128)(2,1)S(1)}, u32[]{:S(2)}, u32[]{:S(2)}) collective-permute-start(bf16[3,1536]{1,0:T(4,128)(2,1)S(1)} %pad_maximum_fusion.6), channel_id=1, source_target_pairs={{0,4},{4,8},{8,12},{1,5},{5,9},{9,13},{2,6},{6,10},{10,14},{3,7},{... | collective-permute-start | bytes 27656 | tf_op jit(solution)/shard_map/ppermute | solution.py:20
  16.0 13.8 %copy-start.8 = (f32[3,8,2,128]{3,1,2,0:T(8,128)}, f32[3,8,2,128]{3,1,2,0:T(8,128)S(1)}, u32[]{:S(2)}) copy-start(f32[3,8,2,128]{3,1,2,0:T(8,128)S(1)} %copy.107) | copy-start | bytes 73732
  17.0 12.8 %copy-start.9 = (f32[3,8,2,128]{3,1,2,0:T(8,128)}, f32[3,8,2,128]{3,1,2,0:T(8,128)S(1)}, u32[]{:S(2)}) copy-start(f32[3,8,2,128]{3,1,2,0:T(8,128)S(1)} %copy.108) | copy-start | bytes 73732
  17.8 8.3 %collective-permute-start.3 = (f32[20]{0:T(128)S(1)}, f32[20]{0:T(128)S(1)}, u32[]{:S(2)}, u32[]{:S(2)}) collective-permute-start(f32[20]{0:T(128)S(1)} %get-tuple-element.55), channel_id=1, source_target_pairs={{0,4},{4,8},{8,12},{1,5},{5,9},{9,13},{2,6},{6,10},{10,14},{3,7},{... | collective-permute-start | bytes 248 | tf_op jit(solution)/shard_map/ppermute | solution.py:20
  34.7 9.7 %collective-permute-start.1 = (bf16[20,64,128]{2,1,0:T(8,128)(2,1)S(1)}, bf16[20,64,128]{2,1,0:T(8,128)(2,1)S(1)}, u32[]{:S(2)}, u32[]{:S(2)}) collective-permute-start(bf16[20,64,128]{2,1,0:T(8,128)(2,1)S(1)} %get-tuple-element.57), channel_id=1, source_target_pairs={{0,4},{4,8},{8,12},{1,5},{5,9},{9,13},{2,6},{6,10},{10,14},{3,7},{... | collective-permute-start | bytes 983048 | tf_op jit(solution)/shard_map/ppermute | solution.py:20
  37.5 3.9 %copy-start.7 = (f32[256,256]{1,0:T(8,128)S(1)}, f32[256,256]{1,0:T(8,128)}, u32[]{:S(2)}) copy-start(f32[256,256]{1,0:T(8,128)} %fusion.57) | copy-start | bytes 786436
  37.6 3.9 %copy-start.10 = (f32[3,8,2,128]{3,1,2,0:T(8,128)S(1)}, f32[3,8,2,128]{3,1,2,0:T(8,128)}, u32[]{:S(2)}) copy-start(f32[3,8,2,128]{3,1,2,0:T(8,128)} %copy-done.9) | copy-start | bytes 73732
  37.6 3.9 %copy-start.15 = (pred[256,256]{1,0:T(8,128)(4,1)S(1)}, pred[256,256]{1,0:T(8,128)(4,1)}, u32[]{:S(2)}) copy-start(pred[256,256]{1,0:T(8,128)(4,1)} %iota_compare_fusion) | copy-start | bytes 196612
  37.6 3.9 %copy-start.16 = (f32[20,256]{1,0:T(8,128)S(1)}, f32[20,256]{1,0:T(8,128)}, u32[]{:S(2)}) copy-start(f32[20,256]{1,0:T(8,128)} %get-tuple-element.41) | copy-start | bytes 61444
  41.5 2.9 %copy-start.20 = (f32[20]{0:T(128)S(1)}, f32[20]{0:T(128)}, u32[]{:S(2)}) copy-start(f32[20]{0:T(128)} %get-tuple-element.54) | copy-start | bytes 244
  44.6 7.8 %collective-permute-start.2 = (bf16[20,64,128]{2,1,0:T(8,128)(2,1)S(1)}, bf16[20,64,128]{2,1,0:T(8,128)(2,1)S(1)}, u32[]{:S(2)}, u32[]{:S(2)}) collective-permute-start(bf16[20,64,128]{2,1,0:T(8,128)(2,1)S(1)} %fusion.27), channel_id=1, source_target_pairs={{0,8},{4,12},{1,9},{5,13},{2,10},{6,14},{3,11},{7,15},{16,24},{20,... | collective-permute-start | bytes 983048 | tf_op jit(solution)/shard_map/ppermute | solution.py:20
  48.4 4.4 %copy-start.18 = (f32[20]{0:T(128)S(1)}, f32[20]{0:T(128)}, u32[]{:S(2)}) copy-start(f32[20]{0:T(128)} %get-tuple-element.52) | copy-start | bytes 244
  51.9 1.3 %copy-start.4 = (f32[20,64,256]{2,1,0:T(8,128)S(1)}, f32[20,64,256]{2,1,0:T(8,128)}, u32[]{:S(2)}) copy-start(f32[20,64,256]{2,1,0:T(8,128)} %fusion) | copy-start | bytes 3932164
  51.9 1.3 %copy-start.12 = (f32[20,256]{1,0:T(8,128)S(1)}, f32[20,256]{1,0:T(8,128)}, u32[]{:S(2)}) copy-start(f32[20,256]{1,0:T(8,128)} %get-tuple-element.45) | copy-start | bytes 61444
  53.2 1.3 %copy-start.5 = (f32[20,64,256]{2,1,0:T(8,128)S(1)}, f32[20,64,256]{2,1,0:T(8,128)}, u32[]{:S(2)}) copy-start(f32[20,64,256]{2,1,0:T(8,128)} %fusion.1) | copy-start | bytes 3932164
  53.2 1.3 %copy-start.11 = (f32[20,256]{1,0:T(8,128)S(1)}, f32[20,256]{1,0:T(8,128)}, u32[]{:S(2)}) copy-start(f32[20,256]{1,0:T(8,128)} %get-tuple-element.44) | copy-start | bytes 61444
  54.5 1.3 %copy-start.1 = (bf16[512,1280]{0,1:T(8,128)(2,1)S(1)}, bf16[512,1280]{0,1:T(8,128)(2,1)}, u32[]{:S(2)}) copy-start(bf16[512,1280]{0,1:T(8,128)(2,1)} %copy.91) | copy-start | bytes 3932164
  54.5 1.7 %copy-start.2 = (bf16[512,1280]{0,1:T(8,128)(2,1)S(1)}, bf16[512,1280]{0,1:T(8,128)(2,1)}, u32[]{:S(2)}) copy-start(bf16[512,1280]{0,1:T(8,128)(2,1)} %copy.92) | copy-start | bytes 3932164
  56.2 4.2 %copy-start.23 = (s32[128]{0:T(128)S(1)}, s32[128]{0:T(128)}, u32[]{:S(2)}) copy-start(s32[128]{0:T(128)} %iota_add_fusion) | copy-start | bytes 1540
  56.2 6.3 %copy-start.17 = (f32[1280]{0:T(1024)S(1)}, f32[1280]{0:T(1024)}, u32[]{:S(2)}) copy-start(f32[1280]{0:T(1024)} %param.21) | copy-start | bytes 15364
  57.7 1.2 %collective-permute-start.4 = (f32[512]{0:T(512)S(1)}, f32[512]{0:T(512)S(1)}, u32[]{:S(2)}, u32[]{:S(2)}) collective-permute-start(f32[512]{0:T(512)S(1)} %get-tuple-element.28), channel_id=1, source_target_pairs={{0,1},{1,0},{2,3},{3,2},{4,5},{5,4},{6,7},{7,6},{8,9},{9,8},{10,11... | collective-permute-start | bytes 6152 | tf_op jit(solution)/shard_map/ppermute | solution.py:84
  58.9 3.6 %collective-permute-start.5 = (f32[512]{0:T(512)S(1)}, f32[512]{0:T(512)S(1)}, u32[]{:S(2)}, u32[]{:S(2)}) collective-permute-start(f32[512]{0:T(512)S(1)} %add.148), channel_id=1, source_target_pairs={{0,2},{1,3},{2,0},{3,1},{4,6},{5,7},{6,4},{7,5},{8,10},{9,11},{10,... | collective-permute-start | bytes 6152 | tf_op jit(solution)/shard_map/ppermute | solution.py:84
  63.9 2.8 %copy-start.6 = (bf16[160,8,160]{2,1,0:T(8,128)(2,1)S(1)}, bf16[160,8,160]{2,1,0:T(8,128)(2,1)}, u32[]{:S(2)}) copy-start(bf16[160,8,160]{2,1,0:T(8,128)(2,1)} %reshape.244) | copy-start | bytes 1228804
  63.9 2.8 %copy-start.21 = (pred[128]{0:T(512)(128)(4,1)S(1)}, pred[128]{0:T(512)(128)(4,1)}, u32[]{:S(2)}) copy-start(pred[128]{0:T(512)(128)(4,1)} %get-tuple-element.26) | copy-start | bytes 388
  65.6 1.7 %copy-start = (bf16[512,1280]{1,0:T(8,128)(2,1)}, bf16[512,1280]{1,0:T(8,128)(2,1)S(1)}, u32[]{:S(2)}) copy-start(bf16[512,1280]{1,0:T(8,128)(2,1)S(1)} %copy.104) | copy-start | bytes 3932164
  69.1 13.9 %collective-permute-start.9 = (bf16[40,1304]{1,0:T(8,128)(2,1)S(1)}, bf16[40,1304]{1,0:T(8,128)(2,1)S(1)}, u32[]{:S(2)}, u32[]{:S(2)}) collective-permute-start(bf16[40,1304]{1,0:T(8,128)(2,1)S(1)} %get-tuple-element.37), channel_id=1, source_target_pairs={{0,12},{4,0},{8,4},{12,8},{1,13},{5,1},{9,5},{13,9},{2,14},{6,2},{... | collective-permute-start | bytes 312968 | tf_op jit(solution)/shard_map/ppermute | solution.py:219
  79.5 9.5 %collective-permute-start.10 = (bf16[40,1304]{1,0:T(8,128)(2,1)S(1)}, bf16[40,1304]{1,0:T(8,128)(2,1)S(1)}, u32[]{:S(2)}, u32[]{:S(2)}) collective-permute-start(bf16[40,1304]{1,0:T(8,128)(2,1)S(1)} %get-tuple-element.36), channel_id=1, source_target_pairs={{0,8},{4,12},{8,0},{12,4},{1,9},{5,13},{9,1},{13,5},{2,10},{6,14},... | collective-permute-start | bytes 312968 | tf_op jit(solution)/shard_map/ppermute | solution.py:219
  79.5 9.5 %collective-permute-start.11 = (bf16[40,1304]{1,0:T(8,128)(2,1)S(1)}, bf16[40,1304]{1,0:T(8,128)(2,1)S(1)}, u32[]{:S(2)}, u32[]{:S(2)}) collective-permute-start(bf16[40,1304]{1,0:T(8,128)(2,1)S(1)} %get-tuple-element.35), channel_id=1, source_target_pairs={{0,4},{4,8},{8,12},{12,0},{1,5},{5,9},{9,13},{13,1},{2,6},{6,10},{... | collective-permute-start | bytes 312968 | tf_op jit(solution)/shard_map/ppermute | solution.py:219
  (4 other events, 3.7 us)

commit v12 on v10

--- a/solution.py
+++ b/solution.py
@@ -171,12 +171,15 @@
     gated = with_layout_constraint(gated, Layout(major_to_minor=(0, 1)))
     square_sum = butterfly_sum(jnp.sum(gated * gated, axis=0), "tensor")
     width_all = channels * lax.axis_size("tensor")
-    mixed_major = (
-        gated * lax.rsqrt(square_sum / width_all + EPSILON)[None, :] * norm_gain[:, None]
-    ).astype(jnp.bfloat16)
+    row_scale = lax.rsqrt(square_sum / width_all + EPSILON)
+    mixed_major = (gated * row_scale[None, :] * norm_gain[:, None]).astype(jnp.bfloat16)
     mixed_seq = mixed_major.T
     local_ends = seg_ends - lax.axis_index("seq") * tok_rows
-    summaries = jnp.take(mixed_seq, local_ends, axis=0)
+    summaries = (
+        jnp.take(gated, local_ends, axis=1)
+        * jnp.take(row_scale, local_ends)[None, :]
+        * norm_gain[:, None]
+    ).astype(jnp.bfloat16).T
     pool_heads_local = POOL_HEADS // lax.axis_size("tensor")
     pool_width = channels // pool_heads_local
     scale_factor = 1.0 / math.sqrt(pool_width)

time: 91.7 us -> 101 us (1.10)
  local copies, waits for them, and re-layouts: 19.4 us -> 28.8 us
  waiting for transfers between devices: 11.3 us -> 7.5 us
  matrix products: 10.9 us -> 13.1 us
    ppermute x3, waiting for transfers between devices: 7.51 us -> 3.71 us  [local(): lax.ppermute(chunk, 'seq', [(i, (i + shift) % seq_count) for i in range(s...]
    gather x2, local copies, waits for them, and re-layouts: 1.1 us -> 4.42 us  [the longest x1 3.03 us: local(): jnp.take(gated, local_ends, axis=1)]
    another operation x9 -> x10, local copies, waits for them, and re-layouts: 0.44 us -> 2.55 us  [the longest x1 2.11 us: local(): gated = with_layout_constraint(gated, Layout(major_to_minor=(0, 1)))]
    convert_element_type x0 -> x1, local copies, waits for them, and re-layouts: none -> 1.19 us  [local(): summaries = (jnp.take(gated, local_ends, axis=1) * jnp.take(row_scale, lo...]
    dot_general x1, matrix products: 0.57 us -> 1.76 us  [local(): jnp.einsum('pad,rad->apr', queries, keys_block, preferred_element_type=jn...]
    unnamed x61 -> x67, local copies, waits for them, and re-layouts: 3.97 us -> 5.02 us
    convert_element_type x0 -> x1, other arithmetic: none -> 1.04 us  [local(): summaries = (jnp.take(gated, local_ends, axis=1) * jnp.take(row_scale, lo...]
  transfers between devices with their start and end apart: 10 -> 10, of which waited for: 4 -> 3; matrix products, arithmetic and copies ran while one was open for 33% -> 39% of each run, Pallas kernels for 0% -> 0%
where the time goes in v12:
time: 101 us; the launch traced here: 99.7 us
  starting transfers between devices  32.7 us (32%)
  local copies, waits for them, and re-layouts  28.8 us (29%)
  other arithmetic  16.2 us (16%)
  matrix products  13.1 us (13%)
  waiting for transfers between devices  7.5 us (7%)
  between operations  1.41 us (1%)
    ppermute x4, starting transfers between devices, passed_along(): lax.ppermute(value, axis, [(source, source + steps) for source in range(l...  17.8 us
    ppermute x3, starting transfers between devices, local(): lax.ppermute(chunk, 'seq', [(i, (i + shift) % seq_count) for i in range(s...  9.24 us
    dot_general x2, matrix products, stretch_local(): jnp.einsum('hij,jhp->hpi', mixing, x_block, preferred_element_type=jnp.fl...  5.84 us
    unnamed x67, local copies, waits for them, and re-layouts  5.02 us
    all_to_all x1, starting transfers between devices, local(): lax.all_to_all(query_rows.reshape(seq_count * pools_local, -1), 'seq', 0,...  4.11 us
    ppermute x3, waiting for transfers between devices, local(): lax.ppermute(chunk, 'seq', [(i, (i + shift) % seq_count) for i in range(s...  3.71 us
    gather x1, local copies, waits for them, and re-layouts, local(): jnp.take(gated, local_ends, axis=1)  3.03 us
    ppermute x4, waiting for transfers between devices, passed_along(): lax.ppermute(value, axis, [(source, source + steps) for source in range(l...  2.9 us
  transfers between devices with their start and end apart: 10, of which 3 were waited for; matrix products, arithmetic and copies ran while one was open for 39% of the time, Pallas kernels for 0%

profile of v12, /device:TPU:0, one launch (start us, length us, event | category | flops | bytes accessed | tf_op | source)
XLA Modules:
  0.0 99.7 jit_solution(17109862422231800047)
XLA Ops:
  2.2 5.0 %collective-permute-start = (bf16[3,1536]{1,0:T(4,128)(2,1)S(1)}, bf16[3,1536]{1,0:T(4,128)(2,1)S(1)}, u32[]{:S(2)}, u32[]{:S(2)}) collective-permute-start(bf16[3,1536]{1,0:T(4,128)(2,1)S(1)} %pad_maximum_fusion.5), channel_id=1, source_target_pairs={{0,4},{4,8},{8,12},{1,5},{5,9},{9,13},{2,6},{6,10},{10,14},{3,7},{... | collective-permute-start | bytes 27656 | tf_op jit(solution)/shard_map/ppermute | solution.py:20
  10.7 3.5 %collective-permute-start.3 = (f32[20]{0:T(128)S(1)}, f32[20]{0:T(128)S(1)}, u32[]{:S(2)}, u32[]{:S(2)}) collective-permute-start(f32[20]{0:T(128)S(1)} %get-tuple-element.53), channel_id=1, source_target_pairs={{0,4},{4,8},{8,12},{1,5},{5,9},{9,13},{2,6},{6,10},{10,14},{3,7},{... | collective-permute-start | bytes 248 | tf_op jit(solution)/shard_map/ppermute | solution.py:20
  15.1 1.0 concatenate.32
  16.9 4.1 %all-to-all-start = ((bf16[4,40,1284]{2,1,0:T(8,128)(2,1)}), bf16[4,40,1284]{2,1,0:T(8,128)(2,1)}, u32[]{:S(2)}, u32[]{:S(2)}) async-start(bf16[4,40,1284]{2,1,0:T(8,128)(2,1)} %broadcast_in_dim.126), calls=%async_computation | async-start | bytes 901120 | tf_op jit(solution)/shard_map/all_to_all | solution.py:125
  25.1 1.8 %divide_convert_fusion = bf16[512,1280]{1,0:T(8,128)(2,1)S(1)} fusion(bf16[512,1280]{1,0:T(8,128)(2,1)S(1)} %copy-done.4, bf16[3,1280]{1,0:T(4,128)(2,1)S(1)} %slice.204, f32[1280]{0:T(1024)S(1)} %get-tuple-element.18, f32[1280]{0:T(1024)S(1)} %get-tuple-element.19, f32[1280]{0:T(1024)S(1)} %get-tuple-element.17, f32[1280]{0:T(1024)S(1)} %get-tuple-element.16), kind=kLoop, calls=%fused_computation.24 | loop fusion | flops 15728640 | bytes 2649600 | tf_op jit(solution)/shard_map/convert_element_type | solution.py:36
  27.9 1.0 %divide_convert_fusion.1 = bf16[512,256]{1,0:T(8,128)(2,1)S(1)} fusion(bf16[512,256]{1,0:T(8,128)(2,1)S(1)} %copy-done.8, bf16[3,256]{1,0:T(4,128)(2,1)S(1)} %slice-done, f32[256]{0:T(256)} %bitcast.129, f32[256]{0:T(256)} %bitcast.130, f32[256]{0:T(256)} %bitcast.128, f32[256]{0:T(256)} %bitcast.127), kind=kLoop, calls=%fused_computation.61 | loop fusion | flops 3145728 | bytes 529920 | tf_op jit(solution)/shard_map/convert_element_type | solution.py:36
  29.1 1.1 %convolution_add_fusion.3 = f32[20,64,128]{2,1,0:T(8,128)S(1)} fusion(bf16[256,20,64]{0,2,1:T(8,128)(2,1)S(1)} %bitcast.102, f32[256,20]{0,1:T(8,128)} %get-tuple-element.37, f32[20]{0:T(128)} %get-tuple-element.51, bf16[512,256]{1,0:T(8,128)(2,1)S(1)} %divide_convert_fusion.1), kind=kOutput, calls=%fused_computation.44 | convolution fusion | flops 85032960 | bytes 1396816 | tf_op jit(solution)/shard_map/jhp,js->hps/dot_general | solution.py:52
  30.2 1.1 %fusion.83 = (bf16[20,64,128]{2,1,0:T(8,128)(2,1)S(1)}, f32[20,64,128]{2,1,0:T(8,128)S(1)}) fusion(bf16[512,256]{1,0:T(8,128)(2,1)S(1)} %divide_convert_fusion.1, bf16[256,20,64]{0,2,1:T(8,128)(2,1)S(1)} %bitcast.105, f32[256,20]{0,1:T(8,128)} %get-tuple-element.38, f32[20,64,128]{2,1,0:T(8,128)S(1)} %convolution_add_fusion.3, f32[20]{0:T(128)} %get-tuple-element.54), kind=kOutput, calls=%fused_computation.166 | convolution fusion | flops 85360640 | bytes 2379856 | tf_op jit(solution)/shard_map/jhp,js->hps/dot_general | solution.py:52
  31.3 3.9 %collective-permute-start.1 = (bf16[20,64,128]{2,1,0:T(8,128)(2,1)S(1)}, bf16[20,64,128]{2,1,0:T(8,128)(2,1)S(1)}, u32[]{:S(2)}, u32[]{:S(2)}) collective-permute-start(bf16[20,64,128]{2,1,0:T(8,128)(2,1)S(1)} %get-tuple-element.55), channel_id=1, source_target_pairs={{0,4},{4,8},{8,12},{1,5},{5,9},{9,13},{2,6},{6,10},{10,14},{3,7},{... | collective-permute-start | bytes 983048 | tf_op jit(solution)/shard_map/ppermute | solution.py:20
  35.2 2.9 %fusion = f32[20,64,256]{2,1,0:T(8,128)} fusion(bf16[256,20,64]{0,2,1:T(8,128)(2,1)S(1)} %bitcast.103, f32[20,256]{1,0:T(8,128)S(1)} %copy-done.20, f32[256,256]{1,0:T(8,128)S(1)} %fusion.58, f32[20,256]{1,0:T(8,128)S(1)} %bitcast.120, pred[256,256]{1,0:T(8,128)(4,1)S(1)} %copy-done.15), kind=kOutput, calls=%fused_computation.4 | convolution fusion | flops 175636480 | bytes 2334720 | tf_op jit(solution)/shard_map/hij,jhp->hpi/dot_general | solution.py:49
  38.4 2.9 %collective-permute-done.1 = bf16[20,64,128]{2,1,0:T(8,128)(2,1)S(1)} collective-permute-done((bf16[20,64,128]{2,1,0:T(8,128)(2,1)S(1)}, bf16[20,64,128]{2,1,0:T(8,128)(2,1)S(1)}, u32[]{:S(2)}, u32[]{:S(2)}) %collective-permute-start.1) | collective-permute-done | bytes 327712 | tf_op jit(solution)/shard_map/ppermute | solution.py:20
  41.4 5.5 %collective-permute-start.2 = (bf16[20,64,128]{2,1,0:T(8,128)(2,1)S(1)}, bf16[20,64,128]{2,1,0:T(8,128)(2,1)S(1)}, u32[]{:S(2)}, u32[]{:S(2)}) collective-permute-start(bf16[20,64,128]{2,1,0:T(8,128)(2,1)S(1)} %fusion.26), channel_id=1, source_target_pairs={{0,8},{4,12},{1,9},{5,13},{2,10},{6,14},{3,11},{7,15},{16,24},{20,... | collective-permute-start | bytes 983048 | tf_op jit(solution)/shard_map/ppermute | solution.py:20
  46.9 2.9 %fusion.1 = f32[20,64,256]{2,1,0:T(8,128)} fusion(bf16[256,20,64]{0,2,1:T(8,128)(2,1)S(1)} %bitcast.106, f32[20,256]{1,0:T(8,128)S(1)} %copy-done.19, f32[256,256]{1,0:T(8,128)S(1)} %fusion.54, f32[20,256]{1,0:T(8,128)S(1)} %bitcast.123, pred[256,256]{1,0:T(8,128)(4,1)S(1)} %copy-done.15), kind=kOutput, calls=%fused_computation.5 | convolution fusion | flops 175636480 | bytes 2334720 | tf_op jit(solution)/shard_map/hij,jhp->hpi/dot_general | solution.py:49
  49.8 1.5 %copy.71 = bf16[512,1280]{0,1:T(8,128)(2,1)} copy(bf16[512,1280]{1,0:T(8,128)(2,1)S(1)} %divide_convert_fusion) | data formatting | bytes 2621440 | tf_op jit(solution)/shard_map/layout_constraint | solution.py:135
  51.3 2.4 %copy.72 = bf16[512,1280]{0,1:T(8,128)(2,1)} copy(bf16[512,1280]{1,0:T(8,128)(2,1)} %param.14) | data formatting | bytes 2621440 | tf_op jit(solution)/shard_map/optimization_barrier | solution.py:69
  58.5 1.5 %multiply_reduce_fusion = (f32[512]{0:T(512)S(1)}, f32[1280,512]{1,0:T(8,128)S(1)}) fusion(bf16[512,1280]{0,1:T(8,128)(2,1)S(1)} %copy-done.1, bf16[512,1280]{0,1:T(8,128)(2,1)S(1)} %copy-done, f32[1280]{0:T(1024)S(1)} %mul.368, f32[1280,256]{1,0:T(8,128)S(1)} %bitcast.101, f32[1280,256]{1,0:T(8,128)S(1)} %bitcast.100), kind=kLoop, calls=%fused_computation.13 | loop fusion | flops 7208448 | bytes 7871488 | tf_op jit(solution)/shard_map/reduce_sum | solution.py:172
  61.2 1.5 %collective-permute-start.5 = (f32[512]{0:T(512)S(1)}, f32[512]{0:T(512)S(1)}, u32[]{:S(2)}, u32[]{:S(2)}) collective-permute-start(f32[512]{0:T(512)S(1)} %add.184), channel_id=1, source_target_pairs={{0,2},{1,3},{2,0},{3,1},{4,6},{5,7},{6,4},{7,5},{8,10},{9,11},{10,... | collective-permute-start | bytes 6152 | tf_op jit(solution)/shard_map/ppermute | solution.py:84
  62.8 1.0 %slice.229 = bf16[160,1280]{1,0:T(8,128)(2,1)S(1)} slice(bf16[160,1284]{1,0:T(8,128)(2,1)} %bitcast.20), slice={[0:160], [0:1280]} | slice | bytes 819200 | tf_op jit(solution)/shard_map/slice | solution.py:128
  63.8 1.7 %reshape.246 = bf16[160,8,160]{2,1,0:T(8,128)(2,1)} reshape(bf16[160,1280]{1,0:T(8,128)(2,1)S(1)} %slice.229) | data formatting | bytes 819200 | tf_op jit(solution)/shard_map/reshape | solution.py:188
  65.5 2.1 %copy.73 = f32[1280,512]{0,1:T(8,128)} copy(f32[1280,512]{1,0:T(8,128)S(1)} %get-tuple-element.27) | data formatting | bytes 5242880 | tf_op jit(solution)/shard_map/layout_constraint | solution.py:171
  67.6 3.0 %gather_fusion = f32[128,1280]{1,0:T(8,128)S(1)} fusion(f32[1280,512]{0,1:T(8,128)} %copy.73, s32[1024]{0:T(1024)} %pad_clamp_fusion), kind=kCustom, calls=%fused_computation | custom fusion | bytes 1311232 | tf_op jit(solution)/shard_map/jit(_take)/gather | solution.py:179
  70.7 1.4 %gather_fusion.1 = f32[128]{0:T(128)S(1)} fusion(f32[512]{0:T(512)S(1)} %add_rsqrt_fusion, s32[1024]{0:T(1024)} %pad_clamp_fusion), kind=kCustom, calls=%fused_computation.1 | custom fusion | bytes 1536 | tf_op jit(solution)/shard_map/jit(_take)/gather | solution.py:180
  72.1 1.0 %multiply_convert_fusion.9 = bf16[128,1280]{1,0:T(8,128)(2,1)} fusion(f32[128,1280]{1,0:T(8,128)S(1)} %gather_fusion, f32[1280]{0:T(1024)S(1)} %copy-done.18, f32[128]{0:T(128)S(1)} %broadcast_select_fusion, pred[128]{0:T(512)(128)(4,1)S(1)} %copy-done.25), kind=kLoop, calls=%fused_computation.52 | loop fusion | flops 655360 | bytes 988800 | tf_op jit(solution)/shard_map/convert_element_type | solution.py:182
  73.2 1.2 %copy.74 = bf16[128,1280]{0,1:T(8,128)(2,1)S(1)} copy(bf16[128,1280]{1,0:T(8,128)(2,1)} %multiply_convert_fusion.9) | data formatting | bytes 655360 | tf_op jit(solution)/shard_map/convert_element_type | solution.py:182
  74.4 1.8 %fusion.84 = (bf16[8,160]{1,0:T(8,128)(2,1)S(1)}, f32[8,160,128]{2,1,0:T(8,128)S(1)}) fusion(bf16[128,8,160]{0,2,1:T(8,128)(2,1)S(1)} %bitcast.108, bf16[160,8,160]{2,1,0:T(8,128)(2,1)} %reshape.246, pred[160,128]{1,0:T(8,128)(4,1)S(1)} %compare_and_fusion), kind=kOutput, calls=%fused_computation.167 | convolution fusion | flops 52919040 | bytes 1415680 | tf_op jit(solution)/shard_map/pad,rad->apr/dot_general | solution.py:193
  76.7 1.4 %convolution_convert_fusion = bf16[8,160,160]{2,1,0:T(8,128)(2,1)S(1)} fusion(bf16[128,8,160]{0,2,1:T(8,128)(2,1)} %bitcast.109, f32[8,160,128]{2,1,0:T(8,128)S(1)} %get-tuple-element.58, f32[8,160]{1,0:T(8,128)S(1)} %convert_element_type.322, pred[160,128]{1,0:T(8,128)(4,1)S(1)} %compare_and_fusion), kind=kOutput, calls=%fused_computation.35 | convolution fusion | flops 53125120 | bytes 1418240 | tf_op jit(solution)/shard_map/apr,rad->pad/dot_general | solution.py:200
  79.5 1.1 %concatenate.33 = bf16[160,1304]{1,0:T(8,128)(2,1)S(1)} concatenate(bf16[160,1280]{1,0:T(8,128)(2,1)} %copy.78, bf16[160,8]{1,0:T(8,128)(2,1)S(1)} %copy.79, bf16[160,8]{1,0:T(8,128)(2,1)S(1)} %copy.80, bf16[160,8]{1,0:T(8,128)(2,1)S(1)} %copy.81), dimensions={1} | concatenate | bytes 834560 | tf_op jit(solution)/shard_map/concatenate | solution.py:205
  80.7 5.8 %collective-permute-start.6 = (bf16[40,1304]{1,0:T(8,128)(2,1)S(1)}, bf16[40,1304]{1,0:T(8,128)(2,1)S(1)}, u32[]{:S(2)}, u32[]{:S(2)}) collective-permute-start(bf16[40,1304]{1,0:T(8,128)(2,1)S(1)} %get-tuple-element.35), channel_id=1, source_target_pairs={{0,4},{4,8},{8,12},{12,0},{1,5},{5,9},{9,13},{13,1},{2,6},{6,10},{... | collective-permute-start | bytes 312968 | tf_op jit(solution)/shard_map/ppermute | solution.py:220
  86.6 3.4 %collective-permute-start.7 = (bf16[40,1304]{1,0:T(8,128)(2,1)S(1)}, bf16[40,1304]{1,0:T(8,128)(2,1)S(1)}, u32[]{:S(2)}, u32[]{:S(2)}) collective-permute-start(bf16[40,1304]{1,0:T(8,128)(2,1)S(1)} %get-tuple-element.34), channel_id=1, source_target_pairs={{0,8},{4,12},{8,0},{12,4},{1,9},{5,13},{9,1},{13,5},{2,10},{6,14},... | collective-permute-start | bytes 312968 | tf_op jit(solution)/shard_map/ppermute | solution.py:220
  89.9 1.4 %fusion.23 = bf16[512,1280]{0,1:T(8,128)(2,1)} fusion(f32[1280,512]{1,0:T(8,128)S(1)} %get-tuple-element.27, f32[1280]{0:T(1024)S(1)} %copy-done.18, f32[512]{0:T(512)S(1)} %add_rsqrt_fusion), kind=kLoop, calls=%fused_computation.38 | loop fusion | flops 1966080 | bytes 3939328 | tf_op jit(solution)/shard_map/transpose | solution.py:176
  91.3 2.4 %copy.86 = bf16[512,1280]{1,0:T(8,128)(2,1)} copy(bf16[512,1280]{0,1:T(8,128)(2,1)} %fusion.23) | data formatting | bytes 2621440
  93.7 3.7 %collective-permute-done.7 = bf16[40,1304]{1,0:T(8,128)(2,1)S(1)} collective-permute-done((bf16[40,1304]{1,0:T(8,128)(2,1)S(1)}, bf16[40,1304]{1,0:T(8,128)(2,1)S(1)}, u32[]{:S(2)}, u32[]{:S(2)}) %collective-permute-start.7) | collective-permute-done | bytes 104352 | tf_op jit(solution)/shard_map/ppermute | solution.py:220
  (151 shorter events, 22.3 us)
Async XLA Ops:
  0.6 24.4 %copy-start.4 = (bf16[512,1280]{1,0:T(8,128)(2,1)S(1)}, bf16[512,1280]{1,0:T(8,128)(2,1)}, u32[]{:S(2)}) copy-start(bf16[512,1280]{1,0:T(8,128)(2,1)} %param.13) | copy-start | bytes 3932164
  0.6 21.0 %copy-start.16 = (f32[20,512]{1,0:T(8,128)S(1)}, f32[20,512]{1,0:T(8,128)}, u32[]{:S(2)}) copy-start(f32[20,512]{1,0:T(8,128)} %param.16) | copy-start | bytes 122884
  0.7 21.8 %copy-start.22 = (bf16[4,256]{1,0:T(4,128)(2,1)S(1)}, bf16[4,256]{1,0:T(4,128)(2,1)}, u32[]{:S(2)}) copy-start(bf16[4,256]{1,0:T(4,128)(2,1)} %param.20) | copy-start | bytes 6148
  0.7 22.3 %copy-start.17 = (bf16[4,1280]{1,0:T(4,128)(2,1)S(1)}, bf16[4,1280]{1,0:T(4,128)(2,1)}, u32[]{:S(2)}) copy-start(bf16[4,1280]{1,0:T(4,128)(2,1)} %param.19) | copy-start | bytes 30724
  0.7 22.4 %copy-start.30 = (s32[128]{0:T(128)S(1)}, s32[128]{0:T(128)}, u32[]{:S(2)}) copy-start(s32[128]{0:T(128)} %param.22) | copy-start | bytes 1540
  0.7 24.2 %copy-start.28 = (f32[20]{0:T(128)S(1)}, f32[20]{0:T(128)}, u32[]{:S(2)}) copy-start(f32[20]{0:T(128)} %param.18) | copy-start | bytes 244
  2.2 22.8 %collective-permute-start = (bf16[3,1536]{1,0:T(4,128)(2,1)S(1)}, bf16[3,1536]{1,0:T(4,128)(2,1)S(1)}, u32[]{:S(2)}, u32[]{:S(2)}) collective-permute-start(bf16[3,1536]{1,0:T(4,128)(2,1)S(1)} %pad_maximum_fusion.5), channel_id=1, source_target_pairs={{0,4},{4,8},{8,12},{1,5},{5,9},{9,13},{2,6},{6,10},{10,14},{3,7},{... | collective-permute-start | bytes 27656 | tf_op jit(solution)/shard_map/ppermute | solution.py:20
  8.9 16.1 %copy-start.9 = (f32[3,8,2,128]{3,1,2,0:T(8,128)}, f32[3,8,2,128]{3,1,2,0:T(8,128)S(1)}, u32[]{:S(2)}) copy-start(f32[3,8,2,128]{3,1,2,0:T(8,128)S(1)} %copy.88) | copy-start | bytes 73732
  9.9 15.2 %copy-start.11 = (f32[3,8,2,128]{3,1,2,0:T(8,128)}, f32[3,8,2,128]{3,1,2,0:T(8,128)S(1)}, u32[]{:S(2)}) copy-start(f32[3,8,2,128]{3,1,2,0:T(8,128)S(1)} %copy.89) | copy-start | bytes 73732
  10.7 14.3 %collective-permute-start.3 = (f32[20]{0:T(128)S(1)}, f32[20]{0:T(128)S(1)}, u32[]{:S(2)}, u32[]{:S(2)}) collective-permute-start(f32[20]{0:T(128)S(1)} %get-tuple-element.53), channel_id=1, source_target_pairs={{0,4},{4,8},{8,12},{1,5},{5,9},{9,13},{2,6},{6,10},{10,14},{3,7},{... | collective-permute-start | bytes 248 | tf_op jit(solution)/shard_map/ppermute | solution.py:20
  16.9 36.9 %all-to-all-start = ((bf16[4,40,1284]{2,1,0:T(8,128)(2,1)}), bf16[4,40,1284]{2,1,0:T(8,128)(2,1)}, u32[]{:S(2)}, u32[]{:S(2)}) async-start(bf16[4,40,1284]{2,1,0:T(8,128)(2,1)} %broadcast_in_dim.126), calls=%async_computation | async-start | bytes 901120 | tf_op jit(solution)/shard_map/all_to_all | solution.py:125
  25.0 2.0 %copy-start.21 = (bf16[3,1536]{1,0:T(4,128)(2,1)}, bf16[3,1536]{1,0:T(4,128)(2,1)S(1)}, u32[]{:S(2)}) copy-start(bf16[3,1536]{1,0:T(4,128)(2,1)S(1)} %collective-permute-done) | copy-start | bytes 27652
  27.5 3.7 %copy-start.2 = (bf16[256,1280]{0,1:T(8,128)(2,1)}, bf16[256,1280]{0,1:T(8,128)(2,1)S(1)}, u32[]{:S(2)}) copy-start(bf16[256,1280]{0,1:T(8,128)(2,1)S(1)} %copy.70) | copy-start | bytes 1966084
  27.5 7.6 %copy-start.10 = (f32[3,8,2,128]{3,1,2,0:T(8,128)S(1)}, f32[3,8,2,128]{3,1,2,0:T(8,128)}, u32[]{:S(2)}) copy-start(f32[3,8,2,128]{3,1,2,0:T(8,128)} %copy-done.9) | copy-start | bytes 73732
  27.5 7.6 %copy-start.15 = (pred[256,256]{1,0:T(8,128)(4,1)S(1)}, pred[256,256]{1,0:T(8,128)(4,1)}, u32[]{:S(2)}) copy-start(pred[256,256]{1,0:T(8,128)(4,1)} %iota_compare_fusion) | copy-start | bytes 196612
  27.5 7.6 %copy-start.20 = (f32[20,256]{1,0:T(8,128)S(1)}, f32[20,256]{1,0:T(8,128)}, u32[]{:S(2)}) copy-start(f32[20,256]{1,0:T(8,128)} %get-tuple-element.36) | copy-start | bytes 61444
  31.3 10.0 %collective-permute-start.1 = (bf16[20,64,128]{2,1,0:T(8,128)(2,1)S(1)}, bf16[20,64,128]{2,1,0:T(8,128)(2,1)S(1)}, u32[]{:S(2)}, u32[]{:S(2)}) collective-permute-start(bf16[20,64,128]{2,1,0:T(8,128)(2,1)S(1)} %get-tuple-element.55), channel_id=1, source_target_pairs={{0,4},{4,8},{8,12},{1,5},{5,9},{9,13},{2,6},{6,10},{10,14},{3,7},{... | collective-permute-start | bytes 983048 | tf_op jit(solution)/shard_map/ppermute | solution.py:20
  35.2 6.1 %copy-start.24 = (f32[20]{0:T(128)S(1)}, f32[20]{0:T(128)}, u32[]{:S(2)}) copy-start(f32[20]{0:T(128)} %get-tuple-element.52) | copy-start | bytes 244
  35.2 11.7 %copy-start.3 = (bf16[256,1280]{0,1:T(8,128)(2,1)S(1)}, bf16[256,1280]{0,1:T(8,128)(2,1)}, u32[]{:S(2)}) copy-start(bf16[256,1280]{0,1:T(8,128)(2,1)} %copy-done.2) | copy-start | bytes 1966084
  35.2 11.7 %copy-start.12 = (f32[3,8,2,128]{3,1,2,0:T(8,128)S(1)}, f32[3,8,2,128]{3,1,2,0:T(8,128)}, u32[]{:S(2)}) copy-start(f32[3,8,2,128]{3,1,2,0:T(8,128)} %copy-done.11) | copy-start | bytes 73732
  35.2 11.7 %copy-start.19 = (f32[20,256]{1,0:T(8,128)S(1)}, f32[20,256]{1,0:T(8,128)}, u32[]{:S(2)}) copy-start(f32[20,256]{1,0:T(8,128)} %get-tuple-element.39) | copy-start | bytes 61444
  41.4 13.2 %collective-permute-start.2 = (bf16[20,64,128]{2,1,0:T(8,128)(2,1)S(1)}, bf16[20,64,128]{2,1,0:T(8,128)(2,1)S(1)}, u32[]{:S(2)}, u32[]{:S(2)}) collective-permute-start(bf16[20,64,128]{2,1,0:T(8,128)(2,1)S(1)} %fusion.26), channel_id=1, source_target_pairs={{0,8},{4,12},{1,9},{5,13},{2,10},{6,14},{3,11},{7,15},{16,24},{20,... | collective-permute-start | bytes 983048 | tf_op jit(solution)/shard_map/ppermute | solution.py:20
  51.3 3.7 %copy-start.23 = (f32[20]{0:T(128)S(1)}, f32[20]{0:T(128)}, u32[]{:S(2)}) copy-start(f32[20]{0:T(128)} %get-tuple-element.50) | copy-start | bytes 244
  58.5 4.2 %copy-start.29 = (s32[128]{0:T(128)S(1)}, s32[128]{0:T(128)}, u32[]{:S(2)}) copy-start(s32[128]{0:T(128)} %iota_add_fusion) | copy-start | bytes 1540
  60.0 1.2 %collective-permute-start.4 = (f32[512]{0:T(512)S(1)}, f32[512]{0:T(512)S(1)}, u32[]{:S(2)}, u32[]{:S(2)}) collective-permute-start(f32[512]{0:T(512)S(1)} %get-tuple-element.26), channel_id=1, source_target_pairs={{0,1},{1,0},{2,3},{3,2},{4,5},{5,4},{6,7},{7,6},{8,9},{9,8},{10,11... | collective-permute-start | bytes 6152 | tf_op jit(solution)/shard_map/ppermute | solution.py:84
  61.2 9.5 %collective-permute-start.5 = (f32[512]{0:T(512)S(1)}, f32[512]{0:T(512)S(1)}, u32[]{:S(2)}, u32[]{:S(2)}) collective-permute-start(f32[512]{0:T(512)S(1)} %add.184), channel_id=1, source_target_pairs={{0,2},{1,3},{2,0},{3,1},{4,6},{5,7},{6,4},{7,5},{8,10},{9,11},{10,... | collective-permute-start | bytes 6152 | tf_op jit(solution)/shard_map/ppermute | solution.py:84
  67.6 4.5 %copy-start.27 = (s32[128]{0:T(128)S(1)}, s32[128]{0:T(128)}, u32[]{:S(2)}) copy-start(s32[128]{0:T(128)} %copy-done.26) | copy-start | bytes 1540
  67.6 4.5 %copy-start.18 = (f32[1280]{0:T(1024)S(1)}, f32[1280]{0:T(1024)}, u32[]{:S(2)}) copy-start(f32[1280]{0:T(1024)} %param.21) | copy-start | bytes 15364
  67.6 4.5 %copy-start.25 = (pred[128]{0:T(512)(128)(4,1)S(1)}, pred[128]{0:T(512)(128)(4,1)}, u32[]{:S(2)}) copy-start(pred[128]{0:T(512)(128)(4,1)} %get-tuple-element.24) | copy-start | bytes 388
  80.7 13.0 %collective-permute-start.6 = (bf16[40,1304]{1,0:T(8,128)(2,1)S(1)}, bf16[40,1304]{1,0:T(8,128)(2,1)S(1)}, u32[]{:S(2)}, u32[]{:S(2)}) collective-permute-start(bf16[40,1304]{1,0:T(8,128)(2,1)S(1)} %get-tuple-element.35), channel_id=1, source_target_pairs={{0,4},{4,8},{8,12},{12,0},{1,5},{5,9},{9,13},{13,1},{2,6},{6,10},{... | collective-permute-start | bytes 312968 | tf_op jit(solution)/shard_map/ppermute | solution.py:220
  86.6 10.9 %collective-permute-start.7 = (bf16[40,1304]{1,0:T(8,128)(2,1)S(1)}, bf16[40,1304]{1,0:T(8,128)(2,1)S(1)}, u32[]{:S(2)}, u32[]{:S(2)}) collective-permute-start(bf16[40,1304]{1,0:T(8,128)(2,1)S(1)} %get-tuple-element.34), channel_id=1, source_target_pairs={{0,8},{4,12},{8,0},{12,4},{1,9},{5,13},{9,1},{13,5},{2,10},{6,14},... | collective-permute-start | bytes 312968 | tf_op jit(solution)/shard_map/ppermute | solution.py:220
  89.9 7.5 %collective-permute-start.8 = (bf16[40,1304]{1,0:T(8,128)(2,1)S(1)}, bf16[40,1304]{1,0:T(8,128)(2,1)S(1)}, u32[]{:S(2)}, u32[]{:S(2)}) collective-permute-start(bf16[40,1304]{1,0:T(8,128)(2,1)S(1)} %get-tuple-element.33), channel_id=1, source_target_pairs={{0,12},{4,0},{8,4},{12,8},{1,13},{5,1},{9,5},{13,9},{2,14},{6,2},{... | collective-permute-start | bytes 312968 | tf_op jit(solution)/shard_map/ppermute | solution.py:220
  (10 other events, 14.1 us)

commit v13 on v10

--- a/solution.py
+++ b/solution.py
@@ -176,7 +176,12 @@
     ).astype(jnp.bfloat16)
     mixed_seq = mixed_major.T
     local_ends = seg_ends - lax.axis_index("seq") * tok_rows
-    summaries = jnp.take(mixed_seq, local_ends, axis=0)
+    picks = (
+        lax.broadcasted_iota(jnp.int32, (tok_rows, local_ends.shape[0]), 0) == local_ends[None, :]
+    ).astype(jnp.bfloat16)
+    summaries = (
+        jnp.einsum("ct,ts->sc", mixed_major, picks, preferred_element_type=jnp.float32)
+    ).astype(jnp.bfloat16)
     pool_heads_local = POOL_HEADS // lax.axis_size("tensor")
     pool_width = channels // pool_heads_local
     scale_factor = 1.0 / math.sqrt(pool_width)

time: 91.7 us -> 92 us (level)
  waiting for transfers between devices: 11.3 us -> 7.5 us
  matrix products: 10.9 us -> 13.8 us
  local copies, waits for them, and re-layouts: 19.4 us -> 21.3 us
    ppermute x3, waiting for transfers between devices: 7.51 us -> 3.72 us  [local(): lax.ppermute(chunk, 'seq', [(i, (i + shift) % seq_count) for i in range(s...]
    dot_general x1, matrix products: 0.57 us -> 1.76 us  [local(): jnp.einsum('pad,rad->apr', queries, keys_block, preferred_element_type=jn...]
    gather x2 -> x0, local copies, waits for them, and re-layouts: 1.1 us -> none  [local(): summaries = jnp.take(mixed_seq, local_ends, axis=0)]
    unnamed x61 -> x63, local copies, waits for them, and re-layouts: 3.97 us -> 5.02 us
    concatenate x1, local copies, waits for them, and re-layouts: 0.13 us -> 1.13 us  [local(): jnp.concatenate([numer.reshape(pools_all, channels).astype(jnp.bfloat16),...]
    dot_general x1, matrix products: 0.44 us -> 1.41 us  [local(): jnp.einsum('apr,rad->pad', expo.astype(jnp.bfloat16), keys_block, preferr...]
  transfers between devices with their start and end apart: 10 -> 10, of which waited for: 4 -> 3; matrix products, arithmetic and copies ran while one was open for 33% -> 36% of each run, Pallas kernels for 0% -> 0%
where the time goes in v13:
time: 92 us; the launch traced here: 91.1 us
  starting transfers between devices  32.7 us (36%)
  local copies, waits for them, and re-layouts  21.3 us (23%)
  other arithmetic  14.4 us (16%)
  matrix products  13.8 us (15%)
  waiting for transfers between devices  7.5 us (8%)
  between operations  1.36 us (1%)
    ppermute x4, starting transfers between devices, passed_along(): lax.ppermute(value, axis, [(source, source + steps) for source in range(l...  17.8 us
    ppermute x3, starting transfers between devices, local(): lax.ppermute(chunk, 'seq', [(i, (i + shift) % seq_count) for i in range(s...  9.23 us
    dot_general x2, matrix products, stretch_local(): jnp.einsum('hij,jhp->hpi', mixing, x_block, preferred_element_type=jnp.fl...  5.85 us
    unnamed x63, local copies, waits for them, and re-layouts  5.02 us
    all_to_all x1, starting transfers between devices, local(): lax.all_to_all(query_rows.reshape(seq_count * pools_local, -1), 'seq', 0,...  4.12 us
    ppermute x3, waiting for transfers between devices, local(): lax.ppermute(chunk, 'seq', [(i, (i + shift) % seq_count) for i in range(s...  3.72 us
    ppermute x4, waiting for transfers between devices, passed_along(): lax.ppermute(value, axis, [(source, source + steps) for source in range(l...  2.89 us
    convert_element_type x2, other arithmetic, causal_conv(): return silu_act(summed).astype(jnp.bfloat16)  2.85 us
  transfers between devices with their start and end apart: 10, of which 3 were waited for; matrix products, arithmetic and copies ran while one was open for 36% of the time, Pallas kernels for 0%

profile of v13, /device:TPU:0, one launch (start us, length us, event | category | flops | bytes accessed | tf_op | source)
XLA Modules:
  0.0 91.1 jit_solution(1462708356814112471)
XLA Ops:
  2.2 5.0 %collective-permute-start = (bf16[3,1536]{1,0:T(4,128)(2,1)S(1)}, bf16[3,1536]{1,0:T(4,128)(2,1)S(1)}, u32[]{:S(2)}, u32[]{:S(2)}) collective-permute-start(bf16[3,1536]{1,0:T(4,128)(2,1)S(1)} %pad_maximum_fusion.5), channel_id=1, source_target_pairs={{0,4},{4,8},{8,12},{1,5},{5,9},{9,13},{2,6},{6,10},{10,14},{3,7},{... | collective-permute-start | bytes 27656 | tf_op jit(solution)/shard_map/ppermute | solution.py:20
  10.6 3.5 %collective-permute-start.3 = (f32[20]{0:T(128)S(1)}, f32[20]{0:T(128)S(1)}, u32[]{:S(2)}, u32[]{:S(2)}) collective-permute-start(f32[20]{0:T(128)S(1)} %get-tuple-element.51), channel_id=1, source_target_pairs={{0,4},{4,8},{8,12},{1,5},{5,9},{9,13},{2,6},{6,10},{10,14},{3,7},{... | collective-permute-start | bytes 248 | tf_op jit(solution)/shard_map/ppermute | solution.py:20
  15.0 1.0 %concatenate.32 = bf16[40,1284]{1,0:T(8,128)(2,1)S(1)} concatenate(bf16[40,1280]{1,0:T(8,128)(2,1)} %param.23, bf16[40,2]{1,0:T(8,128)(2,1)S(1)} %copy.71, bf16[40,2]{1,0:T(8,128)(2,1)S(1)} %copy.72), dimensions={1} | concatenate | bytes 205440 | tf_op jit(solution)/shard_map/concatenate | solution.py:123
  16.8 4.1 %all-to-all-start = ((bf16[4,40,1284]{2,1,0:T(8,128)(2,1)}), bf16[4,40,1284]{2,1,0:T(8,128)(2,1)}, u32[]{:S(2)}, u32[]{:S(2)}) async-start(bf16[4,40,1284]{2,1,0:T(8,128)(2,1)} %broadcast_in_dim.51), calls=%async_computation | async-start | bytes 901120 | tf_op jit(solution)/shard_map/all_to_all | solution.py:125
  24.4 1.8 %divide_convert_fusion = bf16[512,1280]{1,0:T(8,128)(2,1)S(1)} fusion(bf16[512,1280]{1,0:T(8,128)(2,1)S(1)} %copy-done.4, bf16[3,1280]{1,0:T(4,128)(2,1)S(1)} %slice.200, f32[1280]{0:T(1024)S(1)} %get-tuple-element.18, f32[1280]{0:T(1024)S(1)} %get-tuple-element.19, f32[1280]{0:T(1024)S(1)} %get-tuple-element.17, f32[1280]{0:T(1024)S(1)} %get-tuple-element.16), kind=kLoop, calls=%fused_computation.22 | loop fusion | flops 15728640 | bytes 2649600 | tf_op jit(solution)/shard_map/convert_element_type | solution.py:36
  27.2 1.0 %divide_convert_fusion.1 = bf16[512,256]{1,0:T(8,128)(2,1)S(1)} fusion(bf16[512,256]{1,0:T(8,128)(2,1)S(1)} %copy-done.8, bf16[3,256]{1,0:T(4,128)(2,1)S(1)} %slice-done, f32[256]{0:T(256)} %bitcast.129, f32[256]{0:T(256)} %bitcast.130, f32[256]{0:T(256)} %bitcast.128, f32[256]{0:T(256)} %bitcast.127), kind=kLoop, calls=%fused_computation.58 | loop fusion | flops 3145728 | bytes 529920 | tf_op jit(solution)/shard_map/convert_element_type | solution.py:36
  28.4 1.1 %convolution_add_fusion.3 = f32[20,64,128]{2,1,0:T(8,128)S(1)} fusion(bf16[256,20,64]{0,2,1:T(8,128)(2,1)S(1)} %bitcast.102, f32[256,20]{0,1:T(8,128)} %get-tuple-element.35, f32[20]{0:T(128)} %get-tuple-element.49, bf16[512,256]{1,0:T(8,128)(2,1)S(1)} %divide_convert_fusion.1), kind=kOutput, calls=%fused_computation.42 | convolution fusion | flops 85032960 | bytes 1396816 | tf_op jit(solution)/shard_map/jhp,js->hps/dot_general | solution.py:52
  29.5 1.1 %fusion.86 = (bf16[20,64,128]{2,1,0:T(8,128)(2,1)S(1)}, f32[20,64,128]{2,1,0:T(8,128)S(1)}) fusion(bf16[512,256]{1,0:T(8,128)(2,1)S(1)} %divide_convert_fusion.1, bf16[256,20,64]{0,2,1:T(8,128)(2,1)S(1)} %bitcast.105, f32[256,20]{0,1:T(8,128)} %get-tuple-element.36, f32[20,64,128]{2,1,0:T(8,128)S(1)} %convolution_add_fusion.3, f32[20]{0:T(128)} %get-tuple-element.52), kind=kOutput, calls=%fused_computation.164 | convolution fusion | flops 85360640 | bytes 2379856 | tf_op jit(solution)/shard_map/jhp,js->hps/dot_general | solution.py:52
  30.6 3.9 %collective-permute-start.1 = (bf16[20,64,128]{2,1,0:T(8,128)(2,1)S(1)}, bf16[20,64,128]{2,1,0:T(8,128)(2,1)S(1)}, u32[]{:S(2)}, u32[]{:S(2)}) collective-permute-start(bf16[20,64,128]{2,1,0:T(8,128)(2,1)S(1)} %get-tuple-element.53), channel_id=1, source_target_pairs={{0,4},{4,8},{8,12},{1,5},{5,9},{9,13},{2,6},{6,10},{10,14},{3,7},{... | collective-permute-start | bytes 983048 | tf_op jit(solution)/shard_map/ppermute | solution.py:20
  34.5 2.9 %fusion = f32[20,64,256]{2,1,0:T(8,128)} fusion(bf16[256,20,64]{0,2,1:T(8,128)(2,1)S(1)} %bitcast.103, f32[20,256]{1,0:T(8,128)S(1)} %copy-done.20, f32[256,256]{1,0:T(8,128)S(1)} %fusion.60, f32[20,256]{1,0:T(8,128)S(1)} %bitcast.120, pred[256,256]{1,0:T(8,128)(4,1)S(1)} %copy-done.15), kind=kOutput, calls=%fused_computation.2 | convolution fusion | flops 175636480 | bytes 2334720 | tf_op jit(solution)/shard_map/hij,jhp->hpi/dot_general | solution.py:49
  37.7 2.9 %collective-permute-done.1 = bf16[20,64,128]{2,1,0:T(8,128)(2,1)S(1)} collective-permute-done((bf16[20,64,128]{2,1,0:T(8,128)(2,1)S(1)}, bf16[20,64,128]{2,1,0:T(8,128)(2,1)S(1)}, u32[]{:S(2)}, u32[]{:S(2)}) %collective-permute-start.1) | collective-permute-done | bytes 327712 | tf_op jit(solution)/shard_map/ppermute | solution.py:20
  40.7 5.5 %collective-permute-start.2 = (bf16[20,64,128]{2,1,0:T(8,128)(2,1)S(1)}, bf16[20,64,128]{2,1,0:T(8,128)(2,1)S(1)}, u32[]{:S(2)}, u32[]{:S(2)}) collective-permute-start(bf16[20,64,128]{2,1,0:T(8,128)(2,1)S(1)} %fusion.25), channel_id=1, source_target_pairs={{0,8},{4,12},{1,9},{5,13},{2,10},{6,14},{3,11},{7,15},{16,24},{20,... | collective-permute-start | bytes 983048 | tf_op jit(solution)/shard_map/ppermute | solution.py:20
  46.2 2.9 %fusion.1 = f32[20,64,256]{2,1,0:T(8,128)} fusion(bf16[256,20,64]{0,2,1:T(8,128)(2,1)S(1)} %bitcast.106, f32[20,256]{1,0:T(8,128)S(1)} %copy-done.19, f32[256,256]{1,0:T(8,128)S(1)} %fusion.56, f32[20,256]{1,0:T(8,128)S(1)} %bitcast.123, pred[256,256]{1,0:T(8,128)(4,1)S(1)} %copy-done.15), kind=kOutput, calls=%fused_computation.3 | convolution fusion | flops 175636480 | bytes 2334720 | tf_op jit(solution)/shard_map/hij,jhp->hpi/dot_general | solution.py:49
  49.1 1.5 %copy.68 = bf16[512,1280]{0,1:T(8,128)(2,1)} copy(bf16[512,1280]{1,0:T(8,128)(2,1)S(1)} %divide_convert_fusion) | data formatting | bytes 2621440 | tf_op jit(solution)/shard_map/layout_constraint | solution.py:135
  50.6 2.4 %copy.69 = bf16[512,1280]{0,1:T(8,128)(2,1)} copy(bf16[512,1280]{1,0:T(8,128)(2,1)} %param.14) | data formatting | bytes 2621440 | tf_op jit(solution)/shard_map/optimization_barrier | solution.py:69
  53.1 0.9 slice_convert_fusion
  55.2 0.9 copy-done.7
  56.5 0.9 copy-done
  57.8 1.5 %multiply_reduce_fusion = (f32[512]{0:T(512)S(1)}, f32[1280,512]{1,0:T(8,128)S(1)}) fusion(bf16[512,1280]{0,1:T(8,128)(2,1)S(1)} %copy-done.1, bf16[512,1280]{0,1:T(8,128)(2,1)S(1)} %copy-done, f32[1280]{0:T(1024)S(1)} %mul.348, f32[1280,256]{1,0:T(8,128)S(1)} %bitcast.101, f32[1280,256]{1,0:T(8,128)S(1)} %bitcast.100), kind=kLoop, calls=%fused_computation.11 | loop fusion | flops 7208448 | bytes 7871488 | tf_op jit(solution)/shard_map/reduce_sum | solution.py:172
  59.6 0.9 collective-permute-done.4
  60.5 1.5 %collective-permute-start.5 = (f32[512]{0:T(512)S(1)}, f32[512]{0:T(512)S(1)}, u32[]{:S(2)}, u32[]{:S(2)}) collective-permute-start(f32[512]{0:T(512)S(1)} %add.172), channel_id=1, source_target_pairs={{0,2},{1,3},{2,0},{3,1},{4,6},{5,7},{6,4},{7,5},{8,10},{9,11},{10,... | collective-permute-start | bytes 6152 | tf_op jit(solution)/shard_map/ppermute | solution.py:84
  62.1 1.0 %slice.225 = bf16[160,1280]{1,0:T(8,128)(2,1)S(1)} slice(bf16[160,1284]{1,0:T(8,128)(2,1)} %bitcast.20), slice={[0:160], [0:1280]} | slice | bytes 819200 | tf_op jit(solution)/shard_map/slice | solution.py:128
  63.2 1.7 %reshape.237 = bf16[160,8,160]{2,1,0:T(8,128)(2,1)} reshape(bf16[160,1280]{1,0:T(8,128)(2,1)S(1)} %slice.225) | data formatting | bytes 819200 | tf_op jit(solution)/shard_map/reshape | solution.py:190
  65.8 1.8 %fusion.87 = (bf16[8,160]{1,0:T(8,128)(2,1)S(1)}, f32[8,160,128]{2,1,0:T(8,128)S(1)}) fusion(bf16[128,8,160]{0,2,1:T(8,128)(2,1)S(1)} %bitcast.108, bf16[160,8,160]{2,1,0:T(8,128)(2,1)} %reshape.237, pred[160,128]{1,0:T(8,128)(4,1)S(1)} %compare_and_fusion), kind=kOutput, calls=%fused_computation.165 | convolution fusion | flops 52919040 | bytes 1415680 | tf_op jit(solution)/shard_map/pad,rad->apr/dot_general | solution.py:195
  68.2 1.4 %convolution_convert_fusion.1 = bf16[8,160,160]{2,1,0:T(8,128)(2,1)S(1)} fusion(bf16[128,8,160]{0,2,1:T(8,128)(2,1)} %bitcast.109, f32[8,160,128]{2,1,0:T(8,128)S(1)} %get-tuple-element.56, f32[8,160]{1,0:T(8,128)S(1)} %convert_element_type.318, pred[160,128]{1,0:T(8,128)(4,1)S(1)} %compare_and_fusion), kind=kOutput, calls=%fused_computation.34 | convolution fusion | flops 53125120 | bytes 1418240 | tf_op jit(solution)/shard_map/apr,rad->pad/dot_general | solution.py:202
  69.9 1.0 %copy.74 = bf16[160,1280]{1,0:T(8,128)(2,1)} copy(bf16[160,1280]{0,1:T(8,128)(2,1)S(1)} %bitcast.104) | data formatting | bytes 819200 | tf_op jit(solution)/shard_map/convert_element_type | solution.py:209
  71.0 1.1 %concatenate.33 = bf16[160,1304]{1,0:T(8,128)(2,1)S(1)} concatenate(bf16[160,1280]{1,0:T(8,128)(2,1)} %copy.74, bf16[160,8]{1,0:T(8,128)(2,1)S(1)} %copy.75, bf16[160,8]{1,0:T(8,128)(2,1)S(1)} %copy.76, bf16[160,8]{1,0:T(8,128)(2,1)S(1)} %copy.77), dimensions={1} | concatenate | bytes 834560 | tf_op jit(solution)/shard_map/concatenate | solution.py:207
  72.2 5.8 %collective-permute-start.6 = (bf16[40,1304]{1,0:T(8,128)(2,1)S(1)}, bf16[40,1304]{1,0:T(8,128)(2,1)S(1)}, u32[]{:S(2)}, u32[]{:S(2)}) collective-permute-start(bf16[40,1304]{1,0:T(8,128)(2,1)S(1)} %get-tuple-element.33), channel_id=1, source_target_pairs={{0,4},{4,8},{8,12},{12,0},{1,5},{5,9},{9,13},{13,1},{2,6},{6,10},{... | collective-permute-start | bytes 312968 | tf_op jit(solution)/shard_map/ppermute | solution.py:222
  78.0 3.4 %collective-permute-start.7 = (bf16[40,1304]{1,0:T(8,128)(2,1)S(1)}, bf16[40,1304]{1,0:T(8,128)(2,1)S(1)}, u32[]{:S(2)}, u32[]{:S(2)}) collective-permute-start(bf16[40,1304]{1,0:T(8,128)(2,1)S(1)} %get-tuple-element.32), channel_id=1, source_target_pairs={{0,8},{4,12},{8,0},{12,4},{1,9},{5,13},{9,1},{13,5},{2,10},{6,14},... | collective-permute-start | bytes 312968 | tf_op jit(solution)/shard_map/ppermute | solution.py:222
  81.4 1.4 %fusion.78 = bf16[512,1280]{0,1:T(8,128)(2,1)} fusion(f32[1280]{0:T(1024)S(1)} %copy-done.18, f32[1280,512]{1,0:T(8,128)S(1)} %get-tuple-element.25, f32[512]{0:T(512)S(1)} %add_rsqrt_fusion), kind=kLoop, calls=%fused_computation.158 | loop fusion | flops 1966080 | bytes 3939328 | tf_op jit(solution)/shard_map/transpose | solution.py:177
  82.8 2.4 %copy.82 = bf16[512,1280]{1,0:T(8,128)(2,1)} copy(bf16[512,1280]{0,1:T(8,128)(2,1)} %fusion.78) | data formatting | bytes 2621440
  85.2 3.7 %collective-permute-done.7 = bf16[40,1304]{1,0:T(8,128)(2,1)S(1)} collective-permute-done((bf16[40,1304]{1,0:T(8,128)(2,1)S(1)}, bf16[40,1304]{1,0:T(8,128)(2,1)S(1)}, u32[]{:S(2)}, u32[]{:S(2)}) %collective-permute-start.7) | collective-permute-done | bytes 104352 | tf_op jit(solution)/shard_map/ppermute | solution.py:222
  (142 shorter events, 18.0 us)
Async XLA Ops:
  0.6 23.7 %copy-start.4 = (bf16[512,1280]{1,0:T(8,128)(2,1)S(1)}, bf16[512,1280]{1,0:T(8,128)(2,1)}, u32[]{:S(2)}) copy-start(bf16[512,1280]{1,0:T(8,128)(2,1)} %param.13) | copy-start | bytes 3932164
  0.6 21.0 %copy-start.16 = (f32[20,512]{1,0:T(8,128)S(1)}, f32[20,512]{1,0:T(8,128)}, u32[]{:S(2)}) copy-start(f32[20,512]{1,0:T(8,128)} %param.16) | copy-start | bytes 122884
  0.7 21.7 %copy-start.22 = (bf16[4,256]{1,0:T(4,128)(2,1)S(1)}, bf16[4,256]{1,0:T(4,128)(2,1)}, u32[]{:S(2)}) copy-start(bf16[4,256]{1,0:T(4,128)(2,1)} %param.20) | copy-start | bytes 6148
  0.7 22.3 %copy-start.17 = (bf16[4,1280]{1,0:T(4,128)(2,1)S(1)}, bf16[4,1280]{1,0:T(4,128)(2,1)}, u32[]{:S(2)}) copy-start(bf16[4,1280]{1,0:T(4,128)(2,1)} %param.19) | copy-start | bytes 30724
  0.7 22.3 %copy-start.28 = (s32[128]{0:T(128)S(1)}, s32[128]{0:T(128)}, u32[]{:S(2)}) copy-start(s32[128]{0:T(128)} %param.22) | copy-start | bytes 1540
  0.7 23.5 %copy-start.25 = (f32[20]{0:T(128)S(1)}, f32[20]{0:T(128)}, u32[]{:S(2)}) copy-start(f32[20]{0:T(128)} %param.18) | copy-start | bytes 244
  2.2 22.1 %collective-permute-start = (bf16[3,1536]{1,0:T(4,128)(2,1)S(1)}, bf16[3,1536]{1,0:T(4,128)(2,1)S(1)}, u32[]{:S(2)}, u32[]{:S(2)}) collective-permute-start(bf16[3,1536]{1,0:T(4,128)(2,1)S(1)} %pad_maximum_fusion.5), channel_id=1, source_target_pairs={{0,4},{4,8},{8,12},{1,5},{5,9},{9,13},{2,6},{6,10},{10,14},{3,7},{... | collective-permute-start | bytes 27656 | tf_op jit(solution)/shard_map/ppermute | solution.py:20
  8.9 15.4 %copy-start.9 = (f32[3,8,2,128]{3,1,2,0:T(8,128)}, f32[3,8,2,128]{3,1,2,0:T(8,128)S(1)}, u32[]{:S(2)}) copy-start(f32[3,8,2,128]{3,1,2,0:T(8,128)S(1)} %copy.84) | copy-start | bytes 73732
  9.9 14.5 %copy-start.11 = (f32[3,8,2,128]{3,1,2,0:T(8,128)}, f32[3,8,2,128]{3,1,2,0:T(8,128)S(1)}, u32[]{:S(2)}) copy-start(f32[3,8,2,128]{3,1,2,0:T(8,128)S(1)} %copy.85) | copy-start | bytes 73732
  10.6 13.7 %collective-permute-start.3 = (f32[20]{0:T(128)S(1)}, f32[20]{0:T(128)S(1)}, u32[]{:S(2)}, u32[]{:S(2)}) collective-permute-start(f32[20]{0:T(128)S(1)} %get-tuple-element.51), channel_id=1, source_target_pairs={{0,4},{4,8},{8,12},{1,5},{5,9},{9,13},{2,6},{6,10},{10,14},{3,7},{... | collective-permute-start | bytes 248 | tf_op jit(solution)/shard_map/ppermute | solution.py:20
  16.8 36.2 %all-to-all-start = ((bf16[4,40,1284]{2,1,0:T(8,128)(2,1)}), bf16[4,40,1284]{2,1,0:T(8,128)(2,1)}, u32[]{:S(2)}, u32[]{:S(2)}) async-start(bf16[4,40,1284]{2,1,0:T(8,128)(2,1)} %broadcast_in_dim.51), calls=%async_computation | async-start | bytes 901120 | tf_op jit(solution)/shard_map/all_to_all | solution.py:125
  24.3 2.0 %copy-start.21 = (bf16[3,1536]{1,0:T(4,128)(2,1)}, bf16[3,1536]{1,0:T(4,128)(2,1)S(1)}, u32[]{:S(2)}) copy-start(bf16[3,1536]{1,0:T(4,128)(2,1)S(1)} %collective-permute-done) | copy-start | bytes 27652
  26.8 3.7 %copy-start.2 = (bf16[256,1280]{0,1:T(8,128)(2,1)}, bf16[256,1280]{0,1:T(8,128)(2,1)S(1)}, u32[]{:S(2)}) copy-start(bf16[256,1280]{0,1:T(8,128)(2,1)S(1)} %copy.67) | copy-start | bytes 1966084
  26.8 7.6 %copy-start.10 = (f32[3,8,2,128]{3,1,2,0:T(8,128)S(1)}, f32[3,8,2,128]{3,1,2,0:T(8,128)}, u32[]{:S(2)}) copy-start(f32[3,8,2,128]{3,1,2,0:T(8,128)} %copy-done.9) | copy-start | bytes 73732
  26.8 7.6 %copy-start.15 = (pred[256,256]{1,0:T(8,128)(4,1)S(1)}, pred[256,256]{1,0:T(8,128)(4,1)}, u32[]{:S(2)}) copy-start(pred[256,256]{1,0:T(8,128)(4,1)} %iota_compare_fusion.1) | copy-start | bytes 196612
  26.9 7.6 %copy-start.20 = (f32[20,256]{1,0:T(8,128)S(1)}, f32[20,256]{1,0:T(8,128)}, u32[]{:S(2)}) copy-start(f32[20,256]{1,0:T(8,128)} %get-tuple-element.34) | copy-start | bytes 61444
  30.6 10.0 %collective-permute-start.1 = (bf16[20,64,128]{2,1,0:T(8,128)(2,1)S(1)}, bf16[20,64,128]{2,1,0:T(8,128)(2,1)S(1)}, u32[]{:S(2)}, u32[]{:S(2)}) collective-permute-start(bf16[20,64,128]{2,1,0:T(8,128)(2,1)S(1)} %get-tuple-element.53), channel_id=1, source_target_pairs={{0,4},{4,8},{8,12},{1,5},{5,9},{9,13},{2,6},{6,10},{10,14},{3,7},{... | collective-permute-start | bytes 983048 | tf_op jit(solution)/shard_map/ppermute | solution.py:20
  34.5 6.1 %copy-start.24 = (f32[20]{0:T(128)S(1)}, f32[20]{0:T(128)}, u32[]{:S(2)}) copy-start(f32[20]{0:T(128)} %get-tuple-element.50) | copy-start | bytes 244
  34.5 11.7 %copy-start.3 = (bf16[256,1280]{0,1:T(8,128)(2,1)S(1)}, bf16[256,1280]{0,1:T(8,128)(2,1)}, u32[]{:S(2)}) copy-start(bf16[256,1280]{0,1:T(8,128)(2,1)} %copy-done.2) | copy-start | bytes 1966084
  34.5 11.7 %copy-start.12 = (f32[3,8,2,128]{3,1,2,0:T(8,128)S(1)}, f32[3,8,2,128]{3,1,2,0:T(8,128)}, u32[]{:S(2)}) copy-start(f32[3,8,2,128]{3,1,2,0:T(8,128)} %copy-done.11) | copy-start | bytes 73732
  34.5 11.7 %copy-start.19 = (f32[20,256]{1,0:T(8,128)S(1)}, f32[20,256]{1,0:T(8,128)}, u32[]{:S(2)}) copy-start(f32[20,256]{1,0:T(8,128)} %get-tuple-element.37) | copy-start | bytes 61444
  40.7 13.2 %collective-permute-start.2 = (bf16[20,64,128]{2,1,0:T(8,128)(2,1)S(1)}, bf16[20,64,128]{2,1,0:T(8,128)(2,1)S(1)}, u32[]{:S(2)}, u32[]{:S(2)}) collective-permute-start(bf16[20,64,128]{2,1,0:T(8,128)(2,1)S(1)} %fusion.25), channel_id=1, source_target_pairs={{0,8},{4,12},{1,9},{5,13},{2,10},{6,14},{3,11},{7,15},{16,24},{20,... | collective-permute-start | bytes 983048 | tf_op jit(solution)/shard_map/ppermute | solution.py:20
  50.6 3.7 %copy-start.23 = (f32[20]{0:T(128)S(1)}, f32[20]{0:T(128)}, u32[]{:S(2)}) copy-start(f32[20]{0:T(128)} %get-tuple-element.48) | copy-start | bytes 244
  57.8 4.2 %copy-start.26 = (s32[128]{0:T(128)S(1)}, s32[128]{0:T(128)}, u32[]{:S(2)}) copy-start(s32[128]{0:T(128)} %iota_add_fusion) | copy-start | bytes 1540
  57.8 7.0 %copy-start.18 = (f32[1280]{0:T(1024)S(1)}, f32[1280]{0:T(1024)}, u32[]{:S(2)}) copy-start(f32[1280]{0:T(1024)} %param.21) | copy-start | bytes 15364
  57.8 7.1 %copy-start.27 = (s32[128]{0:T(128)S(1)}, s32[128]{0:T(128)}, u32[]{:S(2)}) copy-start(s32[128]{0:T(128)} %broadcast_subtract_fusion) | copy-start | bytes 1540
  59.3 1.2 %collective-permute-start.4 = (f32[512]{0:T(512)S(1)}, f32[512]{0:T(512)S(1)}, u32[]{:S(2)}, u32[]{:S(2)}) collective-permute-start(f32[512]{0:T(512)S(1)} %get-tuple-element.24), channel_id=1, source_target_pairs={{0,1},{1,0},{2,3},{3,2},{4,5},{5,4},{6,7},{7,6},{8,9},{9,8},{10,11... | collective-permute-start | bytes 6152 | tf_op jit(solution)/shard_map/ppermute | solution.py:84
  60.5 4.3 %collective-permute-start.5 = (f32[512]{0:T(512)S(1)}, f32[512]{0:T(512)S(1)}, u32[]{:S(2)}, u32[]{:S(2)}) collective-permute-start(f32[512]{0:T(512)S(1)} %add.172), channel_id=1, source_target_pairs={{0,2},{1,3},{2,0},{3,1},{4,6},{5,7},{6,4},{7,5},{8,10},{9,11},{10,... | collective-permute-start | bytes 6152 | tf_op jit(solution)/shard_map/ppermute | solution.py:84
  65.8 1.8 %copy-start.6 = (bf16[128,1280]{0,1:T(8,128)(2,1)}, bf16[128,1280]{0,1:T(8,128)(2,1)S(1)}, u32[]{:S(2)}) copy-start(bf16[128,1280]{0,1:T(8,128)(2,1)S(1)} %copy.70) | copy-start | bytes 983044
  72.2 13.0 %collective-permute-start.6 = (bf16[40,1304]{1,0:T(8,128)(2,1)S(1)}, bf16[40,1304]{1,0:T(8,128)(2,1)S(1)}, u32[]{:S(2)}, u32[]{:S(2)}) collective-permute-start(bf16[40,1304]{1,0:T(8,128)(2,1)S(1)} %get-tuple-element.33), channel_id=1, source_target_pairs={{0,4},{4,8},{8,12},{12,0},{1,5},{5,9},{9,13},{13,1},{2,6},{6,10},{... | collective-permute-start | bytes 312968 | tf_op jit(solution)/shard_map/ppermute | solution.py:222
  78.0 10.9 %collective-permute-start.7 = (bf16[40,1304]{1,0:T(8,128)(2,1)S(1)}, bf16[40,1304]{1,0:T(8,128)(2,1)S(1)}, u32[]{:S(2)}, u32[]{:S(2)}) collective-permute-start(bf16[40,1304]{1,0:T(8,128)(2,1)S(1)} %get-tuple-element.32), channel_id=1, source_target_pairs={{0,8},{4,12},{8,0},{12,4},{1,9},{5,13},{9,1},{13,5},{2,10},{6,14},... | collective-permute-start | bytes 312968 | tf_op jit(solution)/shard_map/ppermute | solution.py:222
  81.4 7.5 %collective-permute-start.8 = (bf16[40,1304]{1,0:T(8,128)(2,1)S(1)}, bf16[40,1304]{1,0:T(8,128)(2,1)S(1)}, u32[]{:S(2)}, u32[]{:S(2)}) collective-permute-start(bf16[40,1304]{1,0:T(8,128)(2,1)S(1)} %get-tuple-element.31), channel_id=1, source_target_pairs={{0,12},{4,0},{8,4},{12,8},{1,13},{5,1},{9,5},{13,9},{2,14},{6,2},{... | collective-permute-start | bytes 312968 | tf_op jit(solution)/shard_map/ppermute | solution.py:222
  (8 other events, 10.9 us)

commit v14 on v10

--- a/solution.py
+++ b/solution.py
@@ -57,22 +57,30 @@
     return (earlier[0] * jnp.exp(later[1])[:, None, None] + later[0], earlier[1] + later[1])
 
 
-def exclusive_scan(state, decay, axis, rider):
+def exclusive_scan(state, decays_all, axis, rider):
     count = lax.axis_size(axis)
-    window = (state, decay)
-    before = (jnp.zeros_like(state), jnp.zeros_like(decay))
+    place = lax.axis_index(axis)
+    order = lax.iota(jnp.int32, count)
+
+    def span_decay(first, last):
+        inside = (order >= first) & (order <= last)
+        return jnp.sum(jnp.where(inside[:, None], decays_all, 0.0), axis=0)
+
+    window = state
+    before = jnp.zeros_like(state)
     shift = 1
     while shift < count:
-        sent_state = passed_along(window[0].astype(jnp.bfloat16), axis, shift)
-        sent_decay = passed_along(window[1], axis, shift)
+        received = passed_along(window.astype(jnp.bfloat16), axis, shift)
         if shift == 1:
-            sent_state, rider = lax.optimization_barrier((sent_state, rider))
-        received = (sent_state.astype(jnp.float32), sent_decay)
-        before = combine(received, before)
+            received, rider = lax.optimization_barrier((received, rider))
+        received = received.astype(jnp.float32)
+        before_decay = span_decay(place - shift + 1, place - 1)
+        before = received * jnp.exp(before_decay)[:, None, None] + before
         if shift * 2 < count:
-            window = combine(received, window)
+            window_decay = span_decay(place - shift + 1, place)
+            window = received * jnp.exp(window_decay)[:, None, None] + window
         shift *= 2
-    return before[0], rider
+    return before, rider
 
 
 def butterfly_sum(value, axis):
@@ -118,13 +126,29 @@
     rim_rows = conv_x.shape[0] - 1
     seq_count = lax.axis_size("seq")
     pools_local = pool_query.shape[0]
+    decay_local = jnp.sum(log_keep, axis=1)
+    decay_high = decay_local.astype(jnp.bfloat16)
+    decay_rest = decay_local - decay_high.astype(jnp.float32)
+    decay_mid = decay_rest.astype(jnp.bfloat16)
+    decay_low = (decay_rest - decay_mid.astype(jnp.float32)).astype(jnp.bfloat16)
     bounds = jnp.stack([pool_start, pool_stop], axis=1)
     bounds_split = jnp.concatenate([bounds // 64, bounds % 64], axis=1).astype(jnp.bfloat16)
     query_rows = jnp.concatenate([pool_query, bounds_split], axis=1)
+    query_width = query_rows.shape[1]
+    decay_row = jnp.concatenate([decay_high, decay_mid, decay_low])
+    decay_row = jnp.pad(decay_row, (0, query_width - decay_row.shape[0]))
+    query_rows = jnp.concatenate([query_rows, decay_row[None, :]], axis=0)
     query_rows = jnp.broadcast_to(query_rows[None], (seq_count,) + query_rows.shape)
     query_rows = lax.all_to_all(
-        query_rows.reshape(seq_count * pools_local, -1), "seq", 0, 0, tiled=True
-    )
+        query_rows.reshape(seq_count * (pools_local + 1), -1), "seq", 0, 0, tiled=True
+    ).reshape(seq_count, pools_local + 1, query_width)
+    decay_parts = query_rows[:, pools_local, : 3 * heads_local].astype(jnp.float32)
+    decays_all = (
+        decay_parts[:, :heads_local]
+        + decay_parts[:, heads_local : 2 * heads_local]
+        + decay_parts[:, 2 * heads_local :]
+    )
+    query_rows = query_rows[:, :pools_local].reshape(seq_count * pools_local, query_width)
     queries_all = query_rows[:, :channels]
     bounds_all = query_rows[:, channels:].astype(jnp.int32)
     start_all = bounds_all[:, 0] * 64 + bounds_all[:, 2]
@@ -154,7 +178,7 @@
         saved_parts.append((intra_part, cumul_keep, entry_state, decay_total))
         entry_state = jnp.exp(cumul_keep[:, -1])[:, None, None] * entry_state + stretch_state
         decay_total = decay_total + cumul_keep[:, -1]
-    incoming, z_late = exclusive_scan(entry_state, decay_total, "seq", z_gate)
+    incoming, z_late = exclusive_scan(entry_state, decays_all, "seq", z_gate)
     x_major = x_conv.T.reshape(heads_local, head_width, tok_rows)
     z_major = z_late.T
     pieces_out = []

time: 91.7 us -> 93.8 us (1.023)
  starting transfers between devices: 32.7 us -> 28.2 us
  other arithmetic: 15.3 us -> 18.6 us
  matrix products: 10.9 us -> 12.9 us
    ppermute x4 -> x3, starting transfers between devices: 17.8 us -> 14.3 us  [passed_along(): lax.ppermute(value, axis, [(source, source + steps) for source in range(l...]
    convert_element_type x1 -> x3, other arithmetic: 0.15 us -> 1.95 us  [the longest x1 1.24 us: exclusive_scan(): received = passed_along(window.astype(jnp.bfloat16), axis, shift)]
    and x0 -> x2, other arithmetic: none -> 1.18 us  [span_decay(): inside = (order >= first) & (order <= last)]
    dot_general x2, matrix products: 5.85 us -> 6.97 us  [stretch_local(): jnp.einsum('hij,jhp->hpi', mixing, x_block, preferred_element_type=jnp.fl...]
    ppermute x3, starting transfers between devices: 9.22 us -> 8.12 us  [local(): lax.ppermute(chunk, 'seq', [(i, (i + shift) % seq_count) for i in range(s...]
    slice x1 -> x2, local copies, waits for them, and re-layouts: 0.16 us -> 1.22 us  [the longest x1 1.06 us: local(): query_rows[:, :pools_local].reshape(seq_count * pools_local, query_width)]
    reduce_sum x0 -> x2, other arithmetic: none -> 1.01 us  [the longest x1 0.92 us: local(): decay_local = jnp.sum(log_keep, axis=1)]
    slice x1, local copies, waits for them, and re-layouts: 1.03 us -> 0.03 us  [local(): queries_all = query_rows[:, :channels]]
  transfers between devices with their start and end apart: 10 -> 9, of which waited for: 4 -> 5; matrix products, arithmetic and copies ran while one was open for 33% -> 37% of each run, Pallas kernels for 0% -> 0%
where the time goes in v14:
time: 93.8 us; the launch traced here: 92.9 us
  starting transfers between devices  28.2 us (30%)
  local copies, waits for them, and re-layouts  20.3 us (22%)
  other arithmetic  18.6 us (20%)
  matrix products  12.9 us (14%)
  waiting for transfers between devices  11.6 us (12%)
  between operations  1.28 us (1%)
    ppermute x3, starting transfers between devices, passed_along(): lax.ppermute(value, axis, [(source, source + steps) for source in range(l...  14.3 us
    ppermute x3, starting transfers between devices, local(): lax.ppermute(chunk, 'seq', [(i, (i + shift) % seq_count) for i in range(s...  8.12 us
    ppermute x3, waiting for transfers between devices, local(): lax.ppermute(chunk, 'seq', [(i, (i + shift) % seq_count) for i in range(s...  7.3 us
    dot_general x2, matrix products, stretch_local(): jnp.einsum('hij,jhp->hpi', mixing, x_block, preferred_element_type=jnp.fl...  6.97 us
    all_to_all x1, starting transfers between devices, local(): lax.all_to_all(query_rows.reshape(seq_count * (pools_local + 1), -1), 'se...  4.14 us
    unnamed x59, local copies, waits for them, and re-layouts  4.07 us
    convert_element_type x2, other arithmetic, causal_conv(): return silu_act(summed).astype(jnp.bfloat16)  3.73 us
    ppermute x3, waiting for transfers between devices, passed_along(): lax.ppermute(value, axis, [(source, source + steps) for source in range(l...  3.18 us
  transfers between devices with their start and end apart: 9, of which 5 were waited for; matrix products, arithmetic and copies ran while one was open for 37% of the time, Pallas kernels for 0%

profile of v14, /device:TPU:0, one launch (start us, length us, event | category | flops | bytes accessed | tf_op | source)
XLA Modules:
  0.0 92.9 jit_solution(11612527921323740087)
XLA Ops:
  0.7 0.8 slice.167
  2.2 5.0 %collective-permute-start = (bf16[3,1536]{1,0:T(4,128)(2,1)S(1)}, bf16[3,1536]{1,0:T(4,128)(2,1)S(1)}, u32[]{:S(2)}, u32[]{:S(2)}) collective-permute-start(bf16[3,1536]{1,0:T(4,128)(2,1)S(1)} %pad_maximum_fusion.6), channel_id=1, source_target_pairs={{0,4},{4,8},{8,12},{1,5},{5,9},{9,13},{2,6},{6,10},{10,14},{3,7},{... | collective-permute-start | bytes 27656 | tf_op jit(solution)/shard_map/ppermute | solution.py:20
  7.2 0.9 reduce_sum.74
  9.1 1.0 %concatenate.35 = bf16[40,1284]{1,0:T(8,128)(2,1)S(1)} concatenate(bf16[40,1280]{1,0:T(8,128)(2,1)} %param.23, bf16[40,2]{1,0:T(8,128)(2,1)S(1)} %copy.70, bf16[40,2]{1,0:T(8,128)(2,1)S(1)} %copy.71), dimensions={1} | concatenate | bytes 205440 | tf_op jit(solution)/shard_map/concatenate | solution.py:136
  10.1 0.8 broadcast_in_dim.147
  11.0 4.1 %all-to-all-start = ((bf16[4,41,1284]{2,1,0:T(8,128)(2,1)}), bf16[4,41,1284]{2,1,0:T(8,128)(2,1)}, u32[]{:S(2)}, u32[]{:S(2)}) async-start(bf16[4,41,1284]{2,1,0:T(8,128)(2,1)} %broadcast_in_dim.147), calls=%async_computation | async-start | bytes 1081344 | tf_op jit(solution)/shard_map/all_to_all | solution.py:142
  15.1 0.8 fusion.93
  24.0 1.8 %divide_convert_fusion = bf16[512,1280]{1,0:T(8,128)(2,1)S(1)} fusion(bf16[512,1280]{1,0:T(8,128)(2,1)S(1)} %copy-done.4, bf16[3,1280]{1,0:T(4,128)(2,1)S(1)} %slice.221, f32[1280]{0:T(1024)S(1)} %get-tuple-element.18, f32[1280]{0:T(1024)S(1)} %get-tuple-element.19, f32[1280]{0:T(1024)S(1)} %get-tuple-element.17, f32[1280]{0:T(1024)S(1)} %get-tuple-element.16), kind=kLoop, calls=%fused_computation.23 | loop fusion | flops 15728640 | bytes 2649600 | tf_op jit(solution)/shard_map/convert_element_type | solution.py:36
  26.4 1.9 %divide_convert_fusion.1 = bf16[512,256]{1,0:T(8,128)(2,1)S(1)} fusion(bf16[512,256]{1,0:T(8,128)(2,1)} %param.15, bf16[3,256]{1,0:T(4,128)(2,1)S(1)} %slice.228, f32[256]{0:T(256)} %bitcast.131, f32[256]{0:T(256)} %bitcast.132, f32[256]{0:T(256)} %bitcast.130, f32[256]{0:T(256)S(1)} %bitcast.129), kind=kLoop, calls=%fused_computation.60 | loop fusion | flops 3145728 | bytes 529920 | tf_op jit(solution)/shard_map/convert_element_type | solution.py:36
  28.5 1.1 %convolution_add_fusion.3 = f32[20,64,128]{2,1,0:T(8,128)S(1)} fusion(bf16[256,20,64]{0,2,1:T(8,128)(2,1)S(1)} %bitcast.101, f32[256,20]{0,1:T(8,128)} %get-tuple-element.38, f32[20]{0:T(128)} %get-tuple-element.52, bf16[512,256]{1,0:T(8,128)(2,1)S(1)} %divide_convert_fusion.1), kind=kOutput, calls=%fused_computation.43 | convolution fusion | flops 85032960 | bytes 1396816 | tf_op jit(solution)/shard_map/jhp,js->hps/dot_general | solution.py:52
  29.6 1.9 %fusion.96 = (bf16[20,64,128]{2,1,0:T(8,128)(2,1)S(1)}, f32[20,64,128]{2,1,0:T(8,128)}) fusion(bf16[512,256]{1,0:T(8,128)(2,1)S(1)} %divide_convert_fusion.1, bf16[256,20,64]{0,2,1:T(8,128)(2,1)S(1)} %bitcast.104, f32[256,20]{0,1:T(8,128)} %get-tuple-element.39, f32[20,64,128]{2,1,0:T(8,128)S(1)} %convolution_add_fusion.3, f32[20]{0:T(128)} %exp.85), kind=kOutput, calls=%fused_computation.189 | convolution fusion | flops 85360640 | bytes 2379856 | tf_op jit(solution)/shard_map/jhp,js->hps/dot_general | solution.py:52
  31.6 3.9 %collective-permute-start.1 = (bf16[20,64,128]{2,1,0:T(8,128)(2,1)S(1)}, bf16[20,64,128]{2,1,0:T(8,128)(2,1)S(1)}, u32[]{:S(2)}, u32[]{:S(2)}) collective-permute-start(bf16[20,64,128]{2,1,0:T(8,128)(2,1)S(1)} %get-tuple-element.56), channel_id=1, source_target_pairs={{0,4},{4,8},{8,12},{1,5},{5,9},{9,13},{2,6},{6,10},{10,14},{3,7},{... | collective-permute-start | bytes 983048 | tf_op jit(solution)/shard_map/ppermute | solution.py:20
  35.5 2.9 %fusion = f32[20,64,256]{2,1,0:T(8,128)} fusion(bf16[256,20,64]{0,2,1:T(8,128)(2,1)S(1)} %bitcast.102, f32[20,256]{1,0:T(8,128)S(1)} %copy-done.16, f32[256,256]{1,0:T(8,128)S(1)} %fusion.63, f32[20,256]{1,0:T(8,128)S(1)} %bitcast.124, pred[256,256]{1,0:T(8,128)(4,1)S(1)} %copy-done.13), kind=kOutput, calls=%fused_computation.3 | convolution fusion | flops 175636480 | bytes 2334720 | tf_op jit(solution)/shard_map/hij,jhp->hpi/dot_general | solution.py:49
  38.6 3.2 %collective-permute-done.1 = bf16[20,64,128]{2,1,0:T(8,128)(2,1)S(1)} collective-permute-done((bf16[20,64,128]{2,1,0:T(8,128)(2,1)S(1)}, bf16[20,64,128]{2,1,0:T(8,128)(2,1)S(1)}, u32[]{:S(2)}, u32[]{:S(2)}) %collective-permute-start.1) | collective-permute-done | bytes 327712 | tf_op jit(solution)/shard_map/ppermute | solution.py:20
  42.6 1.2 %fusion.26 = bf16[20,64,128]{2,1,0:T(8,128)(2,1)S(1)} fusion(f32[20,64,128]{2,1,0:T(8,128)} %get-tuple-element.57, bf16[20,64,128]{2,1,0:T(8,128)(2,1)S(1)} %collective-permute-done.1, f32[20]{0:T(128)S(1)} %exp.89), kind=kLoop, calls=%fused_computation.49 | loop fusion | flops 655360 | bytes 1310800 | tf_op jit(solution)/shard_map/convert_element_type | solution.py:73
  43.9 5.5 %collective-permute-start.2 = (bf16[20,64,128]{2,1,0:T(8,128)(2,1)S(1)}, bf16[20,64,128]{2,1,0:T(8,128)(2,1)S(1)}, u32[]{:S(2)}, u32[]{:S(2)}) collective-permute-start(bf16[20,64,128]{2,1,0:T(8,128)(2,1)S(1)} %fusion.26), channel_id=1, source_target_pairs={{0,8},{4,12},{1,9},{5,13},{2,10},{6,14},{3,11},{7,15},{16,24},{20,... | collective-permute-start | bytes 983048 | tf_op jit(solution)/shard_map/ppermute | solution.py:20
  49.4 4.0 %fusion.1 = f32[20,64,256]{2,1,0:T(8,128)} fusion(bf16[256,20,64]{0,2,1:T(8,128)(2,1)} %bitcast.105, f32[20,256]{1,0:T(8,128)} %get-tuple-element.40, f32[256,256]{1,0:T(8,128)S(1)} %fusion.59, f32[20,256]{1,0:T(8,128)} %bitcast.121, pred[256,256]{1,0:T(8,128)(4,1)} %iota_compare_fusion), kind=kOutput, calls=%fused_computation.4 | convolution fusion | flops 175636480 | bytes 2334720 | tf_op jit(solution)/shard_map/hij,jhp->hpi/dot_general | solution.py:49
  53.4 1.5 %copy.72 = bf16[512,1280]{0,1:T(8,128)(2,1)} copy(bf16[512,1280]{1,0:T(8,128)(2,1)S(1)} %divide_convert_fusion) | data formatting | bytes 2621440 | tf_op jit(solution)/shard_map/layout_constraint | solution.py:159
  54.9 2.4 %copy.73 = bf16[512,1280]{0,1:T(8,128)(2,1)} copy(bf16[512,1280]{1,0:T(8,128)(2,1)} %param.14) | data formatting | bytes 2621440 | tf_op jit(solution)/shard_map/optimization_barrier | solution.py:75
  57.3 1.1 %slice.242 = bf16[4,40,1284]{2,1,0:T(8,128)(2,1)S(1)} slice(bf16[4,41,1284]{2,1,0:T(8,128)(2,1)} %all-to-all-done), slice={[0:4], [0:40], [0:1284]} | slice | bytes 821760 | tf_op jit(solution)/shard_map/slice | solution.py:151
  61.1 0.9 copy-done.1
  62.4 1.5 %multiply_reduce_fusion = (f32[512]{0:T(512)S(1)}, f32[1280,512]{1,0:T(8,128)S(1)}) fusion(bf16[512,1280]{0,1:T(8,128)(2,1)S(1)} %copy-done.2, bf16[512,1280]{0,1:T(8,128)(2,1)S(1)} %copy-done.1, f32[1280]{0:T(1024)S(1)} %mul.358, f32[1280,256]{1,0:T(8,128)S(1)} %bitcast.100, f32[1280,256]{1,0:T(8,128)S(1)} %bitcast.99), kind=kLoop, calls=%fused_computation.12 | loop fusion | flops 7208448 | bytes 7871488 | tf_op jit(solution)/shard_map/reduce_sum | solution.py:196
  64.2 0.9 collective-permute-done.3
  65.1 1.5 %collective-permute-start.4 = (f32[512]{0:T(512)S(1)}, f32[512]{0:T(512)S(1)}, u32[]{:S(2)}, u32[]{:S(2)}) collective-permute-start(f32[512]{0:T(512)S(1)} %add.195), channel_id=1, source_target_pairs={{0,2},{1,3},{2,0},{3,1},{4,6},{5,7},{6,4},{7,5},{8,10},{9,11},{10,... | collective-permute-start | bytes 6152 | tf_op jit(solution)/shard_map/ppermute | solution.py:92
  66.7 1.7 %reshape.268 = bf16[160,8,160]{2,1,0:T(8,128)(2,1)} reshape(bf16[160,1280]{1,0:T(8,128)(2,1)S(1)} %slice.248) | data formatting | bytes 819200 | tf_op jit(solution)/shard_map/reshape | solution.py:209
  68.7 1.4 %fusion.23 = bf16[512,1280]{0,1:T(8,128)(2,1)} fusion(f32[1280,512]{1,0:T(8,128)S(1)} %get-tuple-element.30, f32[1280]{0:T(1024)S(1)} %copy-done.17, f32[512]{0:T(512)S(1)} %add_rsqrt_fusion), kind=kLoop, calls=%fused_computation.37 | loop fusion | flops 1966080 | bytes 3939328 | tf_op jit(solution)/shard_map/transpose | solution.py:201
  70.0 1.7 %copy.85 = bf16[512,1280]{1,0:T(8,128)(2,1)S(1)} copy(bf16[512,1280]{0,1:T(8,128)(2,1)} %fusion.23) | data formatting | bytes 2621440
  71.7 0.9 gather_fusion
  75.3 4.7 %collective-permute-start.5 = (bf16[40,1304]{1,0:T(8,128)(2,1)S(1)}, bf16[40,1304]{1,0:T(8,128)(2,1)S(1)}, u32[]{:S(2)}, u32[]{:S(2)}) collective-permute-start(bf16[40,1304]{1,0:T(8,128)(2,1)S(1)} %get-tuple-element.36), channel_id=1, source_target_pairs={{0,4},{4,8},{8,12},{12,0},{1,5},{5,9},{9,13},{13,1},{2,6},{6,10},{... | collective-permute-start | bytes 312968 | tf_op jit(solution)/shard_map/ppermute | solution.py:241
  80.0 3.4 %collective-permute-start.6 = (bf16[40,1304]{1,0:T(8,128)(2,1)S(1)}, bf16[40,1304]{1,0:T(8,128)(2,1)S(1)}, u32[]{:S(2)}, u32[]{:S(2)}) collective-permute-start(bf16[40,1304]{1,0:T(8,128)(2,1)S(1)} %get-tuple-element.35), channel_id=1, source_target_pairs={{0,8},{4,12},{8,0},{12,4},{1,9},{5,13},{9,1},{13,5},{2,10},{6,14},... | collective-permute-start | bytes 312968 | tf_op jit(solution)/shard_map/ppermute | solution.py:241
  83.4 3.5 %collective-permute-done.5 = bf16[40,1304]{1,0:T(8,128)(2,1)S(1)} collective-permute-done((bf16[40,1304]{1,0:T(8,128)(2,1)S(1)}, bf16[40,1304]{1,0:T(8,128)(2,1)S(1)}, u32[]{:S(2)}, u32[]{:S(2)}) %collective-permute-start.5) | collective-permute-done | bytes 104352 | tf_op jit(solution)/shard_map/ppermute | solution.py:241
  86.9 3.8 %collective-permute-done.6 = bf16[40,1304]{1,0:T(8,128)(2,1)S(1)} collective-permute-done((bf16[40,1304]{1,0:T(8,128)(2,1)S(1)}, bf16[40,1304]{1,0:T(8,128)(2,1)S(1)}, u32[]{:S(2)}, u32[]{:S(2)}) %collective-permute-start.6) | collective-permute-done | bytes 104352 | tf_op jit(solution)/shard_map/ppermute | solution.py:241
  (150 shorter events, 20.0 us)
Async XLA Ops:
  0.6 23.3 %copy-start.4 = (bf16[512,1280]{1,0:T(8,128)(2,1)S(1)}, bf16[512,1280]{1,0:T(8,128)(2,1)}, u32[]{:S(2)}) copy-start(bf16[512,1280]{1,0:T(8,128)(2,1)} %param.13) | copy-start | bytes 3932164
  0.6 19.4 %copy-start.18 = (bf16[4,256]{1,0:T(4,128)(2,1)S(1)}, bf16[4,256]{1,0:T(4,128)(2,1)}, u32[]{:S(2)}) copy-start(bf16[4,256]{1,0:T(4,128)(2,1)} %param.20) | copy-start | bytes 6148
  0.7 20.0 %copy-start.15 = (bf16[4,1280]{1,0:T(4,128)(2,1)S(1)}, bf16[4,1280]{1,0:T(4,128)(2,1)}, u32[]{:S(2)}) copy-start(bf16[4,1280]{1,0:T(4,128)(2,1)} %param.19) | copy-start | bytes 30724
  0.7 20.6 %copy-start.26 = (s32[128]{0:T(128)S(1)}, s32[128]{0:T(128)}, u32[]{:S(2)}) copy-start(s32[128]{0:T(128)} %param.22) | copy-start | bytes 1540
  0.7 21.2 %copy-start.14 = (f32[20,512]{1,0:T(8,128)S(1)}, f32[20,512]{1,0:T(8,128)}, u32[]{:S(2)}) copy-start(f32[20,512]{1,0:T(8,128)} %param.16) | copy-start | bytes 122884
  0.7 23.1 %copy-start.23 = (f32[20]{0:T(128)S(1)}, f32[20]{0:T(128)}, u32[]{:S(2)}) copy-start(f32[20]{0:T(128)} %param.18) | copy-start | bytes 244
  2.2 21.7 %collective-permute-start = (bf16[3,1536]{1,0:T(4,128)(2,1)S(1)}, bf16[3,1536]{1,0:T(4,128)(2,1)S(1)}, u32[]{:S(2)}, u32[]{:S(2)}) collective-permute-start(bf16[3,1536]{1,0:T(4,128)(2,1)S(1)} %pad_maximum_fusion.6), channel_id=1, source_target_pairs={{0,4},{4,8},{8,12},{1,5},{5,9},{9,13},{2,6},{6,10},{10,14},{3,7},{... | collective-permute-start | bytes 27656 | tf_op jit(solution)/shard_map/ppermute | solution.py:20
  11.0 30.8 %all-to-all-start = ((bf16[4,41,1284]{2,1,0:T(8,128)(2,1)}), bf16[4,41,1284]{2,1,0:T(8,128)(2,1)}, u32[]{:S(2)}, u32[]{:S(2)}) async-start(bf16[4,41,1284]{2,1,0:T(8,128)(2,1)} %broadcast_in_dim.147), calls=%async_computation | async-start | bytes 1081344 | tf_op jit(solution)/shard_map/all_to_all | solution.py:142
  18.7 5.2 %copy-start.9 = (f32[3,8,2,128]{3,1,2,0:T(8,128)}, f32[3,8,2,128]{3,1,2,0:T(8,128)S(1)}, u32[]{:S(2)}) copy-start(f32[3,8,2,128]{3,1,2,0:T(8,128)S(1)} %copy.87) | copy-start | bytes 73732
  19.8 4.1 %copy-start.8 = (f32[3,8,2,128]{3,1,2,0:T(8,128)}, f32[3,8,2,128]{3,1,2,0:T(8,128)S(1)}, u32[]{:S(2)}) copy-start(f32[3,8,2,128]{3,1,2,0:T(8,128)S(1)} %copy.88) | copy-start | bytes 73732
  26.4 5.2 %copy-start.3 = (bf16[256,1280]{0,1:T(8,128)(2,1)}, bf16[256,1280]{0,1:T(8,128)(2,1)S(1)}, u32[]{:S(2)}) copy-start(bf16[256,1280]{0,1:T(8,128)(2,1)S(1)} %copy.69) | copy-start | bytes 1966084
  26.4 9.1 %copy-start.10 = (f32[3,8,2,128]{3,1,2,0:T(8,128)S(1)}, f32[3,8,2,128]{3,1,2,0:T(8,128)}, u32[]{:S(2)}) copy-start(f32[3,8,2,128]{3,1,2,0:T(8,128)} %copy-done.9) | copy-start | bytes 73732
  26.4 9.1 %copy-start.13 = (pred[256,256]{1,0:T(8,128)(4,1)S(1)}, pred[256,256]{1,0:T(8,128)(4,1)}, u32[]{:S(2)}) copy-start(pred[256,256]{1,0:T(8,128)(4,1)} %iota_compare_fusion) | copy-start | bytes 196612
  26.4 9.1 %copy-start.16 = (f32[20,256]{1,0:T(8,128)S(1)}, f32[20,256]{1,0:T(8,128)}, u32[]{:S(2)}) copy-start(f32[20,256]{1,0:T(8,128)} %get-tuple-element.37) | copy-start | bytes 61444
  31.6 10.3 %collective-permute-start.1 = (bf16[20,64,128]{2,1,0:T(8,128)(2,1)S(1)}, bf16[20,64,128]{2,1,0:T(8,128)(2,1)S(1)}, u32[]{:S(2)}, u32[]{:S(2)}) collective-permute-start(bf16[20,64,128]{2,1,0:T(8,128)(2,1)S(1)} %get-tuple-element.56), channel_id=1, source_target_pairs={{0,4},{4,8},{8,12},{1,5},{5,9},{9,13},{2,6},{6,10},{10,14},{3,7},{... | collective-permute-start | bytes 983048 | tf_op jit(solution)/shard_map/ppermute | solution.py:20
  35.5 7.0 %copy-start.20 = (pred[4]{0:T(512)(128)(4,1)S(1)}, pred[4]{0:T(512)(128)(4,1)}, u32[]{:S(2)}) copy-start(pred[4]{0:T(512)(128)(4,1)} %get-tuple-element.60) | copy-start | bytes 16
  35.5 7.0 %copy-start.21 = (pred[4]{0:T(512)(128)(4,1)S(1)}, pred[4]{0:T(512)(128)(4,1)}, u32[]{:S(2)}) copy-start(pred[4]{0:T(512)(128)(4,1)} %get-tuple-element.61) | copy-start | bytes 16
  35.5 7.0 %copy-start.25 = (pred[4]{0:T(512)(128)(4,1)S(1)}, pred[4]{0:T(512)(128)(4,1)}, u32[]{:S(2)}) copy-start(pred[4]{0:T(512)(128)(4,1)} %compare_and_fusion.2) | copy-start | bytes 16
  43.9 14.5 %collective-permute-start.2 = (bf16[20,64,128]{2,1,0:T(8,128)(2,1)S(1)}, bf16[20,64,128]{2,1,0:T(8,128)(2,1)S(1)}, u32[]{:S(2)}, u32[]{:S(2)}) collective-permute-start(bf16[20,64,128]{2,1,0:T(8,128)(2,1)S(1)} %fusion.26), channel_id=1, source_target_pairs={{0,8},{4,12},{1,9},{5,13},{2,10},{6,14},{3,11},{7,15},{16,24},{20,... | collective-permute-start | bytes 983048 | tf_op jit(solution)/shard_map/ppermute | solution.py:20
  54.9 3.9 %copy-start.22 = (f32[20]{0:T(128)S(1)}, f32[20]{0:T(128)}, u32[]{:S(2)}) copy-start(f32[20]{0:T(128)} %get-tuple-element.51) | copy-start | bytes 244
  59.2 1.4 %copy-start.6 = (f32[20,64,256]{2,1,0:T(8,128)S(1)}, f32[20,64,256]{2,1,0:T(8,128)}, u32[]{:S(2)}) copy-start(f32[20,64,256]{2,1,0:T(8,128)} %fusion.1) | copy-start | bytes 3932164
  60.6 1.7 %copy-start.2 = (bf16[512,1280]{0,1:T(8,128)(2,1)S(1)}, bf16[512,1280]{0,1:T(8,128)(2,1)}, u32[]{:S(2)}) copy-start(bf16[512,1280]{0,1:T(8,128)(2,1)} %copy.73) | copy-start | bytes 3932164
  62.3 4.2 %copy-start.24 = (s32[128]{0:T(128)S(1)}, s32[128]{0:T(128)}, u32[]{:S(2)}) copy-start(s32[128]{0:T(128)} %iota_add_fusion) | copy-start | bytes 1540
  62.3 6.3 %copy-start.17 = (f32[1280]{0:T(1024)S(1)}, f32[1280]{0:T(1024)}, u32[]{:S(2)}) copy-start(f32[1280]{0:T(1024)} %param.21) | copy-start | bytes 15364
  63.8 1.2 %collective-permute-start.3 = (f32[512]{0:T(512)S(1)}, f32[512]{0:T(512)S(1)}, u32[]{:S(2)}, u32[]{:S(2)}) collective-permute-start(f32[512]{0:T(512)S(1)} %get-tuple-element.29), channel_id=1, source_target_pairs={{0,1},{1,0},{2,3},{3,2},{4,5},{5,4},{6,7},{7,6},{8,9},{9,8},{10,11... | collective-permute-start | bytes 6152 | tf_op jit(solution)/shard_map/ppermute | solution.py:92
  65.1 3.6 %collective-permute-start.4 = (f32[512]{0:T(512)S(1)}, f32[512]{0:T(512)S(1)}, u32[]{:S(2)}, u32[]{:S(2)}) collective-permute-start(f32[512]{0:T(512)S(1)} %add.195), channel_id=1, source_target_pairs={{0,2},{1,3},{2,0},{3,1},{4,6},{5,7},{6,4},{7,5},{8,10},{9,11},{10,... | collective-permute-start | bytes 6152 | tf_op jit(solution)/shard_map/ppermute | solution.py:92
  70.0 2.8 %copy-start.7 = (bf16[160,8,160]{2,1,0:T(8,128)(2,1)S(1)}, bf16[160,8,160]{2,1,0:T(8,128)(2,1)}, u32[]{:S(2)}) copy-start(bf16[160,8,160]{2,1,0:T(8,128)(2,1)} %reshape.268) | copy-start | bytes 1228804
  70.0 2.8 %copy-start.19 = (pred[128]{0:T(512)(128)(4,1)S(1)}, pred[128]{0:T(512)(128)(4,1)}, u32[]{:S(2)}) copy-start(pred[128]{0:T(512)(128)(4,1)} %get-tuple-element.27) | copy-start | bytes 388
  71.7 1.7 %copy-start = (bf16[512,1280]{1,0:T(8,128)(2,1)}, bf16[512,1280]{1,0:T(8,128)(2,1)S(1)}, u32[]{:S(2)}) copy-start(bf16[512,1280]{1,0:T(8,128)(2,1)S(1)} %copy.85) | copy-start | bytes 3932164
  75.3 11.6 %collective-permute-start.5 = (bf16[40,1304]{1,0:T(8,128)(2,1)S(1)}, bf16[40,1304]{1,0:T(8,128)(2,1)S(1)}, u32[]{:S(2)}, u32[]{:S(2)}) collective-permute-start(bf16[40,1304]{1,0:T(8,128)(2,1)S(1)} %get-tuple-element.36), channel_id=1, source_target_pairs={{0,4},{4,8},{8,12},{12,0},{1,5},{5,9},{9,13},{13,1},{2,6},{6,10},{... | collective-permute-start | bytes 312968 | tf_op jit(solution)/shard_map/ppermute | solution.py:241
  80.0 10.7 %collective-permute-start.6 = (bf16[40,1304]{1,0:T(8,128)(2,1)S(1)}, bf16[40,1304]{1,0:T(8,128)(2,1)S(1)}, u32[]{:S(2)}, u32[]{:S(2)}) collective-permute-start(bf16[40,1304]{1,0:T(8,128)(2,1)S(1)} %get-tuple-element.35), channel_id=1, source_target_pairs={{0,8},{4,12},{8,0},{12,4},{1,9},{5,13},{9,1},{13,5},{2,10},{6,14},... | collective-permute-start | bytes 312968 | tf_op jit(solution)/shard_map/ppermute | solution.py:241
  83.4 7.3 %collective-permute-start.7 = (bf16[40,1304]{1,0:T(8,128)(2,1)S(1)}, bf16[40,1304]{1,0:T(8,128)(2,1)S(1)}, u32[]{:S(2)}, u32[]{:S(2)}) collective-permute-start(bf16[40,1304]{1,0:T(8,128)(2,1)S(1)} %get-tuple-element.34), channel_id=1, source_target_pairs={{0,12},{4,0},{8,4},{12,8},{1,13},{5,1},{9,5},{13,9},{2,14},{6,2},{... | collective-permute-start | bytes 312968 | tf_op jit(solution)/shard_map/ppermute | solution.py:241
  (4 other events, 5.4 us)

commit v15 on v10

--- a/solution.py
+++ b/solution.py
@@ -182,12 +182,13 @@
     scale_factor = 1.0 / math.sqrt(pool_width)
     pools_all = queries_all.shape[0]
     segs_local = summaries.shape[0]
-    queries = queries_all.reshape(pools_all, pool_heads_local, pool_width)
     seg_index = lax.axis_index("seq") * segs_local + lax.iota(jnp.int32, segs_local)
     inside = (seg_index[None, :] >= start_all[:, None]) & (seg_index[None, :] < stop_all[:, None])
-    keys_block = summaries.reshape(segs_local, pool_heads_local, pool_width)
+    head_of = lax.broadcasted_iota(jnp.int32, (pool_heads_local, channels), 1) // pool_width
+    head_mask = head_of == lax.broadcasted_iota(jnp.int32, (pool_heads_local, channels), 0)
+    keys_masked = jnp.where(head_mask[:, None, :], summaries[None, :, :], jnp.zeros((), summaries.dtype))
     logits = (
-        jnp.einsum("pad,rad->apr", queries, keys_block, preferred_element_type=jnp.float32)
+        jnp.einsum("pc,asc->aps", queries_all, keys_masked, preferred_element_type=jnp.float32)
         * scale_factor
     )
     logits = jnp.where(inside[None], logits, MASKED)
@@ -195,7 +196,7 @@
     expo = jnp.where(inside[None], jnp.exp(logits - peak[:, :, None]), 0.0)
     denom = jnp.sum(expo, axis=2)
     numer = jnp.einsum(
-        "apr,rad->pad", expo.astype(jnp.bfloat16), keys_block, preferred_element_type=jnp.float32
+        "aps,asc->pc", expo.astype(jnp.bfloat16), keys_masked, preferred_element_type=jnp.float32
     )
     denom_high = denom.astype(jnp.bfloat16)
     denom_low = (denom - denom_high.astype(jnp.float32)).astype(jnp.bfloat16)

time: 91.7 us -> 90.3 us (0.985)
  local copies, waits for them, and re-layouts: 19.4 us -> 14.3 us
  matrix products: 10.9 us -> 12.9 us
  waiting for transfers between devices: 11.3 us -> 12.7 us
    ppermute x2, waiting for transfers between devices: 0.88 us -> 2.86 us  [butterfly_sum(): partner = lax.ppermute(value, axis, [(i, i ^ stride) for i in range(count)])]
    dot_general x2, matrix products: 1.01 us -> 2.95 us  [the longest x1 2.23 us: local(): jnp.einsum('pc,asc->aps', queries_all, keys_masked, preferred_element_typ...]
    reshape x3, local copies, waits for them, and re-layouts: 1.69 us -> 0.03 us  [the longest x1 1.67 us: local(): queries = queries_all.reshape(pools_all, pool_heads_local, pool_width)]
    slice x3 -> x1, local copies, waits for them, and re-layouts: 1.26 us -> 0.16 us  [the longest x1 1.03 us: local(): queries_all = query_rows[:, :channels]]
    transpose x1, other arithmetic: 1.36 us -> 0.33 us  [local(): mixed_seq = mixed_major.T]
    unnamed x61 -> x60, local copies, waits for them, and re-layouts: 3.97 us -> 3.42 us
    another operation x7 -> x8, other arithmetic: 2.1 us -> 2.18 us
  transfers between devices with their start and end apart: 10 -> 10, of which waited for: 4 -> 6; matrix products, arithmetic and copies ran while one was open for 33% -> 30% of each run, Pallas kernels for 0% -> 0%
where the time goes in v15:
time: 90.3 us; the launch traced here: 89.6 us
  starting transfers between devices  33.5 us (37%)
  other arithmetic  14.8 us (16%)
  local copies, waits for them, and re-layouts  14.3 us (16%)
  matrix products  12.9 us (14%)
  waiting for transfers between devices  12.7 us (14%)
  between operations  1.4 us (2%)
    ppermute x4, starting transfers between devices, passed_along(): lax.ppermute(value, axis, [(source, source + steps) for source in range(l...  17.8 us
    ppermute x3, starting transfers between devices, local(): lax.ppermute(chunk, 'seq', [(i, (i + shift) % seq_count) for i in range(s...  9.99 us
    ppermute x3, waiting for transfers between devices, local(): lax.ppermute(chunk, 'seq', [(i, (i + shift) % seq_count) for i in range(s...  6.98 us
    dot_general x2, matrix products, stretch_local(): jnp.einsum('hij,jhp->hpi', mixing, x_block, preferred_element_type=jnp.fl...  5.89 us
    all_to_all x1, starting transfers between devices, local(): lax.all_to_all(query_rows.reshape(seq_count * pools_local, -1), 'seq', 0,...  4.12 us
    convert_element_type x2, other arithmetic, causal_conv(): return silu_act(summed).astype(jnp.bfloat16)  3.73 us
    unnamed x60, local copies, waits for them, and re-layouts  3.42 us
    ppermute x4, waiting for transfers between devices, passed_along(): lax.ppermute(value, axis, [(source, source + steps) for source in range(l...  2.89 us
  transfers between devices with their start and end apart: 10, of which 6 were waited for; matrix products, arithmetic and copies ran while one was open for 30% of the time, Pallas kernels for 0%

profile of v15, /device:TPU:0, one launch (start us, length us, event | category | flops | bytes accessed | tf_op | source)
XLA Modules:
  0.0 89.6 jit_solution(7951844967927028354)
XLA Ops:
  0.7 0.8 slice.153
  2.2 5.0 %collective-permute-start = (bf16[3,1536]{1,0:T(4,128)(2,1)S(1)}, bf16[3,1536]{1,0:T(4,128)(2,1)S(1)}, u32[]{:S(2)}, u32[]{:S(2)}) collective-permute-start(bf16[3,1536]{1,0:T(4,128)(2,1)S(1)} %pad_maximum_fusion.3), channel_id=1, source_target_pairs={{0,4},{4,8},{8,12},{1,5},{5,9},{9,13},{2,6},{6,10},{10,14},{3,7},{... | collective-permute-start | bytes 27656 | tf_op jit(solution)/shard_map/ppermute | solution.py:20
  7.2 0.8 fusion.110
  10.7 3.5 %collective-permute-start.3 = (f32[20]{0:T(128)S(1)}, f32[20]{0:T(128)S(1)}, u32[]{:S(2)}, u32[]{:S(2)}) collective-permute-start(f32[20]{0:T(128)S(1)} %get-tuple-element.53), channel_id=1, source_target_pairs={{0,4},{4,8},{8,12},{1,5},{5,9},{9,13},{2,6},{6,10},{10,14},{3,7},{... | collective-permute-start | bytes 248 | tf_op jit(solution)/shard_map/ppermute | solution.py:20
  15.1 1.0 %concatenate.32 = bf16[40,1284]{1,0:T(8,128)(2,1)S(1)} concatenate(bf16[40,1280]{1,0:T(8,128)(2,1)} %param.23, bf16[40,2]{1,0:T(8,128)(2,1)S(1)} %copy.73, bf16[40,2]{1,0:T(8,128)(2,1)S(1)} %copy.74), dimensions={1} | concatenate | bytes 205440 | tf_op jit(solution)/shard_map/concatenate | solution.py:123
  16.1 0.8 broadcast_in_dim.136
  16.9 4.1 %all-to-all-start = ((bf16[4,40,1284]{2,1,0:T(8,128)(2,1)}), bf16[4,40,1284]{2,1,0:T(8,128)(2,1)}, u32[]{:S(2)}, u32[]{:S(2)}) async-start(bf16[4,40,1284]{2,1,0:T(8,128)(2,1)} %broadcast_in_dim.136), calls=%async_computation | async-start | bytes 901120 | tf_op jit(solution)/shard_map/all_to_all | solution.py:125
  25.0 1.8 %divide_convert_fusion = bf16[512,1280]{1,0:T(8,128)(2,1)S(1)} fusion(bf16[512,1280]{1,0:T(8,128)(2,1)S(1)} %copy-done.4, bf16[3,1280]{1,0:T(4,128)(2,1)S(1)} %slice.202, f32[1280]{0:T(1024)S(1)} %get-tuple-element.18, f32[1280]{0:T(1024)S(1)} %get-tuple-element.19, f32[1280]{0:T(1024)S(1)} %get-tuple-element.17, f32[1280]{0:T(1024)S(1)} %get-tuple-element.16), kind=kLoop, calls=%fused_computation.29 | loop fusion | flops 15728640 | bytes 2649600 | tf_op jit(solution)/shard_map/convert_element_type | solution.py:36
  27.5 1.9 %divide_convert_fusion.1 = bf16[512,256]{1,0:T(8,128)(2,1)S(1)} fusion(bf16[512,256]{1,0:T(8,128)(2,1)} %param.15, bf16[3,256]{1,0:T(4,128)(2,1)S(1)} %slice.209, f32[256]{0:T(256)} %bitcast.131, f32[256]{0:T(256)} %bitcast.132, f32[256]{0:T(256)} %bitcast.130, f32[256]{0:T(256)} %bitcast.129), kind=kLoop, calls=%fused_computation.72 | loop fusion | flops 3145728 | bytes 529920 | tf_op jit(solution)/shard_map/convert_element_type | solution.py:36
  29.6 1.1 %convolution_add_fusion.3 = f32[20,64,128]{2,1,0:T(8,128)S(1)} fusion(bf16[256,20,64]{0,2,1:T(8,128)(2,1)S(1)} %bitcast.112, f32[256,20]{0,1:T(8,128)} %get-tuple-element.37, f32[20]{0:T(128)} %get-tuple-element.51, bf16[512,256]{1,0:T(8,128)(2,1)S(1)} %divide_convert_fusion.1), kind=kOutput, calls=%fused_computation.55 | convolution fusion | flops 85032960 | bytes 1396816 | tf_op jit(solution)/shard_map/jhp,js->hps/dot_general | solution.py:52
  30.6 1.1 %fusion.112 = (bf16[20,64,128]{2,1,0:T(8,128)(2,1)S(1)}, f32[20,64,128]{2,1,0:T(8,128)S(1)}) fusion(bf16[512,256]{1,0:T(8,128)(2,1)S(1)} %divide_convert_fusion.1, bf16[256,20,64]{0,2,1:T(8,128)(2,1)S(1)} %bitcast.114, f32[256,20]{0,1:T(8,128)} %get-tuple-element.38, f32[20,64,128]{2,1,0:T(8,128)S(1)} %convolution_add_fusion.3, f32[20]{0:T(128)} %get-tuple-element.54), kind=kOutput, calls=%fused_computation.186 | convolution fusion | flops 85360640 | bytes 2379856 | tf_op jit(solution)/shard_map/jhp,js->hps/dot_general | solution.py:52
  31.7 3.9 %collective-permute-start.1 = (bf16[20,64,128]{2,1,0:T(8,128)(2,1)S(1)}, bf16[20,64,128]{2,1,0:T(8,128)(2,1)S(1)}, u32[]{:S(2)}, u32[]{:S(2)}) collective-permute-start(bf16[20,64,128]{2,1,0:T(8,128)(2,1)S(1)} %get-tuple-element.55), channel_id=1, source_target_pairs={{0,4},{4,8},{8,12},{1,5},{5,9},{9,13},{2,6},{6,10},{10,14},{3,7},{... | collective-permute-start | bytes 983048 | tf_op jit(solution)/shard_map/ppermute | solution.py:20
  35.7 2.9 %fusion.4 = f32[20,64,256]{2,1,0:T(8,128)} fusion(bf16[256,20,64]{0,2,1:T(8,128)(2,1)S(1)} %bitcast.113, f32[20,256]{1,0:T(8,128)S(1)} %copy-done.17, f32[256,256]{1,0:T(8,128)S(1)} %fusion.82, f32[20,256]{1,0:T(8,128)S(1)} %bitcast.119, pred[256,256]{1,0:T(8,128)(4,1)S(1)} %copy-done.13), kind=kOutput, calls=%fused_computation.7 | convolution fusion | flops 175636480 | bytes 2334720 | tf_op jit(solution)/shard_map/hij,jhp->hpi/dot_general | solution.py:49
  38.9 2.9 %collective-permute-done.1 = bf16[20,64,128]{2,1,0:T(8,128)(2,1)S(1)} collective-permute-done((bf16[20,64,128]{2,1,0:T(8,128)(2,1)S(1)}, bf16[20,64,128]{2,1,0:T(8,128)(2,1)S(1)}, u32[]{:S(2)}, u32[]{:S(2)}) %collective-permute-start.1) | collective-permute-done | bytes 327712 | tf_op jit(solution)/shard_map/ppermute | solution.py:20
  41.9 5.5 %collective-permute-start.2 = (bf16[20,64,128]{2,1,0:T(8,128)(2,1)S(1)}, bf16[20,64,128]{2,1,0:T(8,128)(2,1)S(1)}, u32[]{:S(2)}, u32[]{:S(2)}) collective-permute-start(bf16[20,64,128]{2,1,0:T(8,128)(2,1)S(1)} %fusion.51), channel_id=1, source_target_pairs={{0,8},{4,12},{1,9},{5,13},{2,10},{6,14},{3,11},{7,15},{16,24},{20,... | collective-permute-start | bytes 983048 | tf_op jit(solution)/shard_map/ppermute | solution.py:20
  47.4 2.9 %fusion.5 = f32[20,64,256]{2,1,0:T(8,128)} fusion(bf16[256,20,64]{0,2,1:T(8,128)(2,1)S(1)} %bitcast.115, f32[20,256]{1,0:T(8,128)S(1)} %copy-done.16, f32[256,256]{1,0:T(8,128)S(1)} %fusion.78, f32[20,256]{1,0:T(8,128)S(1)} %bitcast.122, pred[256,256]{1,0:T(8,128)(4,1)S(1)} %copy-done.13), kind=kOutput, calls=%fused_computation.8 | convolution fusion | flops 175636480 | bytes 2334720 | tf_op jit(solution)/shard_map/hij,jhp->hpi/dot_general | solution.py:49
  50.4 1.5 %copy.71 = bf16[512,1280]{0,1:T(8,128)(2,1)} copy(bf16[512,1280]{1,0:T(8,128)(2,1)S(1)} %divide_convert_fusion) | data formatting | bytes 2621440 | tf_op jit(solution)/shard_map/layout_constraint | solution.py:135
  51.8 1.6 %copy.72 = bf16[512,1280]{0,1:T(8,128)(2,1)S(1)} copy(bf16[512,1280]{1,0:T(8,128)(2,1)} %param.14) | data formatting | bytes 2621440 | tf_op jit(solution)/shard_map/optimization_barrier | solution.py:69
  53.5 0.9 slice_convert_fusion
  55.6 0.9 copy-done.6
  56.9 0.9 copy-done.1
  57.8 1.5 %multiply_reduce_fusion = (f32[512]{0:T(512)S(1)}, f32[1280,512]{1,0:T(8,128)S(1)}) fusion(bf16[512,1280]{0,1:T(8,128)(2,1)S(1)} %copy.72, bf16[512,1280]{0,1:T(8,128)(2,1)S(1)} %copy-done.1, f32[1280]{0:T(1024)S(1)} %mul.351, f32[1280,256]{1,0:T(8,128)S(1)} %bitcast.111, f32[1280,256]{1,0:T(8,128)S(1)} %bitcast.110), kind=kLoop, calls=%fused_computation.18 | loop fusion | flops 7208448 | bytes 7871488 | tf_op jit(solution)/shard_map/reduce_sum | solution.py:172
  59.7 0.9 collective-permute-done.4
  60.6 1.5 %collective-permute-start.5 = (f32[512]{0:T(512)S(1)}, f32[512]{0:T(512)S(1)}, u32[]{:S(2)}, u32[]{:S(2)}) collective-permute-start(f32[512]{0:T(512)S(1)} %add.182), channel_id=1, source_target_pairs={{0,2},{1,3},{2,0},{3,1},{4,6},{5,7},{6,4},{7,5},{8,10},{9,11},{10,... | collective-permute-start | bytes 6152 | tf_op jit(solution)/shard_map/ppermute | solution.py:84
  62.2 2.0 %collective-permute-done.5 = f32[512]{0:T(512)S(1)} collective-permute-done((f32[512]{0:T(512)S(1)}, f32[512]{0:T(512)S(1)}, u32[]{:S(2)}, u32[]{:S(2)}) %collective-permute-start.5) | collective-permute-done | bytes 2080 | tf_op jit(solution)/shard_map/ppermute | solution.py:84
  65.1 0.9 gather_fusion
  66.2 2.2 %fusion.113 = (bf16[8,160]{1,0:T(8,128)(2,1)S(1)}, f32[8,160,128]{2,1,0:T(8,128)S(1)}) fusion(bf16[160,1284]{1,0:T(8,128)(2,1)} %bitcast.19, pred[8,1280]{1,0:T(8,128)(4,1)S(1)} %copy-done.18, bf16[128,1280]{1,0:T(8,128)(2,1)S(1)} %broadcast_select_fusion, pred[160,128]{1,0:T(8,128)(4,1)S(1)} %compare_and_fusion), kind=kOutput, calls=%fused_computation.187 | convolution fusion | flops 421231360 | bytes 1425920 | tf_op jit(solution)/shard_map/pc,asc->aps/dot_general | solution.py:191
  70.3 6.6 %collective-permute-start.6 = (bf16[40,1304]{1,0:T(8,128)(2,1)S(1)}, bf16[40,1304]{1,0:T(8,128)(2,1)S(1)}, u32[]{:S(2)}, u32[]{:S(2)}) collective-permute-start(bf16[40,1304]{1,0:T(8,128)(2,1)S(1)} %get-tuple-element.35), channel_id=1, source_target_pairs={{0,4},{4,8},{8,12},{12,0},{1,5},{5,9},{9,13},{13,1},{2,6},{6,10},{... | collective-permute-start | bytes 312968 | tf_op jit(solution)/shard_map/ppermute | solution.py:218
  76.9 3.4 %collective-permute-start.7 = (bf16[40,1304]{1,0:T(8,128)(2,1)S(1)}, bf16[40,1304]{1,0:T(8,128)(2,1)S(1)}, u32[]{:S(2)}, u32[]{:S(2)}) collective-permute-start(bf16[40,1304]{1,0:T(8,128)(2,1)S(1)} %get-tuple-element.34), channel_id=1, source_target_pairs={{0,8},{4,12},{8,0},{12,4},{1,9},{5,13},{9,1},{13,5},{2,10},{6,14},... | collective-permute-start | bytes 312968 | tf_op jit(solution)/shard_map/ppermute | solution.py:218
  80.3 3.5 %collective-permute-done.6 = bf16[40,1304]{1,0:T(8,128)(2,1)S(1)} collective-permute-done((bf16[40,1304]{1,0:T(8,128)(2,1)S(1)}, bf16[40,1304]{1,0:T(8,128)(2,1)S(1)}, u32[]{:S(2)}, u32[]{:S(2)}) %collective-permute-start.6) | collective-permute-done | bytes 104352 | tf_op jit(solution)/shard_map/ppermute | solution.py:218
  83.8 3.2 %collective-permute-done.7 = bf16[40,1304]{1,0:T(8,128)(2,1)S(1)} collective-permute-done((bf16[40,1304]{1,0:T(8,128)(2,1)S(1)}, bf16[40,1304]{1,0:T(8,128)(2,1)S(1)}, u32[]{:S(2)}, u32[]{:S(2)}) %collective-permute-start.7) | collective-permute-done | bytes 104352 | tf_op jit(solution)/shard_map/ppermute | solution.py:218
  88.7 0.9 copy.82
  (135 shorter events, 16.0 us)
Async XLA Ops:
  0.6 24.4 %copy-start.4 = (bf16[512,1280]{1,0:T(8,128)(2,1)S(1)}, bf16[512,1280]{1,0:T(8,128)(2,1)}, u32[]{:S(2)}) copy-start(bf16[512,1280]{1,0:T(8,128)(2,1)} %param.13) | copy-start | bytes 3932164
  0.6 21.0 %copy-start.14 = (f32[20,512]{1,0:T(8,128)S(1)}, f32[20,512]{1,0:T(8,128)}, u32[]{:S(2)}) copy-start(f32[20,512]{1,0:T(8,128)} %param.16) | copy-start | bytes 122884
  0.7 21.7 %copy-start.20 = (bf16[4,256]{1,0:T(4,128)(2,1)S(1)}, bf16[4,256]{1,0:T(4,128)(2,1)}, u32[]{:S(2)}) copy-start(bf16[4,256]{1,0:T(4,128)(2,1)} %param.20) | copy-start | bytes 6148
  0.7 22.3 %copy-start.15 = (bf16[4,1280]{1,0:T(4,128)(2,1)S(1)}, bf16[4,1280]{1,0:T(4,128)(2,1)}, u32[]{:S(2)}) copy-start(bf16[4,1280]{1,0:T(4,128)(2,1)} %param.19) | copy-start | bytes 30724
  0.7 22.4 %copy-start.26 = (s32[128]{0:T(128)S(1)}, s32[128]{0:T(128)}, u32[]{:S(2)}) copy-start(s32[128]{0:T(128)} %param.22) | copy-start | bytes 1540
  0.7 24.1 %copy-start.24 = (f32[20]{0:T(128)S(1)}, f32[20]{0:T(128)}, u32[]{:S(2)}) copy-start(f32[20]{0:T(128)} %param.18) | copy-start | bytes 244
  2.2 22.7 %collective-permute-start = (bf16[3,1536]{1,0:T(4,128)(2,1)S(1)}, bf16[3,1536]{1,0:T(4,128)(2,1)S(1)}, u32[]{:S(2)}, u32[]{:S(2)}) collective-permute-start(bf16[3,1536]{1,0:T(4,128)(2,1)S(1)} %pad_maximum_fusion.3), channel_id=1, source_target_pairs={{0,4},{4,8},{8,12},{1,5},{5,9},{9,13},{2,6},{6,10},{10,14},{3,7},{... | collective-permute-start | bytes 27656 | tf_op jit(solution)/shard_map/ppermute | solution.py:20
  8.9 16.1 %copy-start.7 = (f32[3,8,2,128]{3,1,2,0:T(8,128)}, f32[3,8,2,128]{3,1,2,0:T(8,128)S(1)}, u32[]{:S(2)}) copy-start(f32[3,8,2,128]{3,1,2,0:T(8,128)S(1)} %copy.84) | copy-start | bytes 73732
  9.9 15.1 %copy-start.9 = (f32[3,8,2,128]{3,1,2,0:T(8,128)}, f32[3,8,2,128]{3,1,2,0:T(8,128)S(1)}, u32[]{:S(2)}) copy-start(f32[3,8,2,128]{3,1,2,0:T(8,128)S(1)} %copy.85) | copy-start | bytes 73732
  10.7 14.3 %collective-permute-start.3 = (f32[20]{0:T(128)S(1)}, f32[20]{0:T(128)S(1)}, u32[]{:S(2)}, u32[]{:S(2)}) collective-permute-start(f32[20]{0:T(128)S(1)} %get-tuple-element.53), channel_id=1, source_target_pairs={{0,4},{4,8},{8,12},{1,5},{5,9},{9,13},{2,6},{6,10},{10,14},{3,7},{... | collective-permute-start | bytes 248 | tf_op jit(solution)/shard_map/ppermute | solution.py:20
  16.9 36.6 %all-to-all-start = ((bf16[4,40,1284]{2,1,0:T(8,128)(2,1)}), bf16[4,40,1284]{2,1,0:T(8,128)(2,1)}, u32[]{:S(2)}, u32[]{:S(2)}) async-start(bf16[4,40,1284]{2,1,0:T(8,128)(2,1)} %broadcast_in_dim.136), calls=%async_computation | async-start | bytes 901120 | tf_op jit(solution)/shard_map/all_to_all | solution.py:125
  27.4 4.3 %copy-start.2 = (bf16[256,1280]{0,1:T(8,128)(2,1)}, bf16[256,1280]{0,1:T(8,128)(2,1)S(1)}, u32[]{:S(2)}) copy-start(bf16[256,1280]{0,1:T(8,128)(2,1)S(1)} %copy.70) | copy-start | bytes 1966084
  27.4 8.2 %copy-start.8 = (f32[3,8,2,128]{3,1,2,0:T(8,128)S(1)}, f32[3,8,2,128]{3,1,2,0:T(8,128)}, u32[]{:S(2)}) copy-start(f32[3,8,2,128]{3,1,2,0:T(8,128)} %copy-done.7) | copy-start | bytes 73732
  27.4 8.2 %copy-start.13 = (pred[256,256]{1,0:T(8,128)(4,1)S(1)}, pred[256,256]{1,0:T(8,128)(4,1)}, u32[]{:S(2)}) copy-start(pred[256,256]{1,0:T(8,128)(4,1)} %iota_compare_fusion) | copy-start | bytes 196612
  27.4 8.2 %copy-start.17 = (f32[20,256]{1,0:T(8,128)S(1)}, f32[20,256]{1,0:T(8,128)}, u32[]{:S(2)}) copy-start(f32[20,256]{1,0:T(8,128)} %get-tuple-element.36) | copy-start | bytes 61444
  31.7 10.0 %collective-permute-start.1 = (bf16[20,64,128]{2,1,0:T(8,128)(2,1)S(1)}, bf16[20,64,128]{2,1,0:T(8,128)(2,1)S(1)}, u32[]{:S(2)}, u32[]{:S(2)}) collective-permute-start(bf16[20,64,128]{2,1,0:T(8,128)(2,1)S(1)} %get-tuple-element.55), channel_id=1, source_target_pairs={{0,4},{4,8},{8,12},{1,5},{5,9},{9,13},{2,6},{6,10},{10,14},{3,7},{... | collective-permute-start | bytes 983048 | tf_op jit(solution)/shard_map/ppermute | solution.py:20
  35.7 6.1 %copy-start.22 = (f32[20]{0:T(128)S(1)}, f32[20]{0:T(128)}, u32[]{:S(2)}) copy-start(f32[20]{0:T(128)} %get-tuple-element.52) | copy-start | bytes 244
  35.7 11.7 %copy-start.3 = (bf16[256,1280]{0,1:T(8,128)(2,1)S(1)}, bf16[256,1280]{0,1:T(8,128)(2,1)}, u32[]{:S(2)}) copy-start(bf16[256,1280]{0,1:T(8,128)(2,1)} %copy-done.2) | copy-start | bytes 1966084
  35.7 11.7 %copy-start.10 = (f32[3,8,2,128]{3,1,2,0:T(8,128)S(1)}, f32[3,8,2,128]{3,1,2,0:T(8,128)}, u32[]{:S(2)}) copy-start(f32[3,8,2,128]{3,1,2,0:T(8,128)} %copy-done.9) | copy-start | bytes 73732
  35.7 11.7 %copy-start.16 = (f32[20,256]{1,0:T(8,128)S(1)}, f32[20,256]{1,0:T(8,128)}, u32[]{:S(2)}) copy-start(f32[20,256]{1,0:T(8,128)} %get-tuple-element.39) | copy-start | bytes 61444
  41.9 12.5 %collective-permute-start.2 = (bf16[20,64,128]{2,1,0:T(8,128)(2,1)S(1)}, bf16[20,64,128]{2,1,0:T(8,128)(2,1)S(1)}, u32[]{:S(2)}, u32[]{:S(2)}) collective-permute-start(bf16[20,64,128]{2,1,0:T(8,128)(2,1)S(1)} %fusion.51), channel_id=1, source_target_pairs={{0,8},{4,12},{1,9},{5,13},{2,10},{6,14},{3,11},{7,15},{16,24},{20,... | collective-permute-start | bytes 983048 | tf_op jit(solution)/shard_map/ppermute | solution.py:20
  51.8 2.9 %copy-start.21 = (f32[20]{0:T(128)S(1)}, f32[20]{0:T(128)}, u32[]{:S(2)}) copy-start(f32[20]{0:T(128)} %get-tuple-element.50) | copy-start | bytes 244
  53.5 1.7 %copy-start.12 = (f32[20,256]{1,0:T(8,128)S(1)}, f32[20,256]{1,0:T(8,128)}, u32[]{:S(2)}) copy-start(f32[20,256]{1,0:T(8,128)} %get-tuple-element.43) | copy-start | bytes 61444
  53.5 1.7 %copy-start.5 = (f32[20,64,256]{2,1,0:T(8,128)S(1)}, f32[20,64,256]{2,1,0:T(8,128)}, u32[]{:S(2)}) copy-start(f32[20,64,256]{2,1,0:T(8,128)} %fusion.4) | copy-start | bytes 3932164
  57.8 4.2 %copy-start.25 = (s32[128]{0:T(128)S(1)}, s32[128]{0:T(128)}, u32[]{:S(2)}) copy-start(s32[128]{0:T(128)} %iota_add_fusion) | copy-start | bytes 1540
  57.8 6.3 %copy-start.19 = (f32[1280]{0:T(1024)S(1)}, f32[1280]{0:T(1024)}, u32[]{:S(2)}) copy-start(f32[1280]{0:T(1024)} %param.21) | copy-start | bytes 15364
  59.3 1.2 %collective-permute-start.4 = (f32[512]{0:T(512)S(1)}, f32[512]{0:T(512)S(1)}, u32[]{:S(2)}, u32[]{:S(2)}) collective-permute-start(f32[512]{0:T(512)S(1)} %get-tuple-element.26), channel_id=1, source_target_pairs={{0,1},{1,0},{2,3},{3,2},{4,5},{5,4},{6,7},{7,6},{8,9},{9,8},{10,11... | collective-permute-start | bytes 6152 | tf_op jit(solution)/shard_map/ppermute | solution.py:84
  60.6 3.6 %collective-permute-start.5 = (f32[512]{0:T(512)S(1)}, f32[512]{0:T(512)S(1)}, u32[]{:S(2)}, u32[]{:S(2)}) collective-permute-start(f32[512]{0:T(512)S(1)} %add.182), channel_id=1, source_target_pairs={{0,2},{1,3},{2,0},{3,1},{4,6},{5,7},{6,4},{7,5},{8,10},{9,11},{10,... | collective-permute-start | bytes 6152 | tf_op jit(solution)/shard_map/ppermute | solution.py:84
  65.1 3.3 %copy-start = (bf16[512,1280]{1,0:T(8,128)(2,1)}, bf16[512,1280]{1,0:T(8,128)(2,1)S(1)}, u32[]{:S(2)}) copy-start(bf16[512,1280]{1,0:T(8,128)(2,1)S(1)} %copy.81) | copy-start | bytes 3932164
  70.3 13.5 %collective-permute-start.6 = (bf16[40,1304]{1,0:T(8,128)(2,1)S(1)}, bf16[40,1304]{1,0:T(8,128)(2,1)S(1)}, u32[]{:S(2)}, u32[]{:S(2)}) collective-permute-start(bf16[40,1304]{1,0:T(8,128)(2,1)S(1)} %get-tuple-element.35), channel_id=1, source_target_pairs={{0,4},{4,8},{8,12},{12,0},{1,5},{5,9},{9,13},{13,1},{2,6},{6,10},{... | collective-permute-start | bytes 312968 | tf_op jit(solution)/shard_map/ppermute | solution.py:218
  76.9 10.1 %collective-permute-start.7 = (bf16[40,1304]{1,0:T(8,128)(2,1)S(1)}, bf16[40,1304]{1,0:T(8,128)(2,1)S(1)}, u32[]{:S(2)}, u32[]{:S(2)}) collective-permute-start(bf16[40,1304]{1,0:T(8,128)(2,1)S(1)} %get-tuple-element.34), channel_id=1, source_target_pairs={{0,8},{4,12},{8,0},{12,4},{1,9},{5,13},{9,1},{13,5},{2,10},{6,14},... | collective-permute-start | bytes 312968 | tf_op jit(solution)/shard_map/ppermute | solution.py:218
  80.3 7.0 %collective-permute-start.8 = (bf16[40,1304]{1,0:T(8,128)(2,1)S(1)}, bf16[40,1304]{1,0:T(8,128)(2,1)S(1)}, u32[]{:S(2)}, u32[]{:S(2)}) collective-permute-start(bf16[40,1304]{1,0:T(8,128)(2,1)S(1)} %get-tuple-element.33), channel_id=1, source_target_pairs={{0,12},{4,0},{8,4},{12,8},{1,13},{5,1},{9,5},{13,9},{2,14},{6,2},{... | collective-permute-start | bytes 312968 | tf_op jit(solution)/shard_map/ppermute | solution.py:218
  (5 other events, 7.2 us)

commit v16 on v15

--- a/solution.py
+++ b/solution.py
@@ -176,7 +176,12 @@
     ).astype(jnp.bfloat16)
     mixed_seq = mixed_major.T
     local_ends = seg_ends - lax.axis_index("seq") * tok_rows
-    summaries = jnp.take(mixed_seq, local_ends, axis=0)
+    picks = (
+        lax.broadcasted_iota(jnp.int32, (tok_rows, local_ends.shape[0]), 0) == local_ends[None, :]
+    ).astype(jnp.bfloat16)
+    summaries = (
+        jnp.einsum("ct,ts->sc", mixed_major, picks, preferred_element_type=jnp.float32)
+    ).astype(jnp.bfloat16)
     pool_heads_local = POOL_HEADS // lax.axis_size("tensor")
     pool_width = channels // pool_heads_local
     scale_factor = 1.0 / math.sqrt(pool_width)

time: 90.3 us -> 91.5 us (1.013)
  local copies, waits for them, and re-layouts: 14.3 us -> 18.5 us
  waiting for transfers between devices: 12.7 us -> 8.95 us
    ppermute x3, waiting for transfers between devices: 6.98 us -> 3.19 us  [local(): lax.ppermute(chunk, 'seq', [(i, (i + shift) % seq_count) for i in range(s...]
    unnamed x60 -> x58, local copies, waits for them, and re-layouts: 3.42 us -> 5.61 us
    transpose x1, other arithmetic: 0.33 us -> 1.36 us  [local(): mixed_seq = mixed_major.T]
  transfers between devices with their start and end apart: 10 -> 10, of which waited for: 6 -> 5; matrix products, arithmetic and copies ran while one was open for 30% -> 35% of each run, Pallas kernels for 0% -> 0%
where the time goes in v16:
time: 91.5 us; the launch traced here: 90.8 us
  starting transfers between devices  32.7 us (36%)
  local copies, waits for them, and re-layouts  18.5 us (20%)
  other arithmetic  15.7 us (17%)
  matrix products  13.6 us (15%)
  waiting for transfers between devices  8.95 us (10%)
  between operations  1.31 us (1%)
    ppermute x4, starting transfers between devices, passed_along(): lax.ppermute(value, axis, [(source, source + steps) for source in range(l...  17.8 us
    ppermute x3, starting transfers between devices, local(): lax.ppermute(chunk, 'seq', [(i, (i + shift) % seq_count) for i in range(s...  9.22 us
    dot_general x2, matrix products, stretch_local(): jnp.einsum('hij,jhp->hpi', mixing, x_block, preferred_element_type=jnp.fl...  5.85 us
    unnamed x58, local copies, waits for them, and re-layouts  5.61 us
    all_to_all x1, starting transfers between devices, local(): lax.all_to_all(query_rows.reshape(seq_count * pools_local, -1), 'seq', 0,...  4.12 us
    convert_element_type x2, other arithmetic, causal_conv(): return silu_act(summed).astype(jnp.bfloat16)  3.73 us
    ppermute x3, waiting for transfers between devices, local(): lax.ppermute(chunk, 'seq', [(i, (i + shift) % seq_count) for i in range(s...  3.19 us
    ppermute x4, waiting for transfers between devices, passed_along(): lax.ppermute(value, axis, [(source, source + steps) for source in range(l...  2.9 us
  transfers between devices with their start and end apart: 10, of which 5 were waited for; matrix products, arithmetic and copies ran while one was open for 35% of the time, Pallas kernels for 0%

profile of v16, /device:TPU:0, one launch (start us, length us, event | category | flops | bytes accessed | tf_op | source)
XLA Modules:
  0.0 90.8 jit_solution(10109537899436404031)
XLA Ops:
  0.7 0.8 slice.153
  2.2 5.0 %collective-permute-start = (bf16[3,1536]{1,0:T(4,128)(2,1)S(1)}, bf16[3,1536]{1,0:T(4,128)(2,1)S(1)}, u32[]{:S(2)}, u32[]{:S(2)}) collective-permute-start(bf16[3,1536]{1,0:T(4,128)(2,1)S(1)} %pad_maximum_fusion.3), channel_id=1, source_target_pairs={{0,4},{4,8},{8,12},{1,5},{5,9},{9,13},{2,6},{6,10},{10,14},{3,7},{... | collective-permute-start | bytes 27656 | tf_op jit(solution)/shard_map/ppermute | solution.py:20
  10.7 3.5 %collective-permute-start.3 = (f32[20]{0:T(128)S(1)}, f32[20]{0:T(128)S(1)}, u32[]{:S(2)}, u32[]{:S(2)}) collective-permute-start(f32[20]{0:T(128)S(1)} %get-tuple-element.51), channel_id=1, source_target_pairs={{0,4},{4,8},{8,12},{1,5},{5,9},{9,13},{2,6},{6,10},{10,14},{3,7},{... | collective-permute-start | bytes 248 | tf_op jit(solution)/shard_map/ppermute | solution.py:20
  15.1 1.0 %concatenate.32 = bf16[40,1284]{1,0:T(8,128)(2,1)S(1)} concatenate(bf16[40,1280]{1,0:T(8,128)(2,1)} %param.23, bf16[40,2]{1,0:T(8,128)(2,1)S(1)} %copy.70, bf16[40,2]{1,0:T(8,128)(2,1)S(1)} %copy.71), dimensions={1} | concatenate | bytes 205440 | tf_op jit(solution)/shard_map/concatenate | solution.py:123
  16.1 0.8 broadcast_in_dim.75
  16.9 4.1 %all-to-all-start = ((bf16[4,40,1284]{2,1,0:T(8,128)(2,1)}), bf16[4,40,1284]{2,1,0:T(8,128)(2,1)}, u32[]{:S(2)}, u32[]{:S(2)}) async-start(bf16[4,40,1284]{2,1,0:T(8,128)(2,1)} %broadcast_in_dim.75), calls=%async_computation | async-start | bytes 901120 | tf_op jit(solution)/shard_map/all_to_all | solution.py:125
  25.0 1.8 %divide_convert_fusion = bf16[512,1280]{1,0:T(8,128)(2,1)S(1)} fusion(bf16[512,1280]{1,0:T(8,128)(2,1)S(1)} %copy-done.4, bf16[3,1280]{1,0:T(4,128)(2,1)S(1)} %slice.200, f32[1280]{0:T(1024)S(1)} %get-tuple-element.18, f32[1280]{0:T(1024)S(1)} %get-tuple-element.19, f32[1280]{0:T(1024)S(1)} %get-tuple-element.17, f32[1280]{0:T(1024)S(1)} %get-tuple-element.16), kind=kLoop, calls=%fused_computation.28 | loop fusion | flops 15728640 | bytes 2649600 | tf_op jit(solution)/shard_map/convert_element_type | solution.py:36
  27.5 1.9 %divide_convert_fusion.1 = bf16[512,256]{1,0:T(8,128)(2,1)S(1)} fusion(bf16[512,256]{1,0:T(8,128)(2,1)} %param.15, bf16[3,256]{1,0:T(4,128)(2,1)S(1)} %slice.207, f32[256]{0:T(256)} %bitcast.131, f32[256]{0:T(256)} %bitcast.132, f32[256]{0:T(256)} %bitcast.130, f32[256]{0:T(256)} %bitcast.129), kind=kLoop, calls=%fused_computation.71 | loop fusion | flops 3145728 | bytes 529920 | tf_op jit(solution)/shard_map/convert_element_type | solution.py:36
  29.6 1.1 %convolution_add_fusion.3 = f32[20,64,128]{2,1,0:T(8,128)S(1)} fusion(bf16[256,20,64]{0,2,1:T(8,128)(2,1)S(1)} %bitcast.112, f32[256,20]{0,1:T(8,128)} %get-tuple-element.35, f32[20]{0:T(128)} %get-tuple-element.49, bf16[512,256]{1,0:T(8,128)(2,1)S(1)} %divide_convert_fusion.1), kind=kOutput, calls=%fused_computation.54 | convolution fusion | flops 85032960 | bytes 1396816 | tf_op jit(solution)/shard_map/jhp,js->hps/dot_general | solution.py:52
  30.7 1.1 %fusion.115 = (bf16[20,64,128]{2,1,0:T(8,128)(2,1)S(1)}, f32[20,64,128]{2,1,0:T(8,128)S(1)}) fusion(bf16[512,256]{1,0:T(8,128)(2,1)S(1)} %divide_convert_fusion.1, bf16[256,20,64]{0,2,1:T(8,128)(2,1)S(1)} %bitcast.114, f32[256,20]{0,1:T(8,128)} %get-tuple-element.36, f32[20,64,128]{2,1,0:T(8,128)S(1)} %convolution_add_fusion.3, f32[20]{0:T(128)} %get-tuple-element.52), kind=kOutput, calls=%fused_computation.186 | convolution fusion | flops 85360640 | bytes 2379856 | tf_op jit(solution)/shard_map/jhp,js->hps/dot_general | solution.py:52
  31.8 3.9 %collective-permute-start.1 = (bf16[20,64,128]{2,1,0:T(8,128)(2,1)S(1)}, bf16[20,64,128]{2,1,0:T(8,128)(2,1)S(1)}, u32[]{:S(2)}, u32[]{:S(2)}) collective-permute-start(bf16[20,64,128]{2,1,0:T(8,128)(2,1)S(1)} %get-tuple-element.53), channel_id=1, source_target_pairs={{0,4},{4,8},{8,12},{1,5},{5,9},{9,13},{2,6},{6,10},{10,14},{3,7},{... | collective-permute-start | bytes 983048 | tf_op jit(solution)/shard_map/ppermute | solution.py:20
  35.8 2.9 %fusion.4 = f32[20,64,256]{2,1,0:T(8,128)} fusion(bf16[256,20,64]{0,2,1:T(8,128)(2,1)S(1)} %bitcast.113, f32[20,256]{1,0:T(8,128)S(1)} %copy-done.18, f32[256,256]{1,0:T(8,128)S(1)} %fusion.84, f32[20,256]{1,0:T(8,128)S(1)} %bitcast.119, pred[256,256]{1,0:T(8,128)(4,1)S(1)} %copy-done.13), kind=kOutput, calls=%fused_computation.6 | convolution fusion | flops 175636480 | bytes 2334720 | tf_op jit(solution)/shard_map/hij,jhp->hpi/dot_general | solution.py:49
  38.9 2.9 %collective-permute-done.1 = bf16[20,64,128]{2,1,0:T(8,128)(2,1)S(1)} collective-permute-done((bf16[20,64,128]{2,1,0:T(8,128)(2,1)S(1)}, bf16[20,64,128]{2,1,0:T(8,128)(2,1)S(1)}, u32[]{:S(2)}, u32[]{:S(2)}) %collective-permute-start.1) | collective-permute-done | bytes 327712 | tf_op jit(solution)/shard_map/ppermute | solution.py:20
  41.9 5.5 %collective-permute-start.2 = (bf16[20,64,128]{2,1,0:T(8,128)(2,1)S(1)}, bf16[20,64,128]{2,1,0:T(8,128)(2,1)S(1)}, u32[]{:S(2)}, u32[]{:S(2)}) collective-permute-start(bf16[20,64,128]{2,1,0:T(8,128)(2,1)S(1)} %fusion.50), channel_id=1, source_target_pairs={{0,8},{4,12},{1,9},{5,13},{2,10},{6,14},{3,11},{7,15},{16,24},{20,... | collective-permute-start | bytes 983048 | tf_op jit(solution)/shard_map/ppermute | solution.py:20
  47.5 2.9 %fusion.5 = f32[20,64,256]{2,1,0:T(8,128)} fusion(bf16[256,20,64]{0,2,1:T(8,128)(2,1)S(1)} %bitcast.115, f32[20,256]{1,0:T(8,128)S(1)} %copy-done.17, f32[256,256]{1,0:T(8,128)S(1)} %fusion.80, f32[20,256]{1,0:T(8,128)S(1)} %bitcast.122, pred[256,256]{1,0:T(8,128)(4,1)S(1)} %copy-done.13), kind=kOutput, calls=%fused_computation.7 | convolution fusion | flops 175636480 | bytes 2334720 | tf_op jit(solution)/shard_map/hij,jhp->hpi/dot_general | solution.py:49
  50.4 1.5 %copy.68 = bf16[512,1280]{0,1:T(8,128)(2,1)} copy(bf16[512,1280]{1,0:T(8,128)(2,1)S(1)} %divide_convert_fusion) | data formatting | bytes 2621440 | tf_op jit(solution)/shard_map/layout_constraint | solution.py:135
  51.8 2.4 %copy.69 = bf16[512,1280]{0,1:T(8,128)(2,1)} copy(bf16[512,1280]{1,0:T(8,128)(2,1)} %param.14) | data formatting | bytes 2621440 | tf_op jit(solution)/shard_map/optimization_barrier | solution.py:69
  54.3 0.9 slice_convert_fusion
  56.4 0.9 copy-done.6
  57.7 0.9 copy-done
  59.0 1.5 %multiply_reduce_fusion = (f32[512]{0:T(512)S(1)}, f32[1280,512]{1,0:T(8,128)S(1)}) fusion(bf16[512,1280]{0,1:T(8,128)(2,1)S(1)} %copy-done.1, bf16[512,1280]{0,1:T(8,128)(2,1)S(1)} %copy-done, f32[1280]{0:T(1024)S(1)} %mul.351, f32[1280,256]{1,0:T(8,128)S(1)} %bitcast.111, f32[1280,256]{1,0:T(8,128)S(1)} %bitcast.110), kind=kLoop, calls=%fused_computation.17 | loop fusion | flops 7208448 | bytes 7871488 | tf_op jit(solution)/shard_map/reduce_sum | solution.py:172
  60.8 0.9 collective-permute-done.4
  61.7 1.5 %collective-permute-start.5 = (f32[512]{0:T(512)S(1)}, f32[512]{0:T(512)S(1)}, u32[]{:S(2)}, u32[]{:S(2)}) collective-permute-start(f32[512]{0:T(512)S(1)} %add.174), channel_id=1, source_target_pairs={{0,2},{1,3},{2,0},{3,1},{4,6},{5,7},{6,4},{7,5},{8,10},{9,11},{10,... | collective-permute-start | bytes 6152 | tf_op jit(solution)/shard_map/ppermute | solution.py:84
  63.3 2.0 %collective-permute-done.5 = f32[512]{0:T(512)S(1)} collective-permute-done((f32[512]{0:T(512)S(1)}, f32[512]{0:T(512)S(1)}, u32[]{:S(2)}, u32[]{:S(2)}) %collective-permute-start.5) | collective-permute-done | bytes 2080 | tf_op jit(solution)/shard_map/ppermute | solution.py:84
  66.1 2.2 %fusion.116 = (bf16[8,160]{1,0:T(8,128)(2,1)S(1)}, f32[8,160,128]{2,1,0:T(8,128)S(1)}) fusion(bf16[160,1284]{1,0:T(8,128)(2,1)} %bitcast.19, pred[8,1280]{1,0:T(8,128)(4,1)S(1)} %copy-done.19, bf16[128,1280]{1,0:T(8,128)(2,1)S(1)} %convolution_convert_fusion, pred[160,128]{1,0:T(8,128)(4,1)S(1)} %compare_and_fusion), kind=kOutput, calls=%fused_computation.187 | convolution fusion | flops 421231360 | bytes 1425920 | tf_op jit(solution)/shard_map/pc,asc->aps/dot_general | solution.py:196
  71.3 0.9 %concatenate.33 = bf16[160,1304]{1,0:T(8,128)(2,1)S(1)} concatenate(bf16[160,1280]{1,0:T(8,128)(2,1)S(1)} %fusion.27, bf16[160,8]{1,0:T(8,128)(2,1)} %copy.72, bf16[160,8]{1,0:T(8,128)(2,1)S(1)} %copy.73, bf16[160,8]{1,0:T(8,128)(2,1)} %copy.74), dimensions={1} | concatenate | bytes 834560 | tf_op jit(solution)/shard_map/concatenate | solution.py:208
  72.3 5.8 %collective-permute-start.6 = (bf16[40,1304]{1,0:T(8,128)(2,1)S(1)}, bf16[40,1304]{1,0:T(8,128)(2,1)S(1)}, u32[]{:S(2)}, u32[]{:S(2)}) collective-permute-start(bf16[40,1304]{1,0:T(8,128)(2,1)S(1)} %get-tuple-element.33), channel_id=1, source_target_pairs={{0,4},{4,8},{8,12},{12,0},{1,5},{5,9},{9,13},{13,1},{2,6},{6,10},{... | collective-permute-start | bytes 312968 | tf_op jit(solution)/shard_map/ppermute | solution.py:223
  78.1 3.4 %collective-permute-start.7 = (bf16[40,1304]{1,0:T(8,128)(2,1)S(1)}, bf16[40,1304]{1,0:T(8,128)(2,1)S(1)}, u32[]{:S(2)}, u32[]{:S(2)}) collective-permute-start(bf16[40,1304]{1,0:T(8,128)(2,1)S(1)} %get-tuple-element.32), channel_id=1, source_target_pairs={{0,8},{4,12},{8,0},{12,4},{1,9},{5,13},{9,1},{13,5},{2,10},{6,14},... | collective-permute-start | bytes 312968 | tf_op jit(solution)/shard_map/ppermute | solution.py:223
  81.5 1.4 %fusion.107 = bf16[512,1280]{0,1:T(8,128)(2,1)} fusion(f32[1280]{0:T(1024)S(1)} %copy-done.16, f32[1280,512]{1,0:T(8,128)S(1)} %get-tuple-element.25, f32[512]{0:T(512)S(1)} %add_rsqrt_fusion), kind=kLoop, calls=%fused_computation.180 | loop fusion | flops 1966080 | bytes 3939328 | tf_op jit(solution)/shard_map/transpose | solution.py:177
  82.8 2.4 %copy.77 = bf16[512,1280]{1,0:T(8,128)(2,1)} copy(bf16[512,1280]{0,1:T(8,128)(2,1)} %fusion.107) | data formatting | bytes 2621440
  85.3 2.9 %collective-permute-done.7 = bf16[40,1304]{1,0:T(8,128)(2,1)S(1)} collective-permute-done((bf16[40,1304]{1,0:T(8,128)(2,1)S(1)}, bf16[40,1304]{1,0:T(8,128)(2,1)S(1)}, u32[]{:S(2)}, u32[]{:S(2)}) %collective-permute-start.7) | collective-permute-done | bytes 104352 | tf_op jit(solution)/shard_map/ppermute | solution.py:223
  89.9 0.9 copy.78
  (131 shorter events, 17.9 us)
Async XLA Ops:
  0.6 24.4 %copy-start.4 = (bf16[512,1280]{1,0:T(8,128)(2,1)S(1)}, bf16[512,1280]{1,0:T(8,128)(2,1)}, u32[]{:S(2)}) copy-start(bf16[512,1280]{1,0:T(8,128)(2,1)} %param.13) | copy-start | bytes 3932164
  0.6 21.0 %copy-start.14 = (f32[20,512]{1,0:T(8,128)S(1)}, f32[20,512]{1,0:T(8,128)}, u32[]{:S(2)}) copy-start(f32[20,512]{1,0:T(8,128)} %param.16) | copy-start | bytes 122884
  0.7 21.8 %copy-start.20 = (bf16[4,256]{1,0:T(4,128)(2,1)S(1)}, bf16[4,256]{1,0:T(4,128)(2,1)}, u32[]{:S(2)}) copy-start(bf16[4,256]{1,0:T(4,128)(2,1)} %param.20) | copy-start | bytes 6148
  0.7 22.3 %copy-start.15 = (bf16[4,1280]{1,0:T(4,128)(2,1)S(1)}, bf16[4,1280]{1,0:T(4,128)(2,1)}, u32[]{:S(2)}) copy-start(bf16[4,1280]{1,0:T(4,128)(2,1)} %param.19) | copy-start | bytes 30724
  0.7 22.4 %copy-start.25 = (s32[128]{0:T(128)S(1)}, s32[128]{0:T(128)}, u32[]{:S(2)}) copy-start(s32[128]{0:T(128)} %param.22) | copy-start | bytes 1540
  0.7 24.1 %copy-start.22 = (f32[20]{0:T(128)S(1)}, f32[20]{0:T(128)}, u32[]{:S(2)}) copy-start(f32[20]{0:T(128)} %param.18) | copy-start | bytes 244
  2.2 22.8 %collective-permute-start = (bf16[3,1536]{1,0:T(4,128)(2,1)S(1)}, bf16[3,1536]{1,0:T(4,128)(2,1)S(1)}, u32[]{:S(2)}, u32[]{:S(2)}) collective-permute-start(bf16[3,1536]{1,0:T(4,128)(2,1)S(1)} %pad_maximum_fusion.3), channel_id=1, source_target_pairs={{0,4},{4,8},{8,12},{1,5},{5,9},{9,13},{2,6},{6,10},{10,14},{3,7},{... | collective-permute-start | bytes 27656 | tf_op jit(solution)/shard_map/ppermute | solution.py:20
  8.9 16.1 %copy-start.7 = (f32[3,8,2,128]{3,1,2,0:T(8,128)}, f32[3,8,2,128]{3,1,2,0:T(8,128)S(1)}, u32[]{:S(2)}) copy-start(f32[3,8,2,128]{3,1,2,0:T(8,128)S(1)} %copy.80) | copy-start | bytes 73732
  9.9 15.1 %copy-start.9 = (f32[3,8,2,128]{3,1,2,0:T(8,128)}, f32[3,8,2,128]{3,1,2,0:T(8,128)S(1)}, u32[]{:S(2)}) copy-start(f32[3,8,2,128]{3,1,2,0:T(8,128)S(1)} %copy.81) | copy-start | bytes 73732
  10.7 14.3 %collective-permute-start.3 = (f32[20]{0:T(128)S(1)}, f32[20]{0:T(128)S(1)}, u32[]{:S(2)}, u32[]{:S(2)}) collective-permute-start(f32[20]{0:T(128)S(1)} %get-tuple-element.51), channel_id=1, source_target_pairs={{0,4},{4,8},{8,12},{1,5},{5,9},{9,13},{2,6},{6,10},{10,14},{3,7},{... | collective-permute-start | bytes 248 | tf_op jit(solution)/shard_map/ppermute | solution.py:20
  16.9 37.4 %all-to-all-start = ((bf16[4,40,1284]{2,1,0:T(8,128)(2,1)}), bf16[4,40,1284]{2,1,0:T(8,128)(2,1)}, u32[]{:S(2)}, u32[]{:S(2)}) async-start(bf16[4,40,1284]{2,1,0:T(8,128)(2,1)} %broadcast_in_dim.75), calls=%async_computation | async-start | bytes 901120 | tf_op jit(solution)/shard_map/all_to_all | solution.py:125
  27.4 4.3 %copy-start.2 = (bf16[256,1280]{0,1:T(8,128)(2,1)}, bf16[256,1280]{0,1:T(8,128)(2,1)S(1)}, u32[]{:S(2)}) copy-start(bf16[256,1280]{0,1:T(8,128)(2,1)S(1)} %copy.67) | copy-start | bytes 1966084
  27.5 8.2 %copy-start.8 = (f32[3,8,2,128]{3,1,2,0:T(8,128)S(1)}, f32[3,8,2,128]{3,1,2,0:T(8,128)}, u32[]{:S(2)}) copy-start(f32[3,8,2,128]{3,1,2,0:T(8,128)} %copy-done.7) | copy-start | bytes 73732
  27.5 8.2 %copy-start.13 = (pred[256,256]{1,0:T(8,128)(4,1)S(1)}, pred[256,256]{1,0:T(8,128)(4,1)}, u32[]{:S(2)}) copy-start(pred[256,256]{1,0:T(8,128)(4,1)} %iota_compare_fusion.1) | copy-start | bytes 196612
  27.5 8.2 %copy-start.18 = (f32[20,256]{1,0:T(8,128)S(1)}, f32[20,256]{1,0:T(8,128)}, u32[]{:S(2)}) copy-start(f32[20,256]{1,0:T(8,128)} %get-tuple-element.34) | copy-start | bytes 61444
  31.8 10.0 %collective-permute-start.1 = (bf16[20,64,128]{2,1,0:T(8,128)(2,1)S(1)}, bf16[20,64,128]{2,1,0:T(8,128)(2,1)S(1)}, u32[]{:S(2)}, u32[]{:S(2)}) collective-permute-start(bf16[20,64,128]{2,1,0:T(8,128)(2,1)S(1)} %get-tuple-element.53), channel_id=1, source_target_pairs={{0,4},{4,8},{8,12},{1,5},{5,9},{9,13},{2,6},{6,10},{10,14},{3,7},{... | collective-permute-start | bytes 983048 | tf_op jit(solution)/shard_map/ppermute | solution.py:20
  35.7 6.1 %copy-start.21 = (f32[20]{0:T(128)S(1)}, f32[20]{0:T(128)}, u32[]{:S(2)}) copy-start(f32[20]{0:T(128)} %get-tuple-element.50) | copy-start | bytes 244
  35.7 11.7 %copy-start.3 = (bf16[256,1280]{0,1:T(8,128)(2,1)S(1)}, bf16[256,1280]{0,1:T(8,128)(2,1)}, u32[]{:S(2)}) copy-start(bf16[256,1280]{0,1:T(8,128)(2,1)} %copy-done.2) | copy-start | bytes 1966084
  35.7 11.7 %copy-start.10 = (f32[3,8,2,128]{3,1,2,0:T(8,128)S(1)}, f32[3,8,2,128]{3,1,2,0:T(8,128)}, u32[]{:S(2)}) copy-start(f32[3,8,2,128]{3,1,2,0:T(8,128)} %copy-done.9) | copy-start | bytes 73732
  35.7 11.7 %copy-start.17 = (f32[20,256]{1,0:T(8,128)S(1)}, f32[20,256]{1,0:T(8,128)}, u32[]{:S(2)}) copy-start(f32[20,256]{1,0:T(8,128)} %get-tuple-element.37) | copy-start | bytes 61444
  41.9 13.2 %collective-permute-start.2 = (bf16[20,64,128]{2,1,0:T(8,128)(2,1)S(1)}, bf16[20,64,128]{2,1,0:T(8,128)(2,1)S(1)}, u32[]{:S(2)}, u32[]{:S(2)}) collective-permute-start(bf16[20,64,128]{2,1,0:T(8,128)(2,1)S(1)} %fusion.50), channel_id=1, source_target_pairs={{0,8},{4,12},{1,9},{5,13},{2,10},{6,14},{3,11},{7,15},{16,24},{20,... | collective-permute-start | bytes 983048 | tf_op jit(solution)/shard_map/ppermute | solution.py:20
  54.3 1.7 %copy-start.5 = (f32[20,64,256]{2,1,0:T(8,128)S(1)}, f32[20,64,256]{2,1,0:T(8,128)}, u32[]{:S(2)}) copy-start(f32[20,64,256]{2,1,0:T(8,128)} %fusion.4) | copy-start | bytes 3932164
  54.3 1.7 %copy-start.12 = (f32[20,256]{1,0:T(8,128)S(1)}, f32[20,256]{1,0:T(8,128)}, u32[]{:S(2)}) copy-start(f32[20,256]{1,0:T(8,128)} %get-tuple-element.41) | copy-start | bytes 61444
  59.0 4.2 %copy-start.23 = (s32[128]{0:T(128)S(1)}, s32[128]{0:T(128)}, u32[]{:S(2)}) copy-start(s32[128]{0:T(128)} %iota_add_fusion) | copy-start | bytes 1540
  59.0 6.3 %copy-start.16 = (f32[1280]{0:T(1024)S(1)}, f32[1280]{0:T(1024)}, u32[]{:S(2)}) copy-start(f32[1280]{0:T(1024)} %param.21) | copy-start | bytes 15364
  59.0 6.3 %copy-start.24 = (s32[128]{0:T(128)S(1)}, s32[128]{0:T(128)}, u32[]{:S(2)}) copy-start(s32[128]{0:T(128)} %broadcast_subtract_fusion) | copy-start | bytes 1540
  60.5 5.6 %copy-start.19 = (pred[8,1280]{1,0:T(8,128)(4,1)S(1)}, pred[8,1280]{1,0:T(8,128)(4,1)}, u32[]{:S(2)}) copy-start(pred[8,1280]{1,0:T(8,128)(4,1)} %iota_compare_fusion.2) | copy-start | bytes 30724
  60.5 1.2 %collective-permute-start.4 = (f32[512]{0:T(512)S(1)}, f32[512]{0:T(512)S(1)}, u32[]{:S(2)}, u32[]{:S(2)}) collective-permute-start(f32[512]{0:T(512)S(1)} %get-tuple-element.24), channel_id=1, source_target_pairs={{0,1},{1,0},{2,3},{3,2},{4,5},{5,4},{6,7},{7,6},{8,9},{9,8},{10,11... | collective-permute-start | bytes 6152 | tf_op jit(solution)/shard_map/ppermute | solution.py:84
  61.7 3.6 %collective-permute-start.5 = (f32[512]{0:T(512)S(1)}, f32[512]{0:T(512)S(1)}, u32[]{:S(2)}, u32[]{:S(2)}) collective-permute-start(f32[512]{0:T(512)S(1)} %add.174), channel_id=1, source_target_pairs={{0,2},{1,3},{2,0},{3,1},{4,6},{5,7},{6,4},{7,5},{8,10},{9,11},{10,... | collective-permute-start | bytes 6152 | tf_op jit(solution)/shard_map/ppermute | solution.py:84
  72.3 13.0 %collective-permute-start.6 = (bf16[40,1304]{1,0:T(8,128)(2,1)S(1)}, bf16[40,1304]{1,0:T(8,128)(2,1)S(1)}, u32[]{:S(2)}, u32[]{:S(2)}) collective-permute-start(bf16[40,1304]{1,0:T(8,128)(2,1)S(1)} %get-tuple-element.33), channel_id=1, source_target_pairs={{0,4},{4,8},{8,12},{12,0},{1,5},{5,9},{9,13},{13,1},{2,6},{6,10},{... | collective-permute-start | bytes 312968 | tf_op jit(solution)/shard_map/ppermute | solution.py:223
  78.1 10.1 %collective-permute-start.7 = (bf16[40,1304]{1,0:T(8,128)(2,1)S(1)}, bf16[40,1304]{1,0:T(8,128)(2,1)S(1)}, u32[]{:S(2)}, u32[]{:S(2)}) collective-permute-start(bf16[40,1304]{1,0:T(8,128)(2,1)S(1)} %get-tuple-element.32), channel_id=1, source_target_pairs={{0,8},{4,12},{8,0},{12,4},{1,9},{5,13},{9,1},{13,5},{2,10},{6,14},... | collective-permute-start | bytes 312968 | tf_op jit(solution)/shard_map/ppermute | solution.py:223
  81.5 7.0 %collective-permute-start.8 = (bf16[40,1304]{1,0:T(8,128)(2,1)S(1)}, bf16[40,1304]{1,0:T(8,128)(2,1)S(1)}, u32[]{:S(2)}, u32[]{:S(2)}) collective-permute-start(bf16[40,1304]{1,0:T(8,128)(2,1)S(1)} %get-tuple-element.31), channel_id=1, source_target_pairs={{0,12},{4,0},{8,4},{12,8},{1,13},{5,1},{9,5},{13,9},{2,14},{6,2},{... | collective-permute-start | bytes 312968 | tf_op jit(solution)/shard_map/ppermute | solution.py:223
  (4 other events, 5.7 us)

commit v17 on v15

--- a/solution.py
+++ b/solution.py
@@ -200,16 +200,16 @@
     )
     denom_high = denom.astype(jnp.bfloat16)
     denom_low = (denom - denom_high.astype(jnp.float32)).astype(jnp.bfloat16)
+    stats = jnp.concatenate([peak.T.astype(jnp.bfloat16), denom_high.T, denom_low.T], axis=1)
+    stats = stats.reshape(seq_count, -1)
+    stats = jnp.pad(stats, ((0, 0), (0, channels - stats.shape[1])))
     parts = jnp.concatenate(
         [
-            numer.reshape(pools_all, channels).astype(jnp.bfloat16),
-            peak.T.astype(jnp.bfloat16),
-            denom_high.T,
-            denom_low.T,
+            numer.reshape(seq_count, pools_local, channels).astype(jnp.bfloat16),
+            stats[:, None, :],
         ],
         axis=1,
     )
-    parts = parts.reshape(seq_count, pools_local, channels + 3 * pool_heads_local)
     place = lax.axis_index("seq")
     gathered = [lax.dynamic_index_in_dim(parts, place, 0, False)]
     for shift in range(1, seq_count):
@@ -220,10 +220,12 @@
             )
         )
     parts = jnp.stack(gathered).astype(jnp.float32)
-    numer_parts = parts[:, :, :channels].reshape(
+    numer_parts = parts[:, :pools_local].reshape(
         seq_count, pools_local, pool_heads_local, pool_width
     )
-    stats_parts = parts[:, :, channels:].reshape(seq_count, pools_local, 3, pool_heads_local)
+    stats_parts = parts[:, pools_local, : pools_local * 3 * pool_heads_local].reshape(
+        seq_count, pools_local, 3, pool_heads_local
+    )
     peak_parts = stats_parts[:, :, 0]
     denom_parts = stats_parts[:, :, 1] + stats_parts[:, :, 2]
     peak_all = jnp.max(peak_parts, axis=0)

time: 90.3 us -> 90.8 us (level)
    unnamed x60 -> x59, local copies, waits for them, and re-layouts: 3.42 us -> 2.52 us
    another operation x8 -> x7, other arithmetic: 2.18 us -> 2.1 us
where the time goes in v17:
time: 90.8 us; the launch traced here: 90.1 us
  starting transfers between devices  33.5 us (37%)
  other arithmetic  15.3 us (17%)
  local copies, waits for them, and re-layouts  13.7 us (15%)
  waiting for transfers between devices  13.3 us (15%)
  matrix products  12.9 us (14%)
  between operations  1.41 us (2%)
    ppermute x4, starting transfers between devices, passed_along(): lax.ppermute(value, axis, [(source, source + steps) for source in range(l...  17.8 us
    ppermute x3, starting transfers between devices, local(): lax.ppermute(chunk, 'seq', [(i, (i + shift) % seq_count) for i in range(s...  9.99 us
    ppermute x3, waiting for transfers between devices, local(): lax.ppermute(chunk, 'seq', [(i, (i + shift) % seq_count) for i in range(s...  7.53 us
    dot_general x2, matrix products, stretch_local(): jnp.einsum('hij,jhp->hpi', mixing, x_block, preferred_element_type=jnp.fl...  5.89 us
    all_to_all x1, starting transfers between devices, local(): lax.all_to_all(query_rows.reshape(seq_count * pools_local, -1), 'seq', 0,...  4.12 us
    convert_element_type x2, other arithmetic, causal_conv(): return silu_act(summed).astype(jnp.bfloat16)  3.73 us
    ppermute x4, waiting for transfers between devices, passed_along(): lax.ppermute(value, axis, [(source, source + steps) for source in range(l...  2.89 us
    ppermute x2, waiting for transfers between devices, butterfly_sum(): partner = lax.ppermute(value, axis, [(i, i ^ stride) for i in range(count)])  2.86 us
  transfers between devices with their start and end apart: 10, of which 6 were waited for; matrix products, arithmetic and copies ran while one was open for 30% of the time, Pallas kernels for 0%

profile of v17, /device:TPU:0, one launch (start us, length us, event | category | flops | bytes accessed | tf_op | source)
XLA Modules:
  0.0 90.1 jit_solution(17014243804002253351)
XLA Ops:
  0.7 0.8 slice.153
  2.2 5.0 %collective-permute-start = (bf16[3,1536]{1,0:T(4,128)(2,1)S(1)}, bf16[3,1536]{1,0:T(4,128)(2,1)S(1)}, u32[]{:S(2)}, u32[]{:S(2)}) collective-permute-start(bf16[3,1536]{1,0:T(4,128)(2,1)S(1)} %pad_maximum_fusion.5), channel_id=1, source_target_pairs={{0,4},{4,8},{8,12},{1,5},{5,9},{9,13},{2,6},{6,10},{10,14},{3,7},{... | collective-permute-start | bytes 27656 | tf_op jit(solution)/shard_map/ppermute | solution.py:20
  7.2 0.8 fusion.112
  10.7 3.5 %collective-permute-start.3 = (f32[20]{0:T(128)S(1)}, f32[20]{0:T(128)S(1)}, u32[]{:S(2)}, u32[]{:S(2)}) collective-permute-start(f32[20]{0:T(128)S(1)} %get-tuple-element.55), channel_id=1, source_target_pairs={{0,4},{4,8},{8,12},{1,5},{5,9},{9,13},{2,6},{6,10},{10,14},{3,7},{... | collective-permute-start | bytes 248 | tf_op jit(solution)/shard_map/ppermute | solution.py:20
  15.1 1.0 %concatenate.35 = bf16[40,1284]{1,0:T(8,128)(2,1)S(1)} concatenate(bf16[40,1280]{1,0:T(8,128)(2,1)} %param.23, bf16[40,2]{1,0:T(8,128)(2,1)S(1)} %copy.67, bf16[40,2]{1,0:T(8,128)(2,1)S(1)} %copy.68), dimensions={1} | concatenate | bytes 205440 | tf_op jit(solution)/shard_map/concatenate | solution.py:123
  16.1 0.8 broadcast_in_dim.139
  16.9 4.1 %all-to-all-start = ((bf16[4,40,1284]{2,1,0:T(8,128)(2,1)}), bf16[4,40,1284]{2,1,0:T(8,128)(2,1)}, u32[]{:S(2)}, u32[]{:S(2)}) async-start(bf16[4,40,1284]{2,1,0:T(8,128)(2,1)} %broadcast_in_dim.139), calls=%async_computation | async-start | bytes 901120 | tf_op jit(solution)/shard_map/all_to_all | solution.py:125
  25.0 1.8 %divide_convert_fusion = bf16[512,1280]{1,0:T(8,128)(2,1)S(1)} fusion(bf16[512,1280]{1,0:T(8,128)(2,1)S(1)} %copy-done.4, bf16[3,1280]{1,0:T(4,128)(2,1)S(1)} %slice.202, f32[1280]{0:T(1024)S(1)} %get-tuple-element.18, f32[1280]{0:T(1024)S(1)} %get-tuple-element.19, f32[1280]{0:T(1024)S(1)} %get-tuple-element.17, f32[1280]{0:T(1024)S(1)} %get-tuple-element.16), kind=kLoop, calls=%fused_computation.27 | loop fusion | flops 15728640 | bytes 2649600 | tf_op jit(solution)/shard_map/convert_element_type | solution.py:36
  27.5 1.9 %divide_convert_fusion.1 = bf16[512,256]{1,0:T(8,128)(2,1)S(1)} fusion(bf16[512,256]{1,0:T(8,128)(2,1)} %param.15, bf16[3,256]{1,0:T(4,128)(2,1)S(1)} %slice.209, f32[256]{0:T(256)} %bitcast.125, f32[256]{0:T(256)} %bitcast.126, f32[256]{0:T(256)} %bitcast.124, f32[256]{0:T(256)} %bitcast.123), kind=kLoop, calls=%fused_computation.74 | loop fusion | flops 3145728 | bytes 529920 | tf_op jit(solution)/shard_map/convert_element_type | solution.py:36
  29.6 1.1 %convolution_add_fusion.3 = f32[20,64,128]{2,1,0:T(8,128)S(1)} fusion(bf16[256,20,64]{0,2,1:T(8,128)(2,1)S(1)} %bitcast.100, f32[256,20]{0,1:T(8,128)} %get-tuple-element.39, f32[20]{0:T(128)} %get-tuple-element.53, bf16[512,256]{1,0:T(8,128)(2,1)S(1)} %divide_convert_fusion.1), kind=kOutput, calls=%fused_computation.53 | convolution fusion | flops 85032960 | bytes 1396816 | tf_op jit(solution)/shard_map/jhp,js->hps/dot_general | solution.py:52
  30.6 1.1 %fusion.114 = (bf16[20,64,128]{2,1,0:T(8,128)(2,1)S(1)}, f32[20,64,128]{2,1,0:T(8,128)S(1)}) fusion(bf16[512,256]{1,0:T(8,128)(2,1)S(1)} %divide_convert_fusion.1, bf16[256,20,64]{0,2,1:T(8,128)(2,1)S(1)} %bitcast.102, f32[256,20]{0,1:T(8,128)} %get-tuple-element.40, f32[20,64,128]{2,1,0:T(8,128)S(1)} %convolution_add_fusion.3, f32[20]{0:T(128)} %get-tuple-element.56), kind=kOutput, calls=%fused_computation.196 | convolution fusion | flops 85360640 | bytes 2379856 | tf_op jit(solution)/shard_map/jhp,js->hps/dot_general | solution.py:52
  31.7 3.9 %collective-permute-start.1 = (bf16[20,64,128]{2,1,0:T(8,128)(2,1)S(1)}, bf16[20,64,128]{2,1,0:T(8,128)(2,1)S(1)}, u32[]{:S(2)}, u32[]{:S(2)}) collective-permute-start(bf16[20,64,128]{2,1,0:T(8,128)(2,1)S(1)} %get-tuple-element.57), channel_id=1, source_target_pairs={{0,4},{4,8},{8,12},{1,5},{5,9},{9,13},{2,6},{6,10},{10,14},{3,7},{... | collective-permute-start | bytes 983048 | tf_op jit(solution)/shard_map/ppermute | solution.py:20
  35.7 2.9 %fusion.4 = f32[20,64,256]{2,1,0:T(8,128)} fusion(bf16[256,20,64]{0,2,1:T(8,128)(2,1)S(1)} %bitcast.101, f32[20,256]{1,0:T(8,128)S(1)} %copy-done.17, f32[256,256]{1,0:T(8,128)S(1)} %fusion.88, f32[20,256]{1,0:T(8,128)S(1)} %bitcast.116, pred[256,256]{1,0:T(8,128)(4,1)S(1)} %copy-done.13), kind=kOutput, calls=%fused_computation.7 | convolution fusion | flops 175636480 | bytes 2334720 | tf_op jit(solution)/shard_map/hij,jhp->hpi/dot_general | solution.py:49
  38.9 2.9 %collective-permute-done.1 = bf16[20,64,128]{2,1,0:T(8,128)(2,1)S(1)} collective-permute-done((bf16[20,64,128]{2,1,0:T(8,128)(2,1)S(1)}, bf16[20,64,128]{2,1,0:T(8,128)(2,1)S(1)}, u32[]{:S(2)}, u32[]{:S(2)}) %collective-permute-start.1) | collective-permute-done | bytes 327712 | tf_op jit(solution)/shard_map/ppermute | solution.py:20
  41.9 5.5 %collective-permute-start.2 = (bf16[20,64,128]{2,1,0:T(8,128)(2,1)S(1)}, bf16[20,64,128]{2,1,0:T(8,128)(2,1)S(1)}, u32[]{:S(2)}, u32[]{:S(2)}) collective-permute-start(bf16[20,64,128]{2,1,0:T(8,128)(2,1)S(1)} %fusion.50), channel_id=1, source_target_pairs={{0,8},{4,12},{1,9},{5,13},{2,10},{6,14},{3,11},{7,15},{16,24},{20,... | collective-permute-start | bytes 983048 | tf_op jit(solution)/shard_map/ppermute | solution.py:20
  47.4 2.9 %fusion.5 = f32[20,64,256]{2,1,0:T(8,128)} fusion(bf16[256,20,64]{0,2,1:T(8,128)(2,1)S(1)} %bitcast.103, f32[20,256]{1,0:T(8,128)S(1)} %copy-done.16, f32[256,256]{1,0:T(8,128)S(1)} %fusion.84, f32[20,256]{1,0:T(8,128)S(1)} %bitcast.119, pred[256,256]{1,0:T(8,128)(4,1)S(1)} %copy-done.13), kind=kOutput, calls=%fused_computation.8 | convolution fusion | flops 175636480 | bytes 2334720 | tf_op jit(solution)/shard_map/hij,jhp->hpi/dot_general | solution.py:49
  50.4 1.5 %copy.65 = bf16[512,1280]{0,1:T(8,128)(2,1)} copy(bf16[512,1280]{1,0:T(8,128)(2,1)S(1)} %divide_convert_fusion) | data formatting | bytes 2621440 | tf_op jit(solution)/shard_map/layout_constraint | solution.py:135
  51.8 1.6 %copy.66 = bf16[512,1280]{0,1:T(8,128)(2,1)S(1)} copy(bf16[512,1280]{1,0:T(8,128)(2,1)} %param.14) | data formatting | bytes 2621440 | tf_op jit(solution)/shard_map/optimization_barrier | solution.py:69
  53.5 0.9 slice_convert_fusion
  55.6 0.9 copy-done.6
  56.9 0.9 copy-done.1
  57.8 1.5 %multiply_reduce_fusion = (f32[512]{0:T(512)S(1)}, f32[1280,512]{1,0:T(8,128)S(1)}) fusion(bf16[512,1280]{0,1:T(8,128)(2,1)S(1)} %copy.66, bf16[512,1280]{0,1:T(8,128)(2,1)S(1)} %copy-done.1, f32[1280]{0:T(1024)S(1)} %mul.351, f32[1280,256]{1,0:T(8,128)S(1)} %bitcast.99, f32[1280,256]{1,0:T(8,128)S(1)} %bitcast.98), kind=kLoop, calls=%fused_computation.16 | loop fusion | flops 7208448 | bytes 7871488 | tf_op jit(solution)/shard_map/reduce_sum | solution.py:172
  59.7 0.9 collective-permute-done.4
  60.6 1.5 %collective-permute-start.5 = (f32[512]{0:T(512)S(1)}, f32[512]{0:T(512)S(1)}, u32[]{:S(2)}, u32[]{:S(2)}) collective-permute-start(f32[512]{0:T(512)S(1)} %add.184), channel_id=1, source_target_pairs={{0,2},{1,3},{2,0},{3,1},{4,6},{5,7},{6,4},{7,5},{8,10},{9,11},{10,... | collective-permute-start | bytes 6152 | tf_op jit(solution)/shard_map/ppermute | solution.py:84
  62.2 2.0 %collective-permute-done.5 = f32[512]{0:T(512)S(1)} collective-permute-done((f32[512]{0:T(512)S(1)}, f32[512]{0:T(512)S(1)}, u32[]{:S(2)}, u32[]{:S(2)}) %collective-permute-start.5) | collective-permute-done | bytes 2080 | tf_op jit(solution)/shard_map/ppermute | solution.py:84
  65.1 0.9 gather_fusion
  66.2 2.2 %fusion.115 = (bf16[8,160]{1,0:T(8,128)(2,1)S(1)}, f32[8,160,128]{2,1,0:T(8,128)S(1)}) fusion(bf16[160,1284]{1,0:T(8,128)(2,1)} %bitcast.19, pred[8,1280]{1,0:T(8,128)(4,1)S(1)} %copy-done.18, bf16[128,1280]{1,0:T(8,128)(2,1)S(1)} %broadcast_select_fusion, pred[160,128]{1,0:T(8,128)(4,1)S(1)} %compare_and_fusion), kind=kOutput, calls=%fused_computation.197 | convolution fusion | flops 421231360 | bytes 1425920 | tf_op jit(solution)/shard_map/pc,asc->aps/dot_general | solution.py:191
  70.1 6.6 %collective-permute-start.6 = (bf16[41,1280]{1,0:T(8,128)(2,1)S(1)}, bf16[41,1280]{1,0:T(8,128)(2,1)S(1)}, u32[]{:S(2)}, u32[]{:S(2)}) collective-permute-start(bf16[41,1280]{1,0:T(8,128)(2,1)S(1)} %get-tuple-element.33), channel_id=1, source_target_pairs={{0,4},{4,8},{8,12},{12,0},{1,5},{5,9},{9,13},{13,1},{2,6},{6,10},{... | collective-permute-start | bytes 314888 | tf_op jit(solution)/shard_map/ppermute | solution.py:218
  76.7 3.4 %collective-permute-start.7 = (bf16[41,1280]{1,0:T(8,128)(2,1)S(1)}, bf16[41,1280]{1,0:T(8,128)(2,1)S(1)}, u32[]{:S(2)}, u32[]{:S(2)}) collective-permute-start(bf16[41,1280]{1,0:T(8,128)(2,1)S(1)} %get-tuple-element.34), channel_id=1, source_target_pairs={{0,8},{4,12},{8,0},{12,4},{1,9},{5,13},{9,1},{13,5},{2,10},{6,14},... | collective-permute-start | bytes 314888 | tf_op jit(solution)/shard_map/ppermute | solution.py:218
  80.1 3.7 %collective-permute-done.6 = bf16[41,1280]{1,0:T(8,128)(2,1)S(1)} collective-permute-done((bf16[41,1280]{1,0:T(8,128)(2,1)S(1)}, bf16[41,1280]{1,0:T(8,128)(2,1)S(1)}, u32[]{:S(2)}, u32[]{:S(2)}) %collective-permute-start.6) | collective-permute-done | bytes 104992 | tf_op jit(solution)/shard_map/ppermute | solution.py:218
  83.8 3.5 %collective-permute-done.7 = bf16[41,1280]{1,0:T(8,128)(2,1)S(1)} collective-permute-done((bf16[41,1280]{1,0:T(8,128)(2,1)S(1)}, bf16[41,1280]{1,0:T(8,128)(2,1)S(1)}, u32[]{:S(2)}, u32[]{:S(2)}) %collective-permute-start.7) | collective-permute-done | bytes 104992 | tf_op jit(solution)/shard_map/ppermute | solution.py:218
  89.3 0.7 div.57
  (138 shorter events, 16.0 us)
Async XLA Ops:
  0.6 24.4 %copy-start.4 = (bf16[512,1280]{1,0:T(8,128)(2,1)S(1)}, bf16[512,1280]{1,0:T(8,128)(2,1)}, u32[]{:S(2)}) copy-start(bf16[512,1280]{1,0:T(8,128)(2,1)} %param.13) | copy-start | bytes 3932164
  0.6 21.0 %copy-start.14 = (f32[20,512]{1,0:T(8,128)S(1)}, f32[20,512]{1,0:T(8,128)}, u32[]{:S(2)}) copy-start(f32[20,512]{1,0:T(8,128)} %param.16) | copy-start | bytes 122884
  0.7 21.7 %copy-start.20 = (bf16[4,256]{1,0:T(4,128)(2,1)S(1)}, bf16[4,256]{1,0:T(4,128)(2,1)}, u32[]{:S(2)}) copy-start(bf16[4,256]{1,0:T(4,128)(2,1)} %param.20) | copy-start | bytes 6148
  0.7 22.3 %copy-start.15 = (bf16[4,1280]{1,0:T(4,128)(2,1)S(1)}, bf16[4,1280]{1,0:T(4,128)(2,1)}, u32[]{:S(2)}) copy-start(bf16[4,1280]{1,0:T(4,128)(2,1)} %param.19) | copy-start | bytes 30724
  0.7 22.4 %copy-start.26 = (s32[128]{0:T(128)S(1)}, s32[128]{0:T(128)}, u32[]{:S(2)}) copy-start(s32[128]{0:T(128)} %param.22) | copy-start | bytes 1540
  0.7 24.1 %copy-start.24 = (f32[20]{0:T(128)S(1)}, f32[20]{0:T(128)}, u32[]{:S(2)}) copy-start(f32[20]{0:T(128)} %param.18) | copy-start | bytes 244
  2.2 22.7 %collective-permute-start = (bf16[3,1536]{1,0:T(4,128)(2,1)S(1)}, bf16[3,1536]{1,0:T(4,128)(2,1)S(1)}, u32[]{:S(2)}, u32[]{:S(2)}) collective-permute-start(bf16[3,1536]{1,0:T(4,128)(2,1)S(1)} %pad_maximum_fusion.5), channel_id=1, source_target_pairs={{0,4},{4,8},{8,12},{1,5},{5,9},{9,13},{2,6},{6,10},{10,14},{3,7},{... | collective-permute-start | bytes 27656 | tf_op jit(solution)/shard_map/ppermute | solution.py:20
  8.9 16.1 %copy-start.7 = (f32[3,8,2,128]{3,1,2,0:T(8,128)}, f32[3,8,2,128]{3,1,2,0:T(8,128)S(1)}, u32[]{:S(2)}) copy-start(f32[3,8,2,128]{3,1,2,0:T(8,128)S(1)} %copy.75) | copy-start | bytes 73732
  9.9 15.1 %copy-start.9 = (f32[3,8,2,128]{3,1,2,0:T(8,128)}, f32[3,8,2,128]{3,1,2,0:T(8,128)S(1)}, u32[]{:S(2)}) copy-start(f32[3,8,2,128]{3,1,2,0:T(8,128)S(1)} %copy.76) | copy-start | bytes 73732
  10.7 14.3 %collective-permute-start.3 = (f32[20]{0:T(128)S(1)}, f32[20]{0:T(128)S(1)}, u32[]{:S(2)}, u32[]{:S(2)}) collective-permute-start(f32[20]{0:T(128)S(1)} %get-tuple-element.55), channel_id=1, source_target_pairs={{0,4},{4,8},{8,12},{1,5},{5,9},{9,13},{2,6},{6,10},{10,14},{3,7},{... | collective-permute-start | bytes 248 | tf_op jit(solution)/shard_map/ppermute | solution.py:20
  16.9 36.6 %all-to-all-start = ((bf16[4,40,1284]{2,1,0:T(8,128)(2,1)}), bf16[4,40,1284]{2,1,0:T(8,128)(2,1)}, u32[]{:S(2)}, u32[]{:S(2)}) async-start(bf16[4,40,1284]{2,1,0:T(8,128)(2,1)} %broadcast_in_dim.139), calls=%async_computation | async-start | bytes 901120 | tf_op jit(solution)/shard_map/all_to_all | solution.py:125
  27.4 4.3 %copy-start.2 = (bf16[256,1280]{0,1:T(8,128)(2,1)}, bf16[256,1280]{0,1:T(8,128)(2,1)S(1)}, u32[]{:S(2)}) copy-start(bf16[256,1280]{0,1:T(8,128)(2,1)S(1)} %copy.64) | copy-start | bytes 1966084
  27.4 8.2 %copy-start.8 = (f32[3,8,2,128]{3,1,2,0:T(8,128)S(1)}, f32[3,8,2,128]{3,1,2,0:T(8,128)}, u32[]{:S(2)}) copy-start(f32[3,8,2,128]{3,1,2,0:T(8,128)} %copy-done.7) | copy-start | bytes 73732
  27.4 8.2 %copy-start.13 = (pred[256,256]{1,0:T(8,128)(4,1)S(1)}, pred[256,256]{1,0:T(8,128)(4,1)}, u32[]{:S(2)}) copy-start(pred[256,256]{1,0:T(8,128)(4,1)} %iota_compare_fusion) | copy-start | bytes 196612
  27.4 8.2 %copy-start.17 = (f32[20,256]{1,0:T(8,128)S(1)}, f32[20,256]{1,0:T(8,128)}, u32[]{:S(2)}) copy-start(f32[20,256]{1,0:T(8,128)} %get-tuple-element.38) | copy-start | bytes 61444
  31.7 10.0 %collective-permute-start.1 = (bf16[20,64,128]{2,1,0:T(8,128)(2,1)S(1)}, bf16[20,64,128]{2,1,0:T(8,128)(2,1)S(1)}, u32[]{:S(2)}, u32[]{:S(2)}) collective-permute-start(bf16[20,64,128]{2,1,0:T(8,128)(2,1)S(1)} %get-tuple-element.57), channel_id=1, source_target_pairs={{0,4},{4,8},{8,12},{1,5},{5,9},{9,13},{2,6},{6,10},{10,14},{3,7},{... | collective-permute-start | bytes 983048 | tf_op jit(solution)/shard_map/ppermute | solution.py:20
  35.7 6.1 %copy-start.22 = (f32[20]{0:T(128)S(1)}, f32[20]{0:T(128)}, u32[]{:S(2)}) copy-start(f32[20]{0:T(128)} %get-tuple-element.54) | copy-start | bytes 244
  35.7 11.7 %copy-start.3 = (bf16[256,1280]{0,1:T(8,128)(2,1)S(1)}, bf16[256,1280]{0,1:T(8,128)(2,1)}, u32[]{:S(2)}) copy-start(bf16[256,1280]{0,1:T(8,128)(2,1)} %copy-done.2) | copy-start | bytes 1966084
  35.7 11.7 %copy-start.10 = (f32[3,8,2,128]{3,1,2,0:T(8,128)S(1)}, f32[3,8,2,128]{3,1,2,0:T(8,128)}, u32[]{:S(2)}) copy-start(f32[3,8,2,128]{3,1,2,0:T(8,128)} %copy-done.9) | copy-start | bytes 73732
  35.7 11.7 %copy-start.16 = (f32[20,256]{1,0:T(8,128)S(1)}, f32[20,256]{1,0:T(8,128)}, u32[]{:S(2)}) copy-start(f32[20,256]{1,0:T(8,128)} %get-tuple-element.41) | copy-start | bytes 61444
  41.9 12.5 %collective-permute-start.2 = (bf16[20,64,128]{2,1,0:T(8,128)(2,1)S(1)}, bf16[20,64,128]{2,1,0:T(8,128)(2,1)S(1)}, u32[]{:S(2)}, u32[]{:S(2)}) collective-permute-start(bf16[20,64,128]{2,1,0:T(8,128)(2,1)S(1)} %fusion.50), channel_id=1, source_target_pairs={{0,8},{4,12},{1,9},{5,13},{2,10},{6,14},{3,11},{7,15},{16,24},{20,... | collective-permute-start | bytes 983048 | tf_op jit(solution)/shard_map/ppermute | solution.py:20
  51.8 2.9 %copy-start.21 = (f32[20]{0:T(128)S(1)}, f32[20]{0:T(128)}, u32[]{:S(2)}) copy-start(f32[20]{0:T(128)} %get-tuple-element.52) | copy-start | bytes 244
  53.5 1.7 %copy-start.12 = (f32[20,256]{1,0:T(8,128)S(1)}, f32[20,256]{1,0:T(8,128)}, u32[]{:S(2)}) copy-start(f32[20,256]{1,0:T(8,128)} %get-tuple-element.45) | copy-start | bytes 61444
  53.5 1.7 %copy-start.5 = (f32[20,64,256]{2,1,0:T(8,128)S(1)}, f32[20,64,256]{2,1,0:T(8,128)}, u32[]{:S(2)}) copy-start(f32[20,64,256]{2,1,0:T(8,128)} %fusion.4) | copy-start | bytes 3932164
  57.8 4.2 %copy-start.25 = (s32[128]{0:T(128)S(1)}, s32[128]{0:T(128)}, u32[]{:S(2)}) copy-start(s32[128]{0:T(128)} %iota_add_fusion) | copy-start | bytes 1540
  57.8 6.3 %copy-start.19 = (f32[1280]{0:T(1024)S(1)}, f32[1280]{0:T(1024)}, u32[]{:S(2)}) copy-start(f32[1280]{0:T(1024)} %param.21) | copy-start | bytes 15364
  59.3 1.2 %collective-permute-start.4 = (f32[512]{0:T(512)S(1)}, f32[512]{0:T(512)S(1)}, u32[]{:S(2)}, u32[]{:S(2)}) collective-permute-start(f32[512]{0:T(512)S(1)} %get-tuple-element.26), channel_id=1, source_target_pairs={{0,1},{1,0},{2,3},{3,2},{4,5},{5,4},{6,7},{7,6},{8,9},{9,8},{10,11... | collective-permute-start | bytes 6152 | tf_op jit(solution)/shard_map/ppermute | solution.py:84
  60.6 3.6 %collective-permute-start.5 = (f32[512]{0:T(512)S(1)}, f32[512]{0:T(512)S(1)}, u32[]{:S(2)}, u32[]{:S(2)}) collective-permute-start(f32[512]{0:T(512)S(1)} %add.184), channel_id=1, source_target_pairs={{0,2},{1,3},{2,0},{3,1},{4,6},{5,7},{6,4},{7,5},{8,10},{9,11},{10,... | collective-permute-start | bytes 6152 | tf_op jit(solution)/shard_map/ppermute | solution.py:84
  65.1 3.3 %copy-start = (bf16[512,1280]{1,0:T(8,128)(2,1)}, bf16[512,1280]{1,0:T(8,128)(2,1)S(1)}, u32[]{:S(2)}) copy-start(bf16[512,1280]{1,0:T(8,128)(2,1)S(1)} %copy.73) | copy-start | bytes 3932164
  70.1 13.7 %collective-permute-start.6 = (bf16[41,1280]{1,0:T(8,128)(2,1)S(1)}, bf16[41,1280]{1,0:T(8,128)(2,1)S(1)}, u32[]{:S(2)}, u32[]{:S(2)}) collective-permute-start(bf16[41,1280]{1,0:T(8,128)(2,1)S(1)} %get-tuple-element.33), channel_id=1, source_target_pairs={{0,4},{4,8},{8,12},{12,0},{1,5},{5,9},{9,13},{13,1},{2,6},{6,10},{... | collective-permute-start | bytes 314888 | tf_op jit(solution)/shard_map/ppermute | solution.py:218
  76.7 10.7 %collective-permute-start.7 = (bf16[41,1280]{1,0:T(8,128)(2,1)S(1)}, bf16[41,1280]{1,0:T(8,128)(2,1)S(1)}, u32[]{:S(2)}, u32[]{:S(2)}) collective-permute-start(bf16[41,1280]{1,0:T(8,128)(2,1)S(1)} %get-tuple-element.34), channel_id=1, source_target_pairs={{0,8},{4,12},{8,0},{12,4},{1,9},{5,13},{9,1},{13,5},{2,10},{6,14},... | collective-permute-start | bytes 314888 | tf_op jit(solution)/shard_map/ppermute | solution.py:218
  80.1 7.5 %collective-permute-start.8 = (bf16[41,1280]{1,0:T(8,128)(2,1)S(1)}, bf16[41,1280]{1,0:T(8,128)(2,1)S(1)}, u32[]{:S(2)}, u32[]{:S(2)}) collective-permute-start(bf16[41,1280]{1,0:T(8,128)(2,1)S(1)} %get-tuple-element.35), channel_id=1, source_target_pairs={{0,12},{4,0},{8,4},{12,8},{1,13},{5,1},{9,5},{13,9},{2,14},{6,2},{... | collective-permute-start | bytes 314888 | tf_op jit(solution)/shard_map/ppermute | solution.py:218
  (5 other events, 7.2 us)

commit v18 on v15

--- a/solution.py
+++ b/solution.py
@@ -121,14 +121,6 @@
     bounds = jnp.stack([pool_start, pool_stop], axis=1)
     bounds_split = jnp.concatenate([bounds // 64, bounds % 64], axis=1).astype(jnp.bfloat16)
     query_rows = jnp.concatenate([pool_query, bounds_split], axis=1)
-    query_rows = jnp.broadcast_to(query_rows[None], (seq_count,) + query_rows.shape)
-    query_rows = lax.all_to_all(
-        query_rows.reshape(seq_count * pools_local, -1), "seq", 0, 0, tiled=True
-    )
-    queries_all = query_rows[:, :channels]
-    bounds_all = query_rows[:, channels:].astype(jnp.int32)
-    start_all = bounds_all[:, 0] * 64 + bounds_all[:, 2]
-    stop_all = bounds_all[:, 1] * 64 + bounds_all[:, 3]
     edge_rows = jnp.concatenate([x_in[tok_rows - rim_rows :], bc_in[tok_rows - rim_rows :]], axis=1)
     before = passed_along(edge_rows, "seq", 1)
     x_conv = causal_conv(before[:, :channels], x_in, conv_x)
@@ -155,6 +147,15 @@
         entry_state = jnp.exp(cumul_keep[:, -1])[:, None, None] * entry_state + stretch_state
         decay_total = decay_total + cumul_keep[:, -1]
     incoming, z_late = exclusive_scan(entry_state, decay_total, "seq", z_gate)
+    incoming, query_rows = lax.optimization_barrier((incoming, query_rows))
+    query_rows = jnp.broadcast_to(query_rows[None], (seq_count,) + query_rows.shape)
+    query_rows = lax.all_to_all(
+        query_rows.reshape(seq_count * pools_local, -1), "seq", 0, 0, tiled=True
+    )
+    queries_all = query_rows[:, :channels]
+    bounds_all = query_rows[:, channels:].astype(jnp.int32)
+    start_all = bounds_all[:, 0] * 64 + bounds_all[:, 2]
+    stop_all = bounds_all[:, 1] * 64 + bounds_all[:, 3]
     x_major = x_conv.T.reshape(heads_local, head_width, tok_rows)
     z_major = z_late.T
     pieces_out = []

time: 90.3 us -> 109 us (1.21)
  waiting for transfers between devices: 12.7 us -> 20.8 us
  other arithmetic: 14.8 us -> 22.5 us
  local copies, waits for them, and re-layouts: 14.3 us -> 17.8 us
  starting transfers between devices: 33.5 us -> 32 us
    all_to_all x1, waiting for transfers between devices: 0.01 us -> 8.94 us  [local(): lax.all_to_all(query_rows.reshape(seq_count * pools_local, -1), 'seq', 0,...]
    ppermute x3, starting transfers between devices: 9.99 us -> 2.16 us  [local(): lax.ppermute(chunk, 'seq', [(i, (i + shift) % seq_count) for i in range(s...]
    all_to_all x1, starting transfers between devices: 4.12 us -> 11.5 us  [local(): lax.all_to_all(query_rows.reshape(seq_count * pools_local, -1), 'seq', 0,...]
    convert_element_type x2, other arithmetic: 3.73 us -> 5.9 us  [causal_conv(): return silu_act(summed).astype(jnp.bfloat16)]
    unnamed x60 -> x50, local copies, waits for them, and re-layouts: 3.42 us -> 5.16 us
    ppermute x2, waiting for transfers between devices: 2.86 us -> 1.13 us  [butterfly_sum(): partner = lax.ppermute(value, axis, [(i, i ^ stride) for i in range(count)])]
    mul x2, other arithmetic: 0.65 us -> 2.35 us  [causal_conv(): padded[offset:offset + length].astype(jnp.float32)]
    convert_element_type x1, other arithmetic: 0.15 us -> 1.85 us  [exclusive_scan(): sent_state = passed_along(window[0].astype(jnp.bfloat16), axis, shift)]
  transfers between devices with their start and end apart: 10 -> 10, of which waited for: 6 -> 6; matrix products, arithmetic and copies ran while one was open for 30% -> 26% of each run, Pallas kernels for 0% -> 0%
where the time goes in v18:
time: 109 us; the launch traced here: 108 us
  starting transfers between devices  32 us (29%)
  other arithmetic  22.5 us (21%)
  waiting for transfers between devices  20.8 us (19%)
  local copies, waits for them, and re-layouts  17.8 us (16%)
  matrix products  13.6 us (12%)
  between operations  1.18 us (1%)
    ppermute x4, starting transfers between devices, passed_along(): lax.ppermute(value, axis, [(source, source + steps) for source in range(l...  16.8 us
    all_to_all x1, starting transfers between devices, local(): lax.all_to_all(query_rows.reshape(seq_count * pools_local, -1), 'seq', 0,...  11.5 us
    all_to_all x1, waiting for transfers between devices, local(): lax.all_to_all(query_rows.reshape(seq_count * pools_local, -1), 'seq', 0,...  8.94 us
    ppermute x3, waiting for transfers between devices, local(): lax.ppermute(chunk, 'seq', [(i, (i + shift) % seq_count) for i in range(s...  8.48 us
    dot_general x2, matrix products, stretch_local(): jnp.einsum('hij,jhp->hpi', mixing, x_block, preferred_element_type=jnp.fl...  6.72 us
    convert_element_type x2, other arithmetic, causal_conv(): return silu_act(summed).astype(jnp.bfloat16)  5.9 us
    unnamed x50, local copies, waits for them, and re-layouts  5.16 us
    dot_general x2, matrix products, stretch_local(): jnp.einsum('jhp,js->hps', weighted, b_block, preferred_element_type=jnp.f...  3.1 us
  transfers between devices with their start and end apart: 10, of which 6 were waited for; matrix products, arithmetic and copies ran while one was open for 26% of the time, Pallas kernels for 0%

profile of v18, /device:TPU:0, one launch (start us, length us, event | category | flops | bytes accessed | tf_op | source)
XLA Modules:
  0.0 107.8 jit_solution(13892163681773577157)
XLA Ops:
  2.1 5.0 %collective-permute-start = (bf16[3,1536]{1,0:T(4,128)(2,1)S(1)}, bf16[3,1536]{1,0:T(4,128)(2,1)S(1)}, u32[]{:S(2)}, u32[]{:S(2)}) collective-permute-start(bf16[3,1536]{1,0:T(4,128)(2,1)S(1)} %pad_maximum_fusion.3), channel_id=1, source_target_pairs={{0,4},{4,8},{8,12},{1,5},{5,9},{9,13},{2,6},{6,10},{10,14},{3,7},{... | collective-permute-start | bytes 27656 | tf_op jit(solution)/shard_map/ppermute | solution.py:20
  10.5 3.5 %collective-permute-start.3 = (f32[20]{0:T(128)S(1)}, f32[20]{0:T(128)S(1)}, u32[]{:S(2)}, u32[]{:S(2)}) collective-permute-start(f32[20]{0:T(128)S(1)} %get-tuple-element.57), channel_id=1, source_target_pairs={{0,4},{4,8},{8,12},{1,5},{5,9},{9,13},{2,6},{6,10},{10,14},{3,7},{... | collective-permute-start | bytes 248 | tf_op jit(solution)/shard_map/ppermute | solution.py:20
  14.7 1.4 %slice_convert_fusion.4 = (f32[1,256]{1,0:T(1,128)}, f32[1,256]{1,0:T(1,128)}, f32[1,256]{1,0:T(1,128)}, f32[1,256]{1,0:T(1,128)}) fusion(bf16[4,256]{1,0:T(4,128)(2,1)} %param.20), kind=kLoop, calls=%fused_computation.168 | loop fusion | flops 1024 | bytes 6144 | tf_op jit(solution)/shard_map/mul | solution.py:33
  16.1 0.9 convert_reduce_fusion.3
  17.0 1.5 %fusion.107 = (f32[20,256]{1,0:T(8,128)}, f32[256,20]{0,1:T(8,128)}, f32[256,20]{0,1:T(8,128)}, f32[20,256]{1,0:T(8,128)}, f32[20,256]{1,0:T(8,128)}, /*index=5*/f32[20,256]{1,0:T(8,128)}) fusion(f32[20,512]{1,0:T(8,128)} %param.16, f32[20,256]{1,0:T(8,128)S(1)} %bitcast.120, f32[20]{0:T(128)S(1)} %get-tuple-element.63, f32[20,256]{1,0:T(8,128)S(1)} %bitcast.123, ...), kind=kLoop, calls=%fused_computation.182 | loop fusion | flops 20480 | bytes 204960 | tf_op jit(solution)/shard_map/slice | solution.py:143
  18.5 1.2 %compare_and_fusion.1 = (pred[128]{0:T(512)(128)(4,1)}, s32[128]{0:T(128)S(1)}) fusion(s32[128]{0:T(128)} %param.22, s32[]{:T(128)S(6)} %mul.364), kind=kLoop, calls=%fused_computation.157 | loop fusion | flops 896 | bytes 1156 | tf_op jit(solution)/shard_map/jit(_take)/and | solution.py:180
  22.0 1.6 %concatenate.29 = bf16[40,1284]{1,0:T(8,128)(2,1)} concatenate(bf16[40,1280]{1,0:T(8,128)(2,1)} %param.23, bf16[40,2]{1,0:T(8,128)(2,1)S(1)} %copy.71, bf16[40,2]{1,0:T(8,128)(2,1)S(1)} %copy.72), dimensions={1} | concatenate | bytes 205440 | tf_op jit(solution)/shard_map/concatenate | solution.py:123
  24.8 4.0 %divide_convert_fusion = bf16[512,1280]{1,0:T(8,128)(2,1)S(1)} fusion(bf16[512,1280]{1,0:T(8,128)(2,1)} %param.13, bf16[3,1280]{1,0:T(4,128)(2,1)S(1)} %slice.202, f32[1280]{0:T(1024)S(1)} %get-tuple-element.22, f32[1280]{0:T(1024)S(1)} %get-tuple-element.23, f32[1280]{0:T(1024)S(1)} %get-tuple-element.21, f32[1280]{0:T(1024)S(1)} %get-tuple-element.20), kind=kLoop, calls=%fused_computation.29 | loop fusion | flops 15728640 | bytes 2649600 | tf_op jit(solution)/shard_map/convert_element_type | solution.py:36
  29.5 1.9 %divide_convert_fusion.1 = bf16[512,256]{1,0:T(8,128)(2,1)S(1)} fusion(bf16[512,256]{1,0:T(8,128)(2,1)} %param.15, bf16[3,256]{1,0:T(4,128)(2,1)S(1)} %slice-done, f32[256]{0:T(256)} %bitcast.133, f32[256]{0:T(256)} %bitcast.134, f32[256]{0:T(256)} %bitcast.132, f32[256]{0:T(256)} %bitcast.131), kind=kLoop, calls=%fused_computation.72 | loop fusion | flops 3145728 | bytes 529920 | tf_op jit(solution)/shard_map/convert_element_type | solution.py:36
  31.6 1.1 %convolution_add_fusion.3 = f32[20,64,128]{2,1,0:T(8,128)S(1)} fusion(bf16[256,20,64]{0,2,1:T(8,128)(2,1)S(1)} %bitcast.112, f32[256,20]{0,1:T(8,128)} %get-tuple-element.41, f32[20]{0:T(128)} %get-tuple-element.55, bf16[512,256]{1,0:T(8,128)(2,1)S(1)} %divide_convert_fusion.1), kind=kOutput, calls=%fused_computation.55 | convolution fusion | flops 85032960 | bytes 1396816 | tf_op jit(solution)/shard_map/jhp,js->hps/dot_general | solution.py:52
  32.7 2.0 %fusion.110 = (bf16[20,64,128]{2,1,0:T(8,128)(2,1)}, f32[20,64,128]{2,1,0:T(8,128)}) fusion(bf16[512,256]{1,0:T(8,128)(2,1)S(1)} %divide_convert_fusion.1, bf16[256,20,64]{0,2,1:T(8,128)(2,1)S(1)} %bitcast.114, f32[256,20]{0,1:T(8,128)} %get-tuple-element.42, f32[20,64,128]{2,1,0:T(8,128)S(1)} %convolution_add_fusion.3, f32[20]{0:T(128)} %get-tuple-element.58), kind=kOutput, calls=%fused_computation.185 | convolution fusion | flops 85360640 | bytes 2379856 | tf_op jit(solution)/shard_map/jhp,js->hps/dot_general | solution.py:52
  34.7 4.2 %collective-permute-start.1 = (bf16[20,64,128]{2,1,0:T(8,128)(2,1)}, bf16[20,64,128]{2,1,0:T(8,128)(2,1)}, u32[]{:S(2)}, u32[]{:S(2)}) collective-permute-start(bf16[20,64,128]{2,1,0:T(8,128)(2,1)} %get-tuple-element.59), channel_id=1, source_target_pairs={{0,4},{4,8},{8,12},{1,5},{5,9},{9,13},{2,6},{6,10},{10,14},{3,7},{... | collective-permute-start | bytes 983048 | tf_op jit(solution)/shard_map/ppermute | solution.py:20
  38.9 2.9 %fusion.5 = f32[20,64,256]{2,1,0:T(8,128)} fusion(bf16[256,20,64]{0,2,1:T(8,128)(2,1)S(1)} %bitcast.115, f32[20,256]{1,0:T(8,128)S(1)} %copy-done.14, f32[256,256]{1,0:T(8,128)S(1)} %fusion.76, f32[20,256]{1,0:T(8,128)S(1)} %bitcast.124, pred[256,256]{1,0:T(8,128)(4,1)S(1)} %copy-done.13), kind=kOutput, calls=%fused_computation.8 | convolution fusion | flops 175636480 | bytes 2334720 | tf_op jit(solution)/shard_map/hij,jhp->hpi/dot_general | solution.py:49
  41.9 1.5 %copy.73 = bf16[512,1280]{0,1:T(8,128)(2,1)} copy(bf16[512,1280]{1,0:T(8,128)(2,1)S(1)} %divide_convert_fusion) | data formatting | bytes 2621440 | tf_op jit(solution)/shard_map/layout_constraint | solution.py:127
  43.6 1.4 %collective-permute-done.1 = bf16[20,64,128]{2,1,0:T(8,128)(2,1)} collective-permute-done((bf16[20,64,128]{2,1,0:T(8,128)(2,1)}, bf16[20,64,128]{2,1,0:T(8,128)(2,1)}, u32[]{:S(2)}, u32[]{:S(2)}) %collective-permute-start.1) | collective-permute-done | bytes 327712 | tf_op jit(solution)/shard_map/ppermute | solution.py:20
  44.9 1.9 %fusion.51 = bf16[20,64,128]{2,1,0:T(8,128)(2,1)} fusion(f32[20,64,128]{2,1,0:T(8,128)S(1)} %copy-done.3, bf16[20,64,128]{2,1,0:T(8,128)(2,1)} %collective-permute-done.1, f32[20]{0:T(128)S(1)} %copy-done.19), kind=kLoop, calls=%fused_computation.62 | loop fusion | flops 655360 | bytes 1310800 | tf_op jit(solution)/shard_map/convert_element_type | solution.py:66
  46.8 4.1 %collective-permute-start.2 = (bf16[20,64,128]{2,1,0:T(8,128)(2,1)}, bf16[20,64,128]{2,1,0:T(8,128)(2,1)S(1)}, u32[]{:S(2)}, u32[]{:S(2)}) collective-permute-start(bf16[20,64,128]{2,1,0:T(8,128)(2,1)} %fusion.51), channel_id=1, source_target_pairs={{0,8},{4,12},{1,9},{5,13},{2,10},{6,14},{3,11},{7,15},{16,24},{20,... | collective-permute-start | bytes 983048 | tf_op jit(solution)/shard_map/ppermute | solution.py:20
  50.9 3.8 %fusion.4 = f32[20,64,256]{2,1,0:T(8,128)} fusion(bf16[256,20,64]{0,2,1:T(8,128)(2,1)S(1)} %bitcast.113, f32[20,256]{1,0:T(8,128)} %get-tuple-element.40, f32[256,256]{1,0:T(8,128)S(1)} %fusion.80, f32[20,256]{1,0:T(8,128)} %bitcast.121, pred[256,256]{1,0:T(8,128)(4,1)} %iota_compare_fusion), kind=kOutput, calls=%fused_computation.7 | convolution fusion | flops 175636480 | bytes 2334720 | tf_op jit(solution)/shard_map/hij,jhp->hpi/dot_general | solution.py:49
  54.7 1.5 %copy.74 = bf16[512,1280]{0,1:T(8,128)(2,1)} copy(bf16[512,1280]{1,0:T(8,128)(2,1)S(1)} %copy-done.4) | data formatting | bytes 2621440 | tf_op jit(solution)/shard_map/optimization_barrier | solution.py:69
  57.1 1.1 %convert_add_fusion = f32[20,64,128]{2,1,0:T(8,128)S(1)} fusion(bf16[20,64,128]{2,1,0:T(8,128)(2,1)} %collective-permute-done.1, bf16[20,64,128]{2,1,0:T(8,128)(2,1)S(1)} %collective-permute-done.2, f32[20]{0:T(128)S(1)} %copy-done.21), kind=kLoop, calls=%fused_computation.59 | loop fusion | flops 655360 | bytes 1310800 | tf_op jit(solution)/shard_map/add | solution.py:57
  59.9 0.9 copy-done.6
  61.7 1.5 %multiply_reduce_fusion = (f32[512]{0:T(512)S(1)}, f32[1280,512]{1,0:T(8,128)S(1)}) fusion(bf16[512,1280]{0,1:T(8,128)(2,1)S(1)} %copy-done.2, bf16[512,1280]{0,1:T(8,128)(2,1)S(1)} %copy-done.1, f32[1280]{0:T(1024)S(1)} %mul.351, f32[1280,256]{1,0:T(8,128)S(1)} %bitcast.110, f32[1280,256]{1,0:T(8,128)S(1)} %bitcast.111), kind=kLoop, calls=%fused_computation.18 | loop fusion | flops 7208448 | bytes 7871488 | tf_op jit(solution)/shard_map/reduce_sum | solution.py:173
  63.3 1.1 %collective-permute-done.4 = f32[512]{0:T(512)S(1)} collective-permute-done((f32[512]{0:T(512)S(1)}, f32[512]{0:T(512)S(1)}, u32[]{:S(2)}, u32[]{:S(2)}) %collective-permute-start.4) | collective-permute-done | bytes 2080 | tf_op jit(solution)/shard_map/ppermute | solution.py:84
  64.5 1.5 %collective-permute-start.5 = (f32[512]{0:T(512)S(1)}, f32[512]{0:T(512)S(1)}, u32[]{:S(2)}, u32[]{:S(2)}) collective-permute-start(f32[512]{0:T(512)S(1)} %add.183), channel_id=1, source_target_pairs={{0,2},{1,3},{2,0},{3,1},{4,6},{5,7},{6,4},{7,5},{8,10},{9,11},{10,... | collective-permute-start | bytes 6152 | tf_op jit(solution)/shard_map/ppermute | solution.py:84
  66.8 11.5 %all-to-all-start = ((bf16[4,40,1284]{2,1,0:T(8,128)(2,1)}), bf16[4,40,1284]{2,1,0:T(8,128)(2,1)S(1)}, u32[]{:S(2)}, u32[]{:S(2)}) async-start(bf16[4,40,1284]{2,1,0:T(8,128)(2,1)} %broadcast_in_dim.136), calls=%async_computation | async-start | bytes 901120 | tf_op jit(solution)/shard_map/all_to_all | solution.py:152
  78.3 1.4 %fusion.36 = bf16[512,1280]{0,1:T(8,128)(2,1)} fusion(f32[1280,512]{1,0:T(8,128)S(1)} %get-tuple-element.31, f32[1280]{0:T(1024)S(1)} %copy-done.17, f32[512]{0:T(512)S(1)} %add_rsqrt_fusion), kind=kLoop, calls=%fused_computation.46 | loop fusion | flops 1966080 | bytes 3939328 | tf_op jit(solution)/shard_map/transpose | solution.py:178
  79.7 1.6 %copy.81 = bf16[512,1280]{1,0:T(8,128)(2,1)S(1)} copy(bf16[512,1280]{0,1:T(8,128)(2,1)} %fusion.36) | data formatting | bytes 2621440
  82.3 8.9 %all-to-all-done = bf16[4,40,1284]{2,1,0:T(8,128)(2,1)S(1)} async-done(((bf16[4,40,1284]{2,1,0:T(8,128)(2,1)}), bf16[4,40,1284]{2,1,0:T(8,128)(2,1)S(1)}, u32[]{:S(2)}, u32[]{:S(2)}) %all-to-all-start) | async-done | bytes 410912 | tf_op jit(solution)/shard_map/all_to_all | solution.py:152
  91.7 1.2 %fusion.111 = (bf16[8,160]{1,0:T(8,128)(2,1)S(1)}, f32[8,160,128]{2,1,0:T(8,128)S(1)}) fusion(bf16[160,1284]{1,0:T(8,128)(2,1)S(1)} %bitcast.118, pred[8,1280]{1,0:T(8,128)(4,1)S(1)} %copy-done.16, bf16[128,1280]{1,0:T(8,128)(2,1)S(1)} %broadcast_select_fusion, pred[160,128]{1,0:T(8,128)(4,1)S(1)} %compare_and_fusion), kind=kOutput, calls=%fused_computation.186 | convolution fusion | flops 421231360 | bytes 1425920 | tf_op jit(solution)/shard_map/pc,asc->aps/dot_general | solution.py:192
  94.8 1.5 %collective-permute-start.8 = (bf16[40,1304]{1,0:T(8,128)(2,1)S(1)}, bf16[40,1304]{1,0:T(8,128)(2,1)S(1)}, u32[]{:S(2)}, u32[]{:S(2)}) collective-permute-start(bf16[40,1304]{1,0:T(8,128)(2,1)S(1)} %get-tuple-element.37), channel_id=1, source_target_pairs={{0,12},{4,0},{8,4},{12,8},{1,13},{5,1},{9,5},{13,9},{2,14},{6,2},{... | collective-permute-start | bytes 312968 | tf_op jit(solution)/shard_map/ppermute | solution.py:219
  97.0 3.4 %collective-permute-done.8 = bf16[40,1304]{1,0:T(8,128)(2,1)S(1)} collective-permute-done((bf16[40,1304]{1,0:T(8,128)(2,1)S(1)}, bf16[40,1304]{1,0:T(8,128)(2,1)S(1)}, u32[]{:S(2)}, u32[]{:S(2)}) %collective-permute-start.8) | collective-permute-done | bytes 104352 | tf_op jit(solution)/shard_map/ppermute | solution.py:219
  100.4 5.1 %collective-permute-done.7 = bf16[40,1304]{1,0:T(8,128)(2,1)S(1)} collective-permute-done((bf16[40,1304]{1,0:T(8,128)(2,1)S(1)}, bf16[40,1304]{1,0:T(8,128)(2,1)S(1)}, u32[]{:S(2)}, u32[]{:S(2)}) %collective-permute-start.7) | collective-permute-done | bytes 104352 | tf_op jit(solution)/shard_map/ppermute | solution.py:219
  (127 shorter events, 20.5 us)
Async XLA Ops:
  2.1 22.2 %collective-permute-start = (bf16[3,1536]{1,0:T(4,128)(2,1)S(1)}, bf16[3,1536]{1,0:T(4,128)(2,1)S(1)}, u32[]{:S(2)}, u32[]{:S(2)}) collective-permute-start(bf16[3,1536]{1,0:T(4,128)(2,1)S(1)} %pad_maximum_fusion.3), channel_id=1, source_target_pairs={{0,4},{4,8},{8,12},{1,5},{5,9},{9,13},{2,6},{6,10},{10,14},{3,7},{... | collective-permute-start | bytes 27656 | tf_op jit(solution)/shard_map/ppermute | solution.py:20
  8.8 15.5 %copy-start.8 = (f32[3,8,2,128]{3,1,2,0:T(8,128)}, f32[3,8,2,128]{3,1,2,0:T(8,128)S(1)}, u32[]{:S(2)}) copy-start(f32[3,8,2,128]{3,1,2,0:T(8,128)S(1)} %copy.84) | copy-start | bytes 73732
  9.7 7.3 %copy-start.9 = (f32[3,8,2,128]{3,1,2,0:T(8,128)}, f32[3,8,2,128]{3,1,2,0:T(8,128)S(1)}, u32[]{:S(2)}) copy-start(f32[3,8,2,128]{3,1,2,0:T(8,128)S(1)} %copy.85) | copy-start | bytes 73732
  10.5 13.1 %collective-permute-start.3 = (f32[20]{0:T(128)S(1)}, f32[20]{0:T(128)S(1)}, u32[]{:S(2)}, u32[]{:S(2)}) collective-permute-start(f32[20]{0:T(128)S(1)} %get-tuple-element.57), channel_id=1, source_target_pairs={{0,4},{4,8},{8,12},{1,5},{5,9},{9,13},{2,6},{6,10},{10,14},{3,7},{... | collective-permute-start | bytes 248 | tf_op jit(solution)/shard_map/ppermute | solution.py:20
  28.9 0.7 slice-start
  29.4 9.5 %copy-start.10 = (f32[3,8,2,128]{3,1,2,0:T(8,128)S(1)}, f32[3,8,2,128]{3,1,2,0:T(8,128)}, u32[]{:S(2)}) copy-start(f32[3,8,2,128]{3,1,2,0:T(8,128)} %copy-done.9) | copy-start | bytes 73732
  29.5 9.5 %copy-start.13 = (pred[256,256]{1,0:T(8,128)(4,1)S(1)}, pred[256,256]{1,0:T(8,128)(4,1)}, u32[]{:S(2)}) copy-start(pred[256,256]{1,0:T(8,128)(4,1)} %iota_compare_fusion) | copy-start | bytes 196612
  29.5 9.5 %copy-start.14 = (f32[20,256]{1,0:T(8,128)S(1)}, f32[20,256]{1,0:T(8,128)}, u32[]{:S(2)}) copy-start(f32[20,256]{1,0:T(8,128)} %get-tuple-element.43) | copy-start | bytes 61444
  34.7 10.2 %collective-permute-start.1 = (bf16[20,64,128]{2,1,0:T(8,128)(2,1)}, bf16[20,64,128]{2,1,0:T(8,128)(2,1)}, u32[]{:S(2)}, u32[]{:S(2)}) collective-permute-start(bf16[20,64,128]{2,1,0:T(8,128)(2,1)} %get-tuple-element.59), channel_id=1, source_target_pairs={{0,4},{4,8},{8,12},{1,5},{5,9},{9,13},{2,6},{6,10},{10,14},{3,7},{... | collective-permute-start | bytes 983048 | tf_op jit(solution)/shard_map/ppermute | solution.py:20
  41.9 3.0 %copy-start.3 = (f32[20,64,128]{2,1,0:T(8,128)S(1)}, f32[20,64,128]{2,1,0:T(8,128)}, u32[]{:S(2)}) copy-start(f32[20,64,128]{2,1,0:T(8,128)} %get-tuple-element.60) | copy-start | bytes 1966084
  41.9 3.0 %copy-start.19 = (f32[20]{0:T(128)S(1)}, f32[20]{0:T(128)}, u32[]{:S(2)}) copy-start(f32[20]{0:T(128)} %get-tuple-element.56) | copy-start | bytes 244
  46.8 10.3 %collective-permute-start.2 = (bf16[20,64,128]{2,1,0:T(8,128)(2,1)}, bf16[20,64,128]{2,1,0:T(8,128)(2,1)S(1)}, u32[]{:S(2)}, u32[]{:S(2)}) collective-permute-start(bf16[20,64,128]{2,1,0:T(8,128)(2,1)} %fusion.51), channel_id=1, source_target_pairs={{0,8},{4,12},{1,9},{5,13},{2,10},{6,14},{3,11},{7,15},{16,24},{20,... | collective-permute-start | bytes 983048 | tf_op jit(solution)/shard_map/ppermute | solution.py:20
  50.9 3.8 %copy-start.4 = (bf16[512,1280]{1,0:T(8,128)(2,1)S(1)}, bf16[512,1280]{1,0:T(8,128)(2,1)}, u32[]{:S(2)}) copy-start(bf16[512,1280]{1,0:T(8,128)(2,1)} %param.14) | copy-start | bytes 3932164
  54.7 2.4 %copy-start.21 = (f32[20]{0:T(128)S(1)}, f32[20]{0:T(128)}, u32[]{:S(2)}) copy-start(f32[20]{0:T(128)} %exp.79) | copy-start | bytes 244
  54.7 3.8 %copy-start.18 = (f32[20]{0:T(128)S(1)}, f32[20]{0:T(128)}, u32[]{:S(2)}) copy-start(f32[20]{0:T(128)} %get-tuple-element.54) | copy-start | bytes 244
  58.2 1.3 %copy-start.5 = (f32[20,64,256]{2,1,0:T(8,128)S(1)}, f32[20,64,256]{2,1,0:T(8,128)}, u32[]{:S(2)}) copy-start(f32[20,64,256]{2,1,0:T(8,128)} %fusion.5) | copy-start | bytes 3932164
  58.2 1.3 %copy-start.12 = (f32[20,256]{1,0:T(8,128)S(1)}, f32[20,256]{1,0:T(8,128)}, u32[]{:S(2)}) copy-start(f32[20,256]{1,0:T(8,128)} %get-tuple-element.46) | copy-start | bytes 61444
  59.5 1.3 %copy-start.6 = (f32[20,64,256]{2,1,0:T(8,128)S(1)}, f32[20,64,256]{2,1,0:T(8,128)}, u32[]{:S(2)}) copy-start(f32[20,64,256]{2,1,0:T(8,128)} %fusion.4) | copy-start | bytes 3932164
  59.5 1.3 %copy-start.11 = (f32[20,256]{1,0:T(8,128)S(1)}, f32[20,256]{1,0:T(8,128)}, u32[]{:S(2)}) copy-start(f32[20,256]{1,0:T(8,128)} %get-tuple-element.47) | copy-start | bytes 61444
  59.9 1.4 %copy-start.1 = (bf16[512,1280]{0,1:T(8,128)(2,1)S(1)}, bf16[512,1280]{0,1:T(8,128)(2,1)}, u32[]{:S(2)}) copy-start(bf16[512,1280]{0,1:T(8,128)(2,1)} %copy.73) | copy-start | bytes 3932164
  59.9 1.8 %copy-start.2 = (bf16[512,1280]{0,1:T(8,128)(2,1)S(1)}, bf16[512,1280]{0,1:T(8,128)(2,1)}, u32[]{:S(2)}) copy-start(bf16[512,1280]{0,1:T(8,128)(2,1)} %copy.74) | copy-start | bytes 3932164
  61.7 4.2 %copy-start.7 = (bf16[40,1284]{1,0:T(8,128)(2,1)S(1)}, bf16[40,1284]{1,0:T(8,128)(2,1)}, u32[]{:S(2)}) copy-start(bf16[40,1284]{1,0:T(8,128)(2,1)} %concatenate.29) | copy-start | bytes 308164
  61.7 16.6 %copy-start.17 = (f32[1280]{0:T(1024)S(1)}, f32[1280]{0:T(1024)}, u32[]{:S(2)}) copy-start(f32[1280]{0:T(1024)} %param.21) | copy-start | bytes 15364
  63.2 1.2 %collective-permute-start.4 = (f32[512]{0:T(512)S(1)}, f32[512]{0:T(512)S(1)}, u32[]{:S(2)}, u32[]{:S(2)}) collective-permute-start(f32[512]{0:T(512)S(1)} %get-tuple-element.30), channel_id=1, source_target_pairs={{0,1},{1,0},{2,3},{3,2},{4,5},{5,4},{6,7},{7,6},{8,9},{9,8},{10,11... | collective-permute-start | bytes 6152 | tf_op jit(solution)/shard_map/ppermute | solution.py:84
  64.5 13.8 %collective-permute-start.5 = (f32[512]{0:T(512)S(1)}, f32[512]{0:T(512)S(1)}, u32[]{:S(2)}, u32[]{:S(2)}) collective-permute-start(f32[512]{0:T(512)S(1)} %add.183), channel_id=1, source_target_pairs={{0,2},{1,3},{2,0},{3,1},{4,6},{5,7},{6,4},{7,5},{8,10},{9,11},{10,... | collective-permute-start | bytes 6152 | tf_op jit(solution)/shard_map/ppermute | solution.py:84
  66.8 24.5 %all-to-all-start = ((bf16[4,40,1284]{2,1,0:T(8,128)(2,1)}), bf16[4,40,1284]{2,1,0:T(8,128)(2,1)S(1)}, u32[]{:S(2)}, u32[]{:S(2)}) async-start(bf16[4,40,1284]{2,1,0:T(8,128)(2,1)} %broadcast_in_dim.136), calls=%async_computation | async-start | bytes 901120 | tf_op jit(solution)/shard_map/all_to_all | solution.py:152
  79.7 2.5 %copy-start.20 = (pred[128]{0:T(512)(128)(4,1)S(1)}, pred[128]{0:T(512)(128)(4,1)}, u32[]{:S(2)}) copy-start(pred[128]{0:T(512)(128)(4,1)} %get-tuple-element.28) | copy-start | bytes 388
  81.3 11.6 %copy-start = (bf16[512,1280]{1,0:T(8,128)(2,1)}, bf16[512,1280]{1,0:T(8,128)(2,1)S(1)}, u32[]{:S(2)}) copy-start(bf16[512,1280]{1,0:T(8,128)(2,1)S(1)} %copy.81) | copy-start | bytes 3932164
  81.3 10.4 %copy-start.16 = (pred[8,1280]{1,0:T(8,128)(4,1)S(1)}, pred[8,1280]{1,0:T(8,128)(4,1)}, u32[]{:S(2)}) copy-start(pred[8,1280]{1,0:T(8,128)(4,1)} %iota_compare_fusion.1) | copy-start | bytes 30724
  94.8 5.6 %collective-permute-start.8 = (bf16[40,1304]{1,0:T(8,128)(2,1)S(1)}, bf16[40,1304]{1,0:T(8,128)(2,1)S(1)}, u32[]{:S(2)}, u32[]{:S(2)}) collective-permute-start(bf16[40,1304]{1,0:T(8,128)(2,1)S(1)} %get-tuple-element.37), channel_id=1, source_target_pairs={{0,12},{4,0},{8,4},{12,8},{1,13},{5,1},{9,5},{13,9},{2,14},{6,2},{... | collective-permute-start | bytes 312968 | tf_op jit(solution)/shard_map/ppermute | solution.py:219
  96.3 9.1 %collective-permute-start.7 = (bf16[40,1304]{1,0:T(8,128)(2,1)S(1)}, bf16[40,1304]{1,0:T(8,128)(2,1)S(1)}, u32[]{:S(2)}, u32[]{:S(2)}) collective-permute-start(bf16[40,1304]{1,0:T(8,128)(2,1)S(1)} %get-tuple-element.38), channel_id=1, source_target_pairs={{0,8},{4,12},{8,0},{12,4},{1,9},{5,13},{9,1},{13,5},{2,10},{6,14},... | collective-permute-start | bytes 312968 | tf_op jit(solution)/shard_map/ppermute | solution.py:219
  96.3 9.1 %collective-permute-start.6 = (bf16[40,1304]{1,0:T(8,128)(2,1)S(1)}, bf16[40,1304]{1,0:T(8,128)(2,1)S(1)}, u32[]{:S(2)}, u32[]{:S(2)}) collective-permute-start(bf16[40,1304]{1,0:T(8,128)(2,1)S(1)} %get-tuple-element.39), channel_id=1, source_target_pairs={{0,4},{4,8},{8,12},{12,0},{1,5},{5,9},{9,13},{13,1},{2,6},{6,10},{... | collective-permute-start | bytes 312968 | tf_op jit(solution)/shard_map/ppermute | solution.py:219
  (1 other events, 0.6 us)
